TPU v7x, 128 devices: a whole 4x4x4 slice. The times are simulated.
128 devices in a mesh: dom: 16 (over y, z), face: 8 (over x, core).
Axes of the slice: x: 4, y: 4, z: 4, core: 2. Of those that a mesh axis runs over, the one named last changes fastest.
Arguments:
- coefficients: float32 [8192, 4096], P(('dom', 'face')), may hold values from -6 to 6
- diffusion: float32 [8192, 3], P(('dom', 'face')), may hold values from 0.05 to 0.5
- velocity: float32 [8192, 3], P(('dom', 'face')), may hold values from -1 to 1
- orders: int32 [8192], P(('dom', 'face')), may hold values from 4 to 15, as said below
- target: int32 [8192], P(('dom', 'face')), may hold values from 0 to 8191, as said below
- local_faces: int32 [128, 4, 64], P(('dom', 'face')), may hold values from 0 to 63, each once within a row
- partner_faces: int32 [128, 2, 64], P(('dom', 'face')), may hold values from -1 to 63, as said below
- partner_turns: int32 [128, 2, 64], P(('dom', 'face')), may hold values from 0 to 7
Outputs:
- advanced: float32 [8192, 4096], P(('dom', 'face'))
Inputs may be any that keep to these rules, and one draw needn't show every extreme that they name: `target`: a permutation of the new slots; slot s lies in block s // 64; an element of block b has its new slot in block b - 1, b, b + 1 or b + 128 // 2 (taken mod 128), and exactly 4 elements of each block move to each of the blocks b - 1, b + 1 and b + 64. `orders`: an element whose new slot s has s mod 64 < 32 has order below 8; every other element has order 16 // 2 or more. Entries are -1 exactly for face 0 in the blocks of the first partition and for face 1 in the blocks of the last; every other row partner_faces[b, r, :] is a permutation of 0 to 63.
All inputs are finite; a program needn't handle non-finite values.
Results may differ from a plain program's by a relative error of at most 0.0001.
Values sent between devices are 32-bit elements; how exact they have to be, the bound alone decides.
No kernel may reach another device: no remote copies, remote signals or barrier semaphores. Data moves between devices by JAX's collectives and lax.ppermute only.
A program may use at most 128 MiB of HBM per device.

v0:
```python
import functools
import jax
import jax.numpy as jnp
import numpy as np
from jax import lax
from jax.experimental import pallas as pl
from jax.experimental.pallas import tpu as pltpu
from jax.sharding import PartitionSpec as P

P_SIZE = 16
PLANE = P_SIZE * P_SIZE
TIME_STEP = 0.25


def mode_tables():
    ladder = np.arange(P_SIZE)
    spacing = ladder[None, :] - ladder[:, None]
    derivative = np.where(
        (spacing > 0) & (spacing % 2 == 1), (2.0 * ladder[:, None] + 1.0) / P_SIZE, 0.0
    )
    second = derivative @ derivative / P_SIZE
    side_signs = np.stack([(-1.0) ** ladder, np.ones(P_SIZE)])
    weights = (2.0 * ladder + 1.0) / (2.0 * P_SIZE)
    return (derivative, second, side_signs, weights)


def side_table(values_pair):
    identity = np.eye(P_SIZE)
    return np.concatenate(
        [
            np.kron(values_pair[0][:, None], identity),
            np.kron(values_pair[1][:, None], identity),
            np.kron(identity, values_pair[0][:, None]),
            np.kron(identity, values_pair[1][:, None]),
        ],
        axis=1,
    )


def kernel_tables():
    derivative, second, side_signs, weights = mode_tables()
    derivative = derivative.astype(np.float32).astype(np.float64)
    second = second.astype(np.float32).astype(np.float64)
    identity = np.eye(P_SIZE)
    traces = side_table(side_signs)
    swapped = traces[:, [16 * g + j for g in (1, 0, 3, 2) for j in range(P_SIZE)]]
    pad = np.zeros((PLANE, 64))
    spread = np.concatenate(
        [
            np.kron(identity, second.T),
            np.kron(second.T, identity),
            np.kron(identity, derivative.T),
            np.kron(derivative.T, identity),
            traces, pad, swapped, pad,
        ],
        axis=1,
    ).astype(np.float32)
    spread_hi = spread.astype(jnp.bfloat16)
    spread_lo = (spread[:, : 2 * PLANE] - spread_hi[:, : 2 * PLANE].astype(np.float32)).astype(jnp.bfloat16)
    lift_signs = side_signs * weights[None, :]
    lift = np.concatenate([side_table(lift_signs).T, np.zeros((64, PLANE))], axis=0)
    lanes = np.arange(PLANE)
    flip = np.zeros((PLANE, PLANE))
    flip[lanes, (lanes % P_SIZE) * P_SIZE + lanes // P_SIZE] = 1.0
    return (
        jnp.asarray(spread_hi),
        jnp.asarray(spread_lo),
        jnp.asarray(lift, jnp.bfloat16),
        jnp.asarray(flip, jnp.bfloat16),
    )


def top_modes():
    ladder = np.arange(P_SIZE)
    first_idx, second_idx, third_idx = np.meshgrid(ladder, ladder, ladder, indexing="ij")
    return np.maximum(np.maximum(first_idx, second_idx), third_idx).reshape(1, -1).astype(np.int32)


def split_two(x):
    hi = x.astype(jnp.bfloat16)
    lo = (x - hi.astype(jnp.float32)).astype(jnp.bfloat16)
    return hi, lo


def mxu(a, b):
    return jnp.dot(a, b, preferred_element_type=jnp.float32)


def exact_pick(onehot, x):
    hi = x.astype(jnp.bfloat16)
    rest = x - hi.astype(jnp.float32)
    mid = rest.astype(jnp.bfloat16)
    lo = (rest - mid.astype(jnp.float32)).astype(jnp.bfloat16)
    return mxu(onehot, hi) + mxu(onehot, mid) + mxu(onehot, lo)


def end_traces(slabs):
    total = slabs[0] + slabs[1]
    even = slabs[0] - slabs[1]
    for a in range(2, P_SIZE):
        total = total + slabs[a]
        even = even + slabs[a] if a % 2 == 0 else even - slabs[a]
    return even, total


def turn(rows, codes, flip):
    lane = lax.broadcasted_iota(jnp.int32, (1, PLANE), 1)
    swapped = exact_pick_right(rows, flip)
    rows = jnp.where(codes % 2 == 1, swapped, rows)
    row_odd = (lane // P_SIZE) % 2 == 1
    col_odd = lane % 2 == 1
    negate = ((codes // 2) % 2 == 1) & row_odd
    negate = negate != (((codes // 4) % 2 == 1) & col_odd)
    return jnp.where(negate, -rows, rows)


def exact_pick_right(x, onehot):
    hi = x.astype(jnp.bfloat16)
    rest = x - hi.astype(jnp.float32)
    mid = rest.astype(jnp.bfloat16)
    lo = (rest - mid.astype(jnp.float32)).astype(jnp.bfloat16)
    return mxu(hi, onehot) + mxu(mid, onehot) + mxu(lo, onehot)


def section_body(
    v_ref, base_ref, top_ref, order_ref, weight_ref, lower_ref, upper_ref, pick_ref, turn_ref,
    spread_hi_ref, spread_lo_ref, lift_ref, flip_ref, out_ref, ends_ref, *, scale
):
    count = v_ref.shape[0]
    derivative, second, side_signs, weights = mode_tables()
    second = second.astype(np.float32)
    derivative = derivative.astype(np.float32)
    lift_signs = (side_signs * weights[None, :]).astype(np.float32)
    slabs = [v_ref[:, a * PLANE : (a + 1) * PLANE] for a in range(P_SIZE)]
    weight = weight_ref[...]
    diff0 = jnp.broadcast_to(weight[:, 0:1], (count, PLANE))
    vel0 = jnp.broadcast_to(weight[:, 3:4], (count, PLANE))
    first = []
    for k in range(P_SIZE):
        acc_s = None
        acc_d = None
        for n in range(k + 1, P_SIZE):
            if second[k, n] != 0.0:
                term = float(second[k, n]) * slabs[n]
                acc_s = term if acc_s is None else acc_s + term
            if derivative[k, n] != 0.0:
                term = float(derivative[k, n]) * slabs[n]
                acc_d = term if acc_d is None else acc_d + term
        part = jnp.zeros((count, PLANE), jnp.float32)
        if acc_s is not None:
            part = part + diff0 * acc_s
        if acc_d is not None:
            part = part - vel0 * acc_d
        first.append(part)
    stacked = jnp.concatenate(slabs, axis=0)
    hi, lo = split_two(stacked)
    spread_hi = spread_hi_ref[...]
    wide = mxu(hi, spread_hi) + mxu(lo, spread_hi)
    fine = mxu(hi, spread_lo_ref[...])
    weight_rows = jnp.concatenate([weight] * P_SIZE, axis=0)
    inner = (
        weight_rows[:, 2:3] * (wide[:, 0:PLANE] + fine[:, 0:PLANE])
        + weight_rows[:, 1:2] * (wide[:, PLANE : 2 * PLANE] + fine[:, PLANE : 2 * PLANE])
        - weight_rows[:, 5:6] * wide[:, 2 * PLANE : 3 * PLANE]
        - weight_rows[:, 4:5] * wide[:, 3 * PLANE : 4 * PLANE]
    )
    own = jnp.concatenate(
        [wide[a * count : (a + 1) * count, 4 * PLANE : 4 * PLANE + 128] for a in range(P_SIZE)], axis=1
    )
    other = jnp.concatenate(
        [wide[a * count : (a + 1) * count, 4 * PLANE + 128 : 4 * PLANE + 256] for a in range(P_SIZE)], axis=1
    )
    lane = lax.broadcasted_iota(jnp.int32, (1, P_SIZE * 128), 1) % 128
    across = jnp.zeros_like(own)
    for face in range(4):
        gathered = exact_pick(pick_ref[face], other)
        across = jnp.where(lane // P_SIZE == face, gathered, across)
    jump = own - across
    jump_rows = jnp.concatenate([jump[:, a * 128 : (a + 1) * 128] for a in range(P_SIZE)], axis=0)
    jhi, jlo = split_two(jump_rows)
    lift_mat = lift_ref[...]
    lifted = mxu(jhi, lift_mat) + mxu(jlo, lift_mat)
    even, total = end_traces(slabs)
    codes = turn_ref[...]
    flip = flip_ref[...]
    below = turn(exact_pick(pick_ref[4], lower_ref[...]), codes[:, 0:1], flip)
    above = turn(exact_pick(pick_ref[5], upper_ref[...]), codes[:, 1:2], flip)
    jump0 = even - below
    jump1 = total - above
    top = top_ref[...]
    order = order_ref[...]
    news = []
    for a in range(P_SIZE):
        rows = slice(a * count, (a + 1) * count)
        volume = first[a] + inner[rows]
        lift = lifted[rows] + float(lift_signs[0, a]) * jump0 + float(lift_signs[1, a]) * jump1
        live = top[:, a * PLANE : (a + 1) * PLANE] <= order
        update = jnp.where(live, volume - lift, 0.0)
        new = base_ref[:, a * PLANE : (a + 1) * PLANE] + scale * update
        out_ref[:, a * PLANE : (a + 1) * PLANE] = new
        news.append(new)
    even, total = end_traces(news)
    ends_ref[0] = even
    ends_ref[1] = total


def section(v, base, top, order, weight, lower, upper, picks, codes, tables, scale):
    count = v.shape[0]
    spec = pl.BlockSpec(memory_space=pltpu.VMEM)
    return pl.pallas_call(
        functools.partial(section_body, scale=scale),
        out_shape=(
            jax.ShapeDtypeStruct(v.shape, jnp.float32),
            jax.ShapeDtypeStruct((2, count, PLANE), jnp.float32),
        ),
        in_specs=[spec] * 13,
        out_specs=(spec, spec),
        compiler_params=pltpu.CompilerParams(vmem_limit_bytes=60 * 1024 * 1024),
    )(v, base, top, order, weight, lower, upper, picks, codes, *tables)


def prep_body(placed_ref, top_ref, order_ref, field_ref, ends_ref):
    news = []
    for a in range(P_SIZE):
        lanes = slice(a * PLANE, (a + 1) * PLANE)
        live = top_ref[:, lanes] <= order_ref[...]
        new = jnp.where(live, placed_ref[:, lanes], 0.0)
        field_ref[:, lanes] = new
        news.append(new)
    even, total = end_traces(news)
    ends_ref[0] = even
    ends_ref[1] = total


def prep(placed, top, order):
    count = placed.shape[0]
    spec = pl.BlockSpec(memory_space=pltpu.VMEM)
    return pl.pallas_call(
        prep_body,
        out_shape=(
            jax.ShapeDtypeStruct(placed.shape, jnp.float32),
            jax.ShapeDtypeStruct((2, count, PLANE), jnp.float32),
        ),
        in_specs=[spec] * 3,
        out_specs=(spec, spec),
    )(placed, top, order)


def exchange(ends):
    size = lax.axis_size("dom")
    up = [(i, i + 1) for i in range(size - 1)]
    down = [(i + 1, i) for i in range(size - 1)]
    return lax.ppermute(ends[1], "dom", up), lax.ppermute(ends[0], "dom", down)


def pick_rows(chosen, count):
    rank = jnp.cumsum(chosen.astype(jnp.int32)) - 1
    hit = chosen[None, :] & (rank[None, :] == jnp.arange(count, dtype=jnp.int32)[:, None])
    rows = jnp.arange(chosen.shape[0], dtype=jnp.int32)
    return jnp.sum(jnp.where(hit, rows[None, :], 0), axis=1)


def pick_rows_inverse(slots, count):
    hit = slots[None, :] == jnp.arange(count, dtype=jnp.int32)[:, None]
    rows = jnp.arange(slots.shape[0], dtype=jnp.int32)
    return jnp.sum(jnp.where(hit, rows[None, :], 0), axis=1)


def shards(
    coefficients, diffusion, velocity, orders, target, local_faces, partner_faces, partner_turns
):
    element_count = coefficients.shape[0]
    blocks_all = lax.axis_size(("dom", "face"))
    moving = element_count // 16
    destination = target // element_count
    new_slot = target % element_count
    here = lax.axis_index(("dom", "face"))
    side_info = jnp.concatenate(
        [
            diffusion,
            velocity,
            new_slot[:, None].astype(jnp.float32),
            orders[:, None].astype(jnp.float32),
        ],
        axis=1,
    )
    side_width = side_info.shape[1]
    got_coef = [coefficients]
    got_side = [side_info]
    got_slot = [jnp.where(destination == here, new_slot, element_count)]
    for shift in (1, blocks_all - 1, blocks_all // 2):
        picked = pick_rows(destination == (here + shift) % blocks_all, moving)
        side_row = jnp.zeros((1, P_SIZE**3), jnp.float32)
        side_row = side_row.at[0, : moving * side_width].set(side_info[picked].reshape(-1))
        parcel = jnp.concatenate([coefficients[picked], side_row], axis=0)
        pairs = [(i, (i + shift) % blocks_all) for i in range(blocks_all)]
        arrived = lax.ppermute(parcel, ("dom", "face"), pairs)
        arrived_side = arrived[moving, : moving * side_width].reshape(moving, side_width)
        got_coef.append(arrived[:moving])
        got_side.append(arrived_side)
        got_slot.append(arrived_side[:, 6].astype(jnp.int32))
    got_coef = jnp.concatenate(got_coef, axis=0)
    got_side = jnp.concatenate(got_side, axis=0)
    got_slot = jnp.concatenate(got_slot, axis=0)
    source = pick_rows_inverse(got_slot, element_count)
    placed_side = got_side[source]
    weight = jnp.concatenate(
        [placed_side[:, 0:6], jnp.zeros((element_count, 2), jnp.float32)], axis=1
    )
    order = placed_side[:, 7:8].astype(jnp.int32)
    top = jnp.asarray(top_modes())
    tables = kernel_tables()
    neighbours = jnp.concatenate([local_faces[0], partner_faces[0]], axis=0)
    picks = (
        neighbours[:, :, None] == jnp.arange(element_count, dtype=jnp.int32)[None, None, :]
    ).astype(jnp.bfloat16)
    codes = partner_turns[0].T
    field, ends = prep(got_coef[source], top, order)
    lower, upper = exchange(ends)
    half, ends = section(
        field, field, top, order, weight, lower, upper, picks, codes, tables, 0.5 * TIME_STEP
    )
    lower, upper = exchange(ends)
    advanced, _ = section(
        half, field, top, order, weight, lower, upper, picks, codes, tables, TIME_STEP
    )
    return advanced


def solution(mesh):
    in_specs = (
        P(("dom", "face"), None),
        P(("dom", "face"), None),
        P(("dom", "face"), None),
        P(("dom", "face")),
        P(("dom", "face")),
        P(("dom", "face"), None, None),
        P(("dom", "face"), None, None),
        P(("dom", "face"), None, None),
    )
    out_specs = P(("dom", "face"), None)
    return jax.shard_map(shards, mesh=mesh, in_specs=in_specs, out_specs=out_specs, check_vma=False)
```

profile of v0, /device:TPU:8, one launch (start us, length us, event | category | flops | bytes accessed | tf_op | source)
XLA Modules:
  0.0 72.6 jit_solution(15641737943329811412)
XLA Ops:
  0.0 0.6 compare_reduce_fusion
  0.6 0.7 compare_select_fusion.4
  1.3 0.7 convert_bitcast_fusion.3
  2.0 0.7 pad_maximum_fusion.2
  2.7 0.1 copy.42
  2.8 0.1 copy.45
  2.9 0.1 reduce-window.26
  3.0 0.1 add_reduce_fusion
  3.1 0.1 copy.43
  3.2 0.1 reduce-window.25
  3.3 0.1 add_reduce_fusion.1
  3.4 0.0 copy-start.5
  3.4 0.0 copy-start.6
  3.4 0.1 select_reduce_fusion.1
  3.6 0.6 gather_fusion.5
  4.1 0.6 broadcast_select_fusion.1
  4.8 0.1 reshape.278
  4.9 1.8 %gather_fusion.4 = f32[4,4096]{1,0:T(4,128)S(1)} fusion(f32[64,4096]{1,0:T(8,128)} %param.19, s32[1024]{0:T(1024)S(1)} %pad_clamp_fusion.1), kind=kCustom, calls=%fused_computation.4 | custom fusion | bytes 131088 | tf_op jit(solution)/shard_map/gather | solution.py:295
  6.8 2.4 %collective-permute-start.2 = (f32[5,4096]{1,0:T(8,128)S(1)}, f32[5,4096]{1,0:T(8,128)S(1)}, u32[]{:S(2)}, u32[]{:S(2)}) collective-permute-start(f32[5,4096]{1,0:T(8,128)S(1)} %select_maximum_fusion), channel_id=1, source_target_pairs={{0,64},{1,65},{2,66},{3,67},{4,68},{5,69},{6,70},{7,71},{8,72},{9,... | collective-permute-start | bytes 245768 | tf_op jit(solution)/shard_map/ppermute | solution.py:297
  9.1 0.6 gather_fusion.3
  9.7 0.6 gather_fusion.2
  10.3 0.7 broadcast_select_fusion.2
  11.0 0.1 reshape.276
  11.1 6.2 %collective-permute-start.1 = (f32[5,4096]{1,0:T(8,128)S(1)}, f32[5,4096]{1,0:T(8,128)S(1)}, u32[]{:S(2)}, u32[]{:S(2)}) collective-permute-start(f32[5,4096]{1,0:T(8,128)S(1)} %select_maximum_fusion.1), channel_id=1, source_target_pairs={{0,127},{1,0},{2,1},{3,2},{4,3},{5,4},{6,5},{7,6},{8,7},{9,8},{10,... | collective-permute-start | bytes 245768 | tf_op jit(solution)/shard_map/ppermute | solution.py:297
  17.3 0.1 copy.41
  17.4 0.1 reduce-window.24
  17.5 0.1 add_reduce_fusion.2
  17.6 0.1 select_reduce_fusion.3
  17.8 0.6 gather_fusion.1
  18.3 0.6 gather_fusion
  18.9 0.7 broadcast_select_fusion.3
  19.6 0.1 reshape.274
  19.7 0.1 collective-permute-start
  19.8 0.8 %fusion.pick_ref = bf16[6,64,64]{2,1,0:T(8,128)(2,1)} fusion(s32[6,64]{1,0:T(8,128)S(1)} %pad_add_fusion), kind=kLoop, calls=%fused_computation.10 | loop fusion | flops 49152 | bytes 50688 | tf_op jit(solution)/shard_map/convert_element_type | solution.py:316
  20.6 0.7 copy.48
  21.3 0.1 reshape_squeeze.11
  21.4 0.2 convert_reduce_fusion
  21.5 0.0 collective-permute-done.1
  21.6 0.1 reshape_squeeze.10
  21.6 0.2 convert_reduce_fusion.1
  21.8 6.5 %collective-permute-done = f32[5,4096]{1,0:T(8,128)S(1)} collective-permute-done((f32[5,4096]{1,0:T(8,128)S(1)}, f32[5,4096]{1,0:T(8,128)S(1)}, u32[]{:S(2)}, u32[]{:S(2)}) %collective-permute-start) | collective-permute-done | bytes 81952 | tf_op jit(solution)/shard_map/ppermute | solution.py:297
  28.4 0.1 reshape_squeeze.9
  28.5 0.2 convert_reduce_fusion.2
  28.7 0.1 pad_add_fusion.1
  28.7 0.1 select_reduce_fusion
  28.9 0.6 gather_fusion.7
  29.5 0.7 slice_convert_fusion.order_ref
  30.2 0.1 pad_maximum_fusion
  30.3 1.8 %gather_fusion.6 = f32[64,4096]{1,0:T(8,128)} fusion(f32[76,4096]{1,0:T(8,128)S(1)} %pad_maximum_fusion, s32[1024]{0:T(1024)S(1)} %pad_clamp_fusion), kind=kCustom, calls=%fused_computation.6 | custom fusion | bytes 2097408 | tf_op jit(solution)/shard_map/gather | solution.py:318
  32.2 2.5 %shard_map.127 = (f32[64,4096]{1,0:T(8,128)}, f32[2,64,256]{2,1,0:T(8,128)}) custom-call(f32[64,4096]{1,0:T(8,128)} %gather_fusion.6, s32[1,4096]{1,0:T(1,128)} %constant.155.clone.top_ref, s32[64,1]{1,0:T(8,128)} %slice_convert_fusion.order_ref), custom_call_target="tpu_custom_call" | custom-call | tf_op jit(solution)/shard_map/pallas_call | solution.py:238
  34.7 0.9 %slice_bitcast_fusion.2 = (f32[64,256]{1,0:T(8,128)S(1)}, f32[64,256]{1,0:T(8,128)S(1)}) fusion(f32[2,64,256]{2,1,0:T(8,128)} %get-tuple-element.47), kind=kLoop, calls=%fused_computation.17 | loop fusion | bytes 262144 | tf_op jit(solution)/shard_map/squeeze | solution.py:253
  35.5 1.9 %collective-permute-start.4 = (f32[64,256]{1,0:T(8,128)S(1)}, f32[64,256]{1,0:T(8,128)S(1)}, u32[]{:S(2)}, u32[]{:S(2)}) collective-permute-start(f32[64,256]{1,0:T(8,128)S(1)} %get-tuple-element.62), channel_id=1, source_target_pairs={{8,0},{16,8},{24,16},{32,24},{40,32},{48,40},{56,48},{64,56},{72,6... | collective-permute-start | bytes 196616 | tf_op jit(solution)/shard_map/ppermute | solution.py:253
  37.5 3.9 %collective-permute-start.3 = (f32[64,256]{1,0:T(8,128)S(1)}, f32[64,256]{1,0:T(8,128)S(1)}, u32[]{:S(2)}, u32[]{:S(2)}) collective-permute-start(f32[64,256]{1,0:T(8,128)S(1)} %get-tuple-element.63), channel_id=1, source_target_pairs={{0,8},{8,16},{16,24},{24,32},{32,40},{40,48},{48,56},{56,64},{64,7... | collective-permute-start | bytes 196616 | tf_op jit(solution)/shard_map/ppermute | solution.py:253
  41.4 0.6 broadcast_select_fusion.weight_ref
  42.0 3.7 %collective-permute-done.3.lower_ref = f32[64,256]{1,0:T(8,128)S(1)} collective-permute-done((f32[64,256]{1,0:T(8,128)S(1)}, f32[64,256]{1,0:T(8,128)S(1)}, u32[]{:S(2)}, u32[]{:S(2)}) %collective-permute-start.3) | collective-permute-done | bytes 65568 | tf_op jit(solution)/shard_map/ppermute | solution.py:253
  45.7 0.6 copy-done.4
  46.4 7.3 %shard_map.128 = (f32[64,4096]{1,0:T(8,128)}, f32[2,64,256]{2,1,0:T(8,128)}) custom-call(f32[64,4096]{1,0:T(8,128)} %get-tuple-element.46.v_ref.base_ref, f32[64,4096]{1,0:T(8,128)} %get-tuple-element.46.v_ref.base_ref, s32[1,4096]{1,0:T(1,128)} %constant.155.clone.top_ref, s32[64,1]{1,0:T(8,128)} %slice_convert_fusion.order_ref, ...), custom_call_target="tpu_custom_call" | custom-call | tf_op jit(solution)/shard_map/pallas_call | solution.py:210
  53.6 0.9 %slice_bitcast_fusion = (f32[64,256]{1,0:T(8,128)S(1)}, f32[64,256]{1,0:T(8,128)S(1)}) fusion(f32[2,64,256]{2,1,0:T(8,128)} %get-tuple-element.49), kind=kLoop, calls=%fused_computation.15 | loop fusion | bytes 262144 | tf_op jit(solution)/shard_map/squeeze | solution.py:253
  54.5 1.9 %collective-permute-start.6 = (f32[64,256]{1,0:T(8,128)S(1)}, f32[64,256]{1,0:T(8,128)S(1)}, u32[]{:S(2)}, u32[]{:S(2)}) collective-permute-start(f32[64,256]{1,0:T(8,128)S(1)} %get-tuple-element.60), channel_id=1, source_target_pairs={{8,0},{16,8},{24,16},{32,24},{40,32},{48,40},{56,48},{64,56},{72,6... | collective-permute-start | bytes 196616 | tf_op jit(solution)/shard_map/ppermute | solution.py:253
  56.4 4.1 %collective-permute-start.5 = (f32[64,256]{1,0:T(8,128)S(1)}, f32[64,256]{1,0:T(8,128)S(1)}, u32[]{:S(2)}, u32[]{:S(2)}) collective-permute-start(f32[64,256]{1,0:T(8,128)S(1)} %get-tuple-element.61), channel_id=1, source_target_pairs={{0,8},{8,16},{16,24},{24,32},{32,40},{40,48},{48,56},{56,64},{64,7... | collective-permute-start | bytes 196616 | tf_op jit(solution)/shard_map/ppermute | solution.py:253
  60.5 0.1 collective-permute-done.6.upper_ref
  60.7 4.0 %collective-permute-done.5.lower_ref = f32[64,256]{1,0:T(8,128)S(1)} collective-permute-done((f32[64,256]{1,0:T(8,128)S(1)}, f32[64,256]{1,0:T(8,128)S(1)}, u32[]{:S(2)}, u32[]{:S(2)}) %collective-permute-start.5) | collective-permute-done | bytes 65568 | tf_op jit(solution)/shard_map/ppermute | solution.py:253
  64.7 0.6 copy-done.2
  65.3 7.2 %shard_map.129 = (f32[64,4096]{1,0:T(8,128)}, f32[2,64,256]{2,1,0:T(8,128)}) custom-call(f32[64,4096]{1,0:T(8,128)} %get-tuple-element.48.v_ref, f32[64,4096]{1,0:T(8,128)} %get-tuple-element.46.v_ref.base_ref, s32[1,4096]{1,0:T(1,128)} %constant.155.clone.top_ref, s32[64,1]{1,0:T(8,128)} %slice_convert_fusion.order_ref, ...), custom_call_target="tpu_custom_call" | custom-call | tf_op jit(solution)/shard_map/pallas_call | solution.py:210
  (36 shorter events, 0.2 us)
Async XLA Ops:
  0.0 9.7 %copy-start = (f32[64,4096]{1,0:T(8,128)S(1)}, f32[64,4096]{1,0:T(8,128)}, u32[]{:S(2)}) copy-start(f32[64,4096]{1,0:T(8,128)} %param.19) | copy-start | bytes 3145732
  3.4 16.4 %copy-start.5 = (s32[1,4,64]{2,1,0:T(4,128)S(1)}, s32[1,4,64]{2,1,0:T(4,128)}, u32[]{:S(2)}) copy-start(s32[1,4,64]{2,1,0:T(4,128)} %param.24) | copy-start | bytes 3076
  3.4 16.4 %copy-start.6 = (s32[1,2,64]{2,1,0:T(2,128)S(1)}, s32[1,2,64]{2,1,0:T(2,128)}, u32[]{:S(2)}) copy-start(s32[1,2,64]{2,1,0:T(2,128)} %param.25) | copy-start | bytes 1540
  4.9 15.7 %copy-start.7 = (s32[1,2,64]{2,1,0:T(2,128)S(1)}, s32[1,2,64]{2,1,0:T(2,128)}, u32[]{:S(2)}) copy-start(s32[1,2,64]{2,1,0:T(2,128)} %param.26) | copy-start | bytes 1540
  6.8 14.5 %collective-permute-start.2 = (f32[5,4096]{1,0:T(8,128)S(1)}, f32[5,4096]{1,0:T(8,128)S(1)}, u32[]{:S(2)}, u32[]{:S(2)}) collective-permute-start(f32[5,4096]{1,0:T(8,128)S(1)} %select_maximum_fusion), channel_id=1, source_target_pairs={{0,64},{1,65},{2,66},{3,67},{4,68},{5,69},{6,70},{7,71},{8,72},{9,... | collective-permute-start | bytes 245768 | tf_op jit(solution)/shard_map/ppermute | solution.py:297
  11.1 10.5 %collective-permute-start.1 = (f32[5,4096]{1,0:T(8,128)S(1)}, f32[5,4096]{1,0:T(8,128)S(1)}, u32[]{:S(2)}, u32[]{:S(2)}) collective-permute-start(f32[5,4096]{1,0:T(8,128)S(1)} %select_maximum_fusion.1), channel_id=1, source_target_pairs={{0,127},{1,0},{2,1},{3,2},{4,3},{5,4},{6,5},{7,6},{8,7},{9,8},{10,... | collective-permute-start | bytes 245768 | tf_op jit(solution)/shard_map/ppermute | solution.py:297
  19.7 8.7 %collective-permute-start = (f32[5,4096]{1,0:T(8,128)S(1)}, f32[5,4096]{1,0:T(8,128)S(1)}, u32[]{:S(2)}, u32[]{:S(2)}) collective-permute-start(f32[5,4096]{1,0:T(8,128)S(1)} %select_maximum_fusion.2), channel_id=1, source_target_pairs={{0,1},{1,2},{2,3},{3,4},{4,5},{5,6},{6,7},{7,8},{8,9},{9,10},{10,1... | collective-permute-start | bytes 245768 | tf_op jit(solution)/shard_map/ppermute | solution.py:297
  32.2 9.2 %copy-start.8 = (pred[8]{0:T(512)(128)(4,1)S(1)}, pred[8]{0:T(512)(128)(4,1)}, u32[]{:S(2)}) copy-start(pred[8]{0:T(512)(128)(4,1)} %constant.154.clone.1) | copy-start | bytes 28
  35.5 6.5 %collective-permute-start.4 = (f32[64,256]{1,0:T(8,128)S(1)}, f32[64,256]{1,0:T(8,128)S(1)}, u32[]{:S(2)}, u32[]{:S(2)}) collective-permute-start(f32[64,256]{1,0:T(8,128)S(1)} %get-tuple-element.62), channel_id=1, source_target_pairs={{8,0},{16,8},{24,16},{32,24},{40,32},{48,40},{56,48},{64,56},{72,6... | collective-permute-start | bytes 196616 | tf_op jit(solution)/shard_map/ppermute | solution.py:253
  37.5 8.3 %collective-permute-start.3 = (f32[64,256]{1,0:T(8,128)S(1)}, f32[64,256]{1,0:T(8,128)S(1)}, u32[]{:S(2)}, u32[]{:S(2)}) collective-permute-start(f32[64,256]{1,0:T(8,128)S(1)} %get-tuple-element.63), channel_id=1, source_target_pairs={{0,8},{8,16},{16,24},{24,32},{32,40},{40,48},{48,56},{56,64},{64,7... | collective-permute-start | bytes 196616 | tf_op jit(solution)/shard_map/ppermute | solution.py:253
  42.0 3.7 %copy-start.3 = (f32[64,256]{1,0:T(8,128)}, f32[64,256]{1,0:T(8,128)S(1)}, u32[]{:S(2)}) copy-start(f32[64,256]{1,0:T(8,128)S(1)} %collective-permute-done.4.upper_ref) | copy-start | bytes 196612
  45.7 0.6 copy-start.4
  54.5 6.2 %collective-permute-start.6 = (f32[64,256]{1,0:T(8,128)S(1)}, f32[64,256]{1,0:T(8,128)S(1)}, u32[]{:S(2)}, u32[]{:S(2)}) collective-permute-start(f32[64,256]{1,0:T(8,128)S(1)} %get-tuple-element.60), channel_id=1, source_target_pairs={{8,0},{16,8},{24,16},{32,24},{40,32},{48,40},{56,48},{64,56},{72,6... | collective-permute-start | bytes 196616 | tf_op jit(solution)/shard_map/ppermute | solution.py:253
  56.4 8.3 %collective-permute-start.5 = (f32[64,256]{1,0:T(8,128)S(1)}, f32[64,256]{1,0:T(8,128)S(1)}, u32[]{:S(2)}, u32[]{:S(2)}) collective-permute-start(f32[64,256]{1,0:T(8,128)S(1)} %get-tuple-element.61), channel_id=1, source_target_pairs={{0,8},{8,16},{16,24},{24,32},{32,40},{40,48},{48,56},{56,64},{64,7... | collective-permute-start | bytes 196616 | tf_op jit(solution)/shard_map/ppermute | solution.py:253
  60.7 4.0 %copy-start.1 = (f32[64,256]{1,0:T(8,128)}, f32[64,256]{1,0:T(8,128)S(1)}, u32[]{:S(2)}) copy-start(f32[64,256]{1,0:T(8,128)S(1)} %collective-permute-done.6.upper_ref) | copy-start | bytes 196612
  64.7 0.6 copy-start.2
where the time goes:
time: 73 us; the launch traced here: 72.6 us
  starting transfers between devices  20.6 us (28%)
  Pallas kernels  17 us (23%)
  waiting for transfers between devices  14.4 us (20%)
  local copies, waits for them, and re-layouts  11.8 us (16%)
  other arithmetic  8.51 us (12%)
    pallas_call x2, Pallas kernels, section(): pl.pallas_call(functools.partial(section_body, scale=scale), out_shape=(j...  14.5 us
    ppermute x3, starting transfers between devices, shards(): arrived = lax.ppermute(parcel, ('dom', 'face'), pairs)  8.7 us
    ppermute x2, starting transfers between devices, exchange(): lax.ppermute(ends[1], 'dom', up)  8.02 us
    ppermute x2, waiting for transfers between devices, exchange(): lax.ppermute(ends[1], 'dom', up)  7.75 us
    ppermute x3, waiting for transfers between devices, shards(): arrived = lax.ppermute(parcel, ('dom', 'face'), pairs)  6.52 us
    ppermute x2, starting transfers between devices, exchange(): lax.ppermute(ends[0], 'dom', down)  3.84 us
    gather x3, local copies, waits for them, and re-layouts, shards(): parcel = jnp.concatenate([coefficients[picked], side_row], axis=0)  3.02 us
    another operation x8, other arithmetic  2.88 us
  transfers between devices with their start and end apart: 7, of which 4 were waited for; matrix products, arithmetic and copies ran while one was open for 9% of the time, Pallas kernels for 0%

commit v1 on v0

--- a/solution.py
+++ b/solution.py
@@ -253,19 +253,6 @@
     return lax.ppermute(ends[1], "dom", up), lax.ppermute(ends[0], "dom", down)
 
 
-def pick_rows(chosen, count):
-    rank = jnp.cumsum(chosen.astype(jnp.int32)) - 1
-    hit = chosen[None, :] & (rank[None, :] == jnp.arange(count, dtype=jnp.int32)[:, None])
-    rows = jnp.arange(chosen.shape[0], dtype=jnp.int32)
-    return jnp.sum(jnp.where(hit, rows[None, :], 0), axis=1)
-
-
-def pick_rows_inverse(slots, count):
-    hit = slots[None, :] == jnp.arange(count, dtype=jnp.int32)[:, None]
-    rows = jnp.arange(slots.shape[0], dtype=jnp.int32)
-    return jnp.sum(jnp.where(hit, rows[None, :], 0), axis=1)
-
-
 def shards(
     coefficients, diffusion, velocity, orders, target, local_faces, partner_faces, partner_turns
 ):
@@ -285,16 +272,26 @@
         axis=1,
     )
     side_width = side_info.shape[1]
+    shifts = (1, blocks_all - 1, blocks_all // 2)
+    goal = (here + jnp.asarray(shifts, jnp.int32)) % blocks_all
+    chosen = destination[None, :] == goal[:, None]
+    rank = jnp.cumsum(chosen.astype(jnp.int32), axis=1) - 1
+    hit = chosen[:, None, :] & (
+        rank[:, None, :] == jnp.arange(moving, dtype=jnp.int32)[None, :, None]
+    )
+    rows = jnp.arange(element_count, dtype=jnp.int32)
+    picked = jnp.sum(jnp.where(hit, rows[None, None, :], 0), axis=2).reshape(-1)
+    side_rows = side_info[picked].reshape(len(shifts), 1, moving * side_width)
+    side_rows = jnp.pad(side_rows, ((0, 0), (0, 0), (0, P_SIZE**3 - moving * side_width)))
+    parcels = jnp.concatenate(
+        [coefficients[picked].reshape(len(shifts), moving, P_SIZE**3), side_rows], axis=1
+    )
     got_coef = [coefficients]
     got_side = [side_info]
     got_slot = [jnp.where(destination == here, new_slot, element_count)]
-    for shift in (1, blocks_all - 1, blocks_all // 2):
-        picked = pick_rows(destination == (here + shift) % blocks_all, moving)
-        side_row = jnp.zeros((1, P_SIZE**3), jnp.float32)
-        side_row = side_row.at[0, : moving * side_width].set(side_info[picked].reshape(-1))
-        parcel = jnp.concatenate([coefficients[picked], side_row], axis=0)
+    for index, shift in enumerate(shifts):
         pairs = [(i, (i + shift) % blocks_all) for i in range(blocks_all)]
-        arrived = lax.ppermute(parcel, ("dom", "face"), pairs)
+        arrived = lax.ppermute(parcels[index], ("dom", "face"), pairs)
         arrived_side = arrived[moving, : moving * side_width].reshape(moving, side_width)
         got_coef.append(arrived[:moving])
         got_side.append(arrived_side)
@@ -302,7 +299,9 @@
     got_coef = jnp.concatenate(got_coef, axis=0)
     got_side = jnp.concatenate(got_side, axis=0)
     got_slot = jnp.concatenate(got_slot, axis=0)
-    source = pick_rows_inverse(got_slot, element_count)
+    hit = got_slot[None, :] == jnp.arange(element_count, dtype=jnp.int32)[:, None]
+    got_rows = jnp.arange(got_slot.shape[0], dtype=jnp.int32)
+    source = jnp.sum(jnp.where(hit, got_rows[None, :], 0), axis=1)
     placed_side = got_side[source]
     weight = jnp.concatenate(
         [placed_side[:, 0:6], jnp.zeros((element_count, 2), jnp.float32)], axis=1

time: 73 us -> 64 us (0.88)
  waiting for transfers between devices: 14.4 us -> 10.5 us
  local copies, waits for them, and re-layouts: 11.8 us -> 9.35 us
  other arithmetic: 8.51 us -> 6.15 us
    ppermute x3, waiting for transfers between devices: 6.52 us -> 0.46 us  [shards(): arrived = lax.ppermute(parcels[index], ('dom', 'face'), pairs)]
    another operation x8 -> x1, other arithmetic: 2.88 us -> 0.24 us  [shards(): rank = jnp.cumsum(chosen.astype(jnp.int32), axis=1) - 1]
    gather x6 -> x2, local copies, waits for them, and re-layouts: 4.69 us -> 2.48 us  [the longest x1 1.93 us: shards(): coefficients[picked].reshape(len(shifts), moving, P_SIZE ** 3)]
    ppermute x2, starting transfers between devices: 8.02 us -> 5.84 us  [exchange(): lax.ppermute(ends[1], 'dom', up)]
    ppermute x2, starting transfers between devices: 3.84 us -> 5.94 us  [exchange(): lax.ppermute(ends[0], 'dom', down)]
    ppermute x2, waiting for transfers between devices: 7.75 us -> 9.75 us  [exchange(): lax.ppermute(ends[1], 'dom', up)]
  transfers between devices with their start and end apart: 7 -> 7, of which waited for: 4 -> 4; matrix products, arithmetic and copies ran while one was open for 9% -> 4% of each run, Pallas kernels for 0% -> 0%
where the time goes in v1:
time: 64 us; the launch traced here: 63.6 us
  starting transfers between devices  20.4 us (32%)
  Pallas kernels  17 us (27%)
  waiting for transfers between devices  10.5 us (16%)
  local copies, waits for them, and re-layouts  9.35 us (15%)
  other arithmetic  6.15 us (10%)
    pallas_call x2, Pallas kernels, section(): pl.pallas_call(functools.partial(section_body, scale=scale), out_shape=(j...  14.5 us
    ppermute x2, waiting for transfers between devices, exchange(): lax.ppermute(ends[1], 'dom', up)  9.75 us
    ppermute x3, starting transfers between devices, shards(): arrived = lax.ppermute(parcels[index], ('dom', 'face'), pairs)  8.65 us
    ppermute x2, starting transfers between devices, exchange(): lax.ppermute(ends[0], 'dom', down)  5.94 us
    ppermute x2, starting transfers between devices, exchange(): lax.ppermute(ends[1], 'dom', up)  5.84 us
    pallas_call x1, Pallas kernels, prep(): pl.pallas_call(prep_body, out_shape=(jax.ShapeDtypeStruct(placed.shape, j...  2.48 us
    gather x1, local copies, waits for them, and re-layouts, shards(): coefficients[picked].reshape(len(shifts), moving, P_SIZE ** 3)  1.93 us
    gather x1, local copies, waits for them, and re-layouts, shards(): field, ends = prep(got_coef[source], top, order)  1.85 us
  transfers between devices with their start and end apart: 7, of which 4 were waited for; matrix products, arithmetic and copies ran while one was open for 4% of the time, Pallas kernels for 0%

profile of v1, /device:TPU:8, one launch (start us, length us, event | category | flops | bytes accessed | tf_op | source)
XLA Modules:
  0.0 63.6 jit_solution(14803483092798758294)
XLA Ops:
  0.0 0.7 %and_select_fusion.1 = s32[3]{0:T(128)S(1)} fusion(s32[3]{0:T(128)} %constant.81.clone, s32[]{:T(128)S(6)} %add.51), kind=kLoop, calls=%fused_computation.37 | loop fusion | flops 36 | bytes 28 | tf_op jit(solution)/shard_map/jit(remainder)/select_n | solution.py:276
  0.7 0.7 %compare_select_fusion.4 = (s32[64]{0:T(128)S(1)}, s32[64]{0:T(128)S(1)}, s32[64]{0:T(128)S(1)}) fusion(s32[]{:T(128)S(6)} %add.51, s32[64]{0:T(128)} %param.18), kind=kLoop, calls=%fused_computation.35 | loop fusion | flops 1344 | bytes 1028 | tf_op jit(solution)/shard_map/jit(_where)/select_n | solution.py:291
  1.3 0.1 fusion.5
  1.4 0.2 reduce_window_sum.11
  1.7 0.1 select_reduce_fusion.1
  1.8 0.1 reshape.106
  1.9 0.7 %convert_bitcast_fusion = (f32[64,1]{0,1:T(1,128)S(1)}, f32[64,1]{0,1:T(1,128)S(1)}) fusion(s32[64]{0:T(128)} %param.17, s32[64]{0:T(128)S(1)} %get-tuple-element.17), kind=kLoop, calls=%fused_computation.51 | loop fusion | flops 448 | bytes 1024 | tf_op jit(solution)/shard_map/convert_element_type | solution.py:270
  2.6 0.7 %pad_maximum_fusion.2 = f32[64,8]{0,1:T(8,128)S(1)} fusion(f32[64,1]{0,1:T(1,128)S(1)} %get-tuple-element.27, f32[64,1]{0,1:T(1,128)S(1)} %get-tuple-element.28, f32[64,3]{0,1:T(4,128)} %param.16, f32[64,3]{0,1:T(4,128)} %param.15), kind=kLoop, calls=%fused_computation.26 | loop fusion | flops 1536 | bytes 4096 | tf_op jit(solution)/shard_map/concatenate | solution.py:265
  3.3 0.1 copy.34
  3.4 0.6 gather_fusion.1
  3.9 0.1 reshape.141
  4.0 1.9 %gather_fusion = f32[12,4096]{1,0:T(8,128)S(1)} fusion(f32[64,4096]{1,0:T(8,128)} %param.14, s32[1024]{0:T(1024)S(1)} %pad_clamp_fusion.1), kind=kCustom, calls=%fused_computation | custom fusion | bytes 393264 | tf_op jit(solution)/shard_map/gather | solution.py:287
  5.9 0.0 copy-start.5
  6.0 0.0 copy-start.6
  6.0 0.0 copy-start.7
  6.0 0.1 reshape.107
  6.0 0.0 copy-start
  6.1 0.1 collective-permute-start
  6.2 2.4 %collective-permute-start.2 = (f32[5,4096]{1,0:T(8,128)S(1)}, f32[5,4096]{1,0:T(8,128)S(1)}, u32[]{:S(2)}, u32[]{:S(2)}) collective-permute-start(f32[5,4096]{1,0:T(8,128)S(1)} %get-tuple-element.21), channel_id=1, source_target_pairs={{0,64},{1,65},{2,66},{3,67},{4,68},{5,69},{6,70},{7,71},{8,72},{9,... | collective-permute-start | bytes 245768 | tf_op jit(solution)/shard_map/ppermute | solution.py:294
  8.6 6.2 %collective-permute-start.1 = (f32[5,4096]{1,0:T(8,128)S(1)}, f32[5,4096]{1,0:T(8,128)S(1)}, u32[]{:S(2)}, u32[]{:S(2)}) collective-permute-start(f32[5,4096]{1,0:T(8,128)S(1)} %get-tuple-element.22), channel_id=1, source_target_pairs={{0,127},{1,0},{2,1},{3,2},{4,3},{5,4},{6,5},{7,6},{8,7},{9,8},{10,... | collective-permute-start | bytes 245768 | tf_op jit(solution)/shard_map/ppermute | solution.py:294
  14.8 0.0 copy-done.5
  14.8 0.0 copy-done.6
  14.8 0.8 %fusion.pick_ref = bf16[6,64,64]{2,1,0:T(8,128)(2,1)} fusion(s32[6,64]{1,0:T(8,128)S(1)} %pad_add_fusion), kind=kLoop, calls=%fused_computation.8 | loop fusion | flops 49152 | bytes 50688 | tf_op jit(solution)/shard_map/convert_element_type | solution.py:315
  15.6 0.0 copy-done.7
  15.6 0.7 %copy.37 = s32[2,64]{0,1:T(8,128)} copy(s32[2,64]{1,0:T(2,128)S(1)} %bitcast.32) | data formatting | bytes 1024 | tf_op jit(solution)/shard_map/squeeze | solution.py:316
  16.3 0.0 collective-permute-done
  16.3 0.1 reshape_squeeze.9
  16.4 0.2 convert_reduce_fusion.2
  16.6 0.0 collective-permute-done.2
  16.6 0.1 reshape_squeeze.11
  16.7 0.2 convert_reduce_fusion
  16.9 0.5 collective-permute-done.1
  17.3 0.1 reshape_squeeze.10
  17.4 0.2 convert_reduce_fusion.1
  17.6 0.1 pad_add_fusion.1
  17.7 0.1 select_reduce_fusion
  17.8 0.6 gather_fusion.3
  18.4 0.7 %slice_convert_fusion.order_ref = s32[64,1]{1,0:T(8,128)} fusion(f32[64,8]{1,0:T(8,128)S(1)} %gather_fusion.3), kind=kLoop, calls=%fused_computation.17 | loop fusion | flops 64 | bytes 512 | tf_op jit(solution)/shard_map/convert_element_type | solution.py:309
  19.2 0.0 copy-done
  19.2 0.1 pad_maximum_fusion
  19.3 1.8 %gather_fusion.2 = f32[64,4096]{1,0:T(8,128)} fusion(f32[76,4096]{1,0:T(8,128)S(1)} %pad_maximum_fusion, s32[1024]{0:T(1024)S(1)} %pad_clamp_fusion), kind=kCustom, calls=%fused_computation.2 | custom fusion | bytes 2097408 | tf_op jit(solution)/shard_map/gather | solution.py:317
  21.1 0.0 copy-start.8
  21.1 2.5 %shard_map.136 = (f32[64,4096]{1,0:T(8,128)}, f32[2,64,256]{2,1,0:T(8,128)}) custom-call(f32[64,4096]{1,0:T(8,128)} %gather_fusion.2, s32[1,4096]{1,0:T(1,128)} %constant.82.clone.top_ref, s32[64,1]{1,0:T(8,128)} %slice_convert_fusion.order_ref), custom_call_target="tpu_custom_call" | custom-call | tf_op jit(solution)/shard_map/pallas_call | solution.py:238
  23.6 0.9 %slice_bitcast_fusion.5 = (f32[64,256]{1,0:T(8,128)S(1)}, f32[64,256]{1,0:T(8,128)S(1)}) fusion(f32[2,64,256]{2,1,0:T(8,128)} %get-tuple-element.11), kind=kLoop, calls=%fused_computation.14 | loop fusion | bytes 262144 | tf_op jit(solution)/shard_map/squeeze | solution.py:253
  24.5 4.0 %collective-permute-start.4 = (f32[64,256]{1,0:T(8,128)S(1)}, f32[64,256]{1,0:T(8,128)S(1)}, u32[]{:S(2)}, u32[]{:S(2)}) collective-permute-start(f32[64,256]{1,0:T(8,128)S(1)} %get-tuple-element.25), channel_id=1, source_target_pairs={{8,0},{16,8},{24,16},{32,24},{40,32},{48,40},{56,48},{64,56},{72,6... | collective-permute-start | bytes 196616 | tf_op jit(solution)/shard_map/ppermute | solution.py:253
  28.5 1.9 %collective-permute-start.3 = (f32[64,256]{1,0:T(8,128)S(1)}, f32[64,256]{1,0:T(8,128)S(1)}, u32[]{:S(2)}, u32[]{:S(2)}) collective-permute-start(f32[64,256]{1,0:T(8,128)S(1)} %get-tuple-element.26), channel_id=1, source_target_pairs={{0,8},{8,16},{16,24},{24,32},{32,40},{40,48},{48,56},{56,64},{64,7... | collective-permute-start | bytes 196616 | tf_op jit(solution)/shard_map/ppermute | solution.py:253
  30.5 0.0 copy-done.8
  30.5 0.6 broadcast_select_fusion.weight_ref
  31.1 0.0 collective-permute-done.4.upper_ref
  31.1 0.0 copy-start.3
  31.1 5.7 %collective-permute-done.3.lower_ref = f32[64,256]{1,0:T(8,128)S(1)} collective-permute-done((f32[64,256]{1,0:T(8,128)S(1)}, f32[64,256]{1,0:T(8,128)S(1)}, u32[]{:S(2)}, u32[]{:S(2)}) %collective-permute-start.3) | collective-permute-done | bytes 65568 | tf_op jit(solution)/shard_map/ppermute | solution.py:253
  36.8 0.0 copy-start.4
  36.8 0.0 copy-done.3
  36.8 0.6 copy-done.4
  37.4 7.3 %shard_map.137 = (f32[64,4096]{1,0:T(8,128)}, f32[2,64,256]{2,1,0:T(8,128)}) custom-call(f32[64,4096]{1,0:T(8,128)} %get-tuple-element.10.v_ref.base_ref, f32[64,4096]{1,0:T(8,128)} %get-tuple-element.10.v_ref.base_ref, s32[1,4096]{1,0:T(1,128)} %constant.82.clone.top_ref, s32[64,1]{1,0:T(8,128)} %slice_convert_fusion.order_ref, ...), custom_call_target="tpu_custom_call" | custom-call | tf_op jit(solution)/shard_map/pallas_call | solution.py:210
  44.7 0.9 %slice_bitcast_fusion.3 = (f32[64,256]{1,0:T(8,128)S(1)}, f32[64,256]{1,0:T(8,128)S(1)}) fusion(f32[2,64,256]{2,1,0:T(8,128)} %get-tuple-element.13), kind=kLoop, calls=%fused_computation.12 | loop fusion | bytes 262144 | tf_op jit(solution)/shard_map/squeeze | solution.py:253
  45.6 1.9 %collective-permute-start.6 = (f32[64,256]{1,0:T(8,128)S(1)}, f32[64,256]{1,0:T(8,128)S(1)}, u32[]{:S(2)}, u32[]{:S(2)}) collective-permute-start(f32[64,256]{1,0:T(8,128)S(1)} %get-tuple-element.23), channel_id=1, source_target_pairs={{8,0},{16,8},{24,16},{32,24},{40,32},{48,40},{56,48},{64,56},{72,6... | collective-permute-start | bytes 196616 | tf_op jit(solution)/shard_map/ppermute | solution.py:253
  47.5 3.9 %collective-permute-start.5 = (f32[64,256]{1,0:T(8,128)S(1)}, f32[64,256]{1,0:T(8,128)S(1)}, u32[]{:S(2)}, u32[]{:S(2)}) collective-permute-start(f32[64,256]{1,0:T(8,128)S(1)} %get-tuple-element.24), channel_id=1, source_target_pairs={{0,8},{8,16},{16,24},{24,32},{32,40},{40,48},{48,56},{56,64},{64,7... | collective-permute-start | bytes 196616 | tf_op jit(solution)/shard_map/ppermute | solution.py:253
  51.4 0.3 collective-permute-done.6.upper_ref
  51.7 0.0 copy-start.1
  51.7 4.0 %collective-permute-done.5.lower_ref = f32[64,256]{1,0:T(8,128)S(1)} collective-permute-done((f32[64,256]{1,0:T(8,128)S(1)}, f32[64,256]{1,0:T(8,128)S(1)}, u32[]{:S(2)}, u32[]{:S(2)}) %collective-permute-start.5) | collective-permute-done | bytes 65568 | tf_op jit(solution)/shard_map/ppermute | solution.py:253
  55.8 0.0 copy-done.1
  55.8 0.6 copy-done.2
  56.4 7.2 %shard_map.138 = (f32[64,4096]{1,0:T(8,128)}, f32[2,64,256]{2,1,0:T(8,128)}) custom-call(f32[64,4096]{1,0:T(8,128)} %get-tuple-element.12.v_ref, f32[64,4096]{1,0:T(8,128)} %get-tuple-element.10.v_ref.base_ref, s32[1,4096]{1,0:T(1,128)} %constant.82.clone.top_ref, s32[64,1]{1,0:T(8,128)} %slice_convert_fusion.order_ref, ...), custom_call_target="tpu_custom_call" | custom-call | tf_op jit(solution)/shard_map/pallas_call | solution.py:210
  (16 shorter events, 0.2 us)
Async XLA Ops:
  5.9 8.9 %copy-start.5 = (s32[1,4,64]{2,1,0:T(4,128)S(1)}, s32[1,4,64]{2,1,0:T(4,128)}, u32[]{:S(2)}) copy-start(s32[1,4,64]{2,1,0:T(4,128)} %param.19) | copy-start | bytes 3076
  6.0 8.8 %copy-start.6 = (s32[1,2,64]{2,1,0:T(2,128)S(1)}, s32[1,2,64]{2,1,0:T(2,128)}, u32[]{:S(2)}) copy-start(s32[1,2,64]{2,1,0:T(2,128)} %param.20) | copy-start | bytes 1540
  6.0 9.6 %copy-start.7 = (s32[1,2,64]{2,1,0:T(2,128)S(1)}, s32[1,2,64]{2,1,0:T(2,128)}, u32[]{:S(2)}) copy-start(s32[1,2,64]{2,1,0:T(2,128)} %param.21) | copy-start | bytes 1540
  6.0 13.1 %copy-start = (f32[64,4096]{1,0:T(8,128)S(1)}, f32[64,4096]{1,0:T(8,128)}, u32[]{:S(2)}) copy-start(f32[64,4096]{1,0:T(8,128)} %param.14) | copy-start | bytes 3145732
  6.1 10.1 %collective-permute-start = (f32[5,4096]{1,0:T(8,128)S(1)}, f32[5,4096]{1,0:T(8,128)S(1)}, u32[]{:S(2)}, u32[]{:S(2)}) collective-permute-start(f32[5,4096]{1,0:T(8,128)S(1)} %get-tuple-element.20), channel_id=1, source_target_pairs={{0,1},{1,2},{2,3},{3,4},{4,5},{5,6},{6,7},{7,8},{8,9},{9,10},{10,1... | collective-permute-start | bytes 245768 | tf_op jit(solution)/shard_map/ppermute | solution.py:294
  6.2 10.3 %collective-permute-start.2 = (f32[5,4096]{1,0:T(8,128)S(1)}, f32[5,4096]{1,0:T(8,128)S(1)}, u32[]{:S(2)}, u32[]{:S(2)}) collective-permute-start(f32[5,4096]{1,0:T(8,128)S(1)} %get-tuple-element.21), channel_id=1, source_target_pairs={{0,64},{1,65},{2,66},{3,67},{4,68},{5,69},{6,70},{7,71},{8,72},{9,... | collective-permute-start | bytes 245768 | tf_op jit(solution)/shard_map/ppermute | solution.py:294
  8.6 8.7 %collective-permute-start.1 = (f32[5,4096]{1,0:T(8,128)S(1)}, f32[5,4096]{1,0:T(8,128)S(1)}, u32[]{:S(2)}, u32[]{:S(2)}) collective-permute-start(f32[5,4096]{1,0:T(8,128)S(1)} %get-tuple-element.22), channel_id=1, source_target_pairs={{0,127},{1,0},{2,1},{3,2},{4,3},{5,4},{6,5},{7,6},{8,7},{9,8},{10,... | collective-permute-start | bytes 245768 | tf_op jit(solution)/shard_map/ppermute | solution.py:294
  21.1 9.3 %copy-start.8 = (pred[8]{0:T(512)(128)(4,1)S(1)}, pred[8]{0:T(512)(128)(4,1)}, u32[]{:S(2)}) copy-start(pred[8]{0:T(512)(128)(4,1)} %constant.80.clone.1) | copy-start | bytes 28
  24.5 6.6 %collective-permute-start.4 = (f32[64,256]{1,0:T(8,128)S(1)}, f32[64,256]{1,0:T(8,128)S(1)}, u32[]{:S(2)}, u32[]{:S(2)}) collective-permute-start(f32[64,256]{1,0:T(8,128)S(1)} %get-tuple-element.25), channel_id=1, source_target_pairs={{8,0},{16,8},{24,16},{32,24},{40,32},{48,40},{56,48},{64,56},{72,6... | collective-permute-start | bytes 196616 | tf_op jit(solution)/shard_map/ppermute | solution.py:253
  28.5 8.3 %collective-permute-start.3 = (f32[64,256]{1,0:T(8,128)S(1)}, f32[64,256]{1,0:T(8,128)S(1)}, u32[]{:S(2)}, u32[]{:S(2)}) collective-permute-start(f32[64,256]{1,0:T(8,128)S(1)} %get-tuple-element.26), channel_id=1, source_target_pairs={{0,8},{8,16},{16,24},{24,32},{32,40},{40,48},{48,56},{56,64},{64,7... | collective-permute-start | bytes 196616 | tf_op jit(solution)/shard_map/ppermute | solution.py:253
  31.1 5.7 %copy-start.3 = (f32[64,256]{1,0:T(8,128)}, f32[64,256]{1,0:T(8,128)S(1)}, u32[]{:S(2)}) copy-start(f32[64,256]{1,0:T(8,128)S(1)} %collective-permute-done.4.upper_ref) | copy-start | bytes 196612
  36.8 0.6 copy-start.4
  45.6 6.2 %collective-permute-start.6 = (f32[64,256]{1,0:T(8,128)S(1)}, f32[64,256]{1,0:T(8,128)S(1)}, u32[]{:S(2)}, u32[]{:S(2)}) collective-permute-start(f32[64,256]{1,0:T(8,128)S(1)} %get-tuple-element.23), channel_id=1, source_target_pairs={{8,0},{16,8},{24,16},{32,24},{40,32},{48,40},{56,48},{64,56},{72,6... | collective-permute-start | bytes 196616 | tf_op jit(solution)/shard_map/ppermute | solution.py:253
  47.5 8.3 %collective-permute-start.5 = (f32[64,256]{1,0:T(8,128)S(1)}, f32[64,256]{1,0:T(8,128)S(1)}, u32[]{:S(2)}, u32[]{:S(2)}) collective-permute-start(f32[64,256]{1,0:T(8,128)S(1)} %get-tuple-element.24), channel_id=1, source_target_pairs={{0,8},{8,16},{16,24},{24,32},{32,40},{40,48},{48,56},{56,64},{64,7... | collective-permute-start | bytes 196616 | tf_op jit(solution)/shard_map/ppermute | solution.py:253
  51.7 4.0 %copy-start.1 = (f32[64,256]{1,0:T(8,128)}, f32[64,256]{1,0:T(8,128)S(1)}, u32[]{:S(2)}) copy-start(f32[64,256]{1,0:T(8,128)S(1)} %collective-permute-done.6.upper_ref) | copy-start | bytes 196612
  55.8 0.6 copy-start.2

commit v2 on v1

--- a/solution.py
+++ b/solution.py
@@ -124,7 +124,7 @@
 
 def section_body(
     v_ref, base_ref, top_ref, order_ref, weight_ref, lower_ref, upper_ref, pick_ref, turn_ref,
-    spread_hi_ref, spread_lo_ref, lift_ref, flip_ref, out_ref, ends_ref, *, scale
+    spread_hi_ref, spread_lo_ref, lift_ref, flip_ref, out_ref, even_ref, total_ref, *, scale
 ):
     count = v_ref.shape[0]
     derivative, second, side_signs, weights = mode_tables()
@@ -200,8 +200,8 @@
         out_ref[:, a * PLANE : (a + 1) * PLANE] = new
         news.append(new)
     even, total = end_traces(news)
-    ends_ref[0] = even
-    ends_ref[1] = total
+    even_ref[...] = even
+    total_ref[...] = total
 
 
 def section(v, base, top, order, weight, lower, upper, picks, codes, tables, scale):
@@ -211,15 +211,16 @@
         functools.partial(section_body, scale=scale),
         out_shape=(
             jax.ShapeDtypeStruct(v.shape, jnp.float32),
-            jax.ShapeDtypeStruct((2, count, PLANE), jnp.float32),
+            jax.ShapeDtypeStruct((count, PLANE), jnp.float32),
+            jax.ShapeDtypeStruct((count, PLANE), jnp.float32),
         ),
         in_specs=[spec] * 13,
-        out_specs=(spec, spec),
+        out_specs=(spec, spec, spec),
         compiler_params=pltpu.CompilerParams(vmem_limit_bytes=60 * 1024 * 1024),
     )(v, base, top, order, weight, lower, upper, picks, codes, *tables)
 
 
-def prep_body(placed_ref, top_ref, order_ref, field_ref, ends_ref):
+def prep_body(placed_ref, top_ref, order_ref, field_ref, even_ref, total_ref):
     news = []
     for a in range(P_SIZE):
         lanes = slice(a * PLANE, (a + 1) * PLANE)
@@ -228,8 +229,8 @@
         field_ref[:, lanes] = new
         news.append(new)
     even, total = end_traces(news)
-    ends_ref[0] = even
-    ends_ref[1] = total
+    even_ref[...] = even
+    total_ref[...] = total
 
 
 def prep(placed, top, order):
@@ -239,18 +240,19 @@
         prep_body,
         out_shape=(
             jax.ShapeDtypeStruct(placed.shape, jnp.float32),
-            jax.ShapeDtypeStruct((2, count, PLANE), jnp.float32),
+            jax.ShapeDtypeStruct((count, PLANE), jnp.float32),
+            jax.ShapeDtypeStruct((count, PLANE), jnp.float32),
         ),
         in_specs=[spec] * 3,
-        out_specs=(spec, spec),
+        out_specs=(spec, spec, spec),
     )(placed, top, order)
 
 
-def exchange(ends):
+def exchange(even, total):
     size = lax.axis_size("dom")
-    up = [(i, i + 1) for i in range(size - 1)]
-    down = [(i + 1, i) for i in range(size - 1)]
-    return lax.ppermute(ends[1], "dom", up), lax.ppermute(ends[0], "dom", down)
+    up = [(i, (i + 1) % size) for i in range(size)]
+    down = [((i + 1) % size, i) for i in range(size)]
+    return lax.ppermute(total, "dom", up), lax.ppermute(even, "dom", down)
 
 
 def shards(
@@ -314,13 +316,13 @@
         neighbours[:, :, None] == jnp.arange(element_count, dtype=jnp.int32)[None, None, :]
     ).astype(jnp.bfloat16)
     codes = partner_turns[0].T
-    field, ends = prep(got_coef[source], top, order)
-    lower, upper = exchange(ends)
-    half, ends = section(
+    field, even, total = prep(got_coef[source], top, order)
+    lower, upper = exchange(even, total)
+    half, even, total = section(
         field, field, top, order, weight, lower, upper, picks, codes, tables, 0.5 * TIME_STEP
     )
-    lower, upper = exchange(ends)
-    advanced, _ = section(
+    lower, upper = exchange(even, total)
+    advanced, _, _ = section(
         half, field, top, order, weight, lower, upper, picks, codes, tables, TIME_STEP
     )
     return advanced

time: 64 us -> 56.3 us (0.88)
  the two profiles are of different devices: /device:TPU:8 before, /device:TPU:0 now
where the time goes in v2:
time: 56.3 us; the launch traced here: 56 us
  starting transfers between devices  20.5 us (36%)
  Pallas kernels  17 us (30%)
  local copies, waits for them, and re-layouts  7.62 us (14%)
  other arithmetic  6.15 us (11%)
  waiting for transfers between devices  4.54 us (8%)
    pallas_call x2, Pallas kernels, section(): pl.pallas_call(functools.partial(section_body, scale=scale), out_shape=(j...  14.5 us
    ppermute x4, starting transfers between devices, exchange(): return (lax.ppermute(total, 'dom', up), lax.ppermute(even, 'dom', down))  10.9 us
    ppermute x3, starting transfers between devices, shards(): arrived = lax.ppermute(parcels[index], ('dom', 'face'), pairs)  9.63 us
    ppermute x4, waiting for transfers between devices, exchange(): return (lax.ppermute(total, 'dom', up), lax.ppermute(even, 'dom', down))  4.08 us
    pallas_call x1, Pallas kernels, prep(): pl.pallas_call(prep_body, out_shape=(jax.ShapeDtypeStruct(placed.shape, j...  2.47 us
    gather x1, local copies, waits for them, and re-layouts, shards(): coefficients[picked].reshape(len(shifts), moving, P_SIZE ** 3)  1.93 us
    gather x1, local copies, waits for them, and re-layouts, shards(): field, even, total = prep(got_coef[source], top, order)  1.85 us
    unnamed x18, local copies, waits for them, and re-layouts  1.31 us
  transfers between devices with their start and end apart: 7, of which 4 were waited for; matrix products, arithmetic and copies ran while one was open for 5% of the time, Pallas kernels for 0%

profile of v2, /device:TPU:0, one launch (start us, length us, event | category | flops | bytes accessed | tf_op | source)
XLA Modules:
  0.0 56.0 jit_solution(17098828388993735753)
XLA Ops:
  0.0 0.7 %and_select_fusion.1 = s32[3]{0:T(128)S(1)} fusion(s32[3]{0:T(128)} %constant.81.clone, s32[]{:T(128)S(6)} %add.51), kind=kLoop, calls=%fused_computation.33 | loop fusion | flops 36 | bytes 28 | tf_op jit(solution)/shard_map/jit(remainder)/select_n | solution.py:278
  0.7 0.7 %compare_select_fusion.4 = (s32[64]{0:T(128)S(1)}, s32[64]{0:T(128)S(1)}, s32[64]{0:T(128)S(1)}) fusion(s32[]{:T(128)S(6)} %add.51, s32[64]{0:T(128)} %param.18), kind=kLoop, calls=%fused_computation.31 | loop fusion | flops 1344 | bytes 1028 | tf_op jit(solution)/shard_map/jit(_where)/select_n | solution.py:293
  1.3 0.1 fusion.5
  1.4 0.2 reduce_window_sum.11
  1.7 0.1 select_reduce_fusion.1
  1.8 0.1 reshape.106
  1.9 0.7 %convert_bitcast_fusion = (f32[64,1]{0,1:T(1,128)S(1)}, f32[64,1]{0,1:T(1,128)S(1)}) fusion(s32[64]{0:T(128)} %param.17, s32[64]{0:T(128)S(1)} %get-tuple-element.21), kind=kLoop, calls=%fused_computation.47 | loop fusion | flops 448 | bytes 1024 | tf_op jit(solution)/shard_map/convert_element_type | solution.py:272
  2.6 0.7 %pad_maximum_fusion.2 = f32[64,8]{0,1:T(8,128)S(1)} fusion(f32[64,1]{0,1:T(1,128)S(1)} %get-tuple-element.27, f32[64,1]{0,1:T(1,128)S(1)} %get-tuple-element.28, f32[64,3]{0,1:T(4,128)} %param.16, f32[64,3]{0,1:T(4,128)} %param.15), kind=kLoop, calls=%fused_computation.22 | loop fusion | flops 1536 | bytes 4096 | tf_op jit(solution)/shard_map/concatenate | solution.py:267
  3.3 0.1 copy.34
  3.4 0.6 gather_fusion.1
  3.9 0.1 reshape.141
  4.0 1.9 %gather_fusion = f32[12,4096]{1,0:T(8,128)S(1)} fusion(f32[64,4096]{1,0:T(8,128)} %param.14, s32[1024]{0:T(1024)S(1)} %pad_clamp_fusion.1), kind=kCustom, calls=%fused_computation | custom fusion | bytes 393264 | tf_op jit(solution)/shard_map/gather | solution.py:289
  5.9 0.0 copy-start.5
  6.0 0.0 copy-start.6
  6.0 0.0 copy-start.7
  6.0 0.1 reshape.107
  6.0 0.0 copy-start
  6.1 0.1 collective-permute-start
  6.2 3.4 %collective-permute-start.2 = (f32[5,4096]{1,0:T(8,128)S(1)}, f32[5,4096]{1,0:T(8,128)S(1)}, u32[]{:S(2)}, u32[]{:S(2)}) collective-permute-start(f32[5,4096]{1,0:T(8,128)S(1)} %get-tuple-element.25), channel_id=1, source_target_pairs={{0,64},{1,65},{2,66},{3,67},{4,68},{5,69},{6,70},{7,71},{8,72},{9,... | collective-permute-start | bytes 245768 | tf_op jit(solution)/shard_map/ppermute | solution.py:296
  9.6 6.2 %collective-permute-start.1 = (f32[5,4096]{1,0:T(8,128)S(1)}, f32[5,4096]{1,0:T(8,128)S(1)}, u32[]{:S(2)}, u32[]{:S(2)}) collective-permute-start(f32[5,4096]{1,0:T(8,128)S(1)} %get-tuple-element.26), channel_id=1, source_target_pairs={{0,127},{1,0},{2,1},{3,2},{4,3},{5,4},{6,5},{7,6},{8,7},{9,8},{10,... | collective-permute-start | bytes 245768 | tf_op jit(solution)/shard_map/ppermute | solution.py:296
  15.8 0.0 copy-done.5
  15.8 0.0 copy-done.6
  15.8 0.8 %fusion.pick_ref = bf16[6,64,64]{2,1,0:T(8,128)(2,1)} fusion(s32[6,64]{1,0:T(8,128)S(1)} %pad_add_fusion), kind=kLoop, calls=%fused_computation.8 | loop fusion | flops 49152 | bytes 50688 | tf_op jit(solution)/shard_map/convert_element_type | solution.py:317
  16.6 0.0 copy-done.7
  16.6 0.7 %copy.37 = s32[2,64]{0,1:T(8,128)} copy(s32[2,64]{1,0:T(2,128)S(1)} %bitcast.24) | data formatting | bytes 1024 | tf_op jit(solution)/shard_map/squeeze | solution.py:318
  17.2 0.2 collective-permute-done
  17.5 0.1 reshape_squeeze.9
  17.6 0.2 convert_reduce_fusion.2
  17.8 0.0 collective-permute-done.2
  17.8 0.1 reshape_squeeze.11
  17.9 0.2 convert_reduce_fusion
  18.1 0.2 collective-permute-done.1
  18.3 0.1 reshape_squeeze.10
  18.4 0.2 convert_reduce_fusion.1
  18.6 0.1 pad_add_fusion.1
  18.7 0.1 select_reduce_fusion
  18.8 0.6 %gather_fusion.3 = f32[64,8]{1,0:T(8,128)S(1)} fusion(f32[76,8]{1,0:T(8,128)S(1)} %pad_maximum_fusion.1, s32[1024]{0:T(1024)S(1)} %pad_clamp_fusion), kind=kCustom, calls=%fused_computation.3 | custom fusion | bytes 4352 | tf_op jit(solution)/shard_map/gather | solution.py:307
  19.4 0.7 %slice_convert_fusion.order_ref = s32[64,1]{1,0:T(8,128)} fusion(f32[64,8]{1,0:T(8,128)S(1)} %gather_fusion.3), kind=kLoop, calls=%fused_computation.13 | loop fusion | flops 64 | bytes 512 | tf_op jit(solution)/shard_map/convert_element_type | solution.py:311
  20.2 0.0 copy-done
  20.2 0.1 pad_maximum_fusion
  20.3 0.0 copy-start.8
  20.3 1.8 %gather_fusion.2 = f32[64,4096]{1,0:T(8,128)} fusion(f32[76,4096]{1,0:T(8,128)S(1)} %pad_maximum_fusion, s32[1024]{0:T(1024)S(1)} %pad_clamp_fusion), kind=kCustom, calls=%fused_computation.2 | custom fusion | bytes 2097408 | tf_op jit(solution)/shard_map/gather | solution.py:319
  22.1 2.5 %shard_map.136 = (f32[64,4096]{1,0:T(8,128)}, f32[64,256]{1,0:T(8,128)}, f32[64,256]{1,0:T(8,128)}) custom-call(f32[64,4096]{1,0:T(8,128)} %gather_fusion.2, s32[1,4096]{1,0:T(1,128)} %constant.82.clone.top_ref, s32[64,1]{1,0:T(8,128)} %slice_convert_fusion.order_ref), custom_call_target="tpu_custom_call" | custom-call | tf_op jit(solution)/shard_map/pallas_call | solution.py:239
  24.6 0.0 collective-permute-start.3
  24.6 5.3 %collective-permute-start.4 = (f32[64,256]{1,0:T(8,128)}, f32[64,256]{1,0:T(8,128)S(1)}, u32[]{:S(2)}, u32[]{:S(2)}) collective-permute-start(f32[64,256]{1,0:T(8,128)} %get-tuple-element.14), channel_id=1, source_target_pairs={{8,0},{16,8},{24,16},{32,24},{40,32},{48,40},{56,48},{64,56},{72,6... | collective-permute-start | bytes 196616 | tf_op jit(solution)/shard_map/ppermute | solution.py:255
  30.0 0.0 copy-done.8
  30.0 0.6 %broadcast_select_fusion.weight_ref = f32[64,8]{1,0:T(8,128)} fusion(f32[64,8]{1,0:T(8,128)S(1)} %gather_fusion.3, pred[8]{0:T(512)(128)(4,1)S(1)} %copy-done.8), kind=kLoop, calls=%fused_computation.16 | loop fusion | flops 512 | bytes 4104 | tf_op jit(solution)/shard_map/concatenate | solution.py:308
  30.6 1.8 %collective-permute-done.3.lower_ref = f32[64,256]{1,0:T(8,128)S(1)} collective-permute-done((f32[64,256]{1,0:T(8,128)}, f32[64,256]{1,0:T(8,128)S(1)}, u32[]{:S(2)}, u32[]{:S(2)}) %collective-permute-start.3) | collective-permute-done | bytes 65568 | tf_op jit(solution)/shard_map/ppermute | solution.py:255
  32.4 0.0 copy-start.3
  32.4 0.0 collective-permute-done.4.upper_ref
  32.4 0.0 copy-start.4
  32.4 0.6 %copy-done.3 = f32[64,256]{1,0:T(8,128)} copy-done((f32[64,256]{1,0:T(8,128)}, f32[64,256]{1,0:T(8,128)S(1)}, u32[]{:S(2)}) %copy-start.3) | copy-done | bytes 65560
  33.0 0.0 copy-done.4
  33.0 7.3 %shard_map.137 = (f32[64,4096]{1,0:T(8,128)}, f32[64,256]{1,0:T(8,128)}, f32[64,256]{1,0:T(8,128)}) custom-call(f32[64,4096]{1,0:T(8,128)} %get-tuple-element.12.v_ref.base_ref, f32[64,4096]{1,0:T(8,128)} %get-tuple-element.12.v_ref.base_ref, s32[1,4096]{1,0:T(1,128)} %constant.82.clone.top_ref, s32[64,1]{1,0:T(8,128)} %slice_convert_fusion.order_ref, ...), custom_call_target="tpu_custom_call" | custom-call | tf_op jit(solution)/shard_map/pallas_call | solution.py:210
  40.4 0.0 collective-permute-start.5
  40.4 5.6 %collective-permute-start.6 = (f32[64,256]{1,0:T(8,128)}, f32[64,256]{1,0:T(8,128)S(1)}, u32[]{:S(2)}, u32[]{:S(2)}) collective-permute-start(f32[64,256]{1,0:T(8,128)} %get-tuple-element.17), channel_id=1, source_target_pairs={{8,0},{16,8},{24,16},{32,24},{40,32},{48,40},{56,48},{64,56},{72,6... | collective-permute-start | bytes 196616 | tf_op jit(solution)/shard_map/ppermute | solution.py:255
  45.9 2.2 %collective-permute-done.5.lower_ref = f32[64,256]{1,0:T(8,128)S(1)} collective-permute-done((f32[64,256]{1,0:T(8,128)}, f32[64,256]{1,0:T(8,128)S(1)}, u32[]{:S(2)}, u32[]{:S(2)}) %collective-permute-start.5) | collective-permute-done | bytes 65568 | tf_op jit(solution)/shard_map/ppermute | solution.py:255
  48.2 0.0 copy-start.1
  48.2 0.0 collective-permute-done.6.upper_ref
  48.2 0.0 copy-start.2
  48.2 0.6 %copy-done.1 = f32[64,256]{1,0:T(8,128)} copy-done((f32[64,256]{1,0:T(8,128)}, f32[64,256]{1,0:T(8,128)S(1)}, u32[]{:S(2)}) %copy-start.1) | copy-done | bytes 65560
  48.8 0.0 copy-done.2
  48.8 7.2 %shard_map.138 = (f32[64,4096]{1,0:T(8,128)}, f32[64,256]{1,0:T(8,128)}, f32[64,256]{1,0:T(8,128)}) custom-call(f32[64,4096]{1,0:T(8,128)} %get-tuple-element.15.v_ref, f32[64,4096]{1,0:T(8,128)} %get-tuple-element.12.v_ref.base_ref, s32[1,4096]{1,0:T(1,128)} %constant.82.clone.top_ref, s32[64,1]{1,0:T(8,128)} %slice_convert_fusion.order_ref, ...), custom_call_target="tpu_custom_call" | custom-call | tf_op jit(solution)/shard_map/pallas_call | solution.py:210
  (15 shorter events, 0.2 us)
Async XLA Ops:
  5.9 9.8 %copy-start.5 = (s32[1,4,64]{2,1,0:T(4,128)S(1)}, s32[1,4,64]{2,1,0:T(4,128)}, u32[]{:S(2)}) copy-start(s32[1,4,64]{2,1,0:T(4,128)} %param.19) | copy-start | bytes 3076
  6.0 9.8 %copy-start.6 = (s32[1,2,64]{2,1,0:T(2,128)S(1)}, s32[1,2,64]{2,1,0:T(2,128)}, u32[]{:S(2)}) copy-start(s32[1,2,64]{2,1,0:T(2,128)} %param.20) | copy-start | bytes 1540
  6.0 10.6 %copy-start.7 = (s32[1,2,64]{2,1,0:T(2,128)S(1)}, s32[1,2,64]{2,1,0:T(2,128)}, u32[]{:S(2)}) copy-start(s32[1,2,64]{2,1,0:T(2,128)} %param.21) | copy-start | bytes 1540
  6.0 14.1 %copy-start = (f32[64,4096]{1,0:T(8,128)S(1)}, f32[64,4096]{1,0:T(8,128)}, u32[]{:S(2)}) copy-start(f32[64,4096]{1,0:T(8,128)} %param.14) | copy-start | bytes 3145732
  6.1 11.3 %collective-permute-start = (f32[5,4096]{1,0:T(8,128)S(1)}, f32[5,4096]{1,0:T(8,128)S(1)}, u32[]{:S(2)}, u32[]{:S(2)}) collective-permute-start(f32[5,4096]{1,0:T(8,128)S(1)} %get-tuple-element.24), channel_id=1, source_target_pairs={{0,1},{1,2},{2,3},{3,4},{4,5},{5,6},{6,7},{7,8},{8,9},{9,10},{10,1... | collective-permute-start | bytes 245768 | tf_op jit(solution)/shard_map/ppermute | solution.py:296
  6.2 11.5 %collective-permute-start.2 = (f32[5,4096]{1,0:T(8,128)S(1)}, f32[5,4096]{1,0:T(8,128)S(1)}, u32[]{:S(2)}, u32[]{:S(2)}) collective-permute-start(f32[5,4096]{1,0:T(8,128)S(1)} %get-tuple-element.25), channel_id=1, source_target_pairs={{0,64},{1,65},{2,66},{3,67},{4,68},{5,69},{6,70},{7,71},{8,72},{9,... | collective-permute-start | bytes 245768 | tf_op jit(solution)/shard_map/ppermute | solution.py:296
  9.6 8.7 %collective-permute-start.1 = (f32[5,4096]{1,0:T(8,128)S(1)}, f32[5,4096]{1,0:T(8,128)S(1)}, u32[]{:S(2)}, u32[]{:S(2)}) collective-permute-start(f32[5,4096]{1,0:T(8,128)S(1)} %get-tuple-element.26), channel_id=1, source_target_pairs={{0,127},{1,0},{2,1},{3,2},{4,3},{5,4},{6,5},{7,6},{8,7},{9,8},{10,... | collective-permute-start | bytes 245768 | tf_op jit(solution)/shard_map/ppermute | solution.py:296
  20.3 9.7 %copy-start.8 = (pred[8]{0:T(512)(128)(4,1)S(1)}, pred[8]{0:T(512)(128)(4,1)}, u32[]{:S(2)}) copy-start(pred[8]{0:T(512)(128)(4,1)} %constant.80.clone.1) | copy-start | bytes 28
  24.6 7.8 %collective-permute-start.3 = (f32[64,256]{1,0:T(8,128)}, f32[64,256]{1,0:T(8,128)S(1)}, u32[]{:S(2)}, u32[]{:S(2)}) collective-permute-start(f32[64,256]{1,0:T(8,128)} %get-tuple-element.13), channel_id=1, source_target_pairs={{0,8},{8,16},{16,24},{24,32},{32,40},{40,48},{48,56},{56,64},{64,7... | collective-permute-start | bytes 196616 | tf_op jit(solution)/shard_map/ppermute | solution.py:255
  24.6 7.8 %collective-permute-start.4 = (f32[64,256]{1,0:T(8,128)}, f32[64,256]{1,0:T(8,128)S(1)}, u32[]{:S(2)}, u32[]{:S(2)}) collective-permute-start(f32[64,256]{1,0:T(8,128)} %get-tuple-element.14), channel_id=1, source_target_pairs={{8,0},{16,8},{24,16},{32,24},{40,32},{48,40},{56,48},{64,56},{72,6... | collective-permute-start | bytes 196616 | tf_op jit(solution)/shard_map/ppermute | solution.py:255
  32.4 0.6 %copy-start.3 = (f32[64,256]{1,0:T(8,128)}, f32[64,256]{1,0:T(8,128)S(1)}, u32[]{:S(2)}) copy-start(f32[64,256]{1,0:T(8,128)S(1)} %collective-permute-done.3.lower_ref) | copy-start | bytes 196612
  32.4 0.6 %copy-start.4 = (f32[64,256]{1,0:T(8,128)}, f32[64,256]{1,0:T(8,128)S(1)}, u32[]{:S(2)}) copy-start(f32[64,256]{1,0:T(8,128)S(1)} %collective-permute-done.4.upper_ref) | copy-start | bytes 196612
  40.4 7.8 %collective-permute-start.5 = (f32[64,256]{1,0:T(8,128)}, f32[64,256]{1,0:T(8,128)S(1)}, u32[]{:S(2)}, u32[]{:S(2)}) collective-permute-start(f32[64,256]{1,0:T(8,128)} %get-tuple-element.16), channel_id=1, source_target_pairs={{0,8},{8,16},{16,24},{24,32},{32,40},{40,48},{48,56},{56,64},{64,7... | collective-permute-start | bytes 196616 | tf_op jit(solution)/shard_map/ppermute | solution.py:255
  40.4 7.8 %collective-permute-start.6 = (f32[64,256]{1,0:T(8,128)}, f32[64,256]{1,0:T(8,128)S(1)}, u32[]{:S(2)}, u32[]{:S(2)}) collective-permute-start(f32[64,256]{1,0:T(8,128)} %get-tuple-element.17), channel_id=1, source_target_pairs={{8,0},{16,8},{24,16},{32,24},{40,32},{48,40},{56,48},{64,56},{72,6... | collective-permute-start | bytes 196616 | tf_op jit(solution)/shard_map/ppermute | solution.py:255
  48.2 0.6 %copy-start.1 = (f32[64,256]{1,0:T(8,128)}, f32[64,256]{1,0:T(8,128)S(1)}, u32[]{:S(2)}) copy-start(f32[64,256]{1,0:T(8,128)S(1)} %collective-permute-done.5.lower_ref) | copy-start | bytes 196612
  48.2 0.6 %copy-start.2 = (f32[64,256]{1,0:T(8,128)}, f32[64,256]{1,0:T(8,128)S(1)}, u32[]{:S(2)}) copy-start(f32[64,256]{1,0:T(8,128)S(1)} %collective-permute-done.6.upper_ref) | copy-start | bytes 196612

commit v3 on v2

--- a/solution.py
+++ b/solution.py
@@ -122,9 +122,8 @@
     return mxu(hi, onehot) + mxu(mid, onehot) + mxu(lo, onehot)
 
 
-def section_body(
-    v_ref, base_ref, top_ref, order_ref, weight_ref, lower_ref, upper_ref, pick_ref, turn_ref,
-    spread_hi_ref, spread_lo_ref, lift_ref, flip_ref, out_ref, even_ref, total_ref, *, scale
+def inner_body(
+    v_ref, weight_ref, pick_ref, spread_hi_ref, spread_lo_ref, lift_ref, partial_ref
 ):
     count = v_ref.shape[0]
     derivative, second, side_signs, weights = mode_tables()
@@ -181,23 +180,35 @@
     lift_mat = lift_ref[...]
     lifted = mxu(jhi, lift_mat) + mxu(jlo, lift_mat)
     even, total = end_traces(slabs)
+    for a in range(P_SIZE):
+        rows = slice(a * count, (a + 1) * count)
+        own_lift = lifted[rows] + float(lift_signs[0, a]) * even + float(lift_signs[1, a]) * total
+        partial_ref[:, a * PLANE : (a + 1) * PLANE] = first[a] + inner[rows] - own_lift
+
+
+def outer_body(
+    partial_ref, base_ref, top_ref, order_ref, lower_ref, upper_ref, pick_ref, turn_ref, flip_ref,
+    out_ref, even_ref, total_ref, *, scale
+):
+    derivative, second, side_signs, weights = mode_tables()
+    lift_signs = (side_signs * weights[None, :]).astype(np.float32)
     codes = turn_ref[...]
     flip = flip_ref[...]
     below = turn(exact_pick(pick_ref[4], lower_ref[...]), codes[:, 0:1], flip)
     above = turn(exact_pick(pick_ref[5], upper_ref[...]), codes[:, 1:2], flip)
-    jump0 = even - below
-    jump1 = total - above
     top = top_ref[...]
     order = order_ref[...]
     news = []
     for a in range(P_SIZE):
-        rows = slice(a * count, (a + 1) * count)
-        volume = first[a] + inner[rows]
-        lift = lifted[rows] + float(lift_signs[0, a]) * jump0 + float(lift_signs[1, a]) * jump1
-        live = top[:, a * PLANE : (a + 1) * PLANE] <= order
-        update = jnp.where(live, volume - lift, 0.0)
-        new = base_ref[:, a * PLANE : (a + 1) * PLANE] + scale * update
-        out_ref[:, a * PLANE : (a + 1) * PLANE] = new
+        lanes = slice(a * PLANE, (a + 1) * PLANE)
+        update = (
+            partial_ref[:, lanes]
+            + float(lift_signs[0, a]) * below
+            + float(lift_signs[1, a]) * above
+        )
+        live = top[:, lanes] <= order
+        new = base_ref[:, lanes] + scale * jnp.where(live, update, 0.0)
+        out_ref[:, lanes] = new
         news.append(new)
     even, total = end_traces(news)
     even_ref[...] = even
@@ -206,18 +217,29 @@
 
 def section(v, base, top, order, weight, lower, upper, picks, codes, tables, scale):
     count = v.shape[0]
+    spread_hi, spread_lo, lift, flip = tables
     spec = pl.BlockSpec(memory_space=pltpu.VMEM)
+    partial = pl.pallas_call(
+        inner_body,
+        out_shape=jax.ShapeDtypeStruct(v.shape, jnp.float32),
+        in_specs=[spec] * 6,
+        out_specs=spec,
+        compiler_params=pltpu.CompilerParams(vmem_limit_bytes=60 * 1024 * 1024),
+        cost_estimate=pl.CostEstimate(
+            flops=2_500_000_000, transcendentals=0, bytes_accessed=4_000_000
+        ),
+    )(v, weight, picks, spread_hi, spread_lo, lift)
+    lower, upper = exchange(*lower) if isinstance(lower, tuple) else (lower, upper)
     return pl.pallas_call(
-        functools.partial(section_body, scale=scale),
+        functools.partial(outer_body, scale=scale),
         out_shape=(
             jax.ShapeDtypeStruct(v.shape, jnp.float32),
             jax.ShapeDtypeStruct((count, PLANE), jnp.float32),
             jax.ShapeDtypeStruct((count, PLANE), jnp.float32),
         ),
-        in_specs=[spec] * 13,
+        in_specs=[spec] * 9,
         out_specs=(spec, spec, spec),
-        compiler_params=pltpu.CompilerParams(vmem_limit_bytes=60 * 1024 * 1024),
-    )(v, base, top, order, weight, lower, upper, picks, codes, *tables)
+    )(partial, base, top, order, lower, upper, picks, codes, flip)
 
 
 def prep_body(placed_ref, top_ref, order_ref, field_ref, even_ref, total_ref):
@@ -317,13 +339,11 @@
     ).astype(jnp.bfloat16)
     codes = partner_turns[0].T
     field, even, total = prep(got_coef[source], top, order)
-    lower, upper = exchange(even, total)
     half, even, total = section(
-        field, field, top, order, weight, lower, upper, picks, codes, tables, 0.5 * TIME_STEP
-    )
-    lower, upper = exchange(even, total)
+        field, field, top, order, weight, (even, total), None, picks, codes, tables, 0.5 * TIME_STEP
+    )
     advanced, _, _ = section(
-        half, field, top, order, weight, lower, upper, picks, codes, tables, TIME_STEP
+        half, field, top, order, weight, (even, total), None, picks, codes, tables, TIME_STEP
     )
     return advanced
 

time: 56.3 us -> 56.9 us (1.011)
  Pallas kernels: 17 us -> 21.2 us
  waiting for transfers between devices: 4.54 us -> 0.48 us
  local copies, waits for them, and re-layouts: 7.62 us -> 8.2 us
    pallas_call x2 -> x4, Pallas kernels: 14.5 us -> 18.7 us  [the longest x2 12 us: section(): pl.pallas_call(inner_body, out_shape=jax.ShapeDtypeStruct(v.shape, jnp.fl...]
    ppermute x4, waiting for transfers between devices: 4.08 us -> 0.01 us  [exchange(): return (lax.ppermute(total, 'dom', up), lax.ppermute(even, 'dom', down))]
    unnamed x18, local copies, waits for them, and re-layouts: 1.31 us -> 1.89 us
  transfers between devices with their start and end apart: 7 -> 7, of which waited for: 4 -> 2; matrix products, arithmetic and copies ran while one was open for 5% -> 4% of each run, Pallas kernels for 0% -> 21%
where the time goes in v3:
time: 56.9 us; the launch traced here: 56.5 us
  Pallas kernels  21.2 us (37%)
  starting transfers between devices  20.3 us (36%)
  local copies, waits for them, and re-layouts  8.2 us (14%)
  other arithmetic  6.15 us (11%)
    pallas_call x2, Pallas kernels, section(): pl.pallas_call(inner_body, out_shape=jax.ShapeDtypeStruct(v.shape, jnp.fl...  12 us
    ppermute x4, starting transfers between devices, exchange(): return (lax.ppermute(total, 'dom', up), lax.ppermute(even, 'dom', down))  10.7 us
    ppermute x3, starting transfers between devices, shards(): arrived = lax.ppermute(parcels[index], ('dom', 'face'), pairs)  9.63 us
    pallas_call x2, Pallas kernels, section(): pl.pallas_call(functools.partial(outer_body, scale=scale), out_shape=(jax...  6.73 us
    pallas_call x1, Pallas kernels, prep(): pl.pallas_call(prep_body, out_shape=(jax.ShapeDtypeStruct(placed.shape, j...  2.47 us
    gather x1, local copies, waits for them, and re-layouts, shards(): coefficients[picked].reshape(len(shifts), moving, P_SIZE ** 3)  1.93 us
    unnamed x18, local copies, waits for them, and re-layouts  1.89 us
    gather x1, local copies, waits for them, and re-layouts, shards(): field, even, total = prep(got_coef[source], top, order)  1.85 us
  transfers between devices with their start and end apart: 7, of which 2 were waited for; matrix products, arithmetic and copies ran while one was open for 4% of the time, Pallas kernels for 21%

profile of v3, /device:TPU:0, one launch (start us, length us, event | category | flops | bytes accessed | tf_op | source)
XLA Modules:
  0.0 56.5 jit_solution(13454500284965757954)
XLA Ops:
  0.0 0.7 %and_select_fusion.1 = s32[3]{0:T(128)S(1)} fusion(s32[3]{0:T(128)} %constant.81.clone, s32[]{:T(128)S(6)} %add.51), kind=kLoop, calls=%fused_computation.33 | loop fusion | flops 36 | bytes 28 | tf_op jit(solution)/shard_map/jit(remainder)/select_n | solution.py:300
  0.7 0.7 %compare_select_fusion.4 = (s32[64]{0:T(128)S(1)}, s32[64]{0:T(128)S(1)}, s32[64]{0:T(128)S(1)}) fusion(s32[]{:T(128)S(6)} %add.51, s32[64]{0:T(128)} %param.18), kind=kLoop, calls=%fused_computation.31 | loop fusion | flops 1344 | bytes 1028 | tf_op jit(solution)/shard_map/jit(_where)/select_n | solution.py:315
  1.3 0.1 fusion.5
  1.4 0.2 reduce_window_sum.11
  1.7 0.1 select_reduce_fusion.1
  1.8 0.1 reshape.106
  1.9 0.7 %convert_bitcast_fusion = (f32[64,1]{0,1:T(1,128)S(1)}, f32[64,1]{0,1:T(1,128)S(1)}) fusion(s32[64]{0:T(128)} %param.17, s32[64]{0:T(128)S(1)} %get-tuple-element.21), kind=kLoop, calls=%fused_computation.47 | loop fusion | flops 448 | bytes 1024 | tf_op jit(solution)/shard_map/convert_element_type | solution.py:294
  2.6 0.7 %pad_maximum_fusion.2 = f32[64,8]{0,1:T(8,128)S(1)} fusion(f32[64,1]{0,1:T(1,128)S(1)} %get-tuple-element.27, f32[64,1]{0,1:T(1,128)S(1)} %get-tuple-element.28, f32[64,3]{0,1:T(4,128)} %param.16, f32[64,3]{0,1:T(4,128)} %param.15), kind=kLoop, calls=%fused_computation.22 | loop fusion | flops 1536 | bytes 4096 | tf_op jit(solution)/shard_map/concatenate | solution.py:289
  3.3 0.1 copy.34
  3.4 0.6 gather_fusion.1
  3.9 0.1 reshape.141
  4.0 1.9 %gather_fusion = f32[12,4096]{1,0:T(8,128)S(1)} fusion(f32[64,4096]{1,0:T(8,128)} %param.14, s32[1024]{0:T(1024)S(1)} %pad_clamp_fusion.1), kind=kCustom, calls=%fused_computation | custom fusion | bytes 393264 | tf_op jit(solution)/shard_map/gather | solution.py:311
  5.9 0.0 copy-start.5
  6.0 0.0 copy-start.6
  6.0 0.0 copy-start.7
  6.0 0.0 copy-start.8
  6.0 0.1 reshape.107
  6.1 0.0 copy-start
  6.2 0.1 collective-permute-start
  6.2 3.4 %collective-permute-start.2 = (f32[5,4096]{1,0:T(8,128)S(1)}, f32[5,4096]{1,0:T(8,128)S(1)}, u32[]{:S(2)}, u32[]{:S(2)}) collective-permute-start(f32[5,4096]{1,0:T(8,128)S(1)} %get-tuple-element.25), channel_id=1, source_target_pairs={{0,64},{1,65},{2,66},{3,67},{4,68},{5,69},{6,70},{7,71},{8,72},{9,... | collective-permute-start | bytes 245768 | tf_op jit(solution)/shard_map/ppermute | solution.py:318
  9.6 6.2 %collective-permute-start.1 = (f32[5,4096]{1,0:T(8,128)S(1)}, f32[5,4096]{1,0:T(8,128)S(1)}, u32[]{:S(2)}, u32[]{:S(2)}) collective-permute-start(f32[5,4096]{1,0:T(8,128)S(1)} %get-tuple-element.26), channel_id=1, source_target_pairs={{0,127},{1,0},{2,1},{3,2},{4,3},{5,4},{6,5},{7,6},{8,7},{9,8},{10,... | collective-permute-start | bytes 245768 | tf_op jit(solution)/shard_map/ppermute | solution.py:318
  15.8 0.0 copy-done.5
  15.8 0.0 copy-done.6
  15.8 0.8 %fusion.pick_ref = bf16[6,64,64]{2,1,0:T(8,128)(2,1)} fusion(s32[6,64]{1,0:T(8,128)S(1)} %pad_add_fusion), kind=kLoop, calls=%fused_computation.8 | loop fusion | flops 49152 | bytes 50688 | tf_op jit(solution)/shard_map/convert_element_type | solution.py:339
  16.6 0.0 copy-done.7
  16.6 0.7 %copy.37 = s32[2,64]{0,1:T(8,128)} copy(s32[2,64]{1,0:T(2,128)S(1)} %bitcast.24) | data formatting | bytes 1024 | tf_op jit(solution)/shard_map/squeeze | solution.py:340
  17.3 0.2 collective-permute-done
  17.5 0.1 reshape_squeeze.9
  17.6 0.2 convert_reduce_fusion.2
  17.8 0.0 collective-permute-done.2
  17.8 0.1 reshape_squeeze.11
  17.9 0.2 convert_reduce_fusion
  18.1 0.2 collective-permute-done.1
  18.3 0.1 reshape_squeeze.10
  18.4 0.2 convert_reduce_fusion.1
  18.6 0.1 pad_add_fusion.1
  18.7 0.1 select_reduce_fusion
  18.8 0.6 %gather_fusion.3 = f32[64,8]{1,0:T(8,128)S(1)} fusion(f32[76,8]{1,0:T(8,128)S(1)} %pad_maximum_fusion.1, s32[1024]{0:T(1024)S(1)} %pad_clamp_fusion), kind=kCustom, calls=%fused_computation.3 | custom fusion | bytes 4352 | tf_op jit(solution)/shard_map/gather | solution.py:329
  19.4 0.7 %slice_convert_fusion.order_ref = s32[64,1]{1,0:T(8,128)} fusion(f32[64,8]{1,0:T(8,128)S(1)} %gather_fusion.3), kind=kLoop, calls=%fused_computation.13 | loop fusion | flops 64 | bytes 512 | tf_op jit(solution)/shard_map/convert_element_type | solution.py:333
  20.1 0.0 copy-done.8
  20.1 0.6 %broadcast_select_fusion.weight_ref = f32[64,8]{1,0:T(8,128)} fusion(f32[64,8]{1,0:T(8,128)S(1)} %gather_fusion.3, pred[8]{0:T(512)(128)(4,1)S(1)} %copy-done.8), kind=kLoop, calls=%fused_computation.16 | loop fusion | flops 512 | bytes 4104 | tf_op jit(solution)/shard_map/concatenate | solution.py:330
  20.8 0.0 copy-done
  20.8 0.1 pad_maximum_fusion
  20.9 1.8 %gather_fusion.2 = f32[64,4096]{1,0:T(8,128)} fusion(f32[76,4096]{1,0:T(8,128)S(1)} %pad_maximum_fusion, s32[1024]{0:T(1024)S(1)} %pad_clamp_fusion), kind=kCustom, calls=%fused_computation.2 | custom fusion | bytes 2097408 | tf_op jit(solution)/shard_map/gather | solution.py:341
  22.8 2.5 %shard_map.136 = (f32[64,4096]{1,0:T(8,128)}, f32[64,256]{1,0:T(8,128)}, f32[64,256]{1,0:T(8,128)}) custom-call(f32[64,4096]{1,0:T(8,128)} %gather_fusion.2, s32[1,4096]{1,0:T(1,128)} %constant.82.clone.top_ref, s32[64,1]{1,0:T(8,128)} %slice_convert_fusion.order_ref), custom_call_target="tpu_custom_call" | custom-call | tf_op jit(solution)/shard_map/pallas_call | solution.py:261
  25.2 0.0 collective-permute-start.3
  25.2 5.3 %collective-permute-start.4 = (f32[64,256]{1,0:T(8,128)}, f32[64,256]{1,0:T(8,128)S(1)}, u32[]{:S(2)}, u32[]{:S(2)}) collective-permute-start(f32[64,256]{1,0:T(8,128)} %get-tuple-element.14), channel_id=1, source_target_pairs={{8,0},{16,8},{24,16},{32,24},{40,32},{48,40},{56,48},{64,56},{72,6... | collective-permute-start | bytes 196616 | tf_op jit(solution)/shard_map/ppermute | solution.py:277
  30.6 6.0 %shard_map.137.partial_ref = f32[64,4096]{1,0:T(8,128)} custom-call(f32[64,4096]{1,0:T(8,128)} %get-tuple-element.12.v_ref.base_ref, f32[64,8]{1,0:T(8,128)} %broadcast_select_fusion.weight_ref, bf16[6,64,64]{2,1,0:T(8,128)(2,1)} %fusion.pick_ref, bf16[256,1280]{1,0:T(8,128)(2,1)} %constant.83.clone.spread_hi_ref, ...), custom_call_target="tpu_custom_call" | custom-call | flops 2500000000 | bytes 4000000 | tf_op jit(solution)/shard_map/pallas_call | solution.py:222
  36.5 0.0 collective-permute-done.3.lower_ref
  36.5 0.0 copy-start.3
  36.5 0.0 collective-permute-done.4.upper_ref
  36.5 0.0 copy-start.4
  36.6 0.6 %copy-done.3 = f32[64,256]{1,0:T(8,128)} copy-done((f32[64,256]{1,0:T(8,128)}, f32[64,256]{1,0:T(8,128)S(1)}, u32[]{:S(2)}) %copy-start.3) | copy-done | bytes 65560
  37.2 0.0 copy-done.4
  37.2 3.4 %shard_map.138 = (f32[64,4096]{1,0:T(8,128)}, f32[64,256]{1,0:T(8,128)}, f32[64,256]{1,0:T(8,128)}) custom-call(f32[64,4096]{1,0:T(8,128)} %shard_map.137.partial_ref, f32[64,4096]{1,0:T(8,128)} %get-tuple-element.12.v_ref.base_ref, s32[1,4096]{1,0:T(1,128)} %constant.82.clone.top_ref, s32[64,1]{1,0:T(8,128)} %slice_convert_fusion.order_ref, ...), custom_call_target="tpu_custom_call" | custom-call | tf_op jit(solution)/shard_map/pallas_call | solution.py:233
  40.6 0.0 collective-permute-start.5
  40.6 5.3 %collective-permute-start.6 = (f32[64,256]{1,0:T(8,128)}, f32[64,256]{1,0:T(8,128)S(1)}, u32[]{:S(2)}, u32[]{:S(2)}) collective-permute-start(f32[64,256]{1,0:T(8,128)} %get-tuple-element.17), channel_id=1, source_target_pairs={{8,0},{16,8},{24,16},{32,24},{40,32},{48,40},{56,48},{64,56},{72,6... | collective-permute-start | bytes 196616 | tf_op jit(solution)/shard_map/ppermute | solution.py:277
  45.9 6.0 %shard_map.139.partial_ref = f32[64,4096]{1,0:T(8,128)} custom-call(f32[64,4096]{1,0:T(8,128)} %get-tuple-element.15.v_ref, f32[64,8]{1,0:T(8,128)} %broadcast_select_fusion.weight_ref, bf16[6,64,64]{2,1,0:T(8,128)(2,1)} %fusion.pick_ref, bf16[256,1280]{1,0:T(8,128)(2,1)} %constant.83.clone.spread_hi_ref, bf16[256,512]{1,0:T(8,128)(2,1)} %constant.84.clone.spread_lo_ref, ...), custom_call_target="tpu_custom_call" | custom-call | flops 2500000000 | bytes 4000000 | tf_op jit(solution)/shard_map/pallas_call | solution.py:222
  51.9 0.0 collective-permute-done.5.lower_ref
  51.9 0.0 copy-start.1
  51.9 0.0 collective-permute-done.6.upper_ref
  51.9 0.6 %copy-done.1 = f32[64,256]{1,0:T(8,128)} copy-done((f32[64,256]{1,0:T(8,128)}, f32[64,256]{1,0:T(8,128)S(1)}, u32[]{:S(2)}) %copy-start.1) | copy-done | bytes 65560
  52.6 0.6 %copy-done.2 = f32[64,256]{1,0:T(8,128)} copy-done((f32[64,256]{1,0:T(8,128)}, f32[64,256]{1,0:T(8,128)S(1)}, u32[]{:S(2)}) %copy-start.2) | copy-done | bytes 65560
  53.2 3.3 %shard_map.140 = (f32[64,4096]{1,0:T(8,128)}, f32[64,256]{1,0:T(8,128)}, f32[64,256]{1,0:T(8,128)}) custom-call(f32[64,4096]{1,0:T(8,128)} %shard_map.139.partial_ref, f32[64,4096]{1,0:T(8,128)} %get-tuple-element.12.v_ref.base_ref, s32[1,4096]{1,0:T(1,128)} %constant.82.clone.top_ref, s32[64,1]{1,0:T(8,128)} %slice_convert_fusion.order_ref, ...), custom_call_target="tpu_custom_call" | custom-call | tf_op jit(solution)/shard_map/pallas_call | solution.py:233
  (16 shorter events, 0.2 us)
Async XLA Ops:
  5.9 9.9 %copy-start.5 = (s32[1,4,64]{2,1,0:T(4,128)S(1)}, s32[1,4,64]{2,1,0:T(4,128)}, u32[]{:S(2)}) copy-start(s32[1,4,64]{2,1,0:T(4,128)} %param.19) | copy-start | bytes 3076
  6.0 9.8 %copy-start.6 = (s32[1,2,64]{2,1,0:T(2,128)S(1)}, s32[1,2,64]{2,1,0:T(2,128)}, u32[]{:S(2)}) copy-start(s32[1,2,64]{2,1,0:T(2,128)} %param.20) | copy-start | bytes 1540
  6.0 10.6 %copy-start.7 = (s32[1,2,64]{2,1,0:T(2,128)S(1)}, s32[1,2,64]{2,1,0:T(2,128)}, u32[]{:S(2)}) copy-start(s32[1,2,64]{2,1,0:T(2,128)} %param.21) | copy-start | bytes 1540
  6.0 14.1 %copy-start.8 = (pred[8]{0:T(512)(128)(4,1)S(1)}, pred[8]{0:T(512)(128)(4,1)}, u32[]{:S(2)}) copy-start(pred[8]{0:T(512)(128)(4,1)} %constant.80.clone.1) | copy-start | bytes 28
  6.1 14.7 %copy-start = (f32[64,4096]{1,0:T(8,128)S(1)}, f32[64,4096]{1,0:T(8,128)}, u32[]{:S(2)}) copy-start(f32[64,4096]{1,0:T(8,128)} %param.14) | copy-start | bytes 3145732
  6.2 11.3 %collective-permute-start = (f32[5,4096]{1,0:T(8,128)S(1)}, f32[5,4096]{1,0:T(8,128)S(1)}, u32[]{:S(2)}, u32[]{:S(2)}) collective-permute-start(f32[5,4096]{1,0:T(8,128)S(1)} %get-tuple-element.24), channel_id=1, source_target_pairs={{0,1},{1,2},{2,3},{3,4},{4,5},{5,6},{6,7},{7,8},{8,9},{9,10},{10,1... | collective-permute-start | bytes 245768 | tf_op jit(solution)/shard_map/ppermute | solution.py:318
  6.2 11.5 %collective-permute-start.2 = (f32[5,4096]{1,0:T(8,128)S(1)}, f32[5,4096]{1,0:T(8,128)S(1)}, u32[]{:S(2)}, u32[]{:S(2)}) collective-permute-start(f32[5,4096]{1,0:T(8,128)S(1)} %get-tuple-element.25), channel_id=1, source_target_pairs={{0,64},{1,65},{2,66},{3,67},{4,68},{5,69},{6,70},{7,71},{8,72},{9,... | collective-permute-start | bytes 245768 | tf_op jit(solution)/shard_map/ppermute | solution.py:318
  9.6 8.7 %collective-permute-start.1 = (f32[5,4096]{1,0:T(8,128)S(1)}, f32[5,4096]{1,0:T(8,128)S(1)}, u32[]{:S(2)}, u32[]{:S(2)}) collective-permute-start(f32[5,4096]{1,0:T(8,128)S(1)} %get-tuple-element.26), channel_id=1, source_target_pairs={{0,127},{1,0},{2,1},{3,2},{4,3},{5,4},{6,5},{7,6},{8,7},{9,8},{10,... | collective-permute-start | bytes 245768 | tf_op jit(solution)/shard_map/ppermute | solution.py:318
  25.2 11.3 %collective-permute-start.3 = (f32[64,256]{1,0:T(8,128)}, f32[64,256]{1,0:T(8,128)S(1)}, u32[]{:S(2)}, u32[]{:S(2)}) collective-permute-start(f32[64,256]{1,0:T(8,128)} %get-tuple-element.13), channel_id=1, source_target_pairs={{0,8},{8,16},{16,24},{24,32},{32,40},{40,48},{48,56},{56,64},{64,7... | collective-permute-start | bytes 196616 | tf_op jit(solution)/shard_map/ppermute | solution.py:277
  25.2 11.3 %collective-permute-start.4 = (f32[64,256]{1,0:T(8,128)}, f32[64,256]{1,0:T(8,128)S(1)}, u32[]{:S(2)}, u32[]{:S(2)}) collective-permute-start(f32[64,256]{1,0:T(8,128)} %get-tuple-element.14), channel_id=1, source_target_pairs={{8,0},{16,8},{24,16},{32,24},{40,32},{48,40},{56,48},{64,56},{72,6... | collective-permute-start | bytes 196616 | tf_op jit(solution)/shard_map/ppermute | solution.py:277
  36.5 0.6 %copy-start.3 = (f32[64,256]{1,0:T(8,128)}, f32[64,256]{1,0:T(8,128)S(1)}, u32[]{:S(2)}) copy-start(f32[64,256]{1,0:T(8,128)S(1)} %collective-permute-done.3.lower_ref) | copy-start | bytes 196612
  36.5 0.6 %copy-start.4 = (f32[64,256]{1,0:T(8,128)}, f32[64,256]{1,0:T(8,128)S(1)}, u32[]{:S(2)}) copy-start(f32[64,256]{1,0:T(8,128)S(1)} %collective-permute-done.4.upper_ref) | copy-start | bytes 196612
  40.6 11.4 %collective-permute-start.5 = (f32[64,256]{1,0:T(8,128)}, f32[64,256]{1,0:T(8,128)S(1)}, u32[]{:S(2)}, u32[]{:S(2)}) collective-permute-start(f32[64,256]{1,0:T(8,128)} %get-tuple-element.16), channel_id=1, source_target_pairs={{0,8},{8,16},{16,24},{24,32},{32,40},{40,48},{48,56},{56,64},{64,7... | collective-permute-start | bytes 196616 | tf_op jit(solution)/shard_map/ppermute | solution.py:277
  40.6 11.4 %collective-permute-start.6 = (f32[64,256]{1,0:T(8,128)}, f32[64,256]{1,0:T(8,128)S(1)}, u32[]{:S(2)}, u32[]{:S(2)}) collective-permute-start(f32[64,256]{1,0:T(8,128)} %get-tuple-element.17), channel_id=1, source_target_pairs={{8,0},{16,8},{24,16},{32,24},{40,32},{48,40},{56,48},{64,56},{72,6... | collective-permute-start | bytes 196616 | tf_op jit(solution)/shard_map/ppermute | solution.py:277
  51.9 0.6 %copy-start.1 = (f32[64,256]{1,0:T(8,128)}, f32[64,256]{1,0:T(8,128)S(1)}, u32[]{:S(2)}) copy-start(f32[64,256]{1,0:T(8,128)S(1)} %collective-permute-done.5.lower_ref) | copy-start | bytes 196612
  52.6 0.6 %copy-start.2 = (f32[64,256]{1,0:T(8,128)}, f32[64,256]{1,0:T(8,128)S(1)}, u32[]{:S(2)}) copy-start(f32[64,256]{1,0:T(8,128)S(1)} %collective-permute-done.6.upper_ref) | copy-start | bytes 196612

commit v4 on v3

--- a/solution.py
+++ b/solution.py
@@ -122,9 +122,12 @@
     return mxu(hi, onehot) + mxu(mid, onehot) + mxu(lo, onehot)
 
 
-def inner_body(
-    v_ref, weight_ref, pick_ref, spread_hi_ref, spread_lo_ref, lift_ref, partial_ref
-):
+def inner_body(v_ref, *refs, scale, shared):
+    if shared:
+        base_ref = v_ref
+        weight_ref, top_ref, pick_ref, spread_hi_ref, spread_lo_ref, lift_ref, partial_ref = refs
+    else:
+        base_ref, weight_ref, top_ref, pick_ref, spread_hi_ref, spread_lo_ref, lift_ref, partial_ref = refs
     count = v_ref.shape[0]
     derivative, second, side_signs, weights = mode_tables()
     second = second.astype(np.float32)
@@ -180,14 +183,19 @@
     lift_mat = lift_ref[...]
     lifted = mxu(jhi, lift_mat) + mxu(jlo, lift_mat)
     even, total = end_traces(slabs)
+    top = top_ref[...]
+    order = weight[:, 7:8]
     for a in range(P_SIZE):
         rows = slice(a * count, (a + 1) * count)
+        lanes = slice(a * PLANE, (a + 1) * PLANE)
         own_lift = lifted[rows] + float(lift_signs[0, a]) * even + float(lift_signs[1, a]) * total
-        partial_ref[:, a * PLANE : (a + 1) * PLANE] = first[a] + inner[rows] - own_lift
+        live = top[:, lanes] <= order
+        update = jnp.where(live, first[a] + inner[rows] - own_lift, 0.0)
+        partial_ref[:, lanes] = base_ref[:, lanes] + scale * update
 
 
 def outer_body(
-    partial_ref, base_ref, top_ref, order_ref, lower_ref, upper_ref, pick_ref, turn_ref, flip_ref,
+    pre_ref, top_ref, weight_ref, lower_ref, upper_ref, pick_ref, turn_ref, flip_ref,
     out_ref, even_ref, total_ref, *, scale
 ):
     derivative, second, side_signs, weights = mode_tables()
@@ -197,17 +205,13 @@
     below = turn(exact_pick(pick_ref[4], lower_ref[...]), codes[:, 0:1], flip)
     above = turn(exact_pick(pick_ref[5], upper_ref[...]), codes[:, 1:2], flip)
     top = top_ref[...]
-    order = order_ref[...]
+    order = weight_ref[:, 7:8]
     news = []
     for a in range(P_SIZE):
         lanes = slice(a * PLANE, (a + 1) * PLANE)
-        update = (
-            partial_ref[:, lanes]
-            + float(lift_signs[0, a]) * below
-            + float(lift_signs[1, a]) * above
-        )
+        update = float(lift_signs[0, a]) * below + float(lift_signs[1, a]) * above
         live = top[:, lanes] <= order
-        new = base_ref[:, lanes] + scale * jnp.where(live, update, 0.0)
+        new = pre_ref[:, lanes] + scale * jnp.where(live, update, 0.0)
         out_ref[:, lanes] = new
         news.append(new)
     even, total = end_traces(news)
@@ -215,21 +219,23 @@
     total_ref[...] = total
 
 
-def section(v, base, top, order, weight, lower, upper, picks, codes, tables, scale):
+def section(v, base, top, weight, ends, picks, codes, tables, scale):
     count = v.shape[0]
     spread_hi, spread_lo, lift, flip = tables
     spec = pl.BlockSpec(memory_space=pltpu.VMEM)
-    partial = pl.pallas_call(
-        inner_body,
+    shared = base is None
+    operands = (v,) + (() if shared else (base,)) + (weight, top, picks, spread_hi, spread_lo, lift)
+    pre = pl.pallas_call(
+        functools.partial(inner_body, scale=scale, shared=shared),
         out_shape=jax.ShapeDtypeStruct(v.shape, jnp.float32),
-        in_specs=[spec] * 6,
+        in_specs=[spec] * len(operands),
         out_specs=spec,
         compiler_params=pltpu.CompilerParams(vmem_limit_bytes=60 * 1024 * 1024),
         cost_estimate=pl.CostEstimate(
             flops=2_500_000_000, transcendentals=0, bytes_accessed=4_000_000
         ),
-    )(v, weight, picks, spread_hi, spread_lo, lift)
-    lower, upper = exchange(*lower) if isinstance(lower, tuple) else (lower, upper)
+    )(*operands)
+    lower, upper = exchange(*ends)
     return pl.pallas_call(
         functools.partial(outer_body, scale=scale),
         out_shape=(
@@ -237,16 +243,16 @@
             jax.ShapeDtypeStruct((count, PLANE), jnp.float32),
             jax.ShapeDtypeStruct((count, PLANE), jnp.float32),
         ),
-        in_specs=[spec] * 9,
+        in_specs=[spec] * 8,
         out_specs=(spec, spec, spec),
-    )(partial, base, top, order, lower, upper, picks, codes, flip)
-
-
-def prep_body(placed_ref, top_ref, order_ref, field_ref, even_ref, total_ref):
+    )(pre, top, weight, lower, upper, picks, codes, flip)
+
+
+def prep_body(placed_ref, top_ref, weight_ref, field_ref, even_ref, total_ref):
     news = []
     for a in range(P_SIZE):
         lanes = slice(a * PLANE, (a + 1) * PLANE)
-        live = top_ref[:, lanes] <= order_ref[...]
+        live = top_ref[:, lanes] <= weight_ref[:, 7:8]
         new = jnp.where(live, placed_ref[:, lanes], 0.0)
         field_ref[:, lanes] = new
         news.append(new)
@@ -255,7 +261,7 @@
     total_ref[...] = total
 
 
-def prep(placed, top, order):
+def prep(placed, top, weight):
     count = placed.shape[0]
     spec = pl.BlockSpec(memory_space=pltpu.VMEM)
     return pl.pallas_call(
@@ -267,7 +273,7 @@
         ),
         in_specs=[spec] * 3,
         out_specs=(spec, spec, spec),
-    )(placed, top, order)
+    )(placed, top, weight)
 
 
 def exchange(even, total):
@@ -327,23 +333,20 @@
     got_rows = jnp.arange(got_slot.shape[0], dtype=jnp.int32)
     source = jnp.sum(jnp.where(hit, got_rows[None, :], 0), axis=1)
     placed_side = got_side[source]
-    weight = jnp.concatenate(
-        [placed_side[:, 0:6], jnp.zeros((element_count, 2), jnp.float32)], axis=1
-    )
-    order = placed_side[:, 7:8].astype(jnp.int32)
-    top = jnp.asarray(top_modes())
+    weight = placed_side
+    top = jnp.asarray(top_modes().astype(np.float32))
     tables = kernel_tables()
     neighbours = jnp.concatenate([local_faces[0], partner_faces[0]], axis=0)
     picks = (
         neighbours[:, :, None] == jnp.arange(element_count, dtype=jnp.int32)[None, None, :]
     ).astype(jnp.bfloat16)
     codes = partner_turns[0].T
-    field, even, total = prep(got_coef[source], top, order)
+    field, even, total = prep(got_coef[source], top, weight)
     half, even, total = section(
-        field, field, top, order, weight, (even, total), None, picks, codes, tables, 0.5 * TIME_STEP
+        field, None, top, weight, (even, total), picks, codes, tables, 0.5 * TIME_STEP
     )
     advanced, _, _ = section(
-        half, field, top, order, weight, (even, total), None, picks, codes, tables, TIME_STEP
+        half, field, top, weight, (even, total), picks, codes, tables, TIME_STEP
     )
     return advanced
 

time: 56.9 us -> 56 us (0.984)
  other arithmetic: 6.15 us -> 4.85 us
  local copies, waits for them, and re-layouts: 8.2 us -> 8.77 us
    convert_element_type x1 -> x0, other arithmetic: 0.68 us -> none  [shards(): order = placed_side[:, 7:8].astype(jnp.int32)]
    pallas_call x2, Pallas kernels: 6.73 us -> 6.11 us  [section(): pl.pallas_call(functools.partial(outer_body, scale=scale), out_shape=(jax...]
    concatenate x1 -> x0, other arithmetic: 0.61 us -> none  [shards(): jnp.concatenate([placed_side[:, 0:6], jnp.zeros((element_count, 2), jnp.f...]
    gather x1, local copies, waits for them, and re-layouts: 0.6 us -> 1.18 us  [shards(): placed_side = got_side[source]]
    unnamed x18 -> x16, local copies, waits for them, and re-layouts: 1.89 us -> 1.87 us
  transfers between devices with their start and end apart: 7 -> 7, of which waited for: 2 -> 2; matrix products, arithmetic and copies ran while one was open for 4% -> 4% of each run, Pallas kernels for 21% -> 22%
where the time goes in v4:
time: 56 us; the launch traced here: 55.7 us
  Pallas kernels  21.1 us (38%)
  starting transfers between devices  20.3 us (36%)
  local copies, waits for them, and re-layouts  8.77 us (16%)
  other arithmetic  4.85 us (9%)
    pallas_call x2, Pallas kernels, section(): pl.pallas_call(functools.partial(inner_body, scale=scale, shared=shared),...  12.4 us
    ppermute x4, starting transfers between devices, exchange(): return (lax.ppermute(total, 'dom', up), lax.ppermute(even, 'dom', down))  10.7 us
    ppermute x3, starting transfers between devices, shards(): arrived = lax.ppermute(parcels[index], ('dom', 'face'), pairs)  9.63 us
    pallas_call x2, Pallas kernels, section(): pl.pallas_call(functools.partial(outer_body, scale=scale), out_shape=(jax...  6.11 us
    pallas_call x1, Pallas kernels, prep(): pl.pallas_call(prep_body, out_shape=(jax.ShapeDtypeStruct(placed.shape, j...  2.55 us
    gather x1, local copies, waits for them, and re-layouts, shards(): coefficients[picked].reshape(len(shifts), moving, P_SIZE ** 3)  1.93 us
    unnamed x16, local copies, waits for them, and re-layouts  1.87 us
    gather x1, local copies, waits for them, and re-layouts, shards(): field, even, total = prep(got_coef[source], top, weight)  1.85 us
  transfers between devices with their start and end apart: 7, of which 2 were waited for; matrix products, arithmetic and copies ran while one was open for 4% of the time, Pallas kernels for 22%

profile of v4, /device:TPU:0, one launch (start us, length us, event | category | flops | bytes accessed | tf_op | source)
XLA Modules:
  0.0 55.7 jit_solution(12668783286467133788)
XLA Ops:
  0.0 0.7 %and_select_fusion.1 = s32[3]{0:T(128)S(1)} fusion(s32[3]{0:T(128)} %constant.78.clone, s32[]{:T(128)S(6)} %add.51), kind=kLoop, calls=%fused_computation.31 | loop fusion | flops 36 | bytes 28 | tf_op jit(solution)/shard_map/jit(remainder)/select_n | solution.py:306
  0.7 0.7 %compare_select_fusion.4 = (s32[64]{0:T(128)S(1)}, s32[64]{0:T(128)S(1)}, s32[64]{0:T(128)S(1)}) fusion(s32[]{:T(128)S(6)} %add.51, s32[64]{0:T(128)} %param.18), kind=kLoop, calls=%fused_computation.29 | loop fusion | flops 1344 | bytes 1028 | tf_op jit(solution)/shard_map/jit(_where)/select_n | solution.py:321
  1.3 0.1 fusion.5
  1.4 0.2 reduce_window_sum.11
  1.7 0.1 select_reduce_fusion.1
  1.8 0.1 reshape.106
  1.9 0.7 %convert_bitcast_fusion = (f32[64,1]{0,1:T(1,128)S(1)}, f32[64,1]{0,1:T(1,128)S(1)}) fusion(s32[64]{0:T(128)} %param.17, s32[64]{0:T(128)S(1)} %get-tuple-element.21), kind=kLoop, calls=%fused_computation.45 | loop fusion | flops 448 | bytes 1024 | tf_op jit(solution)/shard_map/convert_element_type | solution.py:300
  2.6 0.7 %pad_maximum_fusion.2 = f32[64,8]{0,1:T(8,128)S(1)} fusion(f32[64,1]{0,1:T(1,128)S(1)} %get-tuple-element.27, f32[64,1]{0,1:T(1,128)S(1)} %get-tuple-element.28, f32[64,3]{0,1:T(4,128)} %param.16, f32[64,3]{0,1:T(4,128)} %param.15), kind=kLoop, calls=%fused_computation.20 | loop fusion | flops 1536 | bytes 4096 | tf_op jit(solution)/shard_map/concatenate | solution.py:295
  3.3 0.1 copy.34
  3.4 0.6 gather_fusion.1
  3.9 0.1 reshape.141
  4.0 1.9 %gather_fusion = f32[12,4096]{1,0:T(8,128)S(1)} fusion(f32[64,4096]{1,0:T(8,128)} %param.14, s32[1024]{0:T(1024)S(1)} %pad_clamp_fusion.1), kind=kCustom, calls=%fused_computation | custom fusion | bytes 393264 | tf_op jit(solution)/shard_map/gather | solution.py:317
  5.9 0.0 copy-start.5
  6.0 0.0 copy-start.6
  6.0 0.0 copy-start.7
  6.0 0.0 copy-start
  6.0 0.1 reshape.107
  6.1 0.1 collective-permute-start
  6.2 3.4 %collective-permute-start.2 = (f32[5,4096]{1,0:T(8,128)S(1)}, f32[5,4096]{1,0:T(8,128)S(1)}, u32[]{:S(2)}, u32[]{:S(2)}) collective-permute-start(f32[5,4096]{1,0:T(8,128)S(1)} %get-tuple-element.25), channel_id=1, source_target_pairs={{0,64},{1,65},{2,66},{3,67},{4,68},{5,69},{6,70},{7,71},{8,72},{9,... | collective-permute-start | bytes 245768 | tf_op jit(solution)/shard_map/ppermute | solution.py:324
  9.6 6.2 %collective-permute-start.1 = (f32[5,4096]{1,0:T(8,128)S(1)}, f32[5,4096]{1,0:T(8,128)S(1)}, u32[]{:S(2)}, u32[]{:S(2)}) collective-permute-start(f32[5,4096]{1,0:T(8,128)S(1)} %get-tuple-element.26), channel_id=1, source_target_pairs={{0,127},{1,0},{2,1},{3,2},{4,3},{5,4},{6,5},{7,6},{8,7},{9,8},{10,... | collective-permute-start | bytes 245768 | tf_op jit(solution)/shard_map/ppermute | solution.py:324
  15.8 0.0 copy-done.5
  15.8 0.0 copy-done.6
  15.8 0.8 %fusion.refs_2_.pick_ref.refs_3_ = bf16[6,64,64]{2,1,0:T(8,128)(2,1)} fusion(s32[6,64]{1,0:T(8,128)S(1)} %pad_add_fusion), kind=kLoop, calls=%fused_computation.8 | loop fusion | flops 49152 | bytes 50688 | tf_op jit(solution)/shard_map/convert_element_type | solution.py:342
  16.6 0.0 copy-done.7
  16.6 0.7 %copy.37 = s32[2,64]{0,1:T(8,128)} copy(s32[2,64]{1,0:T(2,128)S(1)} %bitcast.24) | data formatting | bytes 1024 | tf_op jit(solution)/shard_map/squeeze | solution.py:343
  17.2 0.2 collective-permute-done
  17.5 0.1 reshape_squeeze.9
  17.6 0.2 convert_reduce_fusion.2
  17.8 0.0 collective-permute-done.2
  17.8 0.1 reshape_squeeze.11
  17.9 0.2 convert_reduce_fusion
  18.1 0.2 collective-permute-done.1
  18.3 0.1 reshape_squeeze.10
  18.4 0.2 convert_reduce_fusion.1
  18.6 0.1 pad_add_fusion.1
  18.7 0.1 select_reduce_fusion
  18.8 1.2 %gather_fusion.3 = f32[64,8]{1,0:T(8,128)} fusion(f32[76,8]{1,0:T(8,128)S(1)} %pad_maximum_fusion.1, s32[1024]{0:T(1024)S(1)} %pad_clamp_fusion), kind=kCustom, calls=%fused_computation.3 | custom fusion | bytes 4352 | tf_op jit(solution)/shard_map/gather | solution.py:335
  20.1 0.0 copy-done
  20.1 0.1 pad_maximum_fusion
  20.2 1.8 %gather_fusion.2 = f32[64,4096]{1,0:T(8,128)} fusion(f32[76,4096]{1,0:T(8,128)S(1)} %pad_maximum_fusion, s32[1024]{0:T(1024)S(1)} %pad_clamp_fusion), kind=kCustom, calls=%fused_computation.2 | custom fusion | bytes 2097408 | tf_op jit(solution)/shard_map/gather | solution.py:344
  22.0 2.6 %shard_map.136 = (f32[64,4096]{1,0:T(8,128)}, f32[64,256]{1,0:T(8,128)}, f32[64,256]{1,0:T(8,128)}) custom-call(f32[64,4096]{1,0:T(8,128)} %gather_fusion.2, f32[1,4096]{1,0:T(1,128)} %constant.79.clone.top_ref.refs_1_.refs_2_, f32[64,8]{1,0:T(8,128)} %gather_fusion.3), custom_call_target="tpu_custom_call" | custom-call | tf_op jit(solution)/shard_map/pallas_call | solution.py:267
  24.6 0.0 collective-permute-start.3
  24.6 5.3 %collective-permute-start.4 = (f32[64,256]{1,0:T(8,128)}, f32[64,256]{1,0:T(8,128)S(1)}, u32[]{:S(2)}, u32[]{:S(2)}) collective-permute-start(f32[64,256]{1,0:T(8,128)} %get-tuple-element.14), channel_id=1, source_target_pairs={{8,0},{16,8},{24,16},{32,24},{40,32},{48,40},{56,48},{64,56},{72,6... | collective-permute-start | bytes 196616 | tf_op jit(solution)/shard_map/ppermute | solution.py:283
  29.9 6.1 %shard_map.137.pre_ref = f32[64,4096]{1,0:T(8,128)} custom-call(f32[64,4096]{1,0:T(8,128)} %get-tuple-element.12.v_ref.refs_0_, f32[64,8]{1,0:T(8,128)} %gather_fusion.3, f32[1,4096]{1,0:T(1,128)} %constant.79.clone.top_ref.refs_1_.refs_2_, bf16[6,64,64]{2,1,0:T(8,128)(2,1)} %fusion.refs_2_.pick_ref.refs_3_, ...), custom_call_target="tpu_custom_call" | custom-call | flops 2500000000 | bytes 4000000 | tf_op jit(solution)/shard_map/pallas_call | solution.py:228
  36.0 0.0 collective-permute-done.3.lower_ref
  36.0 0.0 copy-start.3
  36.0 0.0 collective-permute-done.4.upper_ref
  36.0 0.0 copy-start.4
  36.0 0.6 %copy-done.3 = f32[64,256]{1,0:T(8,128)} copy-done((f32[64,256]{1,0:T(8,128)}, f32[64,256]{1,0:T(8,128)S(1)}, u32[]{:S(2)}) %copy-start.3) | copy-done | bytes 65560
  36.6 0.0 copy-done.4
  36.7 3.1 %shard_map.138 = (f32[64,4096]{1,0:T(8,128)}, f32[64,256]{1,0:T(8,128)}, f32[64,256]{1,0:T(8,128)}) custom-call(f32[64,4096]{1,0:T(8,128)} %shard_map.137.pre_ref, f32[1,4096]{1,0:T(1,128)} %constant.79.clone.top_ref.refs_1_.refs_2_, f32[64,8]{1,0:T(8,128)} %gather_fusion.3, f32[64,256]{1,0:T(8,128)} %copy-done.3, f32[64,256]{1,0:T(8,128)} %copy-done.4, ...), custom_call_target="tpu_custom_call" | custom-call | tf_op jit(solution)/shard_map/pallas_call | solution.py:239
  39.7 0.0 collective-permute-start.5
  39.7 5.3 %collective-permute-start.6 = (f32[64,256]{1,0:T(8,128)}, f32[64,256]{1,0:T(8,128)S(1)}, u32[]{:S(2)}, u32[]{:S(2)}) collective-permute-start(f32[64,256]{1,0:T(8,128)} %get-tuple-element.17), channel_id=1, source_target_pairs={{8,0},{16,8},{24,16},{32,24},{40,32},{48,40},{56,48},{64,56},{72,6... | collective-permute-start | bytes 196616 | tf_op jit(solution)/shard_map/ppermute | solution.py:283
  45.1 6.4 %shard_map.139.pre_ref = f32[64,4096]{1,0:T(8,128)} custom-call(f32[64,4096]{1,0:T(8,128)} %get-tuple-element.15.v_ref, f32[64,4096]{1,0:T(8,128)} %get-tuple-element.12.v_ref.refs_0_, f32[64,8]{1,0:T(8,128)} %gather_fusion.3, f32[1,4096]{1,0:T(1,128)} %constant.79.clone.top_ref.refs_1_.refs_2_, bf16[6,64,64]{2,1,0:T(8,128)(2,1)} %fusion.refs_2_.pick_ref.refs_3_, ...), custom_call_target="tpu_custom_call" | custom-call | flops 2500000000 | bytes 4000000 | tf_op jit(solution)/shard_map/pallas_call | solution.py:228
  51.4 0.0 collective-permute-done.5.lower_ref
  51.4 0.0 copy-start.1
  51.4 0.0 collective-permute-done.6.upper_ref
  51.4 0.6 %copy-done.1 = f32[64,256]{1,0:T(8,128)} copy-done((f32[64,256]{1,0:T(8,128)}, f32[64,256]{1,0:T(8,128)S(1)}, u32[]{:S(2)}) %copy-start.1) | copy-done | bytes 65560
  52.1 0.0 copy-start.2
  52.1 0.6 %copy-done.2 = f32[64,256]{1,0:T(8,128)} copy-done((f32[64,256]{1,0:T(8,128)}, f32[64,256]{1,0:T(8,128)S(1)}, u32[]{:S(2)}) %copy-start.2) | copy-done | bytes 65560
  52.7 3.0 %shard_map.140 = (f32[64,4096]{1,0:T(8,128)}, f32[64,256]{1,0:T(8,128)}, f32[64,256]{1,0:T(8,128)}) custom-call(f32[64,4096]{1,0:T(8,128)} %shard_map.139.pre_ref, f32[1,4096]{1,0:T(1,128)} %constant.79.clone.top_ref.refs_1_.refs_2_, f32[64,8]{1,0:T(8,128)} %gather_fusion.3, f32[64,256]{1,0:T(8,128)} %copy-done.1, f32[64,256]{1,0:T(8,128)} %copy-done.2, ...), custom_call_target="tpu_custom_call" | custom-call | tf_op jit(solution)/shard_map/pallas_call | solution.py:239
  (15 shorter events, 0.2 us)
Async XLA Ops:
  5.9 9.8 %copy-start.5 = (s32[1,4,64]{2,1,0:T(4,128)S(1)}, s32[1,4,64]{2,1,0:T(4,128)}, u32[]{:S(2)}) copy-start(s32[1,4,64]{2,1,0:T(4,128)} %param.19) | copy-start | bytes 3076
  6.0 9.8 %copy-start.6 = (s32[1,2,64]{2,1,0:T(2,128)S(1)}, s32[1,2,64]{2,1,0:T(2,128)}, u32[]{:S(2)}) copy-start(s32[1,2,64]{2,1,0:T(2,128)} %param.20) | copy-start | bytes 1540
  6.0 10.6 %copy-start.7 = (s32[1,2,64]{2,1,0:T(2,128)S(1)}, s32[1,2,64]{2,1,0:T(2,128)}, u32[]{:S(2)}) copy-start(s32[1,2,64]{2,1,0:T(2,128)} %param.21) | copy-start | bytes 1540
  6.0 14.1 %copy-start = (f32[64,4096]{1,0:T(8,128)S(1)}, f32[64,4096]{1,0:T(8,128)}, u32[]{:S(2)}) copy-start(f32[64,4096]{1,0:T(8,128)} %param.14) | copy-start | bytes 3145732
  6.1 11.3 %collective-permute-start = (f32[5,4096]{1,0:T(8,128)S(1)}, f32[5,4096]{1,0:T(8,128)S(1)}, u32[]{:S(2)}, u32[]{:S(2)}) collective-permute-start(f32[5,4096]{1,0:T(8,128)S(1)} %get-tuple-element.24), channel_id=1, source_target_pairs={{0,1},{1,2},{2,3},{3,4},{4,5},{5,6},{6,7},{7,8},{8,9},{9,10},{10,1... | collective-permute-start | bytes 245768 | tf_op jit(solution)/shard_map/ppermute | solution.py:324
  6.2 11.5 %collective-permute-start.2 = (f32[5,4096]{1,0:T(8,128)S(1)}, f32[5,4096]{1,0:T(8,128)S(1)}, u32[]{:S(2)}, u32[]{:S(2)}) collective-permute-start(f32[5,4096]{1,0:T(8,128)S(1)} %get-tuple-element.25), channel_id=1, source_target_pairs={{0,64},{1,65},{2,66},{3,67},{4,68},{5,69},{6,70},{7,71},{8,72},{9,... | collective-permute-start | bytes 245768 | tf_op jit(solution)/shard_map/ppermute | solution.py:324
  9.6 8.7 %collective-permute-start.1 = (f32[5,4096]{1,0:T(8,128)S(1)}, f32[5,4096]{1,0:T(8,128)S(1)}, u32[]{:S(2)}, u32[]{:S(2)}) collective-permute-start(f32[5,4096]{1,0:T(8,128)S(1)} %get-tuple-element.26), channel_id=1, source_target_pairs={{0,127},{1,0},{2,1},{3,2},{4,3},{5,4},{6,5},{7,6},{8,7},{9,8},{10,... | collective-permute-start | bytes 245768 | tf_op jit(solution)/shard_map/ppermute | solution.py:324
  24.6 11.4 %collective-permute-start.3 = (f32[64,256]{1,0:T(8,128)}, f32[64,256]{1,0:T(8,128)S(1)}, u32[]{:S(2)}, u32[]{:S(2)}) collective-permute-start(f32[64,256]{1,0:T(8,128)} %get-tuple-element.13), channel_id=1, source_target_pairs={{0,8},{8,16},{16,24},{24,32},{32,40},{40,48},{48,56},{56,64},{64,7... | collective-permute-start | bytes 196616 | tf_op jit(solution)/shard_map/ppermute | solution.py:283
  24.6 11.4 %collective-permute-start.4 = (f32[64,256]{1,0:T(8,128)}, f32[64,256]{1,0:T(8,128)S(1)}, u32[]{:S(2)}, u32[]{:S(2)}) collective-permute-start(f32[64,256]{1,0:T(8,128)} %get-tuple-element.14), channel_id=1, source_target_pairs={{8,0},{16,8},{24,16},{32,24},{40,32},{48,40},{56,48},{64,56},{72,6... | collective-permute-start | bytes 196616 | tf_op jit(solution)/shard_map/ppermute | solution.py:283
  36.0 0.6 %copy-start.3 = (f32[64,256]{1,0:T(8,128)}, f32[64,256]{1,0:T(8,128)S(1)}, u32[]{:S(2)}) copy-start(f32[64,256]{1,0:T(8,128)S(1)} %collective-permute-done.3.lower_ref) | copy-start | bytes 196612
  36.0 0.6 %copy-start.4 = (f32[64,256]{1,0:T(8,128)}, f32[64,256]{1,0:T(8,128)S(1)}, u32[]{:S(2)}) copy-start(f32[64,256]{1,0:T(8,128)S(1)} %collective-permute-done.4.upper_ref) | copy-start | bytes 196612
  39.7 11.7 %collective-permute-start.5 = (f32[64,256]{1,0:T(8,128)}, f32[64,256]{1,0:T(8,128)S(1)}, u32[]{:S(2)}, u32[]{:S(2)}) collective-permute-start(f32[64,256]{1,0:T(8,128)} %get-tuple-element.16), channel_id=1, source_target_pairs={{0,8},{8,16},{16,24},{24,32},{32,40},{40,48},{48,56},{56,64},{64,7... | collective-permute-start | bytes 196616 | tf_op jit(solution)/shard_map/ppermute | solution.py:283
  39.7 11.7 %collective-permute-start.6 = (f32[64,256]{1,0:T(8,128)}, f32[64,256]{1,0:T(8,128)S(1)}, u32[]{:S(2)}, u32[]{:S(2)}) collective-permute-start(f32[64,256]{1,0:T(8,128)} %get-tuple-element.17), channel_id=1, source_target_pairs={{8,0},{16,8},{24,16},{32,24},{40,32},{48,40},{56,48},{64,56},{72,6... | collective-permute-start | bytes 196616 | tf_op jit(solution)/shard_map/ppermute | solution.py:283
  51.4 0.6 %copy-start.1 = (f32[64,256]{1,0:T(8,128)}, f32[64,256]{1,0:T(8,128)S(1)}, u32[]{:S(2)}) copy-start(f32[64,256]{1,0:T(8,128)S(1)} %collective-permute-done.5.lower_ref) | copy-start | bytes 196612
  52.1 0.6 %copy-start.2 = (f32[64,256]{1,0:T(8,128)}, f32[64,256]{1,0:T(8,128)S(1)}, u32[]{:S(2)}) copy-start(f32[64,256]{1,0:T(8,128)S(1)} %collective-permute-done.6.upper_ref) | copy-start | bytes 196612

commit v5 on v4

--- a/solution.py
+++ b/solution.py
@@ -122,19 +122,37 @@
     return mxu(hi, onehot) + mxu(mid, onehot) + mxu(lo, onehot)
 
 
-def inner_body(v_ref, *refs, scale, shared):
-    if shared:
+def face_lift(below, above, live, a, scale):
+    derivative, second, side_signs, weights = mode_tables()
+    lift_signs = (side_signs * weights[None, :]).astype(np.float32)
+    update = float(lift_signs[0, a]) * below + float(lift_signs[1, a]) * above
+    return scale * jnp.where(live, update, 0.0)
+
+
+def inner_body(*refs, scale, carried):
+    if carried is None:
+        v_ref, weight_ref, top_ref, pick_ref, spread_hi_ref, spread_lo_ref, lift_ref = refs[:7]
         base_ref = v_ref
-        weight_ref, top_ref, pick_ref, spread_hi_ref, spread_lo_ref, lift_ref, partial_ref = refs
     else:
-        base_ref, weight_ref, top_ref, pick_ref, spread_hi_ref, spread_lo_ref, lift_ref, partial_ref = refs
+        v_ref, below_ref, above_ref, base_ref, weight_ref, top_ref, pick_ref = refs[:7]
+        spread_hi_ref, spread_lo_ref, lift_ref = refs[7:10]
+    partial_ref, even_ref, total_ref = refs[-3:]
     count = v_ref.shape[0]
     derivative, second, side_signs, weights = mode_tables()
     second = second.astype(np.float32)
     derivative = derivative.astype(np.float32)
     lift_signs = (side_signs * weights[None, :]).astype(np.float32)
+    weight = weight_ref[...]
+    top = top_ref[...]
+    order = weight[:, 7:8]
     slabs = [v_ref[:, a * PLANE : (a + 1) * PLANE] for a in range(P_SIZE)]
-    weight = weight_ref[...]
+    if carried is not None:
+        below = below_ref[...]
+        above = above_ref[...]
+        slabs = [
+            slabs[a] + face_lift(below, above, top[:, a * PLANE : (a + 1) * PLANE] <= order, a, carried)
+            for a in range(P_SIZE)
+        ]
     diff0 = jnp.broadcast_to(weight[:, 0:1], (count, PLANE))
     vel0 = jnp.broadcast_to(weight[:, 3:4], (count, PLANE))
     first = []
@@ -183,15 +201,40 @@
     lift_mat = lift_ref[...]
     lifted = mxu(jhi, lift_mat) + mxu(jlo, lift_mat)
     even, total = end_traces(slabs)
-    top = top_ref[...]
-    order = weight[:, 7:8]
+    news = []
     for a in range(P_SIZE):
         rows = slice(a * count, (a + 1) * count)
         lanes = slice(a * PLANE, (a + 1) * PLANE)
         own_lift = lifted[rows] + float(lift_signs[0, a]) * even + float(lift_signs[1, a]) * total
         live = top[:, lanes] <= order
         update = jnp.where(live, first[a] + inner[rows] - own_lift, 0.0)
-        partial_ref[:, lanes] = base_ref[:, lanes] + scale * update
+        new = base_ref[:, lanes] + scale * update
+        partial_ref[:, lanes] = new
+        news.append(new)
+    even, total = end_traces(news)
+    even_ref[...] = even
+    total_ref[...] = total
+
+
+def faces_body(
+    lower_ref, upper_ref, pick_ref, turn_ref, flip_ref, top_ref, weight_ref, even_ref, total_ref,
+    below_ref, above_ref, new_even_ref, new_total_ref, *, scale
+):
+    codes = turn_ref[...]
+    flip = flip_ref[...]
+    below = turn(exact_pick(pick_ref[4], lower_ref[...]), codes[:, 0:1], flip)
+    above = turn(exact_pick(pick_ref[5], upper_ref[...]), codes[:, 1:2], flip)
+    below_ref[...] = below
+    above_ref[...] = above
+    top = top_ref[...]
+    order = weight_ref[:, 7:8]
+    parts = [
+        face_lift(below, above, top[:, a * PLANE : (a + 1) * PLANE] <= order, a, scale)
+        for a in range(P_SIZE)
+    ]
+    even, total = end_traces(parts)
+    new_even_ref[...] = even_ref[...] + even
+    new_total_ref[...] = total_ref[...] + total
 
 
 def outer_body(
@@ -219,27 +262,44 @@
     total_ref[...] = total
 
 
-def section(v, base, top, weight, ends, picks, codes, tables, scale):
-    count = v.shape[0]
-    spread_hi, spread_lo, lift, flip = tables
+def inner(operands, scale, carried):
+    count = operands[0].shape[0]
     spec = pl.BlockSpec(memory_space=pltpu.VMEM)
-    shared = base is None
-    operands = (v,) + (() if shared else (base,)) + (weight, top, picks, spread_hi, spread_lo, lift)
-    pre = pl.pallas_call(
-        functools.partial(inner_body, scale=scale, shared=shared),
-        out_shape=jax.ShapeDtypeStruct(v.shape, jnp.float32),
+    return pl.pallas_call(
+        functools.partial(inner_body, scale=scale, carried=carried),
+        out_shape=(
+            jax.ShapeDtypeStruct(operands[0].shape, jnp.float32),
+            jax.ShapeDtypeStruct((count, PLANE), jnp.float32),
+            jax.ShapeDtypeStruct((count, PLANE), jnp.float32),
+        ),
         in_specs=[spec] * len(operands),
-        out_specs=spec,
+        out_specs=(spec, spec, spec),
         compiler_params=pltpu.CompilerParams(vmem_limit_bytes=60 * 1024 * 1024),
         cost_estimate=pl.CostEstimate(
             flops=2_500_000_000, transcendentals=0, bytes_accessed=4_000_000
         ),
     )(*operands)
-    lower, upper = exchange(*ends)
+
+
+def faces(lower, upper, picks, codes, flip, top, weight, even, total, scale):
+    count = lower.shape[0]
+    spec = pl.BlockSpec(memory_space=pltpu.VMEM)
+    square = jax.ShapeDtypeStruct((count, PLANE), jnp.float32)
+    return pl.pallas_call(
+        functools.partial(faces_body, scale=scale),
+        out_shape=(square,) * 4,
+        in_specs=[spec] * 9,
+        out_specs=(spec,) * 4,
+    )(lower, upper, picks, codes, flip, top, weight, even, total)
+
+
+def outer(pre, top, weight, lower, upper, picks, codes, flip, scale):
+    count = pre.shape[0]
+    spec = pl.BlockSpec(memory_space=pltpu.VMEM)
     return pl.pallas_call(
         functools.partial(outer_body, scale=scale),
         out_shape=(
-            jax.ShapeDtypeStruct(v.shape, jnp.float32),
+            jax.ShapeDtypeStruct(pre.shape, jnp.float32),
             jax.ShapeDtypeStruct((count, PLANE), jnp.float32),
             jax.ShapeDtypeStruct((count, PLANE), jnp.float32),
         ),
@@ -341,13 +401,23 @@
         neighbours[:, :, None] == jnp.arange(element_count, dtype=jnp.int32)[None, None, :]
     ).astype(jnp.bfloat16)
     codes = partner_turns[0].T
+    spread_hi, spread_lo, lift, flip = tables
     field, even, total = prep(got_coef[source], top, weight)
-    half, even, total = section(
-        field, None, top, weight, (even, total), picks, codes, tables, 0.5 * TIME_STEP
-    )
-    advanced, _, _ = section(
-        half, field, top, weight, (even, total), picks, codes, tables, TIME_STEP
-    )
+    first_step = 0.5 * TIME_STEP
+    lower, upper = exchange(even, total)
+    pre, even, total = inner(
+        (field, weight, top, picks, spread_hi, spread_lo, lift), first_step, None
+    )
+    below, above, even, total = faces(
+        lower, upper, picks, codes, flip, top, weight, even, total, first_step
+    )
+    lower, upper = exchange(even, total)
+    pre, _, _ = inner(
+        (pre, below, above, field, weight, top, picks, spread_hi, spread_lo, lift),
+        TIME_STEP,
+        first_step,
+    )
+    advanced, _, _ = outer(pre, top, weight, lower, upper, picks, codes, flip, TIME_STEP)
     return advanced
 
 

time: 56 us -> 55.3 us (0.987)
  local copies, waits for them, and re-layouts: 8.77 us -> 8.18 us
    unnamed x16, local copies, waits for them, and re-layouts: 1.87 us -> 1.28 us
  transfers between devices with their start and end apart: 7 -> 7, of which waited for: 2 -> 2; matrix products, arithmetic and copies ran while one was open for 4% -> 4% of each run, Pallas kernels for 22% -> 24%
where the time goes in v5:
time: 55.3 us; the launch traced here: 55 us
  Pallas kernels  21 us (38%)
  starting transfers between devices  20.3 us (37%)
  local copies, waits for them, and re-layouts  8.18 us (15%)
  other arithmetic  4.86 us (9%)
    pallas_call x2, Pallas kernels, inner(): pl.pallas_call(functools.partial(inner_body, scale=scale, carried=carried...  13 us
    ppermute x4, starting transfers between devices, exchange(): return (lax.ppermute(total, 'dom', up), lax.ppermute(even, 'dom', down))  10.7 us
    ppermute x3, starting transfers between devices, shards(): arrived = lax.ppermute(parcels[index], ('dom', 'face'), pairs)  9.63 us
    pallas_call x1, Pallas kernels, outer(): pl.pallas_call(functools.partial(outer_body, scale=scale), out_shape=(jax...  3.04 us
    pallas_call x1, Pallas kernels, prep(): pl.pallas_call(prep_body, out_shape=(jax.ShapeDtypeStruct(placed.shape, j...  2.51 us
    pallas_call x1, Pallas kernels, faces(): pl.pallas_call(functools.partial(faces_body, scale=scale), out_shape=(squ...  2.44 us
    gather x1, local copies, waits for them, and re-layouts, shards(): coefficients[picked].reshape(len(shifts), moving, P_SIZE ** 3)  1.93 us
    gather x1, local copies, waits for them, and re-layouts, shards(): field, even, total = prep(got_coef[source], top, weight)  1.85 us
  transfers between devices with their start and end apart: 7, of which 2 were waited for; matrix products, arithmetic and copies ran while one was open for 4% of the time, Pallas kernels for 24%

profile of v5, /device:TPU:0, one launch (start us, length us, event | category | flops | bytes accessed | tf_op | source)
XLA Modules:
  0.0 55.0 jit_solution(5579106050191719570)
XLA Ops:
  0.0 0.7 %and_select_fusion.1 = s32[3]{0:T(128)S(1)} fusion(s32[3]{0:T(128)} %constant.78.clone, s32[]{:T(128)S(6)} %add.51), kind=kLoop, calls=%fused_computation.31 | loop fusion | flops 36 | bytes 28 | tf_op jit(solution)/shard_map/jit(remainder)/select_n | solution.py:366
  0.7 0.7 %compare_select_fusion.4 = (s32[64]{0:T(128)S(1)}, s32[64]{0:T(128)S(1)}, s32[64]{0:T(128)S(1)}) fusion(s32[]{:T(128)S(6)} %add.51, s32[64]{0:T(128)} %param.18), kind=kLoop, calls=%fused_computation.29 | loop fusion | flops 1344 | bytes 1028 | tf_op jit(solution)/shard_map/jit(_where)/select_n | solution.py:381
  1.3 0.1 fusion.5
  1.4 0.2 reduce_window_sum.11
  1.7 0.1 select_reduce_fusion.1
  1.8 0.1 reshape.106
  1.9 0.7 %convert_bitcast_fusion = (f32[64,1]{0,1:T(1,128)S(1)}, f32[64,1]{0,1:T(1,128)S(1)}) fusion(s32[64]{0:T(128)} %param.17, s32[64]{0:T(128)S(1)} %get-tuple-element.31), kind=kLoop, calls=%fused_computation.45 | loop fusion | flops 448 | bytes 1024 | tf_op jit(solution)/shard_map/convert_element_type | solution.py:360
  2.6 0.7 %pad_maximum_fusion.2 = f32[64,8]{0,1:T(8,128)S(1)} fusion(f32[64,1]{0,1:T(1,128)S(1)} %get-tuple-element.37, f32[64,1]{0,1:T(1,128)S(1)} %get-tuple-element.38, f32[64,3]{0,1:T(4,128)} %param.16, f32[64,3]{0,1:T(4,128)} %param.15), kind=kLoop, calls=%fused_computation.20 | loop fusion | flops 1536 | bytes 4096 | tf_op jit(solution)/shard_map/concatenate | solution.py:355
  3.3 0.1 copy.34
  3.4 0.6 %gather_fusion.1 = f32[12,8]{1,0:T(8,128)S(1)} fusion(f32[64,8]{1,0:T(8,128)S(1)} %copy.34, s32[1024]{0:T(1024)S(1)} %pad_clamp_fusion.1), kind=kCustom, calls=%fused_computation.1 | custom fusion | bytes 816 | tf_op jit(solution)/shard_map/gather | solution.py:374
  3.9 0.1 reshape.141
  4.0 1.9 %gather_fusion = f32[12,4096]{1,0:T(8,128)S(1)} fusion(f32[64,4096]{1,0:T(8,128)} %param.14, s32[1024]{0:T(1024)S(1)} %pad_clamp_fusion.1), kind=kCustom, calls=%fused_computation | custom fusion | bytes 393264 | tf_op jit(solution)/shard_map/gather | solution.py:377
  5.9 0.0 copy-start.5
  6.0 0.0 copy-start.6
  6.0 0.0 copy-start.7
  6.0 0.0 copy-start
  6.0 0.1 reshape.107
  6.1 0.1 collective-permute-start
  6.2 3.4 %collective-permute-start.2 = (f32[5,4096]{1,0:T(8,128)S(1)}, f32[5,4096]{1,0:T(8,128)S(1)}, u32[]{:S(2)}, u32[]{:S(2)}) collective-permute-start(f32[5,4096]{1,0:T(8,128)S(1)} %get-tuple-element.35), channel_id=1, source_target_pairs={{0,64},{1,65},{2,66},{3,67},{4,68},{5,69},{6,70},{7,71},{8,72},{9,... | collective-permute-start | bytes 245768 | tf_op jit(solution)/shard_map/ppermute | solution.py:384
  9.6 6.2 %collective-permute-start.1 = (f32[5,4096]{1,0:T(8,128)S(1)}, f32[5,4096]{1,0:T(8,128)S(1)}, u32[]{:S(2)}, u32[]{:S(2)}) collective-permute-start(f32[5,4096]{1,0:T(8,128)S(1)} %get-tuple-element.36), channel_id=1, source_target_pairs={{0,127},{1,0},{2,1},{3,2},{4,3},{5,4},{6,5},{7,6},{8,7},{9,8},{10,... | collective-permute-start | bytes 245768 | tf_op jit(solution)/shard_map/ppermute | solution.py:384
  15.8 0.0 copy-done.5
  15.8 0.0 copy-done.6
  15.8 0.8 %fusion.refs_3_.pick_ref.refs_6_ = bf16[6,64,64]{2,1,0:T(8,128)(2,1)} fusion(s32[6,64]{1,0:T(8,128)S(1)} %pad_add_fusion), kind=kLoop, calls=%fused_computation.8 | loop fusion | flops 49152 | bytes 50688 | tf_op jit(solution)/shard_map/convert_element_type | solution.py:402
  16.6 0.0 copy-done.7
  16.6 0.7 %copy.37 = s32[2,64]{0,1:T(8,128)} copy(s32[2,64]{1,0:T(2,128)S(1)} %bitcast.24) | data formatting | bytes 1024 | tf_op jit(solution)/shard_map/squeeze | solution.py:403
  17.3 0.2 collective-permute-done
  17.5 0.1 reshape_squeeze.9
  17.6 0.2 convert_reduce_fusion.2
  17.8 0.0 collective-permute-done.2
  17.8 0.1 reshape_squeeze.11
  17.9 0.2 convert_reduce_fusion
  18.1 0.2 collective-permute-done.1
  18.3 0.1 reshape_squeeze.10
  18.4 0.2 convert_reduce_fusion.1
  18.6 0.1 pad_add_fusion.1
  18.7 0.1 select_reduce_fusion
  18.8 1.2 %gather_fusion.3 = f32[64,8]{1,0:T(8,128)} fusion(f32[76,8]{1,0:T(8,128)S(1)} %pad_maximum_fusion.1, s32[1024]{0:T(1024)S(1)} %pad_clamp_fusion), kind=kCustom, calls=%fused_computation.3 | custom fusion | bytes 4352 | tf_op jit(solution)/shard_map/gather | solution.py:395
  20.1 0.0 copy-done
  20.1 0.1 pad_maximum_fusion
  20.2 1.8 %gather_fusion.2 = f32[64,4096]{1,0:T(8,128)} fusion(f32[76,4096]{1,0:T(8,128)S(1)} %pad_maximum_fusion, s32[1024]{0:T(1024)S(1)} %pad_clamp_fusion), kind=kCustom, calls=%fused_computation.2 | custom fusion | bytes 2097408 | tf_op jit(solution)/shard_map/gather | solution.py:405
  22.0 2.5 %shard_map.136 = (f32[64,4096]{1,0:T(8,128)}, f32[64,256]{1,0:T(8,128)}, f32[64,256]{1,0:T(8,128)}) custom-call(f32[64,4096]{1,0:T(8,128)} %gather_fusion.2, f32[1,4096]{1,0:T(1,128)} %constant.79.clone.top_ref.refs_2_.refs_5_, f32[64,8]{1,0:T(8,128)} %gather_fusion.3), custom_call_target="tpu_custom_call" | custom-call | tf_op jit(solution)/shard_map/pallas_call | solution.py:327
  24.5 0.0 collective-permute-start.3
  24.5 5.3 %collective-permute-start.4 = (f32[64,256]{1,0:T(8,128)}, f32[64,256]{1,0:T(8,128)S(1)}, u32[]{:S(2)}, u32[]{:S(2)}) collective-permute-start(f32[64,256]{1,0:T(8,128)} %get-tuple-element.20), channel_id=1, source_target_pairs={{8,0},{16,8},{24,16},{32,24},{40,32},{48,40},{56,48},{64,56},{72,6... | collective-permute-start | bytes 196616 | tf_op jit(solution)/shard_map/ppermute | solution.py:343
  29.9 6.2 %shard_map.137 = (f32[64,4096]{1,0:T(8,128)}, f32[64,256]{1,0:T(8,128)}, f32[64,256]{1,0:T(8,128)}) custom-call(f32[64,4096]{1,0:T(8,128)} %get-tuple-element.17.refs_0_.refs_3_, f32[64,8]{1,0:T(8,128)} %gather_fusion.3, f32[1,4096]{1,0:T(1,128)} %constant.79.clone.top_ref.refs_2_.refs_5_, bf16[6,64,64]{2,1,0:T(8,128)(2,1)} %fusion.refs_3_.pick_ref.refs_6_, ...), custom_call_target="tpu_custom_call" | custom-call | flops 2500000000 | bytes 4000000 | tf_op jit(solution)/shard_map/pallas_call | solution.py:268
  36.1 0.0 collective-permute-done.3.lower_ref
  36.1 0.0 copy-start.3
  36.1 0.0 collective-permute-done.4.upper_ref
  36.1 0.0 copy-start.4
  36.1 0.6 %copy-done.3 = f32[64,256]{1,0:T(8,128)} copy-done((f32[64,256]{1,0:T(8,128)}, f32[64,256]{1,0:T(8,128)S(1)}, u32[]{:S(2)}) %copy-start.3) | copy-done | bytes 65560
  36.7 0.0 copy-done.4
  36.7 2.4 %shard_map.138 = (f32[64,256]{1,0:T(8,128)}, f32[64,256]{1,0:T(8,128)}, f32[64,256]{1,0:T(8,128)}, f32[64,256]{1,0:T(8,128)}) custom-call(f32[64,256]{1,0:T(8,128)} %copy-done.3, f32[64,256]{1,0:T(8,128)} %copy-done.4, bf16[6,64,64]{2,1,0:T(8,128)(2,1)} %fusion.refs_3_.pick_ref.refs_6_, s32[64,2]{1,0:T(8,128)} %bitcast.20, ...), custom_call_target="tpu_custom_call" | custom-call | tf_op jit(solution)/shard_map/pallas_call | solution.py:288
  39.2 0.0 collective-permute-start.5
  39.2 5.3 %collective-permute-start.6 = (f32[64,256]{1,0:T(8,128)}, f32[64,256]{1,0:T(8,128)S(1)}, u32[]{:S(2)}, u32[]{:S(2)}) collective-permute-start(f32[64,256]{1,0:T(8,128)} %get-tuple-element.27), channel_id=1, source_target_pairs={{8,0},{16,8},{24,16},{32,24},{40,32},{48,40},{56,48},{64,56},{72,6... | collective-permute-start | bytes 196616 | tf_op jit(solution)/shard_map/ppermute | solution.py:343
  44.5 6.8 %shard_map.139 = (f32[64,4096]{1,0:T(8,128)}, f32[64,256]{1,0:T(8,128)}, f32[64,256]{1,0:T(8,128)}) custom-call(f32[64,4096]{1,0:T(8,128)} %get-tuple-element.18.refs_0_, f32[64,256]{1,0:T(8,128)} %get-tuple-element.23.refs_1_, f32[64,256]{1,0:T(8,128)} %get-tuple-element.24.refs_2_, f32[64,4096]{1,0:T(8,128)} %get-tuple-element.17.refs_0_.refs_3_, ...), custom_call_target="tpu_custom_call" | custom-call | flops 2500000000 | bytes 4000000 | tf_op jit(solution)/shard_map/pallas_call | solution.py:268
  51.3 0.0 collective-permute-done.5.lower_ref
  51.3 0.0 copy-start.1
  51.3 0.0 collective-permute-done.6.upper_ref
  51.4 0.0 copy-start.2
  51.4 0.6 %copy-done.1 = f32[64,256]{1,0:T(8,128)} copy-done((f32[64,256]{1,0:T(8,128)}, f32[64,256]{1,0:T(8,128)S(1)}, u32[]{:S(2)}) %copy-start.1) | copy-done | bytes 65560
  52.0 0.0 copy-done.2
  52.0 3.0 %shard_map.140 = (f32[64,4096]{1,0:T(8,128)}, f32[64,256]{1,0:T(8,128)}, f32[64,256]{1,0:T(8,128)}) custom-call(f32[64,4096]{1,0:T(8,128)} %get-tuple-element.25.pre_ref, f32[1,4096]{1,0:T(1,128)} %constant.79.clone.top_ref.refs_2_.refs_5_, f32[64,8]{1,0:T(8,128)} %gather_fusion.3, f32[64,256]{1,0:T(8,128)} %copy-done.1, f32[64,256]{1,0:T(8,128)} %copy-done.2, ...), custom_call_target="tpu_custom_call" | custom-call | tf_op jit(solution)/shard_map/pallas_call | solution.py:299
  (15 shorter events, 0.2 us)
Async XLA Ops:
  5.9 9.8 %copy-start.5 = (s32[1,4,64]{2,1,0:T(4,128)S(1)}, s32[1,4,64]{2,1,0:T(4,128)}, u32[]{:S(2)}) copy-start(s32[1,4,64]{2,1,0:T(4,128)} %param.19) | copy-start | bytes 3076
  6.0 9.8 %copy-start.6 = (s32[1,2,64]{2,1,0:T(2,128)S(1)}, s32[1,2,64]{2,1,0:T(2,128)}, u32[]{:S(2)}) copy-start(s32[1,2,64]{2,1,0:T(2,128)} %param.20) | copy-start | bytes 1540
  6.0 10.6 %copy-start.7 = (s32[1,2,64]{2,1,0:T(2,128)S(1)}, s32[1,2,64]{2,1,0:T(2,128)}, u32[]{:S(2)}) copy-start(s32[1,2,64]{2,1,0:T(2,128)} %param.21) | copy-start | bytes 1540
  6.0 14.1 %copy-start = (f32[64,4096]{1,0:T(8,128)S(1)}, f32[64,4096]{1,0:T(8,128)}, u32[]{:S(2)}) copy-start(f32[64,4096]{1,0:T(8,128)} %param.14) | copy-start | bytes 3145732
  6.1 11.3 %collective-permute-start = (f32[5,4096]{1,0:T(8,128)S(1)}, f32[5,4096]{1,0:T(8,128)S(1)}, u32[]{:S(2)}, u32[]{:S(2)}) collective-permute-start(f32[5,4096]{1,0:T(8,128)S(1)} %get-tuple-element.34), channel_id=1, source_target_pairs={{0,1},{1,2},{2,3},{3,4},{4,5},{5,6},{6,7},{7,8},{8,9},{9,10},{10,1... | collective-permute-start | bytes 245768 | tf_op jit(solution)/shard_map/ppermute | solution.py:384
  6.2 11.5 %collective-permute-start.2 = (f32[5,4096]{1,0:T(8,128)S(1)}, f32[5,4096]{1,0:T(8,128)S(1)}, u32[]{:S(2)}, u32[]{:S(2)}) collective-permute-start(f32[5,4096]{1,0:T(8,128)S(1)} %get-tuple-element.35), channel_id=1, source_target_pairs={{0,64},{1,65},{2,66},{3,67},{4,68},{5,69},{6,70},{7,71},{8,72},{9,... | collective-permute-start | bytes 245768 | tf_op jit(solution)/shard_map/ppermute | solution.py:384
  9.6 8.7 %collective-permute-start.1 = (f32[5,4096]{1,0:T(8,128)S(1)}, f32[5,4096]{1,0:T(8,128)S(1)}, u32[]{:S(2)}, u32[]{:S(2)}) collective-permute-start(f32[5,4096]{1,0:T(8,128)S(1)} %get-tuple-element.36), channel_id=1, source_target_pairs={{0,127},{1,0},{2,1},{3,2},{4,3},{5,4},{6,5},{7,6},{8,7},{9,8},{10,... | collective-permute-start | bytes 245768 | tf_op jit(solution)/shard_map/ppermute | solution.py:384
  24.5 11.5 %collective-permute-start.3 = (f32[64,256]{1,0:T(8,128)}, f32[64,256]{1,0:T(8,128)S(1)}, u32[]{:S(2)}, u32[]{:S(2)}) collective-permute-start(f32[64,256]{1,0:T(8,128)} %get-tuple-element.19), channel_id=1, source_target_pairs={{0,8},{8,16},{16,24},{24,32},{32,40},{40,48},{48,56},{56,64},{64,7... | collective-permute-start | bytes 196616 | tf_op jit(solution)/shard_map/ppermute | solution.py:343
  24.5 11.5 %collective-permute-start.4 = (f32[64,256]{1,0:T(8,128)}, f32[64,256]{1,0:T(8,128)S(1)}, u32[]{:S(2)}, u32[]{:S(2)}) collective-permute-start(f32[64,256]{1,0:T(8,128)} %get-tuple-element.20), channel_id=1, source_target_pairs={{8,0},{16,8},{24,16},{32,24},{40,32},{48,40},{56,48},{64,56},{72,6... | collective-permute-start | bytes 196616 | tf_op jit(solution)/shard_map/ppermute | solution.py:343
  36.1 0.6 %copy-start.3 = (f32[64,256]{1,0:T(8,128)}, f32[64,256]{1,0:T(8,128)S(1)}, u32[]{:S(2)}) copy-start(f32[64,256]{1,0:T(8,128)S(1)} %collective-permute-done.3.lower_ref) | copy-start | bytes 196612
  36.1 0.6 %copy-start.4 = (f32[64,256]{1,0:T(8,128)}, f32[64,256]{1,0:T(8,128)S(1)}, u32[]{:S(2)}) copy-start(f32[64,256]{1,0:T(8,128)S(1)} %collective-permute-done.4.upper_ref) | copy-start | bytes 196612
  39.2 12.2 %collective-permute-start.5 = (f32[64,256]{1,0:T(8,128)}, f32[64,256]{1,0:T(8,128)S(1)}, u32[]{:S(2)}, u32[]{:S(2)}) collective-permute-start(f32[64,256]{1,0:T(8,128)} %get-tuple-element.26), channel_id=1, source_target_pairs={{0,8},{8,16},{16,24},{24,32},{32,40},{40,48},{48,56},{56,64},{64,7... | collective-permute-start | bytes 196616 | tf_op jit(solution)/shard_map/ppermute | solution.py:343
  39.2 12.2 %collective-permute-start.6 = (f32[64,256]{1,0:T(8,128)}, f32[64,256]{1,0:T(8,128)S(1)}, u32[]{:S(2)}, u32[]{:S(2)}) collective-permute-start(f32[64,256]{1,0:T(8,128)} %get-tuple-element.27), channel_id=1, source_target_pairs={{8,0},{16,8},{24,16},{32,24},{40,32},{48,40},{56,48},{64,56},{72,6... | collective-permute-start | bytes 196616 | tf_op jit(solution)/shard_map/ppermute | solution.py:343
  51.3 0.6 %copy-start.1 = (f32[64,256]{1,0:T(8,128)}, f32[64,256]{1,0:T(8,128)S(1)}, u32[]{:S(2)}) copy-start(f32[64,256]{1,0:T(8,128)S(1)} %collective-permute-done.5.lower_ref) | copy-start | bytes 196612
  51.4 0.6 %copy-start.2 = (f32[64,256]{1,0:T(8,128)}, f32[64,256]{1,0:T(8,128)S(1)}, u32[]{:S(2)}) copy-start(f32[64,256]{1,0:T(8,128)S(1)} %collective-permute-done.6.upper_ref) | copy-start | bytes 196612

commit v6 on v5

--- a/solution.py
+++ b/solution.py
@@ -86,12 +86,24 @@
     return jnp.dot(a, b, preferred_element_type=jnp.float32)
 
 
-def exact_pick(onehot, x):
+def split_three(x):
     hi = x.astype(jnp.bfloat16)
     rest = x - hi.astype(jnp.float32)
     mid = rest.astype(jnp.bfloat16)
     lo = (rest - mid.astype(jnp.float32)).astype(jnp.bfloat16)
-    return mxu(onehot, hi) + mxu(onehot, mid) + mxu(onehot, lo)
+    return hi, mid, lo
+
+
+def exact_pick(onehot, x):
+    width = x.shape[1]
+    joined = mxu(onehot, jnp.concatenate(split_three(x), axis=1))
+    return joined[:, :width] + joined[:, width : 2 * width] + joined[:, 2 * width :]
+
+
+def exact_rows(x, onehot):
+    count = x.shape[0]
+    joined = mxu(jnp.concatenate(split_three(x), axis=0), onehot)
+    return joined[:count] + joined[count : 2 * count] + joined[2 * count :]
 
 
 def end_traces(slabs):
@@ -103,23 +115,22 @@
     return even, total
 
 
-def turn(rows, codes, flip):
+def turn_pair(lower, upper, picks, codes, flip):
+    count = lower.shape[0]
+    picked = jnp.concatenate([exact_pick(picks[4], lower), exact_pick(picks[5], upper)], axis=0)
+    swapped = exact_rows(picked, flip)
     lane = lax.broadcasted_iota(jnp.int32, (1, PLANE), 1)
-    swapped = exact_pick_right(rows, flip)
-    rows = jnp.where(codes % 2 == 1, swapped, rows)
     row_odd = (lane // P_SIZE) % 2 == 1
     col_odd = lane % 2 == 1
-    negate = ((codes // 2) % 2 == 1) & row_odd
-    negate = negate != (((codes // 4) % 2 == 1) & col_odd)
-    return jnp.where(negate, -rows, rows)
-
-
-def exact_pick_right(x, onehot):
-    hi = x.astype(jnp.bfloat16)
-    rest = x - hi.astype(jnp.float32)
-    mid = rest.astype(jnp.bfloat16)
-    lo = (rest - mid.astype(jnp.float32)).astype(jnp.bfloat16)
-    return mxu(hi, onehot) + mxu(mid, onehot) + mxu(lo, onehot)
+    sides = []
+    for side in range(2):
+        rows = slice(side * count, (side + 1) * count)
+        code = codes[:, side : side + 1]
+        chosen = jnp.where(code % 2 == 1, swapped[rows], picked[rows])
+        negate = ((code // 2) % 2 == 1) & row_odd
+        negate = negate != (((code // 4) % 2 == 1) & col_odd)
+        sides.append(jnp.where(negate, -chosen, chosen))
+    return sides
 
 
 def face_lift(below, above, live, a, scale):
@@ -220,10 +231,7 @@
     lower_ref, upper_ref, pick_ref, turn_ref, flip_ref, top_ref, weight_ref, even_ref, total_ref,
     below_ref, above_ref, new_even_ref, new_total_ref, *, scale
 ):
-    codes = turn_ref[...]
-    flip = flip_ref[...]
-    below = turn(exact_pick(pick_ref[4], lower_ref[...]), codes[:, 0:1], flip)
-    above = turn(exact_pick(pick_ref[5], upper_ref[...]), codes[:, 1:2], flip)
+    below, above = turn_pair(lower_ref[...], upper_ref[...], pick_ref, turn_ref[...], flip_ref[...])
     below_ref[...] = below
     above_ref[...] = above
     top = top_ref[...]
@@ -243,10 +251,7 @@
 ):
     derivative, second, side_signs, weights = mode_tables()
     lift_signs = (side_signs * weights[None, :]).astype(np.float32)
-    codes = turn_ref[...]
-    flip = flip_ref[...]
-    below = turn(exact_pick(pick_ref[4], lower_ref[...]), codes[:, 0:1], flip)
-    above = turn(exact_pick(pick_ref[5], upper_ref[...]), codes[:, 1:2], flip)
+    below, above = turn_pair(lower_ref[...], upper_ref[...], pick_ref, turn_ref[...], flip_ref[...])
     top = top_ref[...]
     order = weight_ref[:, 7:8]
     news = []

time: 55.3 us -> 55.3 us (level)
  no operation moved by 1% of the time
where the time goes in v6:
time: 55.3 us; the launch traced here: 55 us
  Pallas kernels  21 us (38%)
  starting transfers between devices  20.3 us (37%)
  local copies, waits for them, and re-layouts  8.18 us (15%)
  other arithmetic  4.86 us (9%)
    pallas_call x2, Pallas kernels, inner(): pl.pallas_call(functools.partial(inner_body, scale=scale, carried=carried...  13 us
    ppermute x4, starting transfers between devices, exchange(): return (lax.ppermute(total, 'dom', up), lax.ppermute(even, 'dom', down))  10.7 us
    ppermute x3, starting transfers between devices, shards(): arrived = lax.ppermute(parcels[index], ('dom', 'face'), pairs)  9.63 us
    pallas_call x1, Pallas kernels, outer(): pl.pallas_call(functools.partial(outer_body, scale=scale), out_shape=(jax...  3.02 us
    pallas_call x1, Pallas kernels, prep(): pl.pallas_call(prep_body, out_shape=(jax.ShapeDtypeStruct(placed.shape, j...  2.51 us
    pallas_call x1, Pallas kernels, faces(): pl.pallas_call(functools.partial(faces_body, scale=scale), out_shape=(squ...  2.42 us
    gather x1, local copies, waits for them, and re-layouts, shards(): coefficients[picked].reshape(len(shifts), moving, P_SIZE ** 3)  1.93 us
    gather x1, local copies, waits for them, and re-layouts, shards(): field, even, total = prep(got_coef[source], top, weight)  1.85 us
  transfers between devices with their start and end apart: 7, of which 2 were waited for; matrix products, arithmetic and copies ran while one was open for 4% of the time, Pallas kernels for 24%

profile of v6, /device:TPU:0, one launch (start us, length us, event | category | flops | bytes accessed | tf_op | source)
XLA Modules:
  0.0 55.0 jit_solution(17822937891514481244)
XLA Ops:
  0.0 0.7 %and_select_fusion.1 = s32[3]{0:T(128)S(1)} fusion(s32[3]{0:T(128)} %constant.78.clone, s32[]{:T(128)S(6)} %add.51), kind=kLoop, calls=%fused_computation.31 | loop fusion | flops 36 | bytes 28 | tf_op jit(solution)/shard_map/jit(remainder)/select_n | solution.py:371
  0.7 0.7 %compare_select_fusion.4 = (s32[64]{0:T(128)S(1)}, s32[64]{0:T(128)S(1)}, s32[64]{0:T(128)S(1)}) fusion(s32[]{:T(128)S(6)} %add.51, s32[64]{0:T(128)} %param.18), kind=kLoop, calls=%fused_computation.29 | loop fusion | flops 1344 | bytes 1028 | tf_op jit(solution)/shard_map/jit(_where)/select_n | solution.py:386
  1.3 0.1 fusion.5
  1.4 0.2 reduce_window_sum.11
  1.7 0.1 select_reduce_fusion.1
  1.8 0.1 reshape.106
  1.9 0.7 %convert_bitcast_fusion = (f32[64,1]{0,1:T(1,128)S(1)}, f32[64,1]{0,1:T(1,128)S(1)}) fusion(s32[64]{0:T(128)} %param.17, s32[64]{0:T(128)S(1)} %get-tuple-element.31), kind=kLoop, calls=%fused_computation.45 | loop fusion | flops 448 | bytes 1024 | tf_op jit(solution)/shard_map/convert_element_type | solution.py:365
  2.6 0.7 %pad_maximum_fusion.2 = f32[64,8]{0,1:T(8,128)S(1)} fusion(f32[64,1]{0,1:T(1,128)S(1)} %get-tuple-element.37, f32[64,1]{0,1:T(1,128)S(1)} %get-tuple-element.38, f32[64,3]{0,1:T(4,128)} %param.16, f32[64,3]{0,1:T(4,128)} %param.15), kind=kLoop, calls=%fused_computation.20 | loop fusion | flops 1536 | bytes 4096 | tf_op jit(solution)/shard_map/concatenate | solution.py:360
  3.3 0.1 copy.34
  3.4 0.6 %gather_fusion.1 = f32[12,8]{1,0:T(8,128)S(1)} fusion(f32[64,8]{1,0:T(8,128)S(1)} %copy.34, s32[1024]{0:T(1024)S(1)} %pad_clamp_fusion.1), kind=kCustom, calls=%fused_computation.1 | custom fusion | bytes 816 | tf_op jit(solution)/shard_map/gather | solution.py:379
  3.9 0.1 reshape.141
  4.0 1.9 %gather_fusion = f32[12,4096]{1,0:T(8,128)S(1)} fusion(f32[64,4096]{1,0:T(8,128)} %param.14, s32[1024]{0:T(1024)S(1)} %pad_clamp_fusion.1), kind=kCustom, calls=%fused_computation | custom fusion | bytes 393264 | tf_op jit(solution)/shard_map/gather | solution.py:382
  5.9 0.0 copy-start.5
  6.0 0.0 copy-start.6
  6.0 0.0 copy-start.7
  6.0 0.0 copy-start
  6.0 0.1 reshape.107
  6.1 0.1 collective-permute-start
  6.2 3.4 %collective-permute-start.2 = (f32[5,4096]{1,0:T(8,128)S(1)}, f32[5,4096]{1,0:T(8,128)S(1)}, u32[]{:S(2)}, u32[]{:S(2)}) collective-permute-start(f32[5,4096]{1,0:T(8,128)S(1)} %get-tuple-element.35), channel_id=1, source_target_pairs={{0,64},{1,65},{2,66},{3,67},{4,68},{5,69},{6,70},{7,71},{8,72},{9,... | collective-permute-start | bytes 245768 | tf_op jit(solution)/shard_map/ppermute | solution.py:389
  9.6 6.2 %collective-permute-start.1 = (f32[5,4096]{1,0:T(8,128)S(1)}, f32[5,4096]{1,0:T(8,128)S(1)}, u32[]{:S(2)}, u32[]{:S(2)}) collective-permute-start(f32[5,4096]{1,0:T(8,128)S(1)} %get-tuple-element.36), channel_id=1, source_target_pairs={{0,127},{1,0},{2,1},{3,2},{4,3},{5,4},{6,5},{7,6},{8,7},{9,8},{10,... | collective-permute-start | bytes 245768 | tf_op jit(solution)/shard_map/ppermute | solution.py:389
  15.8 0.0 copy-done.5
  15.8 0.0 copy-done.6
  15.8 0.8 %fusion.refs_3_.pick_ref.refs_6_ = bf16[6,64,64]{2,1,0:T(8,128)(2,1)} fusion(s32[6,64]{1,0:T(8,128)S(1)} %pad_add_fusion), kind=kLoop, calls=%fused_computation.8 | loop fusion | flops 49152 | bytes 50688 | tf_op jit(solution)/shard_map/convert_element_type | solution.py:407
  16.6 0.0 copy-done.7
  16.6 0.7 %copy.37 = s32[2,64]{0,1:T(8,128)} copy(s32[2,64]{1,0:T(2,128)S(1)} %bitcast.24) | data formatting | bytes 1024 | tf_op jit(solution)/shard_map/squeeze | solution.py:408
  17.3 0.2 collective-permute-done
  17.5 0.1 reshape_squeeze.9
  17.6 0.2 convert_reduce_fusion.2
  17.8 0.0 collective-permute-done.2
  17.8 0.1 reshape_squeeze.11
  17.9 0.2 convert_reduce_fusion
  18.1 0.2 collective-permute-done.1
  18.3 0.1 reshape_squeeze.10
  18.4 0.2 convert_reduce_fusion.1
  18.6 0.1 pad_add_fusion.1
  18.7 0.1 select_reduce_fusion
  18.8 1.2 %gather_fusion.3 = f32[64,8]{1,0:T(8,128)} fusion(f32[76,8]{1,0:T(8,128)S(1)} %pad_maximum_fusion.1, s32[1024]{0:T(1024)S(1)} %pad_clamp_fusion), kind=kCustom, calls=%fused_computation.3 | custom fusion | bytes 4352 | tf_op jit(solution)/shard_map/gather | solution.py:400
  20.1 0.0 copy-done
  20.1 0.1 pad_maximum_fusion
  20.2 1.8 %gather_fusion.2 = f32[64,4096]{1,0:T(8,128)} fusion(f32[76,4096]{1,0:T(8,128)S(1)} %pad_maximum_fusion, s32[1024]{0:T(1024)S(1)} %pad_clamp_fusion), kind=kCustom, calls=%fused_computation.2 | custom fusion | bytes 2097408 | tf_op jit(solution)/shard_map/gather | solution.py:410
  22.0 2.5 %shard_map.136 = (f32[64,4096]{1,0:T(8,128)}, f32[64,256]{1,0:T(8,128)}, f32[64,256]{1,0:T(8,128)}) custom-call(f32[64,4096]{1,0:T(8,128)} %gather_fusion.2, f32[1,4096]{1,0:T(1,128)} %constant.79.clone.top_ref.refs_2_.refs_5_, f32[64,8]{1,0:T(8,128)} %gather_fusion.3), custom_call_target="tpu_custom_call" | custom-call | tf_op jit(solution)/shard_map/pallas_call | solution.py:332
  24.5 0.0 collective-permute-start.3
  24.5 5.3 %collective-permute-start.4 = (f32[64,256]{1,0:T(8,128)}, f32[64,256]{1,0:T(8,128)S(1)}, u32[]{:S(2)}, u32[]{:S(2)}) collective-permute-start(f32[64,256]{1,0:T(8,128)} %get-tuple-element.20), channel_id=1, source_target_pairs={{8,0},{16,8},{24,16},{32,24},{40,32},{48,40},{56,48},{64,56},{72,6... | collective-permute-start | bytes 196616 | tf_op jit(solution)/shard_map/ppermute | solution.py:348
  29.9 6.2 %shard_map.137 = (f32[64,4096]{1,0:T(8,128)}, f32[64,256]{1,0:T(8,128)}, f32[64,256]{1,0:T(8,128)}) custom-call(f32[64,4096]{1,0:T(8,128)} %get-tuple-element.17.refs_0_.refs_3_, f32[64,8]{1,0:T(8,128)} %gather_fusion.3, f32[1,4096]{1,0:T(1,128)} %constant.79.clone.top_ref.refs_2_.refs_5_, bf16[6,64,64]{2,1,0:T(8,128)(2,1)} %fusion.refs_3_.pick_ref.refs_6_, ...), custom_call_target="tpu_custom_call" | custom-call | flops 2500000000 | bytes 4000000 | tf_op jit(solution)/shard_map/pallas_call | solution.py:273
  36.1 0.0 collective-permute-done.3.lower_ref
  36.1 0.0 copy-start.3
  36.1 0.0 collective-permute-done.4.upper_ref
  36.1 0.0 copy-start.4
  36.1 0.6 %copy-done.3 = f32[64,256]{1,0:T(8,128)} copy-done((f32[64,256]{1,0:T(8,128)}, f32[64,256]{1,0:T(8,128)S(1)}, u32[]{:S(2)}) %copy-start.3) | copy-done | bytes 65560
  36.7 0.0 copy-done.4
  36.7 2.4 %shard_map.138 = (f32[64,256]{1,0:T(8,128)}, f32[64,256]{1,0:T(8,128)}, f32[64,256]{1,0:T(8,128)}, f32[64,256]{1,0:T(8,128)}) custom-call(f32[64,256]{1,0:T(8,128)} %copy-done.3, f32[64,256]{1,0:T(8,128)} %copy-done.4, bf16[6,64,64]{2,1,0:T(8,128)(2,1)} %fusion.refs_3_.pick_ref.refs_6_, s32[64,2]{1,0:T(8,128)} %bitcast.20, ...), custom_call_target="tpu_custom_call" | custom-call | tf_op jit(solution)/shard_map/pallas_call | solution.py:293
  39.1 0.0 collective-permute-start.5
  39.1 5.3 %collective-permute-start.6 = (f32[64,256]{1,0:T(8,128)}, f32[64,256]{1,0:T(8,128)S(1)}, u32[]{:S(2)}, u32[]{:S(2)}) collective-permute-start(f32[64,256]{1,0:T(8,128)} %get-tuple-element.27), channel_id=1, source_target_pairs={{8,0},{16,8},{24,16},{32,24},{40,32},{48,40},{56,48},{64,56},{72,6... | collective-permute-start | bytes 196616 | tf_op jit(solution)/shard_map/ppermute | solution.py:348
  44.5 6.8 %shard_map.139 = (f32[64,4096]{1,0:T(8,128)}, f32[64,256]{1,0:T(8,128)}, f32[64,256]{1,0:T(8,128)}) custom-call(f32[64,4096]{1,0:T(8,128)} %get-tuple-element.18.refs_0_, f32[64,256]{1,0:T(8,128)} %get-tuple-element.23.refs_1_, f32[64,256]{1,0:T(8,128)} %get-tuple-element.24.refs_2_, f32[64,4096]{1,0:T(8,128)} %get-tuple-element.17.refs_0_.refs_3_, ...), custom_call_target="tpu_custom_call" | custom-call | flops 2500000000 | bytes 4000000 | tf_op jit(solution)/shard_map/pallas_call | solution.py:273
  51.3 0.0 collective-permute-done.5.lower_ref
  51.3 0.0 copy-start.1
  51.3 0.0 collective-permute-done.6.upper_ref
  51.3 0.0 copy-start.2
  51.3 0.6 %copy-done.1 = f32[64,256]{1,0:T(8,128)} copy-done((f32[64,256]{1,0:T(8,128)}, f32[64,256]{1,0:T(8,128)S(1)}, u32[]{:S(2)}) %copy-start.1) | copy-done | bytes 65560
  51.9 0.0 copy-done.2
  52.0 3.0 %shard_map.140 = (f32[64,4096]{1,0:T(8,128)}, f32[64,256]{1,0:T(8,128)}, f32[64,256]{1,0:T(8,128)}) custom-call(f32[64,4096]{1,0:T(8,128)} %get-tuple-element.25.pre_ref, f32[1,4096]{1,0:T(1,128)} %constant.79.clone.top_ref.refs_2_.refs_5_, f32[64,8]{1,0:T(8,128)} %gather_fusion.3, f32[64,256]{1,0:T(8,128)} %copy-done.1, f32[64,256]{1,0:T(8,128)} %copy-done.2, ...), custom_call_target="tpu_custom_call" | custom-call | tf_op jit(solution)/shard_map/pallas_call | solution.py:304
  (15 shorter events, 0.2 us)
Async XLA Ops:
  5.9 9.8 %copy-start.5 = (s32[1,4,64]{2,1,0:T(4,128)S(1)}, s32[1,4,64]{2,1,0:T(4,128)}, u32[]{:S(2)}) copy-start(s32[1,4,64]{2,1,0:T(4,128)} %param.19) | copy-start | bytes 3076
  6.0 9.8 %copy-start.6 = (s32[1,2,64]{2,1,0:T(2,128)S(1)}, s32[1,2,64]{2,1,0:T(2,128)}, u32[]{:S(2)}) copy-start(s32[1,2,64]{2,1,0:T(2,128)} %param.20) | copy-start | bytes 1540
  6.0 10.6 %copy-start.7 = (s32[1,2,64]{2,1,0:T(2,128)S(1)}, s32[1,2,64]{2,1,0:T(2,128)}, u32[]{:S(2)}) copy-start(s32[1,2,64]{2,1,0:T(2,128)} %param.21) | copy-start | bytes 1540
  6.0 14.1 %copy-start = (f32[64,4096]{1,0:T(8,128)S(1)}, f32[64,4096]{1,0:T(8,128)}, u32[]{:S(2)}) copy-start(f32[64,4096]{1,0:T(8,128)} %param.14) | copy-start | bytes 3145732
  6.1 11.3 %collective-permute-start = (f32[5,4096]{1,0:T(8,128)S(1)}, f32[5,4096]{1,0:T(8,128)S(1)}, u32[]{:S(2)}, u32[]{:S(2)}) collective-permute-start(f32[5,4096]{1,0:T(8,128)S(1)} %get-tuple-element.34), channel_id=1, source_target_pairs={{0,1},{1,2},{2,3},{3,4},{4,5},{5,6},{6,7},{7,8},{8,9},{9,10},{10,1... | collective-permute-start | bytes 245768 | tf_op jit(solution)/shard_map/ppermute | solution.py:389
  6.2 11.5 %collective-permute-start.2 = (f32[5,4096]{1,0:T(8,128)S(1)}, f32[5,4096]{1,0:T(8,128)S(1)}, u32[]{:S(2)}, u32[]{:S(2)}) collective-permute-start(f32[5,4096]{1,0:T(8,128)S(1)} %get-tuple-element.35), channel_id=1, source_target_pairs={{0,64},{1,65},{2,66},{3,67},{4,68},{5,69},{6,70},{7,71},{8,72},{9,... | collective-permute-start | bytes 245768 | tf_op jit(solution)/shard_map/ppermute | solution.py:389
  9.6 8.7 %collective-permute-start.1 = (f32[5,4096]{1,0:T(8,128)S(1)}, f32[5,4096]{1,0:T(8,128)S(1)}, u32[]{:S(2)}, u32[]{:S(2)}) collective-permute-start(f32[5,4096]{1,0:T(8,128)S(1)} %get-tuple-element.36), channel_id=1, source_target_pairs={{0,127},{1,0},{2,1},{3,2},{4,3},{5,4},{6,5},{7,6},{8,7},{9,8},{10,... | collective-permute-start | bytes 245768 | tf_op jit(solution)/shard_map/ppermute | solution.py:389
  24.5 11.5 %collective-permute-start.3 = (f32[64,256]{1,0:T(8,128)}, f32[64,256]{1,0:T(8,128)S(1)}, u32[]{:S(2)}, u32[]{:S(2)}) collective-permute-start(f32[64,256]{1,0:T(8,128)} %get-tuple-element.19), channel_id=1, source_target_pairs={{0,8},{8,16},{16,24},{24,32},{32,40},{40,48},{48,56},{56,64},{64,7... | collective-permute-start | bytes 196616 | tf_op jit(solution)/shard_map/ppermute | solution.py:348
  24.5 11.5 %collective-permute-start.4 = (f32[64,256]{1,0:T(8,128)}, f32[64,256]{1,0:T(8,128)S(1)}, u32[]{:S(2)}, u32[]{:S(2)}) collective-permute-start(f32[64,256]{1,0:T(8,128)} %get-tuple-element.20), channel_id=1, source_target_pairs={{8,0},{16,8},{24,16},{32,24},{40,32},{48,40},{56,48},{64,56},{72,6... | collective-permute-start | bytes 196616 | tf_op jit(solution)/shard_map/ppermute | solution.py:348
  36.1 0.6 %copy-start.3 = (f32[64,256]{1,0:T(8,128)}, f32[64,256]{1,0:T(8,128)S(1)}, u32[]{:S(2)}) copy-start(f32[64,256]{1,0:T(8,128)S(1)} %collective-permute-done.3.lower_ref) | copy-start | bytes 196612
  36.1 0.6 %copy-start.4 = (f32[64,256]{1,0:T(8,128)}, f32[64,256]{1,0:T(8,128)S(1)}, u32[]{:S(2)}) copy-start(f32[64,256]{1,0:T(8,128)S(1)} %collective-permute-done.4.upper_ref) | copy-start | bytes 196612
  39.1 12.2 %collective-permute-start.5 = (f32[64,256]{1,0:T(8,128)}, f32[64,256]{1,0:T(8,128)S(1)}, u32[]{:S(2)}, u32[]{:S(2)}) collective-permute-start(f32[64,256]{1,0:T(8,128)} %get-tuple-element.26), channel_id=1, source_target_pairs={{0,8},{8,16},{16,24},{24,32},{32,40},{40,48},{48,56},{56,64},{64,7... | collective-permute-start | bytes 196616 | tf_op jit(solution)/shard_map/ppermute | solution.py:348
  39.1 12.2 %collective-permute-start.6 = (f32[64,256]{1,0:T(8,128)}, f32[64,256]{1,0:T(8,128)S(1)}, u32[]{:S(2)}, u32[]{:S(2)}) collective-permute-start(f32[64,256]{1,0:T(8,128)} %get-tuple-element.27), channel_id=1, source_target_pairs={{8,0},{16,8},{24,16},{32,24},{40,32},{48,40},{56,48},{64,56},{72,6... | collective-permute-start | bytes 196616 | tf_op jit(solution)/shard_map/ppermute | solution.py:348
  51.3 0.6 %copy-start.1 = (f32[64,256]{1,0:T(8,128)}, f32[64,256]{1,0:T(8,128)S(1)}, u32[]{:S(2)}) copy-start(f32[64,256]{1,0:T(8,128)S(1)} %collective-permute-done.5.lower_ref) | copy-start | bytes 196612
  51.3 0.6 %copy-start.2 = (f32[64,256]{1,0:T(8,128)}, f32[64,256]{1,0:T(8,128)S(1)}, u32[]{:S(2)}) copy-start(f32[64,256]{1,0:T(8,128)S(1)} %collective-permute-done.6.upper_ref) | copy-start | bytes 196612

commit v7 on v6

--- a/solution.py
+++ b/solution.py
@@ -313,12 +313,28 @@
     )(pre, top, weight, lower, upper, picks, codes, flip)
 
 
-def prep_body(placed_ref, top_ref, weight_ref, field_ref, even_ref, total_ref):
+def prep_body(
+    coef_ref, first_ref, second_ref, third_ref, source_ref, top_ref, weight_ref,
+    field_ref, even_ref, total_ref
+):
+    count = coef_ref.shape[0]
+    source = source_ref[...]
+    lane = lax.broadcasted_iota(jnp.int32, (1, count), 1)
+    local = (source == lane).astype(jnp.bfloat16)
+    pieces = split_three(coef_ref[...])
+    order = weight_ref[:, 7:8]
     news = []
     for a in range(P_SIZE):
         lanes = slice(a * PLANE, (a + 1) * PLANE)
-        live = top_ref[:, lanes] <= weight_ref[:, 7:8]
-        new = jnp.where(live, placed_ref[:, lanes], 0.0)
+        joined = mxu(local, jnp.concatenate([piece[:, lanes] for piece in pieces], axis=1))
+        placed = joined[:, :PLANE] + joined[:, PLANE : 2 * PLANE] + joined[:, 2 * PLANE :]
+        moving = first_ref.shape[0] - 1
+        for index, parcel_ref in enumerate((first_ref, second_ref, third_ref)):
+            for row in range(moving):
+                hit = source == count + moving * index + row
+                placed = jnp.where(hit, parcel_ref[row : row + 1, lanes], placed)
+        live = top_ref[:, lanes] <= order
+        new = jnp.where(live, placed, 0.0)
         field_ref[:, lanes] = new
         news.append(new)
     even, total = end_traces(news)
@@ -326,19 +342,19 @@
     total_ref[...] = total
 
 
-def prep(placed, top, weight):
-    count = placed.shape[0]
+def prep(coefficients, parcels, source, top, weight):
+    count = coefficients.shape[0]
     spec = pl.BlockSpec(memory_space=pltpu.VMEM)
     return pl.pallas_call(
         prep_body,
         out_shape=(
-            jax.ShapeDtypeStruct(placed.shape, jnp.float32),
+            jax.ShapeDtypeStruct(coefficients.shape, jnp.float32),
             jax.ShapeDtypeStruct((count, PLANE), jnp.float32),
             jax.ShapeDtypeStruct((count, PLANE), jnp.float32),
         ),
-        in_specs=[spec] * 3,
+        in_specs=[spec] * 7,
         out_specs=(spec, spec, spec),
-    )(placed, top, weight)
+    )(coefficients, *parcels, source, top, weight)
 
 
 def exchange(even, total):
@@ -381,17 +397,16 @@
     parcels = jnp.concatenate(
         [coefficients[picked].reshape(len(shifts), moving, P_SIZE**3), side_rows], axis=1
     )
-    got_coef = [coefficients]
+    arrivals = []
     got_side = [side_info]
     got_slot = [jnp.where(destination == here, new_slot, element_count)]
     for index, shift in enumerate(shifts):
         pairs = [(i, (i + shift) % blocks_all) for i in range(blocks_all)]
         arrived = lax.ppermute(parcels[index], ("dom", "face"), pairs)
         arrived_side = arrived[moving, : moving * side_width].reshape(moving, side_width)
-        got_coef.append(arrived[:moving])
+        arrivals.append(arrived)
         got_side.append(arrived_side)
         got_slot.append(arrived_side[:, 6].astype(jnp.int32))
-    got_coef = jnp.concatenate(got_coef, axis=0)
     got_side = jnp.concatenate(got_side, axis=0)
     got_slot = jnp.concatenate(got_slot, axis=0)
     hit = got_slot[None, :] == jnp.arange(element_count, dtype=jnp.int32)[:, None]
@@ -407,7 +422,7 @@
     ).astype(jnp.bfloat16)
     codes = partner_turns[0].T
     spread_hi, spread_lo, lift, flip = tables
-    field, even, total = prep(got_coef[source], top, weight)
+    field, even, total = prep(coefficients, arrivals, source[:, None], top, weight)
     first_step = 0.5 * TIME_STEP
     lower, upper = exchange(even, total)
     pre, even, total = inner(

time: 55.3 us -> 62.1 us (1.12)
  waiting for transfers between devices: 0.47 us -> 6.39 us
  local copies, waits for them, and re-layouts: 8.18 us -> 11 us
  other arithmetic: 4.86 us -> 2.1 us
  Pallas kernels: 21 us -> 22.1 us
    ppermute x3, waiting for transfers between devices: 0.46 us -> 6.38 us  [shards(): arrived = lax.ppermute(parcels[index], ('dom', 'face'), pairs)]
    unnamed x16 -> x30, local copies, waits for them, and re-layouts: 1.28 us -> 5.28 us
    gather x1 -> x0, local copies, waits for them, and re-layouts: 1.85 us -> none  [shards(): field, even, total = prep(got_coef[source], top, weight)]
    pallas_call x1, Pallas kernels: 2.51 us -> 3.68 us  [prep(): pl.pallas_call(prep_body, out_shape=(jax.ShapeDtypeStruct(coefficients.sh...]
    broadcast_in_dim x0 -> x1, local copies, waits for them, and re-layouts: none -> 0.71 us  [shards(): source[:, None]]
    concatenate x1, other arithmetic: 0.71 us -> 0.01 us  [shards(): jnp.concatenate([diffusion, velocity, new_slot[:, None].astype(jnp.float3...]
    convert_element_type x1, other arithmetic: 0.66 us -> 0.01 us  [shards(): orders[:, None].astype(jnp.float32)]
    select_n x1, other arithmetic: 0.66 us -> 0.01 us  [shards(): goal = (here + jnp.asarray(shifts, jnp.int32)) % blocks_all]
  transfers between devices with their start and end apart: 7 -> 7, of which waited for: 2 -> 1; matrix products, arithmetic and copies ran while one was open for 4% -> 3% of each run, Pallas kernels for 24% -> 21%
where the time goes in v7:
time: 62.1 us; the launch traced here: 61.7 us
  Pallas kernels  22.1 us (36%)
  starting transfers between devices  19.9 us (32%)
  local copies, waits for them, and re-layouts  11 us (18%)
  waiting for transfers between devices  6.39 us (10%)
  other arithmetic  2.1 us (3%)
    pallas_call x2, Pallas kernels, inner(): pl.pallas_call(functools.partial(inner_body, scale=scale, carried=carried...  13 us
    ppermute x4, starting transfers between devices, exchange(): return (lax.ppermute(total, 'dom', up), lax.ppermute(even, 'dom', down))  10.7 us
    ppermute x3, starting transfers between devices, shards(): arrived = lax.ppermute(parcels[index], ('dom', 'face'), pairs)  9.24 us
    ppermute x3, waiting for transfers between devices, shards(): arrived = lax.ppermute(parcels[index], ('dom', 'face'), pairs)  6.38 us
    unnamed x30, local copies, waits for them, and re-layouts  5.28 us
    pallas_call x1, Pallas kernels, prep(): pl.pallas_call(prep_body, out_shape=(jax.ShapeDtypeStruct(coefficients.sh...  3.68 us
    pallas_call x1, Pallas kernels, outer(): pl.pallas_call(functools.partial(outer_body, scale=scale), out_shape=(jax...  3.02 us
    pallas_call x1, Pallas kernels, faces(): pl.pallas_call(functools.partial(faces_body, scale=scale), out_shape=(squ...  2.42 us
  transfers between devices with their start and end apart: 7, of which 1 were waited for; matrix products, arithmetic and copies ran while one was open for 3% of the time, Pallas kernels for 21%

profile of v7, /device:TPU:0, one launch (start us, length us, event | category | flops | bytes accessed | tf_op | source)
XLA Modules:
  0.0 61.7 jit_solution(5515013965645582414)
XLA Ops:
  0.0 0.0 copy-start.14
  0.0 0.7 %copy-done.14 = s32[3]{0:T(128)S(1)} copy-done((s32[3]{0:T(128)S(1)}, s32[3]{0:T(128)}, u32[]{:S(2)}) %copy-start.14) | copy-done | bytes 36
  0.7 0.0 copy-start.12
  0.7 0.6 %copy-done.12 = s32[64]{0:T(128)S(1)} copy-done((s32[64]{0:T(128)S(1)}, s32[64]{0:T(128)}, u32[]{:S(2)}) %copy-start.12) | copy-done | bytes 280
  1.3 0.1 fusion.5
  1.4 0.2 reduce_window_sum.11
  1.6 0.1 select_reduce_fusion.1
  1.8 0.1 reshape.106
  1.9 0.0 copy-start.13
  1.9 0.6 %copy-done.13 = s32[64]{0:T(128)S(1)} copy-done((s32[64]{0:T(128)S(1)}, s32[64]{0:T(128)}, u32[]{:S(2)}) %copy-start.13) | copy-done | bytes 280
  2.6 0.0 copy-start.9
  2.6 0.0 copy-start.8
  2.6 0.7 %copy-done.9 = f32[64,3]{0,1:T(4,128)S(1)} copy-done((f32[64,3]{0,1:T(4,128)S(1)}, f32[64,3]{0,1:T(4,128)}, u32[]{:S(2)}) %copy-start.9) | copy-done | bytes 792
  3.2 0.0 copy-done.8
  3.3 0.1 copy.37
  3.4 0.6 gather_fusion.1
  3.9 0.1 reshape.133
  4.0 1.9 %gather_fusion = f32[12,4096]{1,0:T(8,128)S(1)} fusion(f32[64,4096]{1,0:T(8,128)} %coef_ref.1, s32[1024]{0:T(1024)S(1)} %pad_clamp_fusion.1), kind=kCustom, calls=%fused_computation | custom fusion | bytes 393264 | tf_op jit(solution)/shard_map/gather | solution.py:398
  5.9 0.1 reshape.107
  6.1 3.4 %collective-permute-start.2 = (f32[5,4096]{1,0:T(8,128)S(1)}, f32[5,4096]{1,0:T(8,128)S(1)}, u32[]{:S(2)}, u32[]{:S(2)}) collective-permute-start(f32[5,4096]{1,0:T(8,128)S(1)} %get-tuple-element.34), channel_id=1, source_target_pairs={{0,64},{1,65},{2,66},{3,67},{4,68},{5,69},{6,70},{7,71},{8,72},{9,... | collective-permute-start | bytes 245768 | tf_op jit(solution)/shard_map/ppermute | solution.py:405
  9.4 5.9 %collective-permute-start.1 = (f32[5,4096]{1,0:T(8,128)S(1)}, f32[5,4096]{1,0:T(8,128)S(1)}, u32[]{:S(2)}, u32[]{:S(2)}) collective-permute-start(f32[5,4096]{1,0:T(8,128)S(1)} %get-tuple-element.35), channel_id=1, source_target_pairs={{0,127},{1,0},{2,1},{3,2},{4,3},{5,4},{6,5},{7,6},{8,7},{9,8},{10,... | collective-permute-start | bytes 245768 | tf_op jit(solution)/shard_map/ppermute | solution.py:405
  15.3 0.0 copy-start.7
  15.3 0.0 collective-permute-start
  15.3 0.7 %copy-done.7 = s32[1,4,64]{2,1,0:T(4,128)S(1)} copy-done((s32[1,4,64]{2,1,0:T(4,128)S(1)}, s32[1,4,64]{2,1,0:T(4,128)}, u32[]{:S(2)}) %copy-start.7) | copy-done | bytes 1048
  16.0 0.0 copy-done.10
  16.0 0.8 %fusion.refs_3_.pick_ref.refs_6_ = bf16[6,64,64]{2,1,0:T(8,128)(2,1)} fusion(s32[6,64]{1,0:T(8,128)S(1)} %pad_add_fusion), kind=kLoop, calls=%fused_computation.6 | loop fusion | flops 49152 | bytes 50688 | tf_op jit(solution)/shard_map/convert_element_type | solution.py:422
  16.8 0.7 %copy-done.11 = s32[1,2,64]{2,1,0:T(2,128)S(1)} copy-done((s32[1,2,64]{2,1,0:T(2,128)S(1)}, s32[1,2,64]{2,1,0:T(2,128)}, u32[]{:S(2)}) %copy-start.11) | copy-done | bytes 536
  17.5 0.7 %copy.41 = s32[2,64]{0,1:T(8,128)} copy(s32[2,64]{1,0:T(2,128)S(1)} %bitcast.24) | data formatting | bytes 1024 | tf_op jit(solution)/shard_map/squeeze | solution.py:423
  18.2 0.0 collective-permute-done.2.third_ref
  18.2 0.1 reshape_squeeze.11
  18.3 0.2 convert_reduce_fusion
  18.5 0.0 collective-permute-done.1.second_ref
  18.5 0.0 copy-start.1
  18.5 0.1 reshape_squeeze.10
  18.6 0.2 convert_reduce_fusion.1
  18.8 6.4 %collective-permute-done.first_ref = f32[5,4096]{1,0:T(8,128)S(1)} collective-permute-done((f32[5,4096]{1,0:T(8,128)S(1)}, f32[5,4096]{1,0:T(8,128)S(1)}, u32[]{:S(2)}, u32[]{:S(2)}) %collective-permute-start) | collective-permute-done | bytes 81952 | tf_op jit(solution)/shard_map/ppermute | solution.py:405
  25.2 0.1 reshape_squeeze.9
  25.3 0.2 convert_reduce_fusion.2
  25.5 0.1 pad_add_fusion.1
  25.5 0.1 select_reduce_fusion
  25.7 0.7 %copy.40.source_ref = s32[64,1]{1,0:T(8,128)} copy(s32[64,1]{0,1:T(1,128)S(1)} %bitcast.25) | data formatting | bytes 512 | tf_op jit(solution)/shard_map/broadcast_in_dim | solution.py:425
  26.4 1.2 %gather_fusion.2 = f32[64,8]{1,0:T(8,128)} fusion(f32[76,8]{1,0:T(8,128)S(1)} %pad_maximum_fusion, s32[1024]{0:T(1024)S(1)} %pad_clamp_fusion), kind=kCustom, calls=%fused_computation.2 | custom fusion | bytes 4352 | tf_op jit(solution)/shard_map/gather | solution.py:415
  27.6 0.0 copy-done
  27.6 0.0 copy-done.1
  27.6 0.0 copy-done.2
  27.6 3.7 %shard_map.136 = (f32[64,4096]{1,0:T(8,128)}, f32[64,256]{1,0:T(8,128)}, f32[64,256]{1,0:T(8,128)}) custom-call(f32[64,4096]{1,0:T(8,128)} %coef_ref.1, f32[5,4096]{1,0:T(8,128)} %copy-done.2, f32[5,4096]{1,0:T(8,128)} %copy-done.1, f32[5,4096]{1,0:T(8,128)} %copy-done, s32[64,1]{1,0:T(8,128)} %copy.40.source_ref, ...), custom_call_target="tpu_custom_call" | custom-call | tf_op jit(solution)/shard_map/pallas_call | solution.py:348
  31.3 0.0 collective-permute-start.3
  31.3 5.3 %collective-permute-start.4 = (f32[64,256]{1,0:T(8,128)}, f32[64,256]{1,0:T(8,128)S(1)}, u32[]{:S(2)}, u32[]{:S(2)}) collective-permute-start(f32[64,256]{1,0:T(8,128)} %get-tuple-element.20), channel_id=1, source_target_pairs={{8,0},{16,8},{24,16},{32,24},{40,32},{48,40},{56,48},{64,56},{72,6... | collective-permute-start | bytes 196616 | tf_op jit(solution)/shard_map/ppermute | solution.py:364
  36.6 6.2 %shard_map.137 = (f32[64,4096]{1,0:T(8,128)}, f32[64,256]{1,0:T(8,128)}, f32[64,256]{1,0:T(8,128)}) custom-call(f32[64,4096]{1,0:T(8,128)} %get-tuple-element.17.refs_0_.refs_3_, f32[64,8]{1,0:T(8,128)} %gather_fusion.2, f32[1,4096]{1,0:T(1,128)} %constant.79.clone.top_ref.refs_2_.refs_5_, bf16[6,64,64]{2,1,0:T(8,128)(2,1)} %fusion.refs_3_.pick_ref.refs_6_, ...), custom_call_target="tpu_custom_call" | custom-call | flops 2500000000 | bytes 4000000 | tf_op jit(solution)/shard_map/pallas_call | solution.py:273
  42.8 0.0 collective-permute-done.3.lower_ref
  42.8 0.0 collective-permute-done.4.upper_ref
  42.8 0.0 copy-start.6
  42.8 0.6 copy-done.5
  43.5 0.0 copy-done.6
  43.5 2.4 %shard_map.138 = (f32[64,256]{1,0:T(8,128)}, f32[64,256]{1,0:T(8,128)}, f32[64,256]{1,0:T(8,128)}, f32[64,256]{1,0:T(8,128)}) custom-call(f32[64,256]{1,0:T(8,128)} %copy-done.5, f32[64,256]{1,0:T(8,128)} %copy-done.6, bf16[6,64,64]{2,1,0:T(8,128)(2,1)} %fusion.refs_3_.pick_ref.refs_6_, s32[64,2]{1,0:T(8,128)} %bitcast.20, ...), custom_call_target="tpu_custom_call" | custom-call | tf_op jit(solution)/shard_map/pallas_call | solution.py:293
  45.9 0.0 collective-permute-start.5
  45.9 5.3 %collective-permute-start.6 = (f32[64,256]{1,0:T(8,128)}, f32[64,256]{1,0:T(8,128)S(1)}, u32[]{:S(2)}, u32[]{:S(2)}) collective-permute-start(f32[64,256]{1,0:T(8,128)} %get-tuple-element.27), channel_id=1, source_target_pairs={{8,0},{16,8},{24,16},{32,24},{40,32},{48,40},{56,48},{64,56},{72,6... | collective-permute-start | bytes 196616 | tf_op jit(solution)/shard_map/ppermute | solution.py:364
  51.2 6.8 %shard_map.139 = (f32[64,4096]{1,0:T(8,128)}, f32[64,256]{1,0:T(8,128)}, f32[64,256]{1,0:T(8,128)}) custom-call(f32[64,4096]{1,0:T(8,128)} %get-tuple-element.18.refs_0_, f32[64,256]{1,0:T(8,128)} %get-tuple-element.23.refs_1_, f32[64,256]{1,0:T(8,128)} %get-tuple-element.24.refs_2_, f32[64,4096]{1,0:T(8,128)} %get-tuple-element.17.refs_0_.refs_3_, ...), custom_call_target="tpu_custom_call" | custom-call | flops 2500000000 | bytes 4000000 | tf_op jit(solution)/shard_map/pallas_call | solution.py:273
  58.1 0.0 collective-permute-done.5.lower_ref
  58.1 0.0 collective-permute-done.6.upper_ref
  58.1 0.0 copy-start.4
  58.1 0.6 copy-done.3
  58.7 0.0 copy-done.4
  58.7 3.0 %shard_map.140 = (f32[64,4096]{1,0:T(8,128)}, f32[64,256]{1,0:T(8,128)}, f32[64,256]{1,0:T(8,128)}) custom-call(f32[64,4096]{1,0:T(8,128)} %get-tuple-element.25.pre_ref, f32[1,4096]{1,0:T(1,128)} %constant.79.clone.top_ref.refs_2_.refs_5_, f32[64,8]{1,0:T(8,128)} %gather_fusion.2, f32[64,256]{1,0:T(8,128)} %copy-done.3, f32[64,256]{1,0:T(8,128)} %copy-done.4, ...), custom_call_target="tpu_custom_call" | custom-call | tf_op jit(solution)/shard_map/pallas_call | solution.py:304
  (22 shorter events, 0.2 us)
Async XLA Ops:
  0.0 0.7 %copy-start.14 = (s32[3]{0:T(128)S(1)}, s32[3]{0:T(128)}, u32[]{:S(2)}) copy-start(s32[3]{0:T(128)} %constant.78.clone) | copy-start | bytes 40
  0.7 0.7 %copy-start.12 = (s32[64]{0:T(128)S(1)}, s32[64]{0:T(128)}, u32[]{:S(2)}) copy-start(s32[64]{0:T(128)} %param.18) | copy-start | bytes 772
  1.9 0.7 %copy-start.13 = (s32[64]{0:T(128)S(1)}, s32[64]{0:T(128)}, u32[]{:S(2)}) copy-start(s32[64]{0:T(128)} %param.17) | copy-start | bytes 772
  2.6 0.7 %copy-start.9 = (f32[64,3]{0,1:T(4,128)S(1)}, f32[64,3]{0,1:T(4,128)}, u32[]{:S(2)}) copy-start(f32[64,3]{0,1:T(4,128)} %param.15) | copy-start | bytes 2308
  2.6 0.7 %copy-start.8 = (f32[64,3]{0,1:T(4,128)S(1)}, f32[64,3]{0,1:T(4,128)}, u32[]{:S(2)}) copy-start(f32[64,3]{0,1:T(4,128)} %param.16) | copy-start | bytes 2308
  6.1 12.1 %collective-permute-start.2 = (f32[5,4096]{1,0:T(8,128)S(1)}, f32[5,4096]{1,0:T(8,128)S(1)}, u32[]{:S(2)}, u32[]{:S(2)}) collective-permute-start(f32[5,4096]{1,0:T(8,128)S(1)} %get-tuple-element.34), channel_id=1, source_target_pairs={{0,64},{1,65},{2,66},{3,67},{4,68},{5,69},{6,70},{7,71},{8,72},{9,... | collective-permute-start | bytes 245768 | tf_op jit(solution)/shard_map/ppermute | solution.py:405
  9.4 9.0 %collective-permute-start.1 = (f32[5,4096]{1,0:T(8,128)S(1)}, f32[5,4096]{1,0:T(8,128)S(1)}, u32[]{:S(2)}, u32[]{:S(2)}) collective-permute-start(f32[5,4096]{1,0:T(8,128)S(1)} %get-tuple-element.35), channel_id=1, source_target_pairs={{0,127},{1,0},{2,1},{3,2},{4,3},{5,4},{6,5},{7,6},{8,7},{9,8},{10,... | collective-permute-start | bytes 245768 | tf_op jit(solution)/shard_map/ppermute | solution.py:405
  15.3 0.7 %copy-start.7 = (s32[1,4,64]{2,1,0:T(4,128)S(1)}, s32[1,4,64]{2,1,0:T(4,128)}, u32[]{:S(2)}) copy-start(s32[1,4,64]{2,1,0:T(4,128)} %param.19) | copy-start | bytes 3076
  15.3 9.8 %collective-permute-start = (f32[5,4096]{1,0:T(8,128)S(1)}, f32[5,4096]{1,0:T(8,128)S(1)}, u32[]{:S(2)}, u32[]{:S(2)}) collective-permute-start(f32[5,4096]{1,0:T(8,128)S(1)} %get-tuple-element.36), channel_id=1, source_target_pairs={{0,1},{1,2},{2,3},{3,4},{4,5},{5,6},{6,7},{7,8},{8,9},{9,10},{10,1... | collective-permute-start | bytes 245768 | tf_op jit(solution)/shard_map/ppermute | solution.py:405
  15.3 0.7 %copy-start.10 = (s32[1,2,64]{2,1,0:T(2,128)S(1)}, s32[1,2,64]{2,1,0:T(2,128)}, u32[]{:S(2)}) copy-start(s32[1,2,64]{2,1,0:T(2,128)} %param.20) | copy-start | bytes 1540
  16.8 0.7 %copy-start.11 = (s32[1,2,64]{2,1,0:T(2,128)S(1)}, s32[1,2,64]{2,1,0:T(2,128)}, u32[]{:S(2)}) copy-start(s32[1,2,64]{2,1,0:T(2,128)} %param.21) | copy-start | bytes 1540
  18.2 9.4 %copy-start = (f32[5,4096]{1,0:T(8,128)}, f32[5,4096]{1,0:T(8,128)S(1)}, u32[]{:S(2)}) copy-start(f32[5,4096]{1,0:T(8,128)S(1)} %collective-permute-done.2.third_ref) | copy-start | bytes 245764
  18.5 9.1 %copy-start.1 = (f32[5,4096]{1,0:T(8,128)}, f32[5,4096]{1,0:T(8,128)S(1)}, u32[]{:S(2)}) copy-start(f32[5,4096]{1,0:T(8,128)S(1)} %collective-permute-done.1.second_ref) | copy-start | bytes 245764
  25.2 2.4 %copy-start.2 = (f32[5,4096]{1,0:T(8,128)}, f32[5,4096]{1,0:T(8,128)S(1)}, u32[]{:S(2)}) copy-start(f32[5,4096]{1,0:T(8,128)S(1)} %collective-permute-done.first_ref) | copy-start | bytes 245764
  31.3 11.6 %collective-permute-start.3 = (f32[64,256]{1,0:T(8,128)}, f32[64,256]{1,0:T(8,128)S(1)}, u32[]{:S(2)}, u32[]{:S(2)}) collective-permute-start(f32[64,256]{1,0:T(8,128)} %get-tuple-element.19), channel_id=1, source_target_pairs={{0,8},{8,16},{16,24},{24,32},{32,40},{40,48},{48,56},{56,64},{64,7... | collective-permute-start | bytes 196616 | tf_op jit(solution)/shard_map/ppermute | solution.py:364
  31.3 11.6 %collective-permute-start.4 = (f32[64,256]{1,0:T(8,128)}, f32[64,256]{1,0:T(8,128)S(1)}, u32[]{:S(2)}, u32[]{:S(2)}) collective-permute-start(f32[64,256]{1,0:T(8,128)} %get-tuple-element.20), channel_id=1, source_target_pairs={{8,0},{16,8},{24,16},{32,24},{40,32},{48,40},{56,48},{64,56},{72,6... | collective-permute-start | bytes 196616 | tf_op jit(solution)/shard_map/ppermute | solution.py:364
  42.8 0.6 %copy-start.5 = (f32[64,256]{1,0:T(8,128)}, f32[64,256]{1,0:T(8,128)S(1)}, u32[]{:S(2)}) copy-start(f32[64,256]{1,0:T(8,128)S(1)} %collective-permute-done.3.lower_ref) | copy-start | bytes 196612
  42.8 0.6 %copy-start.6 = (f32[64,256]{1,0:T(8,128)}, f32[64,256]{1,0:T(8,128)S(1)}, u32[]{:S(2)}) copy-start(f32[64,256]{1,0:T(8,128)S(1)} %collective-permute-done.4.upper_ref) | copy-start | bytes 196612
  45.9 12.2 %collective-permute-start.5 = (f32[64,256]{1,0:T(8,128)}, f32[64,256]{1,0:T(8,128)S(1)}, u32[]{:S(2)}, u32[]{:S(2)}) collective-permute-start(f32[64,256]{1,0:T(8,128)} %get-tuple-element.26), channel_id=1, source_target_pairs={{0,8},{8,16},{16,24},{24,32},{32,40},{40,48},{48,56},{56,64},{64,7... | collective-permute-start | bytes 196616 | tf_op jit(solution)/shard_map/ppermute | solution.py:364
  45.9 12.2 %collective-permute-start.6 = (f32[64,256]{1,0:T(8,128)}, f32[64,256]{1,0:T(8,128)S(1)}, u32[]{:S(2)}, u32[]{:S(2)}) collective-permute-start(f32[64,256]{1,0:T(8,128)} %get-tuple-element.27), channel_id=1, source_target_pairs={{8,0},{16,8},{24,16},{32,24},{40,32},{48,40},{56,48},{64,56},{72,6... | collective-permute-start | bytes 196616 | tf_op jit(solution)/shard_map/ppermute | solution.py:364
  58.1 0.6 %copy-start.3 = (f32[64,256]{1,0:T(8,128)}, f32[64,256]{1,0:T(8,128)S(1)}, u32[]{:S(2)}) copy-start(f32[64,256]{1,0:T(8,128)S(1)} %collective-permute-done.5.lower_ref) | copy-start | bytes 196612
  58.1 0.6 %copy-start.4 = (f32[64,256]{1,0:T(8,128)}, f32[64,256]{1,0:T(8,128)S(1)}, u32[]{:S(2)}) copy-start(f32[64,256]{1,0:T(8,128)S(1)} %collective-permute-done.6.upper_ref) | copy-start | bytes 196612

commit v8 on v6

--- a/solution.py
+++ b/solution.py
@@ -140,14 +140,18 @@
     return scale * jnp.where(live, update, 0.0)
 
 
-def inner_body(*refs, scale, carried):
+def inner_body(*refs, scale, carried, final):
     if carried is None:
         v_ref, weight_ref, top_ref, pick_ref, spread_hi_ref, spread_lo_ref, lift_ref = refs[:7]
         base_ref = v_ref
     else:
         v_ref, below_ref, above_ref, base_ref, weight_ref, top_ref, pick_ref = refs[:7]
         spread_hi_ref, spread_lo_ref, lift_ref = refs[7:10]
-    partial_ref, even_ref, total_ref = refs[-3:]
+    if final:
+        lower_ref, upper_ref, turn_ref, flip_ref = refs[10:14]
+        partial_ref = refs[-1]
+    else:
+        partial_ref, even_ref, total_ref = refs[-3:]
     count = v_ref.shape[0]
     derivative, second, side_signs, weights = mode_tables()
     second = second.astype(np.float32)
@@ -212,19 +216,26 @@
     lift_mat = lift_ref[...]
     lifted = mxu(jhi, lift_mat) + mxu(jlo, lift_mat)
     even, total = end_traces(slabs)
+    if final:
+        below, above = turn_pair(
+            lower_ref[...], upper_ref[...], pick_ref, turn_ref[...], flip_ref[...]
+        )
     news = []
     for a in range(P_SIZE):
         rows = slice(a * count, (a + 1) * count)
         lanes = slice(a * PLANE, (a + 1) * PLANE)
         own_lift = lifted[rows] + float(lift_signs[0, a]) * even + float(lift_signs[1, a]) * total
+        if final:
+            own_lift = own_lift - float(lift_signs[0, a]) * below - float(lift_signs[1, a]) * above
         live = top[:, lanes] <= order
         update = jnp.where(live, first[a] + inner[rows] - own_lift, 0.0)
         new = base_ref[:, lanes] + scale * update
         partial_ref[:, lanes] = new
         news.append(new)
-    even, total = end_traces(news)
-    even_ref[...] = even
-    total_ref[...] = total
+    if not final:
+        even, total = end_traces(news)
+        even_ref[...] = even
+        total_ref[...] = total
 
 
 def faces_body(
@@ -267,18 +278,16 @@
     total_ref[...] = total
 
 
-def inner(operands, scale, carried):
+def inner(operands, scale, carried, final=False):
     count = operands[0].shape[0]
     spec = pl.BlockSpec(memory_space=pltpu.VMEM)
+    square = jax.ShapeDtypeStruct((count, PLANE), jnp.float32)
+    field = jax.ShapeDtypeStruct(operands[0].shape, jnp.float32)
     return pl.pallas_call(
-        functools.partial(inner_body, scale=scale, carried=carried),
-        out_shape=(
-            jax.ShapeDtypeStruct(operands[0].shape, jnp.float32),
-            jax.ShapeDtypeStruct((count, PLANE), jnp.float32),
-            jax.ShapeDtypeStruct((count, PLANE), jnp.float32),
-        ),
+        functools.partial(inner_body, scale=scale, carried=carried, final=final),
+        out_shape=field if final else (field, square, square),
         in_specs=[spec] * len(operands),
-        out_specs=(spec, spec, spec),
+        out_specs=spec if final else (spec, spec, spec),
         compiler_params=pltpu.CompilerParams(vmem_limit_bytes=60 * 1024 * 1024),
         cost_estimate=pl.CostEstimate(
             flops=2_500_000_000, transcendentals=0, bytes_accessed=4_000_000
@@ -417,12 +426,13 @@
         lower, upper, picks, codes, flip, top, weight, even, total, first_step
     )
     lower, upper = exchange(even, total)
-    pre, _, _ = inner(
-        (pre, below, above, field, weight, top, picks, spread_hi, spread_lo, lift),
+    advanced = inner(
+        (pre, below, above, field, weight, top, picks, spread_hi, spread_lo, lift)
+        + (lower, upper, codes, flip),
         TIME_STEP,
         first_step,
-    )
-    advanced, _, _ = outer(pre, top, weight, lower, upper, picks, codes, flip, TIME_STEP)
+        final=True,
+    )
     return advanced
 
 

time: 55.3 us -> 55.2 us (level)
  Pallas kernels: 21 us -> 18.4 us
  waiting for transfers between devices: 0.47 us -> 2.92 us
    pallas_call x1 -> x0, Pallas kernels: 3.02 us -> none  [outer(): pl.pallas_call(functools.partial(outer_body, scale=scale), out_shape=(jax...]
    ppermute x4, waiting for transfers between devices: 0.01 us -> 2.46 us  [exchange(): return (lax.ppermute(total, 'dom', up), lax.ppermute(even, 'dom', down))]
  transfers between devices with their start and end apart: 7 -> 7, of which waited for: 2 -> 3; matrix products, arithmetic and copies ran while one was open for 4% -> 4% of each run, Pallas kernels for 24% -> 11%
where the time goes in v8:
time: 55.2 us; the launch traced here: 54.9 us
  starting transfers between devices  20.3 us (37%)
  Pallas kernels  18.4 us (33%)
  local copies, waits for them, and re-layouts  8.18 us (15%)
  other arithmetic  4.86 us (9%)
  waiting for transfers between devices  2.92 us (5%)
    pallas_call x2, Pallas kernels, inner(): pl.pallas_call(functools.partial(inner_body, scale=scale, carried=carried...  13.5 us
    ppermute x4, starting transfers between devices, exchange(): return (lax.ppermute(total, 'dom', up), lax.ppermute(even, 'dom', down))  10.7 us
    ppermute x3, starting transfers between devices, shards(): arrived = lax.ppermute(parcels[index], ('dom', 'face'), pairs)  9.63 us
    pallas_call x1, Pallas kernels, prep(): pl.pallas_call(prep_body, out_shape=(jax.ShapeDtypeStruct(placed.shape, j...  2.49 us
    ppermute x4, waiting for transfers between devices, exchange(): return (lax.ppermute(total, 'dom', up), lax.ppermute(even, 'dom', down))  2.46 us
    pallas_call x1, Pallas kernels, faces(): pl.pallas_call(functools.partial(faces_body, scale=scale), out_shape=(squ...  2.41 us
    gather x1, local copies, waits for them, and re-layouts, shards(): coefficients[picked].reshape(len(shifts), moving, P_SIZE ** 3)  1.93 us
    gather x1, local copies, waits for them, and re-layouts, shards(): field, even, total = prep(got_coef[source], top, weight)  1.85 us
  transfers between devices with their start and end apart: 7, of which 3 were waited for; matrix products, arithmetic and copies ran while one was open for 4% of the time, Pallas kernels for 11%

profile of v8, /device:TPU:0, one launch (start us, length us, event | category | flops | bytes accessed | tf_op | source)
XLA Modules:
  0.0 54.9 jit_solution(11021880663323780304)
XLA Ops:
  0.0 0.7 %and_select_fusion.1 = s32[3]{0:T(128)S(1)} fusion(s32[3]{0:T(128)} %constant.78.clone, s32[]{:T(128)S(6)} %add.51), kind=kLoop, calls=%fused_computation.31 | loop fusion | flops 36 | bytes 28 | tf_op jit(solution)/shard_map/jit(remainder)/select_n | solution.py:380
  0.7 0.7 %compare_select_fusion.4 = (s32[64]{0:T(128)S(1)}, s32[64]{0:T(128)S(1)}, s32[64]{0:T(128)S(1)}) fusion(s32[]{:T(128)S(6)} %add.51, s32[64]{0:T(128)} %param.18), kind=kLoop, calls=%fused_computation.29 | loop fusion | flops 1344 | bytes 1028 | tf_op jit(solution)/shard_map/jit(_where)/select_n | solution.py:395
  1.3 0.1 fusion.5
  1.4 0.2 reduce_window_sum.11
  1.7 0.1 select_reduce_fusion.1
  1.8 0.1 reshape.106
  1.9 0.7 %convert_bitcast_fusion = (f32[64,1]{0,1:T(1,128)S(1)}, f32[64,1]{0,1:T(1,128)S(1)}) fusion(s32[64]{0:T(128)} %param.17, s32[64]{0:T(128)S(1)} %get-tuple-element.27), kind=kLoop, calls=%fused_computation.45 | loop fusion | flops 448 | bytes 1024 | tf_op jit(solution)/shard_map/convert_element_type | solution.py:374
  2.6 0.7 %pad_maximum_fusion.2 = f32[64,8]{0,1:T(8,128)S(1)} fusion(f32[64,1]{0,1:T(1,128)S(1)} %get-tuple-element.33, f32[64,1]{0,1:T(1,128)S(1)} %get-tuple-element.34, f32[64,3]{0,1:T(4,128)} %param.16, f32[64,3]{0,1:T(4,128)} %param.15), kind=kLoop, calls=%fused_computation.20 | loop fusion | flops 1536 | bytes 4096 | tf_op jit(solution)/shard_map/concatenate | solution.py:369
  3.3 0.1 copy.34
  3.4 0.6 %gather_fusion.1 = f32[12,8]{1,0:T(8,128)S(1)} fusion(f32[64,8]{1,0:T(8,128)S(1)} %copy.34, s32[1024]{0:T(1024)S(1)} %pad_clamp_fusion.1), kind=kCustom, calls=%fused_computation.1 | custom fusion | bytes 816 | tf_op jit(solution)/shard_map/gather | solution.py:388
  3.9 0.1 reshape.141
  4.0 1.9 %gather_fusion = f32[12,4096]{1,0:T(8,128)S(1)} fusion(f32[64,4096]{1,0:T(8,128)} %param.14, s32[1024]{0:T(1024)S(1)} %pad_clamp_fusion.1), kind=kCustom, calls=%fused_computation | custom fusion | bytes 393264 | tf_op jit(solution)/shard_map/gather | solution.py:391
  5.9 0.0 copy-start.3
  6.0 0.0 copy-start.4
  6.0 0.0 copy-start.5
  6.0 0.0 copy-start
  6.0 0.1 reshape.107
  6.1 0.1 collective-permute-start
  6.2 3.4 %collective-permute-start.2 = (f32[5,4096]{1,0:T(8,128)S(1)}, f32[5,4096]{1,0:T(8,128)S(1)}, u32[]{:S(2)}, u32[]{:S(2)}) collective-permute-start(f32[5,4096]{1,0:T(8,128)S(1)} %get-tuple-element.31), channel_id=1, source_target_pairs={{0,64},{1,65},{2,66},{3,67},{4,68},{5,69},{6,70},{7,71},{8,72},{9,... | collective-permute-start | bytes 245768 | tf_op jit(solution)/shard_map/ppermute | solution.py:398
  9.6 6.2 %collective-permute-start.1 = (f32[5,4096]{1,0:T(8,128)S(1)}, f32[5,4096]{1,0:T(8,128)S(1)}, u32[]{:S(2)}, u32[]{:S(2)}) collective-permute-start(f32[5,4096]{1,0:T(8,128)S(1)} %get-tuple-element.32), channel_id=1, source_target_pairs={{0,127},{1,0},{2,1},{3,2},{4,3},{5,4},{6,5},{7,6},{8,7},{9,8},{10,... | collective-permute-start | bytes 245768 | tf_op jit(solution)/shard_map/ppermute | solution.py:398
  15.8 0.0 copy-done.3
  15.8 0.0 copy-done.4
  15.8 0.8 %fusion.refs_3_.pick_ref.refs_6_ = bf16[6,64,64]{2,1,0:T(8,128)(2,1)} fusion(s32[6,64]{1,0:T(8,128)S(1)} %pad_add_fusion), kind=kLoop, calls=%fused_computation.8 | loop fusion | flops 49152 | bytes 50688 | tf_op jit(solution)/shard_map/convert_element_type | solution.py:416
  16.6 0.0 copy-done.5
  16.6 0.7 %copy.37 = s32[2,64]{0,1:T(8,128)} copy(s32[2,64]{1,0:T(2,128)S(1)} %bitcast.24) | data formatting | bytes 1024 | tf_op jit(solution)/shard_map/squeeze | solution.py:417
  17.3 0.2 collective-permute-done
  17.5 0.1 reshape_squeeze.9
  17.6 0.2 convert_reduce_fusion.2
  17.8 0.0 collective-permute-done.2
  17.8 0.1 reshape_squeeze.11
  17.9 0.2 convert_reduce_fusion
  18.1 0.2 collective-permute-done.1
  18.3 0.1 reshape_squeeze.10
  18.4 0.2 convert_reduce_fusion.1
  18.6 0.1 pad_add_fusion.1
  18.7 0.1 select_reduce_fusion
  18.8 1.2 %gather_fusion.3 = f32[64,8]{1,0:T(8,128)} fusion(f32[76,8]{1,0:T(8,128)S(1)} %pad_maximum_fusion.1, s32[1024]{0:T(1024)S(1)} %pad_clamp_fusion), kind=kCustom, calls=%fused_computation.3 | custom fusion | bytes 4352 | tf_op jit(solution)/shard_map/gather | solution.py:409
  20.1 0.0 copy-done
  20.1 0.1 pad_maximum_fusion
  20.2 1.8 %gather_fusion.2 = f32[64,4096]{1,0:T(8,128)} fusion(f32[76,4096]{1,0:T(8,128)S(1)} %pad_maximum_fusion, s32[1024]{0:T(1024)S(1)} %pad_clamp_fusion), kind=kCustom, calls=%fused_computation.2 | custom fusion | bytes 2097408 | tf_op jit(solution)/shard_map/gather | solution.py:419
  22.0 2.5 %shard_map.136 = (f32[64,4096]{1,0:T(8,128)}, f32[64,256]{1,0:T(8,128)}, f32[64,256]{1,0:T(8,128)}) custom-call(f32[64,4096]{1,0:T(8,128)} %gather_fusion.2, f32[1,4096]{1,0:T(1,128)} %constant.79.clone.top_ref.refs_2_.refs_5_, f32[64,8]{1,0:T(8,128)} %gather_fusion.3), custom_call_target="tpu_custom_call" | custom-call | tf_op jit(solution)/shard_map/pallas_call | solution.py:341
  24.5 0.0 collective-permute-start.3
  24.5 5.3 %collective-permute-start.4 = (f32[64,256]{1,0:T(8,128)}, f32[64,256]{1,0:T(8,128)S(1)}, u32[]{:S(2)}, u32[]{:S(2)}) collective-permute-start(f32[64,256]{1,0:T(8,128)} %get-tuple-element.18), channel_id=1, source_target_pairs={{8,0},{16,8},{24,16},{32,24},{40,32},{48,40},{56,48},{64,56},{72,6... | collective-permute-start | bytes 196616 | tf_op jit(solution)/shard_map/ppermute | solution.py:357
  29.9 6.2 %shard_map.137 = (f32[64,4096]{1,0:T(8,128)}, f32[64,256]{1,0:T(8,128)}, f32[64,256]{1,0:T(8,128)}) custom-call(f32[64,4096]{1,0:T(8,128)} %get-tuple-element.15.refs_0_.refs_3_, f32[64,8]{1,0:T(8,128)} %gather_fusion.3, f32[1,4096]{1,0:T(1,128)} %constant.79.clone.top_ref.refs_2_.refs_5_, bf16[6,64,64]{2,1,0:T(8,128)(2,1)} %fusion.refs_3_.pick_ref.refs_6_, ...), custom_call_target="tpu_custom_call" | custom-call | flops 2500000000 | bytes 4000000 | tf_op jit(solution)/shard_map/pallas_call | solution.py:286
  36.1 0.0 collective-permute-done.3.lower_ref
  36.1 0.0 copy-start.1
  36.1 0.0 collective-permute-done.4.upper_ref
  36.1 0.0 copy-start.2
  36.1 0.6 %copy-done.1 = f32[64,256]{1,0:T(8,128)} copy-done((f32[64,256]{1,0:T(8,128)}, f32[64,256]{1,0:T(8,128)S(1)}, u32[]{:S(2)}) %copy-start.1) | copy-done | bytes 65560
  36.7 0.0 copy-done.2
  36.7 2.4 %shard_map.138 = (f32[64,256]{1,0:T(8,128)}, f32[64,256]{1,0:T(8,128)}, f32[64,256]{1,0:T(8,128)}, f32[64,256]{1,0:T(8,128)}) custom-call(f32[64,256]{1,0:T(8,128)} %copy-done.1, f32[64,256]{1,0:T(8,128)} %copy-done.2, bf16[6,64,64]{2,1,0:T(8,128)(2,1)} %fusion.refs_3_.pick_ref.refs_6_, s32[64,2]{1,0:T(8,128)} %bitcast.20, ...), custom_call_target="tpu_custom_call" | custom-call | tf_op jit(solution)/shard_map/pallas_call | solution.py:302
  39.2 0.0 collective-permute-start.5
  39.2 5.3 %collective-permute-start.6 = (f32[64,256]{1,0:T(8,128)}, f32[64,256]{1,0:T(8,128)S(1)}, u32[]{:S(2)}, u32[]{:S(2)}) collective-permute-start(f32[64,256]{1,0:T(8,128)} %get-tuple-element.24), channel_id=1, source_target_pairs={{8,0},{16,8},{24,16},{32,24},{40,32},{48,40},{56,48},{64,56},{72,6... | collective-permute-start | bytes 196616 | tf_op jit(solution)/shard_map/ppermute | solution.py:357
  44.5 2.4 %collective-permute-done.5.refs_10_ = f32[64,256]{1,0:T(8,128)S(1)} collective-permute-done((f32[64,256]{1,0:T(8,128)}, f32[64,256]{1,0:T(8,128)S(1)}, u32[]{:S(2)}, u32[]{:S(2)}) %collective-permute-start.5) | collective-permute-done | bytes 65568 | tf_op jit(solution)/shard_map/ppermute | solution.py:357
  46.9 0.0 copy-start.6
  47.0 0.0 collective-permute-done.6.refs_11_
  47.0 0.0 copy-start.7
  47.0 0.6 %copy-done.6 = f32[64,256]{1,0:T(8,128)} copy-done((f32[64,256]{1,0:T(8,128)}, f32[64,256]{1,0:T(8,128)S(1)}, u32[]{:S(2)}) %copy-start.6) | copy-done | bytes 65560
  47.6 0.0 copy-done.7
  47.6 7.3 %shard_map.139 = f32[64,4096]{1,0:T(8,128)} custom-call(f32[64,4096]{1,0:T(8,128)} %get-tuple-element.16.refs_0_, f32[64,256]{1,0:T(8,128)} %get-tuple-element.21.refs_1_, f32[64,256]{1,0:T(8,128)} %get-tuple-element.22.refs_2_, f32[64,4096]{1,0:T(8,128)} %get-tuple-element.15.refs_0_.refs_3_, f32[64,8]{1,0:T(8,128)} %gather_fusion.3, ...), custom_call_target="tpu_custom_call" | custom-call | flops 2500000000 | bytes 4000000 | tf_op jit(solution)/shard_map/pallas_call | solution.py:286
  (15 shorter events, 0.2 us)
Async XLA Ops:
  5.9 9.8 %copy-start.3 = (s32[1,4,64]{2,1,0:T(4,128)S(1)}, s32[1,4,64]{2,1,0:T(4,128)}, u32[]{:S(2)}) copy-start(s32[1,4,64]{2,1,0:T(4,128)} %param.19) | copy-start | bytes 3076
  6.0 9.8 %copy-start.4 = (s32[1,2,64]{2,1,0:T(2,128)S(1)}, s32[1,2,64]{2,1,0:T(2,128)}, u32[]{:S(2)}) copy-start(s32[1,2,64]{2,1,0:T(2,128)} %param.20) | copy-start | bytes 1540
  6.0 10.6 %copy-start.5 = (s32[1,2,64]{2,1,0:T(2,128)S(1)}, s32[1,2,64]{2,1,0:T(2,128)}, u32[]{:S(2)}) copy-start(s32[1,2,64]{2,1,0:T(2,128)} %param.21) | copy-start | bytes 1540
  6.0 14.1 %copy-start = (f32[64,4096]{1,0:T(8,128)S(1)}, f32[64,4096]{1,0:T(8,128)}, u32[]{:S(2)}) copy-start(f32[64,4096]{1,0:T(8,128)} %param.14) | copy-start | bytes 3145732
  6.1 11.3 %collective-permute-start = (f32[5,4096]{1,0:T(8,128)S(1)}, f32[5,4096]{1,0:T(8,128)S(1)}, u32[]{:S(2)}, u32[]{:S(2)}) collective-permute-start(f32[5,4096]{1,0:T(8,128)S(1)} %get-tuple-element.30), channel_id=1, source_target_pairs={{0,1},{1,2},{2,3},{3,4},{4,5},{5,6},{6,7},{7,8},{8,9},{9,10},{10,1... | collective-permute-start | bytes 245768 | tf_op jit(solution)/shard_map/ppermute | solution.py:398
  6.2 11.5 %collective-permute-start.2 = (f32[5,4096]{1,0:T(8,128)S(1)}, f32[5,4096]{1,0:T(8,128)S(1)}, u32[]{:S(2)}, u32[]{:S(2)}) collective-permute-start(f32[5,4096]{1,0:T(8,128)S(1)} %get-tuple-element.31), channel_id=1, source_target_pairs={{0,64},{1,65},{2,66},{3,67},{4,68},{5,69},{6,70},{7,71},{8,72},{9,... | collective-permute-start | bytes 245768 | tf_op jit(solution)/shard_map/ppermute | solution.py:398
  9.6 8.7 %collective-permute-start.1 = (f32[5,4096]{1,0:T(8,128)S(1)}, f32[5,4096]{1,0:T(8,128)S(1)}, u32[]{:S(2)}, u32[]{:S(2)}) collective-permute-start(f32[5,4096]{1,0:T(8,128)S(1)} %get-tuple-element.32), channel_id=1, source_target_pairs={{0,127},{1,0},{2,1},{3,2},{4,3},{5,4},{6,5},{7,6},{8,7},{9,8},{10,... | collective-permute-start | bytes 245768 | tf_op jit(solution)/shard_map/ppermute | solution.py:398
  24.5 11.6 %collective-permute-start.3 = (f32[64,256]{1,0:T(8,128)}, f32[64,256]{1,0:T(8,128)S(1)}, u32[]{:S(2)}, u32[]{:S(2)}) collective-permute-start(f32[64,256]{1,0:T(8,128)} %get-tuple-element.17), channel_id=1, source_target_pairs={{0,8},{8,16},{16,24},{24,32},{32,40},{40,48},{48,56},{56,64},{64,7... | collective-permute-start | bytes 196616 | tf_op jit(solution)/shard_map/ppermute | solution.py:357
  24.5 11.6 %collective-permute-start.4 = (f32[64,256]{1,0:T(8,128)}, f32[64,256]{1,0:T(8,128)S(1)}, u32[]{:S(2)}, u32[]{:S(2)}) collective-permute-start(f32[64,256]{1,0:T(8,128)} %get-tuple-element.18), channel_id=1, source_target_pairs={{8,0},{16,8},{24,16},{32,24},{40,32},{48,40},{56,48},{64,56},{72,6... | collective-permute-start | bytes 196616 | tf_op jit(solution)/shard_map/ppermute | solution.py:357
  36.1 0.6 %copy-start.1 = (f32[64,256]{1,0:T(8,128)}, f32[64,256]{1,0:T(8,128)S(1)}, u32[]{:S(2)}) copy-start(f32[64,256]{1,0:T(8,128)S(1)} %collective-permute-done.3.lower_ref) | copy-start | bytes 196612
  36.1 0.6 %copy-start.2 = (f32[64,256]{1,0:T(8,128)}, f32[64,256]{1,0:T(8,128)S(1)}, u32[]{:S(2)}) copy-start(f32[64,256]{1,0:T(8,128)S(1)} %collective-permute-done.4.upper_ref) | copy-start | bytes 196612
  39.2 7.8 %collective-permute-start.5 = (f32[64,256]{1,0:T(8,128)}, f32[64,256]{1,0:T(8,128)S(1)}, u32[]{:S(2)}, u32[]{:S(2)}) collective-permute-start(f32[64,256]{1,0:T(8,128)} %get-tuple-element.23), channel_id=1, source_target_pairs={{0,8},{8,16},{16,24},{24,32},{32,40},{40,48},{48,56},{56,64},{64,7... | collective-permute-start | bytes 196616 | tf_op jit(solution)/shard_map/ppermute | solution.py:357
  39.2 7.8 %collective-permute-start.6 = (f32[64,256]{1,0:T(8,128)}, f32[64,256]{1,0:T(8,128)S(1)}, u32[]{:S(2)}, u32[]{:S(2)}) collective-permute-start(f32[64,256]{1,0:T(8,128)} %get-tuple-element.24), channel_id=1, source_target_pairs={{8,0},{16,8},{24,16},{32,24},{40,32},{48,40},{56,48},{64,56},{72,6... | collective-permute-start | bytes 196616 | tf_op jit(solution)/shard_map/ppermute | solution.py:357
  46.9 0.6 %copy-start.6 = (f32[64,256]{1,0:T(8,128)}, f32[64,256]{1,0:T(8,128)S(1)}, u32[]{:S(2)}) copy-start(f32[64,256]{1,0:T(8,128)S(1)} %collective-permute-done.5.refs_10_) | copy-start | bytes 196612
  47.0 0.6 %copy-start.7 = (f32[64,256]{1,0:T(8,128)}, f32[64,256]{1,0:T(8,128)S(1)}, u32[]{:S(2)}) copy-start(f32[64,256]{1,0:T(8,128)S(1)} %collective-permute-done.6.refs_11_) | copy-start | bytes 196612

commit v9 on v8

--- a/solution.py
+++ b/solution.py
@@ -170,48 +170,69 @@
         ]
     diff0 = jnp.broadcast_to(weight[:, 0:1], (count, PLANE))
     vel0 = jnp.broadcast_to(weight[:, 3:4], (count, PLANE))
+    half = count // 2
+    low = P_SIZE // 2
+
+    def kept(a, x):
+        return x if a < low else x[half:]
+
+    def start(a):
+        return a * count if a < low else low * count + (a - low) * half
+
+    upper_slabs = [s[half:] for s in slabs]
     first = []
     for k in range(P_SIZE):
-        acc_s = None
-        acc_d = None
-        for n in range(k + 1, P_SIZE):
-            if second[k, n] != 0.0:
-                term = float(second[k, n]) * slabs[n]
-                acc_s = term if acc_s is None else acc_s + term
-            if derivative[k, n] != 0.0:
-                term = float(derivative[k, n]) * slabs[n]
-                acc_d = term if acc_d is None else acc_d + term
-        part = jnp.zeros((count, PLANE), jnp.float32)
-        if acc_s is not None:
-            part = part + diff0 * acc_s
-        if acc_d is not None:
-            part = part - vel0 * acc_d
-        first.append(part)
-    stacked = jnp.concatenate(slabs, axis=0)
+        parts = []
+        for rows, source in ((slice(0, half), slabs), (slice(half, count), upper_slabs)):
+            if rows.start == 0 and k >= low:
+                continue
+            acc_s = None
+            acc_d = None
+            top_n = low if rows.start == 0 else P_SIZE
+            for n in range(k + 1, top_n):
+                piece = source[n] if rows.start else source[n][:half]
+                if second[k, n] != 0.0:
+                    term = float(second[k, n]) * piece
+                    acc_s = term if acc_s is None else acc_s + term
+                if derivative[k, n] != 0.0:
+                    term = float(derivative[k, n]) * piece
+                    acc_d = term if acc_d is None else acc_d + term
+            part = jnp.zeros((half, PLANE), jnp.float32)
+            if acc_s is not None:
+                part = part + diff0[rows] * acc_s
+            if acc_d is not None:
+                part = part - vel0[rows] * acc_d
+            parts.append(part)
+        first.append(parts[0] if len(parts) == 1 else jnp.concatenate(parts, axis=0))
+    stacked = jnp.concatenate([kept(a, slabs[a]) for a in range(P_SIZE)], axis=0)
     hi, lo = split_two(stacked)
     spread_hi = spread_hi_ref[...]
     wide = mxu(hi, spread_hi) + mxu(lo, spread_hi)
     fine = mxu(hi, spread_lo_ref[...])
-    weight_rows = jnp.concatenate([weight] * P_SIZE, axis=0)
+    weight_rows = jnp.concatenate([kept(a, weight) for a in range(P_SIZE)], axis=0)
     inner = (
         weight_rows[:, 2:3] * (wide[:, 0:PLANE] + fine[:, 0:PLANE])
         + weight_rows[:, 1:2] * (wide[:, PLANE : 2 * PLANE] + fine[:, PLANE : 2 * PLANE])
         - weight_rows[:, 5:6] * wide[:, 2 * PLANE : 3 * PLANE]
         - weight_rows[:, 4:5] * wide[:, 3 * PLANE : 4 * PLANE]
     )
-    own = jnp.concatenate(
-        [wide[a * count : (a + 1) * count, 4 * PLANE : 4 * PLANE + 128] for a in range(P_SIZE)], axis=1
-    )
-    other = jnp.concatenate(
-        [wide[a * count : (a + 1) * count, 4 * PLANE + 128 : 4 * PLANE + 256] for a in range(P_SIZE)], axis=1
-    )
+    blank = jnp.zeros((half, 128), jnp.float32)
+
+    def trace_block(a, offset):
+        rows = wide[start(a) : start(a) + (count if a < low else half), offset : offset + 128]
+        return rows if a < low else jnp.concatenate([blank, rows], axis=0)
+
+    own = jnp.concatenate([trace_block(a, 4 * PLANE) for a in range(P_SIZE)], axis=1)
+    other = jnp.concatenate([trace_block(a, 4 * PLANE + 128) for a in range(P_SIZE)], axis=1)
     lane = lax.broadcasted_iota(jnp.int32, (1, P_SIZE * 128), 1) % 128
     across = jnp.zeros_like(own)
     for face in range(4):
         gathered = exact_pick(pick_ref[face], other)
         across = jnp.where(lane // P_SIZE == face, gathered, across)
     jump = own - across
-    jump_rows = jnp.concatenate([jump[:, a * 128 : (a + 1) * 128] for a in range(P_SIZE)], axis=0)
+    jump_rows = jnp.concatenate(
+        [kept(a, jump[:, a * 128 : (a + 1) * 128]) for a in range(P_SIZE)], axis=0
+    )
     jhi, jlo = split_two(jump_rows)
     lift_mat = lift_ref[...]
     lifted = mxu(jhi, lift_mat) + mxu(jlo, lift_mat)
@@ -222,14 +243,21 @@
         )
     news = []
     for a in range(P_SIZE):
-        rows = slice(a * count, (a + 1) * count)
+        rows = slice(start(a), start(a) + (count if a < low else half))
         lanes = slice(a * PLANE, (a + 1) * PLANE)
-        own_lift = lifted[rows] + float(lift_signs[0, a]) * even + float(lift_signs[1, a]) * total
+        own_lift = lifted[rows] + float(lift_signs[0, a]) * kept(a, even)
+        own_lift = own_lift + float(lift_signs[1, a]) * kept(a, total)
         if final:
-            own_lift = own_lift - float(lift_signs[0, a]) * below - float(lift_signs[1, a]) * above
-        live = top[:, lanes] <= order
+            own_lift = own_lift - float(lift_signs[0, a]) * kept(a, below)
+            own_lift = own_lift - float(lift_signs[1, a]) * kept(a, above)
+        live = kept(a, top[:, lanes] <= order)
         update = jnp.where(live, first[a] + inner[rows] - own_lift, 0.0)
-        new = base_ref[:, lanes] + scale * update
+        if a < low:
+            new = base_ref[:, lanes] + scale * update
+        else:
+            new = jnp.concatenate(
+                [base_ref[:half, lanes] + 0.0, base_ref[half:, lanes] + scale * update], axis=0
+            )
         partial_ref[:, lanes] = new
         news.append(new)
     if not final:

time: 55.2 us -> 53.5 us (0.969)
  Pallas kernels: 18.4 us -> 16.7 us
    pallas_call x2, Pallas kernels: 13.5 us -> 11.8 us  [inner(): pl.pallas_call(functools.partial(inner_body, scale=scale, carried=carried...]
  transfers between devices with their start and end apart: 7 -> 7, of which waited for: 3 -> 3; matrix products, arithmetic and copies ran while one was open for 4% -> 4% of each run, Pallas kernels for 11% -> 10%
where the time goes in v9:
time: 53.5 us; the launch traced here: 53.2 us
  starting transfers between devices  20.3 us (38%)
  Pallas kernels  16.7 us (31%)
  local copies, waits for them, and re-layouts  8.18 us (15%)
  other arithmetic  4.86 us (9%)
  waiting for transfers between devices  2.92 us (5%)
    pallas_call x2, Pallas kernels, inner(): pl.pallas_call(functools.partial(inner_body, scale=scale, carried=carried...  11.8 us
    ppermute x4, starting transfers between devices, exchange(): return (lax.ppermute(total, 'dom', up), lax.ppermute(even, 'dom', down))  10.7 us
    ppermute x3, starting transfers between devices, shards(): arrived = lax.ppermute(parcels[index], ('dom', 'face'), pairs)  9.63 us
    pallas_call x1, Pallas kernels, prep(): pl.pallas_call(prep_body, out_shape=(jax.ShapeDtypeStruct(placed.shape, j...  2.49 us
    ppermute x4, waiting for transfers between devices, exchange(): return (lax.ppermute(total, 'dom', up), lax.ppermute(even, 'dom', down))  2.46 us
    pallas_call x1, Pallas kernels, faces(): pl.pallas_call(functools.partial(faces_body, scale=scale), out_shape=(squ...  2.42 us
    gather x1, local copies, waits for them, and re-layouts, shards(): coefficients[picked].reshape(len(shifts), moving, P_SIZE ** 3)  1.93 us
    gather x1, local copies, waits for them, and re-layouts, shards(): field, even, total = prep(got_coef[source], top, weight)  1.85 us
  transfers between devices with their start and end apart: 7, of which 3 were waited for; matrix products, arithmetic and copies ran while one was open for 4% of the time, Pallas kernels for 10%

profile of v9, /device:TPU:0, one launch (start us, length us, event | category | flops | bytes accessed | tf_op | source)
XLA Modules:
  0.0 53.2 jit_solution(13778034282183679143)
XLA Ops:
  0.0 0.7 %and_select_fusion.1 = s32[3]{0:T(128)S(1)} fusion(s32[3]{0:T(128)} %constant.78.clone, s32[]{:T(128)S(6)} %add.51), kind=kLoop, calls=%fused_computation.31 | loop fusion | flops 36 | bytes 28 | tf_op jit(solution)/shard_map/jit(remainder)/select_n | solution.py:408
  0.7 0.7 %compare_select_fusion.4 = (s32[64]{0:T(128)S(1)}, s32[64]{0:T(128)S(1)}, s32[64]{0:T(128)S(1)}) fusion(s32[]{:T(128)S(6)} %add.51, s32[64]{0:T(128)} %param.18), kind=kLoop, calls=%fused_computation.29 | loop fusion | flops 1344 | bytes 1028 | tf_op jit(solution)/shard_map/jit(_where)/select_n | solution.py:423
  1.3 0.1 fusion.5
  1.4 0.2 reduce_window_sum.11
  1.7 0.1 select_reduce_fusion.1
  1.8 0.1 reshape.106
  1.9 0.7 %convert_bitcast_fusion = (f32[64,1]{0,1:T(1,128)S(1)}, f32[64,1]{0,1:T(1,128)S(1)}) fusion(s32[64]{0:T(128)} %param.17, s32[64]{0:T(128)S(1)} %get-tuple-element.27), kind=kLoop, calls=%fused_computation.45 | loop fusion | flops 448 | bytes 1024 | tf_op jit(solution)/shard_map/convert_element_type | solution.py:402
  2.6 0.7 %pad_maximum_fusion.2 = f32[64,8]{0,1:T(8,128)S(1)} fusion(f32[64,1]{0,1:T(1,128)S(1)} %get-tuple-element.33, f32[64,1]{0,1:T(1,128)S(1)} %get-tuple-element.34, f32[64,3]{0,1:T(4,128)} %param.16, f32[64,3]{0,1:T(4,128)} %param.15), kind=kLoop, calls=%fused_computation.20 | loop fusion | flops 1536 | bytes 4096 | tf_op jit(solution)/shard_map/concatenate | solution.py:397
  3.3 0.1 copy.34
  3.4 0.6 %gather_fusion.1 = f32[12,8]{1,0:T(8,128)S(1)} fusion(f32[64,8]{1,0:T(8,128)S(1)} %copy.34, s32[1024]{0:T(1024)S(1)} %pad_clamp_fusion.1), kind=kCustom, calls=%fused_computation.1 | custom fusion | bytes 816 | tf_op jit(solution)/shard_map/gather | solution.py:416
  3.9 0.1 reshape.141
  4.0 1.9 %gather_fusion = f32[12,4096]{1,0:T(8,128)S(1)} fusion(f32[64,4096]{1,0:T(8,128)} %param.14, s32[1024]{0:T(1024)S(1)} %pad_clamp_fusion.1), kind=kCustom, calls=%fused_computation | custom fusion | bytes 393264 | tf_op jit(solution)/shard_map/gather | solution.py:419
  5.9 0.0 copy-start.3
  6.0 0.0 copy-start.4
  6.0 0.0 copy-start.5
  6.0 0.0 copy-start
  6.0 0.1 reshape.107
  6.1 0.1 collective-permute-start
  6.2 3.4 %collective-permute-start.2 = (f32[5,4096]{1,0:T(8,128)S(1)}, f32[5,4096]{1,0:T(8,128)S(1)}, u32[]{:S(2)}, u32[]{:S(2)}) collective-permute-start(f32[5,4096]{1,0:T(8,128)S(1)} %get-tuple-element.31), channel_id=1, source_target_pairs={{0,64},{1,65},{2,66},{3,67},{4,68},{5,69},{6,70},{7,71},{8,72},{9,... | collective-permute-start | bytes 245768 | tf_op jit(solution)/shard_map/ppermute | solution.py:426
  9.6 6.2 %collective-permute-start.1 = (f32[5,4096]{1,0:T(8,128)S(1)}, f32[5,4096]{1,0:T(8,128)S(1)}, u32[]{:S(2)}, u32[]{:S(2)}) collective-permute-start(f32[5,4096]{1,0:T(8,128)S(1)} %get-tuple-element.32), channel_id=1, source_target_pairs={{0,127},{1,0},{2,1},{3,2},{4,3},{5,4},{6,5},{7,6},{8,7},{9,8},{10,... | collective-permute-start | bytes 245768 | tf_op jit(solution)/shard_map/ppermute | solution.py:426
  15.8 0.0 copy-done.3
  15.8 0.0 copy-done.4
  15.8 0.8 %fusion.refs_3_.pick_ref.refs_6_ = bf16[6,64,64]{2,1,0:T(8,128)(2,1)} fusion(s32[6,64]{1,0:T(8,128)S(1)} %pad_add_fusion), kind=kLoop, calls=%fused_computation.8 | loop fusion | flops 49152 | bytes 50688 | tf_op jit(solution)/shard_map/convert_element_type | solution.py:444
  16.6 0.0 copy-done.5
  16.6 0.7 %copy.37 = s32[2,64]{0,1:T(8,128)} copy(s32[2,64]{1,0:T(2,128)S(1)} %bitcast.24) | data formatting | bytes 1024 | tf_op jit(solution)/shard_map/squeeze | solution.py:445
  17.3 0.2 collective-permute-done
  17.5 0.1 reshape_squeeze.9
  17.6 0.2 convert_reduce_fusion.2
  17.8 0.0 collective-permute-done.2
  17.8 0.1 reshape_squeeze.11
  17.9 0.2 convert_reduce_fusion
  18.1 0.2 collective-permute-done.1
  18.3 0.1 reshape_squeeze.10
  18.4 0.2 convert_reduce_fusion.1
  18.6 0.1 pad_add_fusion.1
  18.7 0.1 select_reduce_fusion
  18.8 1.2 %gather_fusion.3 = f32[64,8]{1,0:T(8,128)} fusion(f32[76,8]{1,0:T(8,128)S(1)} %pad_maximum_fusion.1, s32[1024]{0:T(1024)S(1)} %pad_clamp_fusion), kind=kCustom, calls=%fused_computation.3 | custom fusion | bytes 4352 | tf_op jit(solution)/shard_map/gather | solution.py:437
  20.1 0.0 copy-done
  20.1 0.1 pad_maximum_fusion
  20.2 1.8 %gather_fusion.2 = f32[64,4096]{1,0:T(8,128)} fusion(f32[76,4096]{1,0:T(8,128)S(1)} %pad_maximum_fusion, s32[1024]{0:T(1024)S(1)} %pad_clamp_fusion), kind=kCustom, calls=%fused_computation.2 | custom fusion | bytes 2097408 | tf_op jit(solution)/shard_map/gather | solution.py:447
  22.0 2.5 %shard_map.136 = (f32[64,4096]{1,0:T(8,128)}, f32[64,256]{1,0:T(8,128)}, f32[64,256]{1,0:T(8,128)}) custom-call(f32[64,4096]{1,0:T(8,128)} %gather_fusion.2, f32[1,4096]{1,0:T(1,128)} %constant.79.clone.top_ref.refs_2_.refs_5_, f32[64,8]{1,0:T(8,128)} %gather_fusion.3), custom_call_target="tpu_custom_call" | custom-call | tf_op jit(solution)/shard_map/pallas_call | solution.py:369
  24.5 0.0 collective-permute-start.3
  24.5 5.3 %collective-permute-start.4 = (f32[64,256]{1,0:T(8,128)}, f32[64,256]{1,0:T(8,128)S(1)}, u32[]{:S(2)}, u32[]{:S(2)}) collective-permute-start(f32[64,256]{1,0:T(8,128)} %get-tuple-element.18), channel_id=1, source_target_pairs={{8,0},{16,8},{24,16},{32,24},{40,32},{48,40},{56,48},{64,56},{72,6... | collective-permute-start | bytes 196616 | tf_op jit(solution)/shard_map/ppermute | solution.py:385
  29.9 5.6 %shard_map.137 = (f32[64,4096]{1,0:T(8,128)}, f32[64,256]{1,0:T(8,128)}, f32[64,256]{1,0:T(8,128)}) custom-call(f32[64,4096]{1,0:T(8,128)} %get-tuple-element.15.refs_0_.refs_3_, f32[64,8]{1,0:T(8,128)} %gather_fusion.3, f32[1,4096]{1,0:T(1,128)} %constant.79.clone.top_ref.refs_2_.refs_5_, bf16[6,64,64]{2,1,0:T(8,128)(2,1)} %fusion.refs_3_.pick_ref.refs_6_, ...), custom_call_target="tpu_custom_call" | custom-call | flops 2500000000 | bytes 4000000 | tf_op jit(solution)/shard_map/pallas_call | solution.py:314
  35.4 0.0 collective-permute-done.3.lower_ref
  35.4 0.0 copy-start.1
  35.4 0.0 collective-permute-done.4.upper_ref
  35.5 0.0 copy-start.2
  35.5 0.6 %copy-done.1 = f32[64,256]{1,0:T(8,128)} copy-done((f32[64,256]{1,0:T(8,128)}, f32[64,256]{1,0:T(8,128)S(1)}, u32[]{:S(2)}) %copy-start.1) | copy-done | bytes 65560
  36.1 0.0 copy-done.2
  36.1 2.4 %shard_map.138 = (f32[64,256]{1,0:T(8,128)}, f32[64,256]{1,0:T(8,128)}, f32[64,256]{1,0:T(8,128)}, f32[64,256]{1,0:T(8,128)}) custom-call(f32[64,256]{1,0:T(8,128)} %copy-done.1, f32[64,256]{1,0:T(8,128)} %copy-done.2, bf16[6,64,64]{2,1,0:T(8,128)(2,1)} %fusion.refs_3_.pick_ref.refs_6_, s32[64,2]{1,0:T(8,128)} %bitcast.20, ...), custom_call_target="tpu_custom_call" | custom-call | tf_op jit(solution)/shard_map/pallas_call | solution.py:330
  38.5 0.0 collective-permute-start.5
  38.5 5.3 %collective-permute-start.6 = (f32[64,256]{1,0:T(8,128)}, f32[64,256]{1,0:T(8,128)S(1)}, u32[]{:S(2)}, u32[]{:S(2)}) collective-permute-start(f32[64,256]{1,0:T(8,128)} %get-tuple-element.24), channel_id=1, source_target_pairs={{8,0},{16,8},{24,16},{32,24},{40,32},{48,40},{56,48},{64,56},{72,6... | collective-permute-start | bytes 196616 | tf_op jit(solution)/shard_map/ppermute | solution.py:385
  43.9 2.4 %collective-permute-done.5.refs_10_ = f32[64,256]{1,0:T(8,128)S(1)} collective-permute-done((f32[64,256]{1,0:T(8,128)}, f32[64,256]{1,0:T(8,128)S(1)}, u32[]{:S(2)}, u32[]{:S(2)}) %collective-permute-start.5) | collective-permute-done | bytes 65568 | tf_op jit(solution)/shard_map/ppermute | solution.py:385
  46.3 0.0 copy-start.6
  46.3 0.0 collective-permute-done.6.refs_11_
  46.3 0.0 copy-start.7
  46.3 0.6 %copy-done.6 = f32[64,256]{1,0:T(8,128)} copy-done((f32[64,256]{1,0:T(8,128)}, f32[64,256]{1,0:T(8,128)S(1)}, u32[]{:S(2)}) %copy-start.6) | copy-done | bytes 65560
  46.9 0.0 copy-done.7
  46.9 6.2 %shard_map.139 = f32[64,4096]{1,0:T(8,128)} custom-call(f32[64,4096]{1,0:T(8,128)} %get-tuple-element.16.refs_0_, f32[64,256]{1,0:T(8,128)} %get-tuple-element.21.refs_1_, f32[64,256]{1,0:T(8,128)} %get-tuple-element.22.refs_2_, f32[64,4096]{1,0:T(8,128)} %get-tuple-element.15.refs_0_.refs_3_, f32[64,8]{1,0:T(8,128)} %gather_fusion.3, ...), custom_call_target="tpu_custom_call" | custom-call | flops 2500000000 | bytes 4000000 | tf_op jit(solution)/shard_map/pallas_call | solution.py:314
  (15 shorter events, 0.2 us)
Async XLA Ops:
  5.9 9.8 %copy-start.3 = (s32[1,4,64]{2,1,0:T(4,128)S(1)}, s32[1,4,64]{2,1,0:T(4,128)}, u32[]{:S(2)}) copy-start(s32[1,4,64]{2,1,0:T(4,128)} %param.19) | copy-start | bytes 3076
  6.0 9.8 %copy-start.4 = (s32[1,2,64]{2,1,0:T(2,128)S(1)}, s32[1,2,64]{2,1,0:T(2,128)}, u32[]{:S(2)}) copy-start(s32[1,2,64]{2,1,0:T(2,128)} %param.20) | copy-start | bytes 1540
  6.0 10.6 %copy-start.5 = (s32[1,2,64]{2,1,0:T(2,128)S(1)}, s32[1,2,64]{2,1,0:T(2,128)}, u32[]{:S(2)}) copy-start(s32[1,2,64]{2,1,0:T(2,128)} %param.21) | copy-start | bytes 1540
  6.0 14.1 %copy-start = (f32[64,4096]{1,0:T(8,128)S(1)}, f32[64,4096]{1,0:T(8,128)}, u32[]{:S(2)}) copy-start(f32[64,4096]{1,0:T(8,128)} %param.14) | copy-start | bytes 3145732
  6.1 11.3 %collective-permute-start = (f32[5,4096]{1,0:T(8,128)S(1)}, f32[5,4096]{1,0:T(8,128)S(1)}, u32[]{:S(2)}, u32[]{:S(2)}) collective-permute-start(f32[5,4096]{1,0:T(8,128)S(1)} %get-tuple-element.30), channel_id=1, source_target_pairs={{0,1},{1,2},{2,3},{3,4},{4,5},{5,6},{6,7},{7,8},{8,9},{9,10},{10,1... | collective-permute-start | bytes 245768 | tf_op jit(solution)/shard_map/ppermute | solution.py:426
  6.2 11.5 %collective-permute-start.2 = (f32[5,4096]{1,0:T(8,128)S(1)}, f32[5,4096]{1,0:T(8,128)S(1)}, u32[]{:S(2)}, u32[]{:S(2)}) collective-permute-start(f32[5,4096]{1,0:T(8,128)S(1)} %get-tuple-element.31), channel_id=1, source_target_pairs={{0,64},{1,65},{2,66},{3,67},{4,68},{5,69},{6,70},{7,71},{8,72},{9,... | collective-permute-start | bytes 245768 | tf_op jit(solution)/shard_map/ppermute | solution.py:426
  9.6 8.7 %collective-permute-start.1 = (f32[5,4096]{1,0:T(8,128)S(1)}, f32[5,4096]{1,0:T(8,128)S(1)}, u32[]{:S(2)}, u32[]{:S(2)}) collective-permute-start(f32[5,4096]{1,0:T(8,128)S(1)} %get-tuple-element.32), channel_id=1, source_target_pairs={{0,127},{1,0},{2,1},{3,2},{4,3},{5,4},{6,5},{7,6},{8,7},{9,8},{10,... | collective-permute-start | bytes 245768 | tf_op jit(solution)/shard_map/ppermute | solution.py:426
  24.5 10.9 %collective-permute-start.3 = (f32[64,256]{1,0:T(8,128)}, f32[64,256]{1,0:T(8,128)S(1)}, u32[]{:S(2)}, u32[]{:S(2)}) collective-permute-start(f32[64,256]{1,0:T(8,128)} %get-tuple-element.17), channel_id=1, source_target_pairs={{0,8},{8,16},{16,24},{24,32},{32,40},{40,48},{48,56},{56,64},{64,7... | collective-permute-start | bytes 196616 | tf_op jit(solution)/shard_map/ppermute | solution.py:385
  24.5 10.9 %collective-permute-start.4 = (f32[64,256]{1,0:T(8,128)}, f32[64,256]{1,0:T(8,128)S(1)}, u32[]{:S(2)}, u32[]{:S(2)}) collective-permute-start(f32[64,256]{1,0:T(8,128)} %get-tuple-element.18), channel_id=1, source_target_pairs={{8,0},{16,8},{24,16},{32,24},{40,32},{48,40},{56,48},{64,56},{72,6... | collective-permute-start | bytes 196616 | tf_op jit(solution)/shard_map/ppermute | solution.py:385
  35.4 0.6 %copy-start.1 = (f32[64,256]{1,0:T(8,128)}, f32[64,256]{1,0:T(8,128)S(1)}, u32[]{:S(2)}) copy-start(f32[64,256]{1,0:T(8,128)S(1)} %collective-permute-done.3.lower_ref) | copy-start | bytes 196612
  35.5 0.6 %copy-start.2 = (f32[64,256]{1,0:T(8,128)}, f32[64,256]{1,0:T(8,128)S(1)}, u32[]{:S(2)}) copy-start(f32[64,256]{1,0:T(8,128)S(1)} %collective-permute-done.4.upper_ref) | copy-start | bytes 196612
  38.5 7.8 %collective-permute-start.5 = (f32[64,256]{1,0:T(8,128)}, f32[64,256]{1,0:T(8,128)S(1)}, u32[]{:S(2)}, u32[]{:S(2)}) collective-permute-start(f32[64,256]{1,0:T(8,128)} %get-tuple-element.23), channel_id=1, source_target_pairs={{0,8},{8,16},{16,24},{24,32},{32,40},{40,48},{48,56},{56,64},{64,7... | collective-permute-start | bytes 196616 | tf_op jit(solution)/shard_map/ppermute | solution.py:385
  38.5 7.8 %collective-permute-start.6 = (f32[64,256]{1,0:T(8,128)}, f32[64,256]{1,0:T(8,128)S(1)}, u32[]{:S(2)}, u32[]{:S(2)}) collective-permute-start(f32[64,256]{1,0:T(8,128)} %get-tuple-element.24), channel_id=1, source_target_pairs={{8,0},{16,8},{24,16},{32,24},{40,32},{48,40},{56,48},{64,56},{72,6... | collective-permute-start | bytes 196616 | tf_op jit(solution)/shard_map/ppermute | solution.py:385
  46.3 0.6 %copy-start.6 = (f32[64,256]{1,0:T(8,128)}, f32[64,256]{1,0:T(8,128)S(1)}, u32[]{:S(2)}) copy-start(f32[64,256]{1,0:T(8,128)S(1)} %collective-permute-done.5.refs_10_) | copy-start | bytes 196612
  46.3 0.6 %copy-start.7 = (f32[64,256]{1,0:T(8,128)}, f32[64,256]{1,0:T(8,128)S(1)}, u32[]{:S(2)}) copy-start(f32[64,256]{1,0:T(8,128)S(1)} %collective-permute-done.6.refs_11_) | copy-start | bytes 196612

commit v10 on v9

--- a/solution.py
+++ b/solution.py
@@ -416,7 +416,13 @@
     side_rows = side_info[picked].reshape(len(shifts), 1, moving * side_width)
     side_rows = jnp.pad(side_rows, ((0, 0), (0, 0), (0, P_SIZE**3 - moving * side_width)))
     parcels = jnp.concatenate(
-        [coefficients[picked].reshape(len(shifts), moving, P_SIZE**3), side_rows], axis=1
+        [
+            jnp.einsum(
+                "qjr,rc->qjc", hit.astype(jnp.float32), coefficients, precision=lax.Precision.HIGHEST
+            ),
+            side_rows,
+        ],
+        axis=1,
     )
     got_coef = [coefficients]
     got_side = [side_info]
@@ -434,6 +440,9 @@
     hit = got_slot[None, :] == jnp.arange(element_count, dtype=jnp.int32)[:, None]
     got_rows = jnp.arange(got_slot.shape[0], dtype=jnp.int32)
     source = jnp.sum(jnp.where(hit, got_rows[None, :], 0), axis=1)
+    placing = (got_slot[None, :] == jnp.arange(element_count, dtype=jnp.int32)[:, None]).astype(
+        jnp.float32
+    )
     placed_side = got_side[source]
     weight = placed_side
     top = jnp.asarray(top_modes().astype(np.float32))
@@ -444,7 +453,8 @@
     ).astype(jnp.bfloat16)
     codes = partner_turns[0].T
     spread_hi, spread_lo, lift, flip = tables
-    field, even, total = prep(got_coef[source], top, weight)
+    placed = jnp.dot(placing, got_coef, precision=lax.Precision.HIGHEST)
+    field, even, total = prep(placed, top, weight)
     first_step = 0.5 * TIME_STEP
     lower, upper = exchange(even, total)
     pre, even, total = inner(

time: 53.5 us -> 53 us (level)
  local copies, waits for them, and re-layouts: 8.18 us -> 4.34 us
  matrix products: 0 us -> 3.5 us
    gather x2 -> x0, local copies, waits for them, and re-layouts: 3.78 us -> none  [the longest x1 1.93 us: shards(): coefficients[picked].reshape(len(shifts), moving, P_SIZE ** 3)]
    dot_general x0 -> x2, matrix products: none -> 3.5 us  [the longest x1 1.78 us: shards(): placed = jnp.dot(placing, got_coef, precision=lax.Precision.HIGHEST)]
  transfers between devices with their start and end apart: 7 -> 7, of which waited for: 3 -> 3; matrix products, arithmetic and copies ran while one was open for 4% -> 4% of each run, Pallas kernels for 10% -> 11%
where the time goes in v10:
time: 53 us; the launch traced here: 52.7 us
  starting transfers between devices  20.3 us (38%)
  Pallas kernels  16.7 us (32%)
  other arithmetic  4.76 us (9%)
  local copies, waits for them, and re-layouts  4.34 us (8%)
  matrix products  3.5 us (7%)
  waiting for transfers between devices  2.92 us (6%)
    pallas_call x2, Pallas kernels, inner(): pl.pallas_call(functools.partial(inner_body, scale=scale, carried=carried...  11.8 us
    ppermute x4, starting transfers between devices, exchange(): return (lax.ppermute(total, 'dom', up), lax.ppermute(even, 'dom', down))  10.7 us
    ppermute x3, starting transfers between devices, shards(): arrived = lax.ppermute(parcels[index], ('dom', 'face'), pairs)  9.63 us
    pallas_call x1, Pallas kernels, prep(): pl.pallas_call(prep_body, out_shape=(jax.ShapeDtypeStruct(placed.shape, j...  2.49 us
    ppermute x4, waiting for transfers between devices, exchange(): return (lax.ppermute(total, 'dom', up), lax.ppermute(even, 'dom', down))  2.46 us
    pallas_call x1, Pallas kernels, faces(): pl.pallas_call(functools.partial(faces_body, scale=scale), out_shape=(squ...  2.42 us
    dot_general x1, matrix products, shards(): placed = jnp.dot(placing, got_coef, precision=lax.Precision.HIGHEST)  1.78 us
    dot_general x1, matrix products, shards(): jnp.einsum('qjr,rc->qjc', hit.astype(jnp.float32), coefficients, precisio...  1.72 us
  transfers between devices with their start and end apart: 7, of which 3 were waited for; matrix products, arithmetic and copies ran while one was open for 4% of the time, Pallas kernels for 11%

profile of v10, /device:TPU:0, one launch (start us, length us, event | category | flops | bytes accessed | tf_op | source)
XLA Modules:
  0.0 52.7 jit_solution(9877165411070112953)
XLA Ops:
  0.0 0.7 %and_select_fusion = s32[3]{0:T(128)S(1)} fusion(s32[3]{0:T(128)} %constant.78.clone, s32[]{:T(128)S(6)} %add.52), kind=kLoop, calls=%fused_computation.39 | loop fusion | flops 36 | bytes 28 | tf_op jit(solution)/shard_map/jit(remainder)/select_n | solution.py:408
  0.7 0.7 %compare_select_fusion.4 = (s32[64]{0:T(128)S(1)}, s32[64]{0:T(128)S(1)}, s32[64]{0:T(128)S(1)}) fusion(s32[]{:T(128)S(6)} %add.52, s32[64]{0:T(128)} %param.18), kind=kLoop, calls=%fused_computation.41 | loop fusion | flops 1344 | bytes 1028 | tf_op jit(solution)/shard_map/jit(_where)/select_n | solution.py:429
  1.3 0.1 fusion.20
  1.4 0.2 reduce_window_sum.11
  1.7 0.1 select_reduce_fusion.1
  1.8 0.1 reshape.103
  1.9 0.7 %convert_bitcast_fusion = (f32[64,1]{0,1:T(1,128)S(1)}, f32[64,1]{0,1:T(1,128)S(1)}) fusion(s32[64]{0:T(128)} %param.17, s32[64]{0:T(128)S(1)} %get-tuple-element.27), kind=kLoop, calls=%fused_computation.55 | loop fusion | flops 448 | bytes 1024 | tf_op jit(solution)/shard_map/convert_element_type | solution.py:402
  2.6 0.7 %pad_maximum_fusion.1 = f32[64,8]{0,1:T(8,128)S(1)} fusion(f32[64,1]{0,1:T(1,128)S(1)} %get-tuple-element.33, f32[64,1]{0,1:T(1,128)S(1)} %get-tuple-element.34, f32[64,3]{0,1:T(4,128)} %param.16, f32[64,3]{0,1:T(4,128)} %param.15), kind=kLoop, calls=%fused_computation.28 | loop fusion | flops 1536 | bytes 4096 | tf_op jit(solution)/shard_map/concatenate | solution.py:397
  3.3 0.1 copy.34
  3.4 0.6 %gather_fusion = f32[12,8]{1,0:T(8,128)S(1)} fusion(f32[64,8]{1,0:T(8,128)S(1)} %copy.34, s32[1024]{0:T(1024)S(1)} %pad_clamp_fusion.1), kind=kCustom, calls=%fused_computation | custom fusion | bytes 816 | tf_op jit(solution)/shard_map/gather | solution.py:416
  3.9 0.1 reshape.122
  4.0 0.0 copy-start.3
  4.0 0.0 copy-start.4
  4.0 1.7 %fusion.8 = f32[3,4,4096]{2,1,0:T(4,128)S(1)} fusion(f32[64,4096]{1,0:T(8,128)} %param.14, s32[3,64]{1,0:T(4,128)S(1)} %broadcast_add_fusion, pred[3,64]{1,0:T(4,128)(4,1)S(1)} %get-tuple-element.29), kind=kOutput, calls=%fused_computation.10 | convolution fusion | flops 37750272 | bytes 1246144 | tf_op jit(solution)/shard_map/qjr,rc->qjc/dot_general | solution.py:420
  5.7 0.0 copy-start.5
  5.7 0.0 copy-start
  5.8 0.1 collective-permute-start
  5.9 3.4 %collective-permute-start.2 = (f32[5,4096]{1,0:T(8,128)S(1)}, f32[5,4096]{1,0:T(8,128)S(1)}, u32[]{:S(2)}, u32[]{:S(2)}) collective-permute-start(f32[5,4096]{1,0:T(8,128)S(1)} %get-tuple-element.31), channel_id=1, source_target_pairs={{0,64},{1,65},{2,66},{3,67},{4,68},{5,69},{6,70},{7,71},{8,72},{9,... | collective-permute-start | bytes 245768 | tf_op jit(solution)/shard_map/ppermute | solution.py:432
  9.3 6.2 %collective-permute-start.1 = (f32[5,4096]{1,0:T(8,128)S(1)}, f32[5,4096]{1,0:T(8,128)S(1)}, u32[]{:S(2)}, u32[]{:S(2)}) collective-permute-start(f32[5,4096]{1,0:T(8,128)S(1)} %get-tuple-element.32), channel_id=1, source_target_pairs={{0,127},{1,0},{2,1},{3,2},{4,3},{5,4},{6,5},{7,6},{8,7},{9,8},{10,... | collective-permute-start | bytes 245768 | tf_op jit(solution)/shard_map/ppermute | solution.py:432
  15.5 0.0 copy-done.3
  15.5 0.0 copy-done.4
  15.5 0.8 %fusion.10.refs_3_.pick_ref.refs_6_ = bf16[6,64,64]{2,1,0:T(8,128)(2,1)} fusion(s32[6,64]{1,0:T(8,128)S(1)} %pad_add_fusion), kind=kLoop, calls=%fused_computation.15 | loop fusion | flops 49152 | bytes 50688 | tf_op jit(solution)/shard_map/convert_element_type | solution.py:453
  16.3 0.0 copy-done.5
  16.3 0.7 %copy.37 = s32[2,64]{0,1:T(8,128)} copy(s32[2,64]{1,0:T(2,128)S(1)} %bitcast.27) | data formatting | bytes 1024 | tf_op jit(solution)/shard_map/squeeze | solution.py:454
  17.0 0.2 collective-permute-done
  17.2 0.1 reshape_squeeze.9
  17.3 0.2 convert_reduce_fusion.2
  17.5 0.0 collective-permute-done.2
  17.5 0.1 reshape_squeeze.11
  17.6 0.2 convert_reduce_fusion
  17.8 0.2 collective-permute-done.1
  18.0 0.1 reshape_squeeze.10
  18.1 0.2 convert_reduce_fusion.1
  18.3 0.1 pad_add_fusion.1
  18.4 0.1 select_reduce_fusion
  18.5 1.2 %gather_fusion.1 = f32[64,8]{1,0:T(8,128)} fusion(f32[76,8]{1,0:T(8,128)S(1)} %pad_maximum_fusion, s32[1024]{0:T(1024)S(1)} %pad_clamp_fusion), kind=kCustom, calls=%fused_computation.1 | custom fusion | bytes 4352 | tf_op jit(solution)/shard_map/gather | solution.py:446
  19.8 0.0 copy-done
  19.8 1.8 %fusion.placed_ref = f32[64,4096]{1,0:T(8,128)} fusion(f32[4,4096]{1,0:T(4,128)S(1)} %slice.60, f32[4,4096]{1,0:T(4,128)S(1)} %slice.59, f32[4,4096]{1,0:T(4,128)S(1)} %slice.58, f32[64,4096]{1,0:T(8,128)S(1)} %copy-done, s32[76]{0:T(128)S(1)} %pad_add_fusion.1), kind=kOutput, calls=%fused_computation.2 | convolution fusion | flops 240014080 | bytes 2294064 | tf_op jit(solution)/shard_map/dot_general | solution.py:456
  21.6 2.5 %shard_map.136 = (f32[64,4096]{1,0:T(8,128)}, f32[64,256]{1,0:T(8,128)}, f32[64,256]{1,0:T(8,128)}) custom-call(f32[64,4096]{1,0:T(8,128)} %fusion.placed_ref, f32[1,4096]{1,0:T(1,128)} %constant.79.clone.top_ref.refs_2_.refs_5_, f32[64,8]{1,0:T(8,128)} %gather_fusion.1), custom_call_target="tpu_custom_call" | custom-call | tf_op jit(solution)/shard_map/pallas_call | solution.py:369
  24.0 0.0 collective-permute-start.3
  24.0 5.3 %collective-permute-start.4 = (f32[64,256]{1,0:T(8,128)}, f32[64,256]{1,0:T(8,128)S(1)}, u32[]{:S(2)}, u32[]{:S(2)}) collective-permute-start(f32[64,256]{1,0:T(8,128)} %get-tuple-element.18), channel_id=1, source_target_pairs={{8,0},{16,8},{24,16},{32,24},{40,32},{48,40},{56,48},{64,56},{72,6... | collective-permute-start | bytes 196616 | tf_op jit(solution)/shard_map/ppermute | solution.py:385
  29.4 5.6 %shard_map.137 = (f32[64,4096]{1,0:T(8,128)}, f32[64,256]{1,0:T(8,128)}, f32[64,256]{1,0:T(8,128)}) custom-call(f32[64,4096]{1,0:T(8,128)} %get-tuple-element.15.refs_0_.refs_3_, f32[64,8]{1,0:T(8,128)} %gather_fusion.1, f32[1,4096]{1,0:T(1,128)} %constant.79.clone.top_ref.refs_2_.refs_5_, bf16[6,64,64]{2,1,0:T(8,128)(2,1)} %fusion.10.refs_3_.pick_ref.refs_6_, ...), custom_call_target="tpu_custom_call" | custom-call | flops 2500000000 | bytes 4000000 | tf_op jit(solution)/shard_map/pallas_call | solution.py:314
  35.0 0.0 collective-permute-done.3.lower_ref
  35.0 0.0 copy-start.1
  35.0 0.0 collective-permute-done.4.upper_ref
  35.0 0.0 copy-start.2
  35.0 0.6 %copy-done.1 = f32[64,256]{1,0:T(8,128)} copy-done((f32[64,256]{1,0:T(8,128)}, f32[64,256]{1,0:T(8,128)S(1)}, u32[]{:S(2)}) %copy-start.1) | copy-done | bytes 65560
  35.6 0.0 copy-done.2
  35.6 2.4 %shard_map.138 = (f32[64,256]{1,0:T(8,128)}, f32[64,256]{1,0:T(8,128)}, f32[64,256]{1,0:T(8,128)}, f32[64,256]{1,0:T(8,128)}) custom-call(f32[64,256]{1,0:T(8,128)} %copy-done.1, f32[64,256]{1,0:T(8,128)} %copy-done.2, bf16[6,64,64]{2,1,0:T(8,128)(2,1)} %fusion.10.refs_3_.pick_ref.refs_6_, s32[64,2]{1,0:T(8,128)} %bitcast.23, ...), custom_call_target="tpu_custom_call" | custom-call | tf_op jit(solution)/shard_map/pallas_call | solution.py:330
  38.0 0.0 collective-permute-start.5
  38.0 5.3 %collective-permute-start.6 = (f32[64,256]{1,0:T(8,128)}, f32[64,256]{1,0:T(8,128)S(1)}, u32[]{:S(2)}, u32[]{:S(2)}) collective-permute-start(f32[64,256]{1,0:T(8,128)} %get-tuple-element.24), channel_id=1, source_target_pairs={{8,0},{16,8},{24,16},{32,24},{40,32},{48,40},{56,48},{64,56},{72,6... | collective-permute-start | bytes 196616 | tf_op jit(solution)/shard_map/ppermute | solution.py:385
  43.4 2.4 %collective-permute-done.5.refs_10_ = f32[64,256]{1,0:T(8,128)S(1)} collective-permute-done((f32[64,256]{1,0:T(8,128)}, f32[64,256]{1,0:T(8,128)S(1)}, u32[]{:S(2)}, u32[]{:S(2)}) %collective-permute-start.5) | collective-permute-done | bytes 65568 | tf_op jit(solution)/shard_map/ppermute | solution.py:385
  45.8 0.0 copy-start.6
  45.8 0.0 collective-permute-done.6.refs_11_
  45.8 0.0 copy-start.7
  45.8 0.6 %copy-done.6 = f32[64,256]{1,0:T(8,128)} copy-done((f32[64,256]{1,0:T(8,128)}, f32[64,256]{1,0:T(8,128)S(1)}, u32[]{:S(2)}) %copy-start.6) | copy-done | bytes 65560
  46.5 0.0 copy-done.7
  46.5 6.2 %shard_map.139 = f32[64,4096]{1,0:T(8,128)} custom-call(f32[64,4096]{1,0:T(8,128)} %get-tuple-element.16.refs_0_, f32[64,256]{1,0:T(8,128)} %get-tuple-element.21.refs_1_, f32[64,256]{1,0:T(8,128)} %get-tuple-element.22.refs_2_, f32[64,4096]{1,0:T(8,128)} %get-tuple-element.15.refs_0_.refs_3_, f32[64,8]{1,0:T(8,128)} %gather_fusion.1, ...), custom_call_target="tpu_custom_call" | custom-call | flops 2500000000 | bytes 4000000 | tf_op jit(solution)/shard_map/pallas_call | solution.py:314
  (15 shorter events, 0.2 us)
Async XLA Ops:
  4.0 11.5 %copy-start.3 = (s32[1,4,64]{2,1,0:T(4,128)S(1)}, s32[1,4,64]{2,1,0:T(4,128)}, u32[]{:S(2)}) copy-start(s32[1,4,64]{2,1,0:T(4,128)} %param.19) | copy-start | bytes 3076
  4.0 11.5 %copy-start.4 = (s32[1,2,64]{2,1,0:T(2,128)S(1)}, s32[1,2,64]{2,1,0:T(2,128)}, u32[]{:S(2)}) copy-start(s32[1,2,64]{2,1,0:T(2,128)} %param.20) | copy-start | bytes 1540
  5.7 10.5 %copy-start.5 = (s32[1,2,64]{2,1,0:T(2,128)S(1)}, s32[1,2,64]{2,1,0:T(2,128)}, u32[]{:S(2)}) copy-start(s32[1,2,64]{2,1,0:T(2,128)} %param.21) | copy-start | bytes 1540
  5.7 14.0 %copy-start = (f32[64,4096]{1,0:T(8,128)S(1)}, f32[64,4096]{1,0:T(8,128)}, u32[]{:S(2)}) copy-start(f32[64,4096]{1,0:T(8,128)} %param.14) | copy-start | bytes 3145732
  5.8 11.3 %collective-permute-start = (f32[5,4096]{1,0:T(8,128)S(1)}, f32[5,4096]{1,0:T(8,128)S(1)}, u32[]{:S(2)}, u32[]{:S(2)}) collective-permute-start(f32[5,4096]{1,0:T(8,128)S(1)} %get-tuple-element.30), channel_id=1, source_target_pairs={{0,1},{1,2},{2,3},{3,4},{4,5},{5,6},{6,7},{7,8},{8,9},{9,10},{10,1... | collective-permute-start | bytes 245768 | tf_op jit(solution)/shard_map/ppermute | solution.py:432
  5.9 11.5 %collective-permute-start.2 = (f32[5,4096]{1,0:T(8,128)S(1)}, f32[5,4096]{1,0:T(8,128)S(1)}, u32[]{:S(2)}, u32[]{:S(2)}) collective-permute-start(f32[5,4096]{1,0:T(8,128)S(1)} %get-tuple-element.31), channel_id=1, source_target_pairs={{0,64},{1,65},{2,66},{3,67},{4,68},{5,69},{6,70},{7,71},{8,72},{9,... | collective-permute-start | bytes 245768 | tf_op jit(solution)/shard_map/ppermute | solution.py:432
  9.3 8.7 %collective-permute-start.1 = (f32[5,4096]{1,0:T(8,128)S(1)}, f32[5,4096]{1,0:T(8,128)S(1)}, u32[]{:S(2)}, u32[]{:S(2)}) collective-permute-start(f32[5,4096]{1,0:T(8,128)S(1)} %get-tuple-element.32), channel_id=1, source_target_pairs={{0,127},{1,0},{2,1},{3,2},{4,3},{5,4},{6,5},{7,6},{8,7},{9,8},{10,... | collective-permute-start | bytes 245768 | tf_op jit(solution)/shard_map/ppermute | solution.py:432
  24.0 10.9 %collective-permute-start.3 = (f32[64,256]{1,0:T(8,128)}, f32[64,256]{1,0:T(8,128)S(1)}, u32[]{:S(2)}, u32[]{:S(2)}) collective-permute-start(f32[64,256]{1,0:T(8,128)} %get-tuple-element.17), channel_id=1, source_target_pairs={{0,8},{8,16},{16,24},{24,32},{32,40},{40,48},{48,56},{56,64},{64,7... | collective-permute-start | bytes 196616 | tf_op jit(solution)/shard_map/ppermute | solution.py:385
  24.0 10.9 %collective-permute-start.4 = (f32[64,256]{1,0:T(8,128)}, f32[64,256]{1,0:T(8,128)S(1)}, u32[]{:S(2)}, u32[]{:S(2)}) collective-permute-start(f32[64,256]{1,0:T(8,128)} %get-tuple-element.18), channel_id=1, source_target_pairs={{8,0},{16,8},{24,16},{32,24},{40,32},{48,40},{56,48},{64,56},{72,6... | collective-permute-start | bytes 196616 | tf_op jit(solution)/shard_map/ppermute | solution.py:385
  35.0 0.6 %copy-start.1 = (f32[64,256]{1,0:T(8,128)}, f32[64,256]{1,0:T(8,128)S(1)}, u32[]{:S(2)}) copy-start(f32[64,256]{1,0:T(8,128)S(1)} %collective-permute-done.3.lower_ref) | copy-start | bytes 196612
  35.0 0.6 %copy-start.2 = (f32[64,256]{1,0:T(8,128)}, f32[64,256]{1,0:T(8,128)S(1)}, u32[]{:S(2)}) copy-start(f32[64,256]{1,0:T(8,128)S(1)} %collective-permute-done.4.upper_ref) | copy-start | bytes 196612
  38.0 7.8 %collective-permute-start.5 = (f32[64,256]{1,0:T(8,128)}, f32[64,256]{1,0:T(8,128)S(1)}, u32[]{:S(2)}, u32[]{:S(2)}) collective-permute-start(f32[64,256]{1,0:T(8,128)} %get-tuple-element.23), channel_id=1, source_target_pairs={{0,8},{8,16},{16,24},{24,32},{32,40},{40,48},{48,56},{56,64},{64,7... | collective-permute-start | bytes 196616 | tf_op jit(solution)/shard_map/ppermute | solution.py:385
  38.0 7.8 %collective-permute-start.6 = (f32[64,256]{1,0:T(8,128)}, f32[64,256]{1,0:T(8,128)S(1)}, u32[]{:S(2)}, u32[]{:S(2)}) collective-permute-start(f32[64,256]{1,0:T(8,128)} %get-tuple-element.24), channel_id=1, source_target_pairs={{8,0},{16,8},{24,16},{32,24},{40,32},{48,40},{56,48},{64,56},{72,6... | collective-permute-start | bytes 196616 | tf_op jit(solution)/shard_map/ppermute | solution.py:385
  45.8 0.6 %copy-start.6 = (f32[64,256]{1,0:T(8,128)}, f32[64,256]{1,0:T(8,128)S(1)}, u32[]{:S(2)}) copy-start(f32[64,256]{1,0:T(8,128)S(1)} %collective-permute-done.5.refs_10_) | copy-start | bytes 196612
  45.8 0.6 %copy-start.7 = (f32[64,256]{1,0:T(8,128)}, f32[64,256]{1,0:T(8,128)S(1)}, u32[]{:S(2)}) copy-start(f32[64,256]{1,0:T(8,128)S(1)} %collective-permute-done.6.refs_11_) | copy-start | bytes 196612

commit v11 on v10

--- a/solution.py
+++ b/solution.py
@@ -141,6 +141,7 @@
 
 
 def inner_body(*refs, scale, carried, final):
+    refs, (hi_buf, lo_buf, lift_buf, table_sems) = refs[:-4], refs[-4:]
     if carried is None:
         v_ref, weight_ref, top_ref, pick_ref, spread_hi_ref, spread_lo_ref, lift_ref = refs[:7]
         base_ref = v_ref
@@ -152,6 +153,14 @@
         partial_ref = refs[-1]
     else:
         partial_ref, even_ref, total_ref = refs[-3:]
+    table_copies = [
+        pltpu.make_async_copy(source, target, table_sems.at[index])
+        for index, (source, target) in enumerate(
+            ((spread_hi_ref, hi_buf), (spread_lo_ref, lo_buf), (lift_ref, lift_buf))
+        )
+    ]
+    for copy in table_copies:
+        copy.start()
     count = v_ref.shape[0]
     derivative, second, side_signs, weights = mode_tables()
     second = second.astype(np.float32)
@@ -206,9 +215,11 @@
         first.append(parts[0] if len(parts) == 1 else jnp.concatenate(parts, axis=0))
     stacked = jnp.concatenate([kept(a, slabs[a]) for a in range(P_SIZE)], axis=0)
     hi, lo = split_two(stacked)
-    spread_hi = spread_hi_ref[...]
+    table_copies[0].wait()
+    table_copies[1].wait()
+    spread_hi = hi_buf[...]
     wide = mxu(hi, spread_hi) + mxu(lo, spread_hi)
-    fine = mxu(hi, spread_lo_ref[...])
+    fine = mxu(hi, lo_buf[...])
     weight_rows = jnp.concatenate([kept(a, weight) for a in range(P_SIZE)], axis=0)
     inner = (
         weight_rows[:, 2:3] * (wide[:, 0:PLANE] + fine[:, 0:PLANE])
@@ -234,7 +245,8 @@
         [kept(a, jump[:, a * 128 : (a + 1) * 128]) for a in range(P_SIZE)], axis=0
     )
     jhi, jlo = split_two(jump_rows)
-    lift_mat = lift_ref[...]
+    table_copies[2].wait()
+    lift_mat = lift_buf[...]
     lifted = mxu(jhi, lift_mat) + mxu(jlo, lift_mat)
     even, total = end_traces(slabs)
     if final:
@@ -311,11 +323,18 @@
     spec = pl.BlockSpec(memory_space=pltpu.VMEM)
     square = jax.ShapeDtypeStruct((count, PLANE), jnp.float32)
     field = jax.ShapeDtypeStruct(operands[0].shape, jnp.float32)
+    first_table = 4 if carried is None else 7
+    in_specs = [spec] * len(operands)
+    for index in range(first_table, first_table + 3):
+        in_specs[index] = pl.BlockSpec(memory_space=pl.ANY)
+    tables = operands[first_table : first_table + 3]
     return pl.pallas_call(
         functools.partial(inner_body, scale=scale, carried=carried, final=final),
         out_shape=field if final else (field, square, square),
-        in_specs=[spec] * len(operands),
+        in_specs=in_specs,
         out_specs=spec if final else (spec, spec, spec),
+        scratch_shapes=[pltpu.VMEM(table.shape, table.dtype) for table in tables]
+        + [pltpu.SemaphoreType.DMA((3,))],
         compiler_params=pltpu.CompilerParams(vmem_limit_bytes=60 * 1024 * 1024),
         cost_estimate=pl.CostEstimate(
             flops=2_500_000_000, transcendentals=0, bytes_accessed=4_000_000

time: 53 us -> 55.1 us (1.040)
  Pallas kernels: 16.7 us -> 18.6 us
    pallas_call x2, Pallas kernels: 11.8 us -> 13.7 us  [inner(): pl.pallas_call(functools.partial(inner_body, scale=scale, carried=carried...]
  transfers between devices with their start and end apart: 7 -> 7, of which waited for: 3 -> 3; matrix products, arithmetic and copies ran while one was open for 4% -> 4% of each run, Pallas kernels for 11% -> 12%
where the time goes in v11:
time: 55.1 us; the launch traced here: 54.7 us
  starting transfers between devices  20.3 us (37%)
  Pallas kernels  18.6 us (34%)
  other arithmetic  4.76 us (9%)
  local copies, waits for them, and re-layouts  4.34 us (8%)
  matrix products  3.5 us (6%)
  waiting for transfers between devices  2.92 us (5%)
    pallas_call x2, Pallas kernels, inner(): pl.pallas_call(functools.partial(inner_body, scale=scale, carried=carried...  13.7 us
    ppermute x4, starting transfers between devices, exchange(): return (lax.ppermute(total, 'dom', up), lax.ppermute(even, 'dom', down))  10.7 us
    ppermute x3, starting transfers between devices, shards(): arrived = lax.ppermute(parcels[index], ('dom', 'face'), pairs)  9.63 us
    pallas_call x1, Pallas kernels, prep(): pl.pallas_call(prep_body, out_shape=(jax.ShapeDtypeStruct(placed.shape, j...  2.49 us
    ppermute x4, waiting for transfers between devices, exchange(): return (lax.ppermute(total, 'dom', up), lax.ppermute(even, 'dom', down))  2.46 us
    pallas_call x1, Pallas kernels, faces(): pl.pallas_call(functools.partial(faces_body, scale=scale), out_shape=(squ...  2.42 us
    dot_general x1, matrix products, shards(): placed = jnp.dot(placing, got_coef, precision=lax.Precision.HIGHEST)  1.78 us
    dot_general x1, matrix products, shards(): jnp.einsum('qjr,rc->qjc', hit.astype(jnp.float32), coefficients, precisio...  1.72 us
  transfers between devices with their start and end apart: 7, of which 3 were waited for; matrix products, arithmetic and copies ran while one was open for 4% of the time, Pallas kernels for 12%

profile of v11, /device:TPU:0, one launch (start us, length us, event | category | flops | bytes accessed | tf_op | source)
XLA Modules:
  0.0 54.7 jit_solution(17384442484395989363)
XLA Ops:
  0.0 0.7 %and_select_fusion = s32[3]{0:T(128)S(1)} fusion(s32[3]{0:T(128)} %constant.78.clone, s32[]{:T(128)S(6)} %add.52), kind=kLoop, calls=%fused_computation.39 | loop fusion | flops 36 | bytes 28 | tf_op jit(solution)/shard_map/jit(remainder)/select_n | solution.py:427
  0.7 0.7 %compare_select_fusion.4 = (s32[64]{0:T(128)S(1)}, s32[64]{0:T(128)S(1)}, s32[64]{0:T(128)S(1)}) fusion(s32[]{:T(128)S(6)} %add.52, s32[64]{0:T(128)} %param.18), kind=kLoop, calls=%fused_computation.41 | loop fusion | flops 1344 | bytes 1028 | tf_op jit(solution)/shard_map/jit(_where)/select_n | solution.py:448
  1.3 0.1 fusion.20
  1.4 0.2 reduce_window_sum.11
  1.7 0.1 select_reduce_fusion.1
  1.8 0.1 reshape.103
  1.9 0.7 %convert_bitcast_fusion = (f32[64,1]{0,1:T(1,128)S(1)}, f32[64,1]{0,1:T(1,128)S(1)}) fusion(s32[64]{0:T(128)} %param.17, s32[64]{0:T(128)S(1)} %get-tuple-element.27), kind=kLoop, calls=%fused_computation.55 | loop fusion | flops 448 | bytes 1024 | tf_op jit(solution)/shard_map/convert_element_type | solution.py:421
  2.6 0.7 %pad_maximum_fusion.1 = f32[64,8]{0,1:T(8,128)S(1)} fusion(f32[64,1]{0,1:T(1,128)S(1)} %get-tuple-element.33, f32[64,1]{0,1:T(1,128)S(1)} %get-tuple-element.34, f32[64,3]{0,1:T(4,128)} %param.16, f32[64,3]{0,1:T(4,128)} %param.15), kind=kLoop, calls=%fused_computation.28 | loop fusion | flops 1536 | bytes 4096 | tf_op jit(solution)/shard_map/concatenate | solution.py:416
  3.3 0.1 copy.34
  3.4 0.6 %gather_fusion = f32[12,8]{1,0:T(8,128)S(1)} fusion(f32[64,8]{1,0:T(8,128)S(1)} %copy.34, s32[1024]{0:T(1024)S(1)} %pad_clamp_fusion.1), kind=kCustom, calls=%fused_computation | custom fusion | bytes 816 | tf_op jit(solution)/shard_map/gather | solution.py:435
  3.9 0.1 reshape.122
  4.0 0.0 copy-start.3
  4.0 0.0 copy-start.4
  4.0 1.7 %fusion.8 = f32[3,4,4096]{2,1,0:T(4,128)S(1)} fusion(f32[64,4096]{1,0:T(8,128)} %param.14, s32[3,64]{1,0:T(4,128)S(1)} %broadcast_add_fusion, pred[3,64]{1,0:T(4,128)(4,1)S(1)} %get-tuple-element.29), kind=kOutput, calls=%fused_computation.10 | convolution fusion | flops 37750272 | bytes 1246144 | tf_op jit(solution)/shard_map/qjr,rc->qjc/dot_general | solution.py:439
  5.7 0.0 copy-start.5
  5.7 0.0 copy-start
  5.8 0.1 collective-permute-start
  5.9 3.4 %collective-permute-start.2 = (f32[5,4096]{1,0:T(8,128)S(1)}, f32[5,4096]{1,0:T(8,128)S(1)}, u32[]{:S(2)}, u32[]{:S(2)}) collective-permute-start(f32[5,4096]{1,0:T(8,128)S(1)} %get-tuple-element.31), channel_id=1, source_target_pairs={{0,64},{1,65},{2,66},{3,67},{4,68},{5,69},{6,70},{7,71},{8,72},{9,... | collective-permute-start | bytes 245768 | tf_op jit(solution)/shard_map/ppermute | solution.py:451
  9.3 6.2 %collective-permute-start.1 = (f32[5,4096]{1,0:T(8,128)S(1)}, f32[5,4096]{1,0:T(8,128)S(1)}, u32[]{:S(2)}, u32[]{:S(2)}) collective-permute-start(f32[5,4096]{1,0:T(8,128)S(1)} %get-tuple-element.32), channel_id=1, source_target_pairs={{0,127},{1,0},{2,1},{3,2},{4,3},{5,4},{6,5},{7,6},{8,7},{9,8},{10,... | collective-permute-start | bytes 245768 | tf_op jit(solution)/shard_map/ppermute | solution.py:451
  15.5 0.0 copy-done.3
  15.5 0.0 copy-done.4
  15.5 0.8 %fusion.10.refs_3_.pick_ref.refs_6_ = bf16[6,64,64]{2,1,0:T(8,128)(2,1)} fusion(s32[6,64]{1,0:T(8,128)S(1)} %pad_add_fusion), kind=kLoop, calls=%fused_computation.15 | loop fusion | flops 49152 | bytes 50688 | tf_op jit(solution)/shard_map/convert_element_type | solution.py:472
  16.3 0.0 copy-done.5
  16.3 0.7 %copy.37 = s32[2,64]{0,1:T(8,128)} copy(s32[2,64]{1,0:T(2,128)S(1)} %bitcast.27) | data formatting | bytes 1024 | tf_op jit(solution)/shard_map/squeeze | solution.py:473
  17.0 0.2 collective-permute-done
  17.2 0.1 reshape_squeeze.9
  17.3 0.2 convert_reduce_fusion.2
  17.5 0.0 collective-permute-done.2
  17.5 0.1 reshape_squeeze.11
  17.6 0.2 convert_reduce_fusion
  17.8 0.2 collective-permute-done.1
  18.0 0.1 reshape_squeeze.10
  18.1 0.2 convert_reduce_fusion.1
  18.3 0.1 pad_add_fusion.1
  18.4 0.1 select_reduce_fusion
  18.5 1.2 %gather_fusion.1 = f32[64,8]{1,0:T(8,128)} fusion(f32[76,8]{1,0:T(8,128)S(1)} %pad_maximum_fusion, s32[1024]{0:T(1024)S(1)} %pad_clamp_fusion), kind=kCustom, calls=%fused_computation.1 | custom fusion | bytes 4352 | tf_op jit(solution)/shard_map/gather | solution.py:465
  19.8 0.0 copy-done
  19.8 1.8 %fusion.placed_ref = f32[64,4096]{1,0:T(8,128)} fusion(f32[4,4096]{1,0:T(4,128)S(1)} %slice.60, f32[4,4096]{1,0:T(4,128)S(1)} %slice.59, f32[4,4096]{1,0:T(4,128)S(1)} %slice.58, f32[64,4096]{1,0:T(8,128)S(1)} %copy-done, s32[76]{0:T(128)S(1)} %pad_add_fusion.1), kind=kOutput, calls=%fused_computation.2 | convolution fusion | flops 240014080 | bytes 2294064 | tf_op jit(solution)/shard_map/dot_general | solution.py:475
  21.6 2.5 %shard_map.136 = (f32[64,4096]{1,0:T(8,128)}, f32[64,256]{1,0:T(8,128)}, f32[64,256]{1,0:T(8,128)}) custom-call(f32[64,4096]{1,0:T(8,128)} %fusion.placed_ref, f32[1,4096]{1,0:T(1,128)} %constant.79.clone.top_ref.refs_2_.refs_5_, f32[64,8]{1,0:T(8,128)} %gather_fusion.1), custom_call_target="tpu_custom_call" | custom-call | tf_op jit(solution)/shard_map/pallas_call | solution.py:388
  24.0 0.0 collective-permute-start.3
  24.0 5.3 %collective-permute-start.4 = (f32[64,256]{1,0:T(8,128)}, f32[64,256]{1,0:T(8,128)S(1)}, u32[]{:S(2)}, u32[]{:S(2)}) collective-permute-start(f32[64,256]{1,0:T(8,128)} %get-tuple-element.18), channel_id=1, source_target_pairs={{8,0},{16,8},{24,16},{32,24},{40,32},{48,40},{56,48},{64,56},{72,6... | collective-permute-start | bytes 196616 | tf_op jit(solution)/shard_map/ppermute | solution.py:404
  29.4 6.6 %shard_map.137 = (f32[64,4096]{1,0:T(8,128)}, f32[64,256]{1,0:T(8,128)}, f32[64,256]{1,0:T(8,128)}) custom-call(f32[64,4096]{1,0:T(8,128)} %get-tuple-element.15.refs_0_.refs_3_, f32[64,8]{1,0:T(8,128)} %gather_fusion.1, f32[1,4096]{1,0:T(1,128)} %constant.79.clone.top_ref.refs_2_.refs_5_, bf16[6,64,64]{2,1,0:T(8,128)(2,1)} %fusion.10.refs_3_.pick_ref.refs_6_, ...), custom_call_target="tpu_custom_call" | custom-call | flops 2500000000 | bytes 4000000 | tf_op jit(solution)/shard_map/pallas_call | solution.py:331
  36.0 0.0 collective-permute-done.3.lower_ref
  36.0 0.0 copy-start.1
  36.0 0.0 collective-permute-done.4.upper_ref
  36.1 0.0 copy-start.2
  36.1 0.6 %copy-done.1 = f32[64,256]{1,0:T(8,128)} copy-done((f32[64,256]{1,0:T(8,128)}, f32[64,256]{1,0:T(8,128)S(1)}, u32[]{:S(2)}) %copy-start.1) | copy-done | bytes 65560
  36.7 0.0 copy-done.2
  36.7 2.4 %shard_map.138 = (f32[64,256]{1,0:T(8,128)}, f32[64,256]{1,0:T(8,128)}, f32[64,256]{1,0:T(8,128)}, f32[64,256]{1,0:T(8,128)}) custom-call(f32[64,256]{1,0:T(8,128)} %copy-done.1, f32[64,256]{1,0:T(8,128)} %copy-done.2, bf16[6,64,64]{2,1,0:T(8,128)(2,1)} %fusion.10.refs_3_.pick_ref.refs_6_, s32[64,2]{1,0:T(8,128)} %bitcast.23, ...), custom_call_target="tpu_custom_call" | custom-call | tf_op jit(solution)/shard_map/pallas_call | solution.py:349
  39.1 0.0 collective-permute-start.5
  39.1 5.3 %collective-permute-start.6 = (f32[64,256]{1,0:T(8,128)}, f32[64,256]{1,0:T(8,128)S(1)}, u32[]{:S(2)}, u32[]{:S(2)}) collective-permute-start(f32[64,256]{1,0:T(8,128)} %get-tuple-element.24), channel_id=1, source_target_pairs={{8,0},{16,8},{24,16},{32,24},{40,32},{48,40},{56,48},{64,56},{72,6... | collective-permute-start | bytes 196616 | tf_op jit(solution)/shard_map/ppermute | solution.py:404
  44.4 2.4 %collective-permute-done.5.refs_10_ = f32[64,256]{1,0:T(8,128)S(1)} collective-permute-done((f32[64,256]{1,0:T(8,128)}, f32[64,256]{1,0:T(8,128)S(1)}, u32[]{:S(2)}, u32[]{:S(2)}) %collective-permute-start.5) | collective-permute-done | bytes 65568 | tf_op jit(solution)/shard_map/ppermute | solution.py:404
  46.9 0.0 copy-start.6
  46.9 0.0 collective-permute-done.6.refs_11_
  46.9 0.0 copy-start.7
  46.9 0.6 %copy-done.6 = f32[64,256]{1,0:T(8,128)} copy-done((f32[64,256]{1,0:T(8,128)}, f32[64,256]{1,0:T(8,128)S(1)}, u32[]{:S(2)}) %copy-start.6) | copy-done | bytes 65560
  47.5 0.0 copy-done.7
  47.5 7.0 %shard_map.139 = f32[64,4096]{1,0:T(8,128)} custom-call(f32[64,4096]{1,0:T(8,128)} %get-tuple-element.16.refs_0_, f32[64,256]{1,0:T(8,128)} %get-tuple-element.21.refs_1_, f32[64,256]{1,0:T(8,128)} %get-tuple-element.22.refs_2_, f32[64,4096]{1,0:T(8,128)} %get-tuple-element.15.refs_0_.refs_3_, f32[64,8]{1,0:T(8,128)} %gather_fusion.1, ...), custom_call_target="tpu_custom_call" | custom-call | flops 2500000000 | bytes 4000000 | tf_op jit(solution)/shard_map/pallas_call | solution.py:331
  (15 shorter events, 0.2 us)
Async XLA Ops:
  4.0 11.5 %copy-start.3 = (s32[1,4,64]{2,1,0:T(4,128)S(1)}, s32[1,4,64]{2,1,0:T(4,128)}, u32[]{:S(2)}) copy-start(s32[1,4,64]{2,1,0:T(4,128)} %param.19) | copy-start | bytes 3076
  4.0 11.5 %copy-start.4 = (s32[1,2,64]{2,1,0:T(2,128)S(1)}, s32[1,2,64]{2,1,0:T(2,128)}, u32[]{:S(2)}) copy-start(s32[1,2,64]{2,1,0:T(2,128)} %param.20) | copy-start | bytes 1540
  5.7 10.5 %copy-start.5 = (s32[1,2,64]{2,1,0:T(2,128)S(1)}, s32[1,2,64]{2,1,0:T(2,128)}, u32[]{:S(2)}) copy-start(s32[1,2,64]{2,1,0:T(2,128)} %param.21) | copy-start | bytes 1540
  5.7 14.0 %copy-start = (f32[64,4096]{1,0:T(8,128)S(1)}, f32[64,4096]{1,0:T(8,128)}, u32[]{:S(2)}) copy-start(f32[64,4096]{1,0:T(8,128)} %param.14) | copy-start | bytes 3145732
  5.8 11.3 %collective-permute-start = (f32[5,4096]{1,0:T(8,128)S(1)}, f32[5,4096]{1,0:T(8,128)S(1)}, u32[]{:S(2)}, u32[]{:S(2)}) collective-permute-start(f32[5,4096]{1,0:T(8,128)S(1)} %get-tuple-element.30), channel_id=1, source_target_pairs={{0,1},{1,2},{2,3},{3,4},{4,5},{5,6},{6,7},{7,8},{8,9},{9,10},{10,1... | collective-permute-start | bytes 245768 | tf_op jit(solution)/shard_map/ppermute | solution.py:451
  5.9 11.5 %collective-permute-start.2 = (f32[5,4096]{1,0:T(8,128)S(1)}, f32[5,4096]{1,0:T(8,128)S(1)}, u32[]{:S(2)}, u32[]{:S(2)}) collective-permute-start(f32[5,4096]{1,0:T(8,128)S(1)} %get-tuple-element.31), channel_id=1, source_target_pairs={{0,64},{1,65},{2,66},{3,67},{4,68},{5,69},{6,70},{7,71},{8,72},{9,... | collective-permute-start | bytes 245768 | tf_op jit(solution)/shard_map/ppermute | solution.py:451
  9.3 8.7 %collective-permute-start.1 = (f32[5,4096]{1,0:T(8,128)S(1)}, f32[5,4096]{1,0:T(8,128)S(1)}, u32[]{:S(2)}, u32[]{:S(2)}) collective-permute-start(f32[5,4096]{1,0:T(8,128)S(1)} %get-tuple-element.32), channel_id=1, source_target_pairs={{0,127},{1,0},{2,1},{3,2},{4,3},{5,4},{6,5},{7,6},{8,7},{9,8},{10,... | collective-permute-start | bytes 245768 | tf_op jit(solution)/shard_map/ppermute | solution.py:451
  24.0 12.0 %collective-permute-start.3 = (f32[64,256]{1,0:T(8,128)}, f32[64,256]{1,0:T(8,128)S(1)}, u32[]{:S(2)}, u32[]{:S(2)}) collective-permute-start(f32[64,256]{1,0:T(8,128)} %get-tuple-element.17), channel_id=1, source_target_pairs={{0,8},{8,16},{16,24},{24,32},{32,40},{40,48},{48,56},{56,64},{64,7... | collective-permute-start | bytes 196616 | tf_op jit(solution)/shard_map/ppermute | solution.py:404
  24.0 12.0 %collective-permute-start.4 = (f32[64,256]{1,0:T(8,128)}, f32[64,256]{1,0:T(8,128)S(1)}, u32[]{:S(2)}, u32[]{:S(2)}) collective-permute-start(f32[64,256]{1,0:T(8,128)} %get-tuple-element.18), channel_id=1, source_target_pairs={{8,0},{16,8},{24,16},{32,24},{40,32},{48,40},{56,48},{64,56},{72,6... | collective-permute-start | bytes 196616 | tf_op jit(solution)/shard_map/ppermute | solution.py:404
  36.0 0.6 %copy-start.1 = (f32[64,256]{1,0:T(8,128)}, f32[64,256]{1,0:T(8,128)S(1)}, u32[]{:S(2)}) copy-start(f32[64,256]{1,0:T(8,128)S(1)} %collective-permute-done.3.lower_ref) | copy-start | bytes 196612
  36.1 0.6 %copy-start.2 = (f32[64,256]{1,0:T(8,128)}, f32[64,256]{1,0:T(8,128)S(1)}, u32[]{:S(2)}) copy-start(f32[64,256]{1,0:T(8,128)S(1)} %collective-permute-done.4.upper_ref) | copy-start | bytes 196612
  39.1 7.8 %collective-permute-start.5 = (f32[64,256]{1,0:T(8,128)}, f32[64,256]{1,0:T(8,128)S(1)}, u32[]{:S(2)}, u32[]{:S(2)}) collective-permute-start(f32[64,256]{1,0:T(8,128)} %get-tuple-element.23), channel_id=1, source_target_pairs={{0,8},{8,16},{16,24},{24,32},{32,40},{40,48},{48,56},{56,64},{64,7... | collective-permute-start | bytes 196616 | tf_op jit(solution)/shard_map/ppermute | solution.py:404
  39.1 7.8 %collective-permute-start.6 = (f32[64,256]{1,0:T(8,128)}, f32[64,256]{1,0:T(8,128)S(1)}, u32[]{:S(2)}, u32[]{:S(2)}) collective-permute-start(f32[64,256]{1,0:T(8,128)} %get-tuple-element.24), channel_id=1, source_target_pairs={{8,0},{16,8},{24,16},{32,24},{40,32},{48,40},{56,48},{64,56},{72,6... | collective-permute-start | bytes 196616 | tf_op jit(solution)/shard_map/ppermute | solution.py:404
  46.9 0.6 %copy-start.6 = (f32[64,256]{1,0:T(8,128)}, f32[64,256]{1,0:T(8,128)S(1)}, u32[]{:S(2)}) copy-start(f32[64,256]{1,0:T(8,128)S(1)} %collective-permute-done.5.refs_10_) | copy-start | bytes 196612
  46.9 0.6 %copy-start.7 = (f32[64,256]{1,0:T(8,128)}, f32[64,256]{1,0:T(8,128)S(1)}, u32[]{:S(2)}) copy-start(f32[64,256]{1,0:T(8,128)S(1)} %collective-permute-done.6.refs_11_) | copy-start | bytes 196612

commit v12 on v10

--- a/solution.py
+++ b/solution.py
@@ -454,7 +454,9 @@
     codes = partner_turns[0].T
     spread_hi, spread_lo, lift, flip = tables
     placed = jnp.dot(placing, got_coef, precision=lax.Precision.HIGHEST)
-    field, even, total = prep(placed, top, weight)
+    field = jnp.where(top <= weight[:, 7:8], placed, 0.0)
+    slabs = [field[:, a * PLANE : (a + 1) * PLANE] for a in range(P_SIZE)]
+    even, total = end_traces(slabs)
     first_step = 0.5 * TIME_STEP
     lower, upper = exchange(even, total)
     pre, even, total = inner(

time: 53 us -> 50.1 us (0.945)
  Pallas kernels: 16.7 us -> 14.2 us
  matrix products: 3.5 us -> 2.55 us
    pallas_call x1 -> x0, Pallas kernels: 2.49 us -> none  [prep(): pl.pallas_call(prep_body, out_shape=(jax.ShapeDtypeStruct(placed.shape, j...]
    dot_general x1, matrix products: 1.78 us -> 0.83 us  [shards(): placed = jnp.dot(placing, got_coef, precision=lax.Precision.HIGHEST)]
    unnamed x16 -> x22, local copies, waits for them, and re-layouts: 1.28 us -> 2.13 us
    gather x1, local copies, waits for them, and re-layouts: 1.18 us -> 0.6 us  [shards(): placed_side = got_side[source]]
where the time goes in v12:
time: 50.1 us; the launch traced here: 49.9 us
  starting transfers between devices  20.3 us (41%)
  Pallas kernels  14.2 us (28%)
  other arithmetic  4.9 us (10%)
  local copies, waits for them, and re-layouts  4.79 us (10%)
  waiting for transfers between devices  2.92 us (6%)
  matrix products  2.55 us (5%)
    pallas_call x2, Pallas kernels, inner(): pl.pallas_call(functools.partial(inner_body, scale=scale, carried=carried...  11.8 us
    ppermute x4, starting transfers between devices, exchange(): return (lax.ppermute(total, 'dom', up), lax.ppermute(even, 'dom', down))  10.7 us
    ppermute x3, starting transfers between devices, shards(): arrived = lax.ppermute(parcels[index], ('dom', 'face'), pairs)  9.63 us
    ppermute x4, waiting for transfers between devices, exchange(): return (lax.ppermute(total, 'dom', up), lax.ppermute(even, 'dom', down))  2.46 us
    pallas_call x1, Pallas kernels, faces(): pl.pallas_call(functools.partial(faces_body, scale=scale), out_shape=(squ...  2.42 us
    unnamed x22, local copies, waits for them, and re-layouts  2.13 us
    dot_general x1, matrix products, shards(): jnp.einsum('qjr,rc->qjc', hit.astype(jnp.float32), coefficients, precisio...  1.72 us
  transfers between devices with their start and end apart: 7, of which 3 were waited for; matrix products, arithmetic and copies ran while one was open for 4% of the time, Pallas kernels for 11%

profile of v12, /device:TPU:0, one launch (start us, length us, event | category | flops | bytes accessed | tf_op | source)
XLA Modules:
  0.0 49.9 jit_solution(3839066132023689167)
XLA Ops:
  0.0 0.7 %and_select_fusion = s32[3]{0:T(128)S(1)} fusion(s32[3]{0:T(128)} %constant.79.clone, s32[]{:T(128)S(6)} %add.119), kind=kLoop, calls=%fused_computation.43 | loop fusion | flops 36 | bytes 28 | tf_op jit(solution)/shard_map/jit(remainder)/select_n | solution.py:408
  0.7 0.7 %compare_select_fusion.4 = (s32[64]{0:T(128)S(1)}, s32[64]{0:T(128)S(1)}, s32[64]{0:T(128)S(1)}) fusion(s32[]{:T(128)S(6)} %add.119, s32[64]{0:T(128)} %param.18), kind=kLoop, calls=%fused_computation.42 | loop fusion | flops 1344 | bytes 1028 | tf_op jit(solution)/shard_map/jit(_where)/select_n | solution.py:429
  1.3 0.1 fusion.19
  1.4 0.2 reduce_window_sum.11
  1.7 0.1 select_reduce_fusion.1
  1.8 0.1 reshape.103
  1.9 0.7 %convert_bitcast_fusion = (f32[64,1]{0,1:T(1,128)S(1)}, f32[64,1]{0,1:T(1,128)S(1)}) fusion(s32[64]{0:T(128)} %param.17, s32[64]{0:T(128)S(1)} %get-tuple-element.21), kind=kLoop, calls=%fused_computation.58 | loop fusion | flops 448 | bytes 1024 | tf_op jit(solution)/shard_map/convert_element_type | solution.py:402
  2.6 0.7 %pad_maximum_fusion.1 = f32[64,8]{0,1:T(8,128)S(1)} fusion(f32[64,1]{0,1:T(1,128)S(1)} %get-tuple-element.27, f32[64,1]{0,1:T(1,128)S(1)} %get-tuple-element.28, f32[64,3]{0,1:T(4,128)} %param.16, f32[64,3]{0,1:T(4,128)} %param.15), kind=kLoop, calls=%fused_computation.31 | loop fusion | flops 1536 | bytes 4096 | tf_op jit(solution)/shard_map/concatenate | solution.py:397
  3.3 0.1 copy.36
  3.4 0.6 %gather_fusion = f32[12,8]{1,0:T(8,128)S(1)} fusion(f32[64,8]{1,0:T(8,128)S(1)} %copy.36, s32[1024]{0:T(1024)S(1)} %pad_clamp_fusion.1), kind=kCustom, calls=%fused_computation | custom fusion | bytes 816 | tf_op jit(solution)/shard_map/gather | solution.py:416
  3.9 0.1 reshape.122
  4.0 0.0 copy-start.5
  4.0 0.0 copy-start.6
  4.0 1.7 %fusion.7 = f32[3,4,4096]{2,1,0:T(4,128)S(1)} fusion(f32[64,4096]{1,0:T(8,128)} %param.14, s32[3,64]{1,0:T(4,128)S(1)} %broadcast_add_fusion, pred[3,64]{1,0:T(4,128)(4,1)S(1)} %get-tuple-element.23), kind=kOutput, calls=%fused_computation.10 | convolution fusion | flops 37750272 | bytes 1246144 | tf_op jit(solution)/shard_map/qjr,rc->qjc/dot_general | solution.py:420
  5.7 0.0 copy-start.7
  5.7 0.0 copy-start.1
  5.8 0.0 copy-start.10
  5.9 0.1 collective-permute-start
  5.9 3.4 %collective-permute-start.2 = (f32[5,4096]{1,0:T(8,128)S(1)}, f32[5,4096]{1,0:T(8,128)S(1)}, u32[]{:S(2)}, u32[]{:S(2)}) collective-permute-start(f32[5,4096]{1,0:T(8,128)S(1)} %get-tuple-element.25), channel_id=1, source_target_pairs={{0,64},{1,65},{2,66},{3,67},{4,68},{5,69},{6,70},{7,71},{8,72},{9,... | collective-permute-start | bytes 245768 | tf_op jit(solution)/shard_map/ppermute | solution.py:432
  9.3 6.2 %collective-permute-start.1 = (f32[5,4096]{1,0:T(8,128)S(1)}, f32[5,4096]{1,0:T(8,128)S(1)}, u32[]{:S(2)}, u32[]{:S(2)}) collective-permute-start(f32[5,4096]{1,0:T(8,128)S(1)} %get-tuple-element.26), channel_id=1, source_target_pairs={{0,127},{1,0},{2,1},{3,2},{4,3},{5,4},{6,5},{7,6},{8,7},{9,8},{10,... | collective-permute-start | bytes 245768 | tf_op jit(solution)/shard_map/ppermute | solution.py:432
  15.5 0.0 copy-done.5
  15.5 0.0 copy-done.6
  15.5 0.8 %fusion.9.refs_3_.pick_ref.refs_6_ = bf16[6,64,64]{2,1,0:T(8,128)(2,1)} fusion(s32[6,64]{1,0:T(8,128)S(1)} %pad_add_fusion), kind=kLoop, calls=%fused_computation.15 | loop fusion | flops 49152 | bytes 50688 | tf_op jit(solution)/shard_map/convert_element_type | solution.py:453
  16.3 0.0 copy-done.7
  16.3 0.7 %copy.37 = s32[2,64]{0,1:T(8,128)} copy(s32[2,64]{1,0:T(2,128)S(1)} %bitcast.27) | data formatting | bytes 1024 | tf_op jit(solution)/shard_map/squeeze | solution.py:454
  17.0 0.2 collective-permute-done
  17.2 0.1 reshape_squeeze.9
  17.3 0.2 convert_reduce_fusion.2
  17.5 0.0 collective-permute-done.2
  17.5 0.1 reshape_squeeze.11
  17.6 0.2 convert_reduce_fusion
  17.8 0.2 collective-permute-done.1
  18.0 0.1 reshape_squeeze.10
  18.1 0.2 convert_reduce_fusion.1
  18.3 0.1 pad_add_fusion.1
  18.4 0.1 select_reduce_fusion
  18.5 0.6 %gather_fusion.1 = f32[64,8]{1,0:T(8,128)S(1)} fusion(f32[76,8]{1,0:T(8,128)S(1)} %pad_maximum_fusion, s32[1024]{0:T(1024)S(1)} %pad_clamp_fusion), kind=kCustom, calls=%fused_computation.1 | custom fusion | bytes 4352 | tf_op jit(solution)/shard_map/gather | solution.py:446
  19.1 0.0 copy-start.2
  19.1 0.2 slice_reduce_fusion
  19.4 0.0 copy-done.1
  19.4 0.0 copy-done.10
  19.4 0.8 %convolution_select_fusion.refs_0_.refs_3_ = f32[64,4096]{1,0:T(8,128)S(1)} fusion(f32[4,4096]{1,0:T(4,128)S(1)} %slice.129, f32[4,4096]{1,0:T(4,128)S(1)} %slice.128, f32[4,4096]{1,0:T(4,128)S(1)} %slice.127, f32[64,4096]{1,0:T(8,128)S(1)} %copy-done.1, f32[4096]{0:T(1024)S(1)} %copy-done.10, f32[64]{0:T(128)S(1)} %slice_reduce_fusion, s32[76]{0:T(128)S(1)} %pad_add_fusion.1), kind=kOutput, calls=%fused_computation.2 | convolution fusion | flops 240538368 | bytes 2310704 | tf_op jit(solution)/shard_map/dot_general | solution.py:456
  20.2 0.0 copy-done.2
  20.2 0.0 copy-start
  20.3 0.1 add_subtract_fusion
  20.3 0.1 add_add_fusion
  20.4 0.8 %copy-done = f32[64,4096]{1,0:T(8,128)} copy-done((f32[64,4096]{1,0:T(8,128)}, f32[64,4096]{1,0:T(8,128)S(1)}, u32[]{:S(2)}) %copy-start) | copy-done | bytes 1048600
  21.2 0.0 collective-permute-start.3
  21.2 5.3 %collective-permute-start.4 = (f32[64,256]{1,0:T(8,128)S(1)}, f32[64,256]{1,0:T(8,128)S(1)}, u32[]{:S(2)}, u32[]{:S(2)}) collective-permute-start(f32[64,256]{1,0:T(8,128)S(1)} %add_subtract_fusion), channel_id=1, source_target_pairs={{8,0},{16,8},{24,16},{32,24},{40,32},{48,40},{56,48},{64,56},{72,6... | collective-permute-start | bytes 196616 | tf_op jit(solution)/shard_map/ppermute | solution.py:385
  26.6 5.6 %shard_map.136 = (f32[64,4096]{1,0:T(8,128)}, f32[64,256]{1,0:T(8,128)}, f32[64,256]{1,0:T(8,128)}) custom-call(f32[64,4096]{1,0:T(8,128)} %copy-done, f32[64,8]{1,0:T(8,128)} %copy-done.2, f32[1,4096]{1,0:T(1,128)} %constant.80.clone.refs_2_.top_ref.refs_5_, bf16[6,64,64]{2,1,0:T(8,128)(2,1)} %fusion.9.refs_3_.pick_ref.refs_6_, ...), custom_call_target="tpu_custom_call" | custom-call | flops 2500000000 | bytes 4000000 | tf_op jit(solution)/shard_map/pallas_call | solution.py:314
  32.2 0.0 collective-permute-done.3.lower_ref
  32.2 0.0 copy-start.3
  32.2 0.0 collective-permute-done.4.upper_ref
  32.2 0.0 copy-start.4
  32.2 0.6 %copy-done.3 = f32[64,256]{1,0:T(8,128)} copy-done((f32[64,256]{1,0:T(8,128)}, f32[64,256]{1,0:T(8,128)S(1)}, u32[]{:S(2)}) %copy-start.3) | copy-done | bytes 65560
  32.8 0.0 copy-done.4
  32.8 2.4 %shard_map.137 = (f32[64,256]{1,0:T(8,128)}, f32[64,256]{1,0:T(8,128)}, f32[64,256]{1,0:T(8,128)}, f32[64,256]{1,0:T(8,128)}) custom-call(f32[64,256]{1,0:T(8,128)} %copy-done.3, f32[64,256]{1,0:T(8,128)} %copy-done.4, bf16[6,64,64]{2,1,0:T(8,128)(2,1)} %fusion.9.refs_3_.pick_ref.refs_6_, s32[64,2]{1,0:T(8,128)} %bitcast.23, ...), custom_call_target="tpu_custom_call" | custom-call | tf_op jit(solution)/shard_map/pallas_call | solution.py:330
  35.2 0.0 collective-permute-start.5
  35.2 5.3 %collective-permute-start.6 = (f32[64,256]{1,0:T(8,128)}, f32[64,256]{1,0:T(8,128)S(1)}, u32[]{:S(2)}, u32[]{:S(2)}) collective-permute-start(f32[64,256]{1,0:T(8,128)} %get-tuple-element.18), channel_id=1, source_target_pairs={{8,0},{16,8},{24,16},{32,24},{40,32},{48,40},{56,48},{64,56},{72,6... | collective-permute-start | bytes 196616 | tf_op jit(solution)/shard_map/ppermute | solution.py:385
  40.6 2.4 %collective-permute-done.5.refs_10_ = f32[64,256]{1,0:T(8,128)S(1)} collective-permute-done((f32[64,256]{1,0:T(8,128)}, f32[64,256]{1,0:T(8,128)S(1)}, u32[]{:S(2)}, u32[]{:S(2)}) %collective-permute-start.5) | collective-permute-done | bytes 65568 | tf_op jit(solution)/shard_map/ppermute | solution.py:385
  43.0 0.0 collective-permute-done.6.refs_11_
  43.0 0.6 %copy-done.8 = f32[64,256]{1,0:T(8,128)} copy-done((f32[64,256]{1,0:T(8,128)}, f32[64,256]{1,0:T(8,128)S(1)}, u32[]{:S(2)}) %copy-start.8) | copy-done | bytes 65560
  43.7 0.0 copy-done.9
  43.7 6.2 %shard_map.138 = f32[64,4096]{1,0:T(8,128)} custom-call(f32[64,4096]{1,0:T(8,128)} %get-tuple-element.12.refs_0_, f32[64,256]{1,0:T(8,128)} %get-tuple-element.15.refs_1_, f32[64,256]{1,0:T(8,128)} %get-tuple-element.16.refs_2_, f32[64,4096]{1,0:T(8,128)} %copy-done, f32[64,8]{1,0:T(8,128)} %copy-done.2, f32[1,4096]{1,0:T(1,128)} %constant.80.clone.refs_2_.top_ref.refs_5_, ...), custom_call_target="tpu_custom_call" | custom-call | flops 2500000000 | bytes 4000000 | tf_op jit(solution)/shard_map/pallas_call | solution.py:314
  (17 shorter events, 0.2 us)
Async XLA Ops:
  4.0 11.5 %copy-start.5 = (s32[1,4,64]{2,1,0:T(4,128)S(1)}, s32[1,4,64]{2,1,0:T(4,128)}, u32[]{:S(2)}) copy-start(s32[1,4,64]{2,1,0:T(4,128)} %param.19) | copy-start | bytes 3076
  4.0 11.5 %copy-start.6 = (s32[1,2,64]{2,1,0:T(2,128)S(1)}, s32[1,2,64]{2,1,0:T(2,128)}, u32[]{:S(2)}) copy-start(s32[1,2,64]{2,1,0:T(2,128)} %param.20) | copy-start | bytes 1540
  5.7 10.5 %copy-start.7 = (s32[1,2,64]{2,1,0:T(2,128)S(1)}, s32[1,2,64]{2,1,0:T(2,128)}, u32[]{:S(2)}) copy-start(s32[1,2,64]{2,1,0:T(2,128)} %param.21) | copy-start | bytes 1540
  5.7 13.6 %copy-start.1 = (f32[64,4096]{1,0:T(8,128)S(1)}, f32[64,4096]{1,0:T(8,128)}, u32[]{:S(2)}) copy-start(f32[64,4096]{1,0:T(8,128)} %param.14) | copy-start | bytes 3145732
  5.8 13.6 %copy-start.10 = (f32[4096]{0:T(1024)S(1)}, f32[4096]{0:T(1024)}, u32[]{:S(2)}) copy-start(f32[4096]{0:T(1024)} %constant.95) | copy-start | bytes 49156
  5.9 11.3 %collective-permute-start = (f32[5,4096]{1,0:T(8,128)S(1)}, f32[5,4096]{1,0:T(8,128)S(1)}, u32[]{:S(2)}, u32[]{:S(2)}) collective-permute-start(f32[5,4096]{1,0:T(8,128)S(1)} %get-tuple-element.24), channel_id=1, source_target_pairs={{0,1},{1,2},{2,3},{3,4},{4,5},{5,6},{6,7},{7,8},{8,9},{9,10},{10,1... | collective-permute-start | bytes 245768 | tf_op jit(solution)/shard_map/ppermute | solution.py:432
  5.9 11.5 %collective-permute-start.2 = (f32[5,4096]{1,0:T(8,128)S(1)}, f32[5,4096]{1,0:T(8,128)S(1)}, u32[]{:S(2)}, u32[]{:S(2)}) collective-permute-start(f32[5,4096]{1,0:T(8,128)S(1)} %get-tuple-element.25), channel_id=1, source_target_pairs={{0,64},{1,65},{2,66},{3,67},{4,68},{5,69},{6,70},{7,71},{8,72},{9,... | collective-permute-start | bytes 245768 | tf_op jit(solution)/shard_map/ppermute | solution.py:432
  9.3 8.7 %collective-permute-start.1 = (f32[5,4096]{1,0:T(8,128)S(1)}, f32[5,4096]{1,0:T(8,128)S(1)}, u32[]{:S(2)}, u32[]{:S(2)}) collective-permute-start(f32[5,4096]{1,0:T(8,128)S(1)} %get-tuple-element.26), channel_id=1, source_target_pairs={{0,127},{1,0},{2,1},{3,2},{4,3},{5,4},{6,5},{7,6},{8,7},{9,8},{10,... | collective-permute-start | bytes 245768 | tf_op jit(solution)/shard_map/ppermute | solution.py:432
  19.1 1.1 %copy-start.2 = (f32[64,8]{1,0:T(8,128)}, f32[64,8]{1,0:T(8,128)S(1)}, u32[]{:S(2)}) copy-start(f32[64,8]{1,0:T(8,128)S(1)} %gather_fusion.1) | copy-start | bytes 6148
  20.2 1.0 %copy-start = (f32[64,4096]{1,0:T(8,128)}, f32[64,4096]{1,0:T(8,128)S(1)}, u32[]{:S(2)}) copy-start(f32[64,4096]{1,0:T(8,128)S(1)} %convolution_select_fusion.refs_0_.refs_3_) | copy-start | bytes 3145732
  21.2 10.9 %collective-permute-start.3 = (f32[64,256]{1,0:T(8,128)S(1)}, f32[64,256]{1,0:T(8,128)S(1)}, u32[]{:S(2)}, u32[]{:S(2)}) collective-permute-start(f32[64,256]{1,0:T(8,128)S(1)} %add_add_fusion), channel_id=1, source_target_pairs={{0,8},{8,16},{16,24},{24,32},{32,40},{40,48},{48,56},{56,64},{64,7... | collective-permute-start | bytes 196616 | tf_op jit(solution)/shard_map/ppermute | solution.py:385
  21.2 10.9 %collective-permute-start.4 = (f32[64,256]{1,0:T(8,128)S(1)}, f32[64,256]{1,0:T(8,128)S(1)}, u32[]{:S(2)}, u32[]{:S(2)}) collective-permute-start(f32[64,256]{1,0:T(8,128)S(1)} %add_subtract_fusion), channel_id=1, source_target_pairs={{8,0},{16,8},{24,16},{32,24},{40,32},{48,40},{56,48},{64,56},{72,6... | collective-permute-start | bytes 196616 | tf_op jit(solution)/shard_map/ppermute | solution.py:385
  32.2 0.6 %copy-start.3 = (f32[64,256]{1,0:T(8,128)}, f32[64,256]{1,0:T(8,128)S(1)}, u32[]{:S(2)}) copy-start(f32[64,256]{1,0:T(8,128)S(1)} %collective-permute-done.3.lower_ref) | copy-start | bytes 196612
  32.2 0.6 %copy-start.4 = (f32[64,256]{1,0:T(8,128)}, f32[64,256]{1,0:T(8,128)S(1)}, u32[]{:S(2)}) copy-start(f32[64,256]{1,0:T(8,128)S(1)} %collective-permute-done.4.upper_ref) | copy-start | bytes 196612
  35.2 7.8 %collective-permute-start.5 = (f32[64,256]{1,0:T(8,128)}, f32[64,256]{1,0:T(8,128)S(1)}, u32[]{:S(2)}, u32[]{:S(2)}) collective-permute-start(f32[64,256]{1,0:T(8,128)} %get-tuple-element.17), channel_id=1, source_target_pairs={{0,8},{8,16},{16,24},{24,32},{32,40},{40,48},{48,56},{56,64},{64,7... | collective-permute-start | bytes 196616 | tf_op jit(solution)/shard_map/ppermute | solution.py:385
  35.2 7.8 %collective-permute-start.6 = (f32[64,256]{1,0:T(8,128)}, f32[64,256]{1,0:T(8,128)S(1)}, u32[]{:S(2)}, u32[]{:S(2)}) collective-permute-start(f32[64,256]{1,0:T(8,128)} %get-tuple-element.18), channel_id=1, source_target_pairs={{8,0},{16,8},{24,16},{32,24},{40,32},{48,40},{56,48},{64,56},{72,6... | collective-permute-start | bytes 196616 | tf_op jit(solution)/shard_map/ppermute | solution.py:385
  43.0 0.6 %copy-start.8 = (f32[64,256]{1,0:T(8,128)}, f32[64,256]{1,0:T(8,128)S(1)}, u32[]{:S(2)}) copy-start(f32[64,256]{1,0:T(8,128)S(1)} %collective-permute-done.5.refs_10_) | copy-start | bytes 196612
  43.0 0.6 %copy-start.9 = (f32[64,256]{1,0:T(8,128)}, f32[64,256]{1,0:T(8,128)S(1)}, u32[]{:S(2)}) copy-start(f32[64,256]{1,0:T(8,128)S(1)} %collective-permute-done.6.refs_11_) | copy-start | bytes 196612

commit v13 on v12

--- a/solution.py
+++ b/solution.py
@@ -411,39 +411,28 @@
     hit = chosen[:, None, :] & (
         rank[:, None, :] == jnp.arange(moving, dtype=jnp.int32)[None, :, None]
     )
-    rows = jnp.arange(element_count, dtype=jnp.int32)
-    picked = jnp.sum(jnp.where(hit, rows[None, None, :], 0), axis=2).reshape(-1)
-    side_rows = side_info[picked].reshape(len(shifts), 1, moving * side_width)
-    side_rows = jnp.pad(side_rows, ((0, 0), (0, 0), (0, P_SIZE**3 - moving * side_width)))
-    parcels = jnp.concatenate(
-        [
-            jnp.einsum(
-                "qjr,rc->qjc", hit.astype(jnp.float32), coefficients, precision=lax.Precision.HIGHEST
-            ),
-            side_rows,
-        ],
+    width = P_SIZE**3
+    carried_rows = jnp.concatenate(
+        [coefficients, side_info, jnp.zeros((element_count, 128 - side_width), jnp.float32)],
         axis=1,
     )
-    got_coef = [coefficients]
-    got_side = [side_info]
+    parcels = jnp.einsum(
+        "qjr,rc->qjc", hit.astype(jnp.float32), carried_rows, precision=lax.Precision.HIGHEST
+    )
+    got_rows = [carried_rows]
     got_slot = [jnp.where(destination == here, new_slot, element_count)]
     for index, shift in enumerate(shifts):
         pairs = [(i, (i + shift) % blocks_all) for i in range(blocks_all)]
         arrived = lax.ppermute(parcels[index], ("dom", "face"), pairs)
-        arrived_side = arrived[moving, : moving * side_width].reshape(moving, side_width)
-        got_coef.append(arrived[:moving])
-        got_side.append(arrived_side)
-        got_slot.append(arrived_side[:, 6].astype(jnp.int32))
-    got_coef = jnp.concatenate(got_coef, axis=0)
-    got_side = jnp.concatenate(got_side, axis=0)
+        got_rows.append(arrived)
+        got_slot.append(arrived[:, width + 6].astype(jnp.int32))
+    got_rows = jnp.concatenate(got_rows, axis=0)
     got_slot = jnp.concatenate(got_slot, axis=0)
-    hit = got_slot[None, :] == jnp.arange(element_count, dtype=jnp.int32)[:, None]
-    got_rows = jnp.arange(got_slot.shape[0], dtype=jnp.int32)
-    source = jnp.sum(jnp.where(hit, got_rows[None, :], 0), axis=1)
     placing = (got_slot[None, :] == jnp.arange(element_count, dtype=jnp.int32)[:, None]).astype(
         jnp.float32
     )
-    placed_side = got_side[source]
+    placed_rows = jnp.dot(placing, got_rows, precision=lax.Precision.HIGHEST)
+    placed_side = placed_rows[:, width : width + side_width]
     weight = placed_side
     top = jnp.asarray(top_modes().astype(np.float32))
     tables = kernel_tables()
@@ -453,7 +442,7 @@
     ).astype(jnp.bfloat16)
     codes = partner_turns[0].T
     spread_hi, spread_lo, lift, flip = tables
-    placed = jnp.dot(placing, got_coef, precision=lax.Precision.HIGHEST)
+    placed = placed_rows[:, :width]
     field = jnp.where(top <= weight[:, 7:8], placed, 0.0)
     slabs = [field[:, a * PLANE : (a + 1) * PLANE] for a in range(P_SIZE)]
     even, total = end_traces(slabs)

time: 50.1 us -> 49.4 us (0.986)
  local copies, waits for them, and re-layouts: 4.79 us -> 6.67 us
  matrix products: 2.55 us -> 1.31 us
  other arithmetic: 4.9 us -> 3.98 us
    unnamed x22 -> x20, local copies, waits for them, and re-layouts: 2.13 us -> 3.65 us
    dot_general x2, matrix products: 2.55 us -> 1.31 us  [the longest x1 0.82 us: shards(): placed_rows = jnp.dot(placing, got_rows, precision=lax.Precision.HIGHEST)]
    concatenate x1, local copies, waits for them, and re-layouts: 0.09 us -> 1.31 us  [shards(): jnp.concatenate([coefficients, side_info, jnp.zeros((element_count, 128 -...]
    gather x2 -> x0, local copies, waits for them, and re-layouts: 1.15 us -> none  [the longest x1 0.6 us: shards(): placed_side = got_side[source]]
    concatenate x3 -> x0, other arithmetic: 0.76 us -> none  [the longest x1 0.71 us: shards(): jnp.concatenate([diffusion, velocity, new_slot[:, None].astype(jnp.float3...]
    slice x6 -> x1, local copies, waits for them, and re-layouts: 0.1 us -> 0.62 us  [shards(): placed_side = placed_rows[:, width:width + side_width]]
  transfers between devices with their start and end apart: 7 -> 7, of which waited for: 3 -> 2; matrix products, arithmetic and copies ran while one was open for 4% -> 4% of each run, Pallas kernels for 11% -> 11%
where the time goes in v13:
time: 49.4 us; the launch traced here: 49.2 us
  starting transfers between devices  20.3 us (41%)
  Pallas kernels  14.2 us (29%)
  local copies, waits for them, and re-layouts  6.67 us (14%)
  other arithmetic  3.98 us (8%)
  waiting for transfers between devices  2.53 us (5%)
  matrix products  1.31 us (3%)
    pallas_call x2, Pallas kernels, inner(): pl.pallas_call(functools.partial(inner_body, scale=scale, carried=carried...  11.8 us
    ppermute x4, starting transfers between devices, exchange(): return (lax.ppermute(total, 'dom', up), lax.ppermute(even, 'dom', down))  10.7 us
    ppermute x3, starting transfers between devices, shards(): arrived = lax.ppermute(parcels[index], ('dom', 'face'), pairs)  9.63 us
    unnamed x20, local copies, waits for them, and re-layouts  3.65 us
    ppermute x4, waiting for transfers between devices, exchange(): return (lax.ppermute(total, 'dom', up), lax.ppermute(even, 'dom', down))  2.46 us
    pallas_call x1, Pallas kernels, faces(): pl.pallas_call(functools.partial(faces_body, scale=scale), out_shape=(squ...  2.42 us
    concatenate x1, local copies, waits for them, and re-layouts, shards(): jnp.concatenate([coefficients, side_info, jnp.zeros((element_count, 128 -...  1.31 us
  transfers between devices with their start and end apart: 7, of which 2 were waited for; matrix products, arithmetic and copies ran while one was open for 4% of the time, Pallas kernels for 11%

profile of v13, /device:TPU:0, one launch (start us, length us, event | category | flops | bytes accessed | tf_op | source)
XLA Modules:
  0.0 49.2 jit_solution(15314568713287158877)
XLA Ops:
  0.0 0.7 %convert_bitcast_fusion = f32[64,1]{0,1:T(1,128)S(1)} fusion(s32[64]{0:T(128)} %param.17), kind=kLoop, calls=%fused_computation.45 | loop fusion | flops 64 | bytes 512 | tf_op jit(solution)/shard_map/convert_element_type | solution.py:402
  0.7 0.7 %and_select_fusion = s32[3]{0:T(128)S(1)} fusion(s32[3]{0:T(128)} %constant.73.clone, s32[]{:T(128)S(6)} %add.93), kind=kLoop, calls=%fused_computation.34 | loop fusion | flops 36 | bytes 28 | tf_op jit(solution)/shard_map/jit(remainder)/select_n | solution.py:408
  1.3 0.7 %compare_select_fusion.2 = (s32[64]{0:T(128)S(1)}, s32[64]{0:T(128)S(1)}, s32[64]{0:T(128)S(1)}) fusion(s32[]{:T(128)S(6)} %add.93, s32[64]{0:T(128)} %param.18), kind=kLoop, calls=%fused_computation.36 | loop fusion | flops 1344 | bytes 1028 | tf_op jit(solution)/shard_map/jit(_where)/select_n | solution.py:423
  2.0 0.1 fusion.21
  2.1 0.2 reduce_window_sum.11
  2.3 0.1 copy.22
  2.4 0.1 copy.23
  2.5 0.8 %copy.20 = f32[64,3]{1,0:T(8,128)S(1)} copy(f32[64,3]{0,1:T(4,128)} %param.15) | data formatting | bytes 1536 | tf_op args[1]
  3.3 0.8 %copy.21 = f32[64,3]{1,0:T(8,128)S(1)} copy(f32[64,3]{0,1:T(4,128)} %param.16) | data formatting | bytes 1536 | tf_op args[2]
  4.1 1.3 %concatenate.12 = f32[64,4224]{1,0:T(8,128)S(1)} concatenate(f32[64,4096]{1,0:T(8,128)} %param.14, f32[64,3]{1,0:T(8,128)S(1)} %copy.20, f32[64,3]{1,0:T(8,128)S(1)} %copy.21, f32[64,1]{1,0:T(8,128)S(1)} %copy.22, f32[64,1]{1,0:T(8,128)S(1)} %copy.23, f32[64,120]{1,0:T(8,128)S(1)} %broadcast_in_dim.6), dimensions={1} | concatenate | bytes 2162688 | tf_op jit(solution)/shard_map/concatenate | solution.py:415
  5.4 0.0 copy-start.4
  5.4 0.0 copy-start.5
  5.4 0.0 copy-start.6
  5.4 0.5 fusion.8
  5.9 0.1 collective-permute-start
  6.0 3.4 %collective-permute-start.2 = (f32[4,4224]{1,0:T(4,128)S(1)}, f32[4,4224]{1,0:T(4,128)S(1)}, u32[]{:S(2)}, u32[]{:S(2)}) collective-permute-start(f32[4,4224]{1,0:T(4,128)S(1)} %get-tuple-element.25), channel_id=1, source_target_pairs={{0,64},{1,65},{2,66},{3,67},{4,68},{5,69},{6,70},{7,71},{8,72},{9,... | collective-permute-start | bytes 202760 | tf_op jit(solution)/shard_map/ppermute | solution.py:426
  9.4 6.2 %collective-permute-start.1 = (f32[4,4224]{1,0:T(4,128)S(1)}, f32[4,4224]{1,0:T(4,128)S(1)}, u32[]{:S(2)}, u32[]{:S(2)}) collective-permute-start(f32[4,4224]{1,0:T(4,128)S(1)} %get-tuple-element.26), channel_id=1, source_target_pairs={{0,127},{1,0},{2,1},{3,2},{4,3},{5,4},{6,5},{7,6},{8,7},{9,8},{10,... | collective-permute-start | bytes 202760 | tf_op jit(solution)/shard_map/ppermute | solution.py:426
  15.6 0.0 copy-done.4
  15.6 0.0 copy-done.5
  15.6 0.8 %fusion.10.refs_3_.pick_ref.refs_6_ = bf16[6,64,64]{2,1,0:T(8,128)(2,1)} fusion(s32[6,64]{1,0:T(8,128)S(1)} %pad_add_fusion), kind=kLoop, calls=%fused_computation.12 | loop fusion | flops 49152 | bytes 50688 | tf_op jit(solution)/shard_map/convert_element_type | solution.py:442
  16.3 0.0 copy-done.6
  16.3 0.7 %copy.24 = s32[2,64]{0,1:T(8,128)} copy(s32[2,64]{1,0:T(2,128)S(1)} %bitcast.21) | data formatting | bytes 1024 | tf_op jit(solution)/shard_map/squeeze | solution.py:443
  17.0 0.0 collective-permute-done
  17.0 0.2 fusion.18
  17.2 0.0 collective-permute-done.2
  17.2 0.2 fusion.16
  17.4 0.1 collective-permute-done.1
  17.5 0.2 fusion.17
  17.7 0.1 pad_add_fusion.1
  17.7 0.0 copy-start.3
  17.8 0.8 %fusion = f32[64,4224]{1,0:T(8,128)S(1)} fusion(f32[4,4224]{1,0:T(4,128)S(1)} %collective-permute-done.2, f32[4,4224]{1,0:T(4,128)S(1)} %collective-permute-done.1, f32[4,4224]{1,0:T(4,128)S(1)} %collective-permute-done, f32[64,4224]{1,0:T(8,128)S(1)} %concatenate.12, s32[76]{0:T(128)S(1)} %pad_add_fusion.1), kind=kOutput, calls=%fused_computation | convolution fusion | flops 247514368 | bytes 2365744 | tf_op jit(solution)/shard_map/dot_general | solution.py:434
  18.6 0.2 slice_reduce_fusion
  18.8 0.6 %slice.109.refs_1_.weight_ref.refs_4_ = f32[64,8]{1,0:T(8,128)} slice(f32[64,4224]{1,0:T(8,128)S(1)} %fusion), slice={[0:64], [4096:4104]} | slice | bytes 4096 | tf_op jit(solution)/shard_map/slice | solution.py:435
  19.4 0.0 copy-done.3
  19.4 0.1 slice_select_fusion.refs_0_.refs_3_
  19.5 0.0 copy-start
  19.5 0.1 add_subtract_fusion
  19.6 0.1 add_add_fusion
  19.7 0.8 %copy-done = f32[64,4096]{1,0:T(8,128)} copy-done((f32[64,4096]{1,0:T(8,128)}, f32[64,4096]{1,0:T(8,128)S(1)}, u32[]{:S(2)}) %copy-start) | copy-done | bytes 1048600
  20.5 0.0 collective-permute-start.3
  20.5 5.3 %collective-permute-start.4 = (f32[64,256]{1,0:T(8,128)S(1)}, f32[64,256]{1,0:T(8,128)S(1)}, u32[]{:S(2)}, u32[]{:S(2)}) collective-permute-start(f32[64,256]{1,0:T(8,128)S(1)} %add_subtract_fusion), channel_id=1, source_target_pairs={{8,0},{16,8},{24,16},{32,24},{40,32},{48,40},{56,48},{64,56},{72,6... | collective-permute-start | bytes 196616 | tf_op jit(solution)/shard_map/ppermute | solution.py:385
  25.9 5.6 %shard_map.136 = (f32[64,4096]{1,0:T(8,128)}, f32[64,256]{1,0:T(8,128)}, f32[64,256]{1,0:T(8,128)}) custom-call(f32[64,4096]{1,0:T(8,128)} %copy-done, f32[64,8]{1,0:T(8,128)} %slice.109.refs_1_.weight_ref.refs_4_, f32[1,4096]{1,0:T(1,128)} %constant.74.clone.refs_2_.top_ref.refs_5_, bf16[6,64,64]{2,1,0:T(8,128)(2,1)} %fusion.10.refs_3_.pick_ref.refs_6_, ...), custom_call_target="tpu_custom_call" | custom-call | flops 2500000000 | bytes 4000000 | tf_op jit(solution)/shard_map/pallas_call | solution.py:314
  31.4 0.0 collective-permute-done.3.lower_ref
  31.4 0.0 copy-start.1
  31.4 0.0 collective-permute-done.4.upper_ref
  31.5 0.0 copy-start.2
  31.5 0.6 %copy-done.1 = f32[64,256]{1,0:T(8,128)} copy-done((f32[64,256]{1,0:T(8,128)}, f32[64,256]{1,0:T(8,128)S(1)}, u32[]{:S(2)}) %copy-start.1) | copy-done | bytes 65560
  32.1 0.0 copy-done.2
  32.1 2.4 %shard_map.137 = (f32[64,256]{1,0:T(8,128)}, f32[64,256]{1,0:T(8,128)}, f32[64,256]{1,0:T(8,128)}, f32[64,256]{1,0:T(8,128)}) custom-call(f32[64,256]{1,0:T(8,128)} %copy-done.1, f32[64,256]{1,0:T(8,128)} %copy-done.2, bf16[6,64,64]{2,1,0:T(8,128)(2,1)} %fusion.10.refs_3_.pick_ref.refs_6_, s32[64,2]{1,0:T(8,128)} %bitcast.17, ...), custom_call_target="tpu_custom_call" | custom-call | tf_op jit(solution)/shard_map/pallas_call | solution.py:330
  34.5 0.0 collective-permute-start.5
  34.5 5.3 %collective-permute-start.6 = (f32[64,256]{1,0:T(8,128)}, f32[64,256]{1,0:T(8,128)S(1)}, u32[]{:S(2)}, u32[]{:S(2)}) collective-permute-start(f32[64,256]{1,0:T(8,128)} %get-tuple-element.18), channel_id=1, source_target_pairs={{8,0},{16,8},{24,16},{32,24},{40,32},{48,40},{56,48},{64,56},{72,6... | collective-permute-start | bytes 196616 | tf_op jit(solution)/shard_map/ppermute | solution.py:385
  39.9 2.4 %collective-permute-done.5.refs_10_ = f32[64,256]{1,0:T(8,128)S(1)} collective-permute-done((f32[64,256]{1,0:T(8,128)}, f32[64,256]{1,0:T(8,128)S(1)}, u32[]{:S(2)}, u32[]{:S(2)}) %collective-permute-start.5) | collective-permute-done | bytes 65568 | tf_op jit(solution)/shard_map/ppermute | solution.py:385
  42.3 0.0 copy-start.7
  42.3 0.0 collective-permute-done.6.refs_11_
  42.3 0.0 copy-start.8
  42.3 0.6 %copy-done.7 = f32[64,256]{1,0:T(8,128)} copy-done((f32[64,256]{1,0:T(8,128)}, f32[64,256]{1,0:T(8,128)S(1)}, u32[]{:S(2)}) %copy-start.7) | copy-done | bytes 65560
  42.9 0.0 copy-done.8
  42.9 6.2 %shard_map.138 = f32[64,4096]{1,0:T(8,128)} custom-call(f32[64,4096]{1,0:T(8,128)} %get-tuple-element.12.refs_0_, f32[64,256]{1,0:T(8,128)} %get-tuple-element.15.refs_1_, f32[64,256]{1,0:T(8,128)} %get-tuple-element.16.refs_2_, f32[64,4096]{1,0:T(8,128)} %copy-done, f32[64,8]{1,0:T(8,128)} %slice.109.refs_1_.weight_ref.refs_4_, ...), custom_call_target="tpu_custom_call" | custom-call | flops 2500000000 | bytes 4000000 | tf_op jit(solution)/shard_map/pallas_call | solution.py:314
  (5 shorter events, 0.0 us)
Async XLA Ops:
  5.4 10.2 %copy-start.4 = (s32[1,4,64]{2,1,0:T(4,128)S(1)}, s32[1,4,64]{2,1,0:T(4,128)}, u32[]{:S(2)}) copy-start(s32[1,4,64]{2,1,0:T(4,128)} %param.19) | copy-start | bytes 3076
  5.4 10.2 %copy-start.5 = (s32[1,2,64]{2,1,0:T(2,128)S(1)}, s32[1,2,64]{2,1,0:T(2,128)}, u32[]{:S(2)}) copy-start(s32[1,2,64]{2,1,0:T(2,128)} %param.20) | copy-start | bytes 1540
  5.4 10.9 %copy-start.6 = (s32[1,2,64]{2,1,0:T(2,128)S(1)}, s32[1,2,64]{2,1,0:T(2,128)}, u32[]{:S(2)}) copy-start(s32[1,2,64]{2,1,0:T(2,128)} %param.21) | copy-start | bytes 1540
  5.9 11.1 %collective-permute-start = (f32[4,4224]{1,0:T(4,128)S(1)}, f32[4,4224]{1,0:T(4,128)S(1)}, u32[]{:S(2)}, u32[]{:S(2)}) collective-permute-start(f32[4,4224]{1,0:T(4,128)S(1)} %get-tuple-element.24), channel_id=1, source_target_pairs={{0,1},{1,2},{2,3},{3,4},{4,5},{5,6},{6,7},{7,8},{8,9},{9,10},{10,1... | collective-permute-start | bytes 202760 | tf_op jit(solution)/shard_map/ppermute | solution.py:426
  6.0 11.2 %collective-permute-start.2 = (f32[4,4224]{1,0:T(4,128)S(1)}, f32[4,4224]{1,0:T(4,128)S(1)}, u32[]{:S(2)}, u32[]{:S(2)}) collective-permute-start(f32[4,4224]{1,0:T(4,128)S(1)} %get-tuple-element.25), channel_id=1, source_target_pairs={{0,64},{1,65},{2,66},{3,67},{4,68},{5,69},{6,70},{7,71},{8,72},{9,... | collective-permute-start | bytes 202760 | tf_op jit(solution)/shard_map/ppermute | solution.py:426
  9.4 8.1 %collective-permute-start.1 = (f32[4,4224]{1,0:T(4,128)S(1)}, f32[4,4224]{1,0:T(4,128)S(1)}, u32[]{:S(2)}, u32[]{:S(2)}) collective-permute-start(f32[4,4224]{1,0:T(4,128)S(1)} %get-tuple-element.26), channel_id=1, source_target_pairs={{0,127},{1,0},{2,1},{3,2},{4,3},{5,4},{6,5},{7,6},{8,7},{9,8},{10,... | collective-permute-start | bytes 202760 | tf_op jit(solution)/shard_map/ppermute | solution.py:426
  17.7 1.6 %copy-start.3 = (f32[4096]{0:T(1024)S(1)}, f32[4096]{0:T(1024)}, u32[]{:S(2)}) copy-start(f32[4096]{0:T(1024)} %constant.87) | copy-start | bytes 49156
  19.5 1.0 %copy-start = (f32[64,4096]{1,0:T(8,128)}, f32[64,4096]{1,0:T(8,128)S(1)}, u32[]{:S(2)}) copy-start(f32[64,4096]{1,0:T(8,128)S(1)} %slice_select_fusion.refs_0_.refs_3_) | copy-start | bytes 3145732
  20.5 10.9 %collective-permute-start.3 = (f32[64,256]{1,0:T(8,128)S(1)}, f32[64,256]{1,0:T(8,128)S(1)}, u32[]{:S(2)}, u32[]{:S(2)}) collective-permute-start(f32[64,256]{1,0:T(8,128)S(1)} %add_add_fusion), channel_id=1, source_target_pairs={{0,8},{8,16},{16,24},{24,32},{32,40},{40,48},{48,56},{56,64},{64,7... | collective-permute-start | bytes 196616 | tf_op jit(solution)/shard_map/ppermute | solution.py:385
  20.5 10.9 %collective-permute-start.4 = (f32[64,256]{1,0:T(8,128)S(1)}, f32[64,256]{1,0:T(8,128)S(1)}, u32[]{:S(2)}, u32[]{:S(2)}) collective-permute-start(f32[64,256]{1,0:T(8,128)S(1)} %add_subtract_fusion), channel_id=1, source_target_pairs={{8,0},{16,8},{24,16},{32,24},{40,32},{48,40},{56,48},{64,56},{72,6... | collective-permute-start | bytes 196616 | tf_op jit(solution)/shard_map/ppermute | solution.py:385
  31.4 0.6 %copy-start.1 = (f32[64,256]{1,0:T(8,128)}, f32[64,256]{1,0:T(8,128)S(1)}, u32[]{:S(2)}) copy-start(f32[64,256]{1,0:T(8,128)S(1)} %collective-permute-done.3.lower_ref) | copy-start | bytes 196612
  31.5 0.6 %copy-start.2 = (f32[64,256]{1,0:T(8,128)}, f32[64,256]{1,0:T(8,128)S(1)}, u32[]{:S(2)}) copy-start(f32[64,256]{1,0:T(8,128)S(1)} %collective-permute-done.4.upper_ref) | copy-start | bytes 196612
  34.5 7.8 %collective-permute-start.5 = (f32[64,256]{1,0:T(8,128)}, f32[64,256]{1,0:T(8,128)S(1)}, u32[]{:S(2)}, u32[]{:S(2)}) collective-permute-start(f32[64,256]{1,0:T(8,128)} %get-tuple-element.17), channel_id=1, source_target_pairs={{0,8},{8,16},{16,24},{24,32},{32,40},{40,48},{48,56},{56,64},{64,7... | collective-permute-start | bytes 196616 | tf_op jit(solution)/shard_map/ppermute | solution.py:385
  34.5 7.8 %collective-permute-start.6 = (f32[64,256]{1,0:T(8,128)}, f32[64,256]{1,0:T(8,128)S(1)}, u32[]{:S(2)}, u32[]{:S(2)}) collective-permute-start(f32[64,256]{1,0:T(8,128)} %get-tuple-element.18), channel_id=1, source_target_pairs={{8,0},{16,8},{24,16},{32,24},{40,32},{48,40},{56,48},{64,56},{72,6... | collective-permute-start | bytes 196616 | tf_op jit(solution)/shard_map/ppermute | solution.py:385
  42.3 0.6 %copy-start.7 = (f32[64,256]{1,0:T(8,128)}, f32[64,256]{1,0:T(8,128)S(1)}, u32[]{:S(2)}) copy-start(f32[64,256]{1,0:T(8,128)S(1)} %collective-permute-done.5.refs_10_) | copy-start | bytes 196612
  42.3 0.6 %copy-start.8 = (f32[64,256]{1,0:T(8,128)}, f32[64,256]{1,0:T(8,128)S(1)}, u32[]{:S(2)}) copy-start(f32[64,256]{1,0:T(8,128)S(1)} %collective-permute-done.6.refs_11_) | copy-start | bytes 196612

commit v14 on v13

--- a/solution.py
+++ b/solution.py
@@ -412,27 +412,45 @@
         rank[:, None, :] == jnp.arange(moving, dtype=jnp.int32)[None, :, None]
     )
     width = P_SIZE**3
-    carried_rows = jnp.concatenate(
-        [coefficients, side_info, jnp.zeros((element_count, 128 - side_width), jnp.float32)],
-        axis=1,
-    )
-    parcels = jnp.einsum(
-        "qjr,rc->qjc", hit.astype(jnp.float32), carried_rows, precision=lax.Precision.HIGHEST
-    )
-    got_rows = [carried_rows]
+    exact = lax.Precision.HIGHEST
+    side_lanes = jnp.concatenate(
+        [
+            diffusion.T,
+            velocity.T,
+            new_slot[None, :].astype(jnp.float32),
+            orders[None, :].astype(jnp.float32),
+            jnp.zeros((128 - side_width, element_count), jnp.float32),
+        ],
+        axis=0,
+    )
+    hit_values = hit.astype(jnp.float32)
+    parcels = jnp.concatenate(
+        [
+            jnp.einsum("qjr,rc->qjc", hit_values, coefficients, precision=exact),
+            jnp.einsum("qjr,cr->qjc", hit_values, side_lanes, precision=exact),
+        ],
+        axis=2,
+    )
+    arrivals = []
     got_slot = [jnp.where(destination == here, new_slot, element_count)]
     for index, shift in enumerate(shifts):
         pairs = [(i, (i + shift) % blocks_all) for i in range(blocks_all)]
         arrived = lax.ppermute(parcels[index], ("dom", "face"), pairs)
-        got_rows.append(arrived)
+        arrivals.append(arrived)
         got_slot.append(arrived[:, width + 6].astype(jnp.int32))
-    got_rows = jnp.concatenate(got_rows, axis=0)
+    arrivals = jnp.concatenate(arrivals, axis=0)
     got_slot = jnp.concatenate(got_slot, axis=0)
     placing = (got_slot[None, :] == jnp.arange(element_count, dtype=jnp.int32)[:, None]).astype(
         jnp.float32
     )
-    placed_rows = jnp.dot(placing, got_rows, precision=lax.Precision.HIGHEST)
-    placed_side = placed_rows[:, width : width + side_width]
+    staying, coming = placing[:, :element_count], placing[:, element_count:]
+    placed = jnp.dot(
+        placing, jnp.concatenate([coefficients, arrivals[:, :width]], axis=0), precision=exact
+    )
+    placed_side = jnp.einsum("sr,cr->sc", staying, side_lanes, precision=exact) + jnp.dot(
+        coming, arrivals[:, width:], precision=exact
+    )
+    placed_side = placed_side[:, :side_width]
     weight = placed_side
     top = jnp.asarray(top_modes().astype(np.float32))
     tables = kernel_tables()
@@ -442,7 +460,6 @@
     ).astype(jnp.bfloat16)
     codes = partner_turns[0].T
     spread_hi, spread_lo, lift, flip = tables
-    placed = placed_rows[:, :width]
     field = jnp.where(top <= weight[:, 7:8], placed, 0.0)
     slabs = [field[:, a * PLANE : (a + 1) * PLANE] for a in range(P_SIZE)]
     even, total = end_traces(slabs)

time: 49.4 us -> 49.4 us (level)
  local copies, waits for them, and re-layouts: 6.67 us -> 4.85 us
  matrix products: 1.31 us -> 3.11 us
    dot_general x2 -> x5, matrix products: 1.31 us -> 3.11 us  [the longest x1 1.78 us: shards(): jnp.einsum('qjr,rc->qjc', hit_values, coefficients, precision=exact)]
    concatenate x1, local copies, waits for them, and re-layouts: 1.31 us -> 0.1 us  [shards(): jnp.concatenate([diffusion.T, velocity.T, new_slot[None, :].astype(jnp.fl...]
    slice x1 -> x0, local copies, waits for them, and re-layouts: 0.62 us -> none  [shards(): placed_side = placed_rows[:, width:width + side_width]]
    unnamed x20 -> x24, local copies, waits for them, and re-layouts: 3.65 us -> 3.67 us
  transfers between devices with their start and end apart: 7 -> 7, of which waited for: 2 -> 1; matrix products, arithmetic and copies ran while one was open for 4% -> 4% of each run, Pallas kernels for 11% -> 11%
where the time goes in v14:
time: 49.4 us; the launch traced here: 49.1 us
  starting transfers between devices  20.3 us (41%)
  Pallas kernels  14.2 us (29%)
  local copies, waits for them, and re-layouts  4.85 us (10%)
  other arithmetic  3.92 us (8%)
  matrix products  3.11 us (6%)
  waiting for transfers between devices  2.51 us (5%)
    pallas_call x2, Pallas kernels, inner(): pl.pallas_call(functools.partial(inner_body, scale=scale, carried=carried...  11.8 us
    ppermute x4, starting transfers between devices, exchange(): return (lax.ppermute(total, 'dom', up), lax.ppermute(even, 'dom', down))  10.7 us
    ppermute x3, starting transfers between devices, shards(): arrived = lax.ppermute(parcels[index], ('dom', 'face'), pairs)  9.63 us
    unnamed x24, local copies, waits for them, and re-layouts  3.67 us
    ppermute x4, waiting for transfers between devices, exchange(): return (lax.ppermute(total, 'dom', up), lax.ppermute(even, 'dom', down))  2.46 us
    pallas_call x1, Pallas kernels, faces(): pl.pallas_call(functools.partial(faces_body, scale=scale), out_shape=(squ...  2.41 us
    dot_general x1, matrix products, shards(): jnp.einsum('qjr,rc->qjc', hit_values, coefficients, precision=exact)  1.78 us
  transfers between devices with their start and end apart: 7, of which 1 were waited for; matrix products, arithmetic and copies ran while one was open for 4% of the time, Pallas kernels for 11%

profile of v14, /device:TPU:0, one launch (start us, length us, event | category | flops | bytes accessed | tf_op | source)
XLA Modules:
  0.0 49.1 jit_solution(15202504957549288008)
XLA Ops:
  0.0 0.7 %convert_bitcast_fusion = f32[1,64]{1,0:T(1,128)S(1)} fusion(s32[64]{0:T(128)} %param.17), kind=kLoop, calls=%fused_computation.61 | loop fusion | flops 64 | bytes 512 | tf_op jit(solution)/shard_map/convert_element_type | solution.py:421
  0.7 0.7 %and_select_fusion = s32[3]{0:T(128)S(1)} fusion(s32[3]{0:T(128)} %constant.73.clone, s32[]{:T(128)S(6)} %add.96), kind=kLoop, calls=%fused_computation.50 | loop fusion | flops 36 | bytes 28 | tf_op jit(solution)/shard_map/jit(remainder)/select_n | solution.py:408
  1.3 0.7 %compare_select_fusion.2 = (s32[64]{0:T(128)S(1)}, s32[64]{0:T(128)S(1)}, s32[64]{0:T(128)S(1)}) fusion(s32[]{:T(128)S(6)} %add.96, s32[64]{0:T(128)} %param.18), kind=kLoop, calls=%fused_computation.52 | loop fusion | flops 1344 | bytes 1028 | tf_op jit(solution)/shard_map/jit(_where)/select_n | solution.py:435
  2.0 0.0 copy-start.5
  2.0 0.0 copy-start.6
  2.0 0.1 fusion.35
  2.1 0.2 reduce_window_sum.11
  2.3 0.1 copy.22
  2.4 0.1 copy.23
  2.5 0.8 %copy.20 = f32[64,3]{1,0:T(8,128)S(1)} copy(f32[64,3]{0,1:T(4,128)} %param.15) | data formatting | bytes 1536 | tf_op args[1]
  3.3 0.0 copy-start.7
  3.3 0.8 %copy.21 = f32[64,3]{1,0:T(8,128)S(1)} copy(f32[64,3]{0,1:T(4,128)} %param.16) | data formatting | bytes 1536 | tf_op args[2]
  4.1 0.1 concatenate.18
  4.2 0.1 fusion.12
  4.4 0.0 copy-start.1
  4.4 0.0 copy-start.10
  4.4 1.8 %fusion.4 = f32[3,4,4096]{2,1,0:T(4,128)S(1)} fusion(f32[64,4096]{1,0:T(8,128)} %param.14, s32[3,64]{1,0:T(4,128)S(1)} %broadcast_add_fusion, pred[3,64]{1,0:T(4,128)(4,1)S(1)} %get-tuple-element.23), kind=kOutput, calls=%fused_computation.7 | convolution fusion | flops 37750272 | bytes 1246144 | tf_op jit(solution)/shard_map/qjr,rc->qjc/dot_general | solution.py:429
  6.2 0.1 fusion.10
  6.2 0.1 collective-permute-start
  6.3 3.4 %collective-permute-start.2 = (f32[4,4224]{1,0:T(4,128)S(1)}, f32[4,4224]{1,0:T(4,128)S(1)}, u32[]{:S(2)}, u32[]{:S(2)}) collective-permute-start(f32[4,4224]{1,0:T(4,128)S(1)} %get-tuple-element.25), channel_id=1, source_target_pairs={{0,64},{1,65},{2,66},{3,67},{4,68},{5,69},{6,70},{7,71},{8,72},{9,... | collective-permute-start | bytes 202760 | tf_op jit(solution)/shard_map/ppermute | solution.py:438
  9.7 6.2 %collective-permute-start.1 = (f32[4,4224]{1,0:T(4,128)S(1)}, f32[4,4224]{1,0:T(4,128)S(1)}, u32[]{:S(2)}, u32[]{:S(2)}) collective-permute-start(f32[4,4224]{1,0:T(4,128)S(1)} %get-tuple-element.26), channel_id=1, source_target_pairs={{0,127},{1,0},{2,1},{3,2},{4,3},{5,4},{6,5},{7,6},{8,7},{9,8},{10,... | collective-permute-start | bytes 202760 | tf_op jit(solution)/shard_map/ppermute | solution.py:438
  15.9 0.0 copy-done.5
  15.9 0.0 copy-done.6
  15.9 0.8 %fusion.6.refs_3_.pick_ref.refs_6_ = bf16[6,64,64]{2,1,0:T(8,128)(2,1)} fusion(s32[6,64]{1,0:T(8,128)S(1)} %pad_add_fusion), kind=kLoop, calls=%fused_computation.12 | loop fusion | flops 49152 | bytes 50688 | tf_op jit(solution)/shard_map/convert_element_type | solution.py:460
  16.6 0.0 copy-done.7
  16.6 0.7 %copy.24 = s32[2,64]{0,1:T(8,128)} copy(s32[2,64]{1,0:T(2,128)S(1)} %bitcast.33) | data formatting | bytes 1024 | tf_op jit(solution)/shard_map/squeeze | solution.py:461
  17.4 0.0 collective-permute-done
  17.4 0.2 fusion.31
  17.5 0.0 collective-permute-done.2
  17.5 0.2 fusion.29
  17.7 0.0 collective-permute-done.1
  17.8 0.2 fusion.30
  18.0 0.1 pad_add_fusion.1
  18.1 0.1 fusion.15
  18.2 0.2 convolution_add_fusion
  18.4 0.0 copy-start.2
  18.4 0.2 slice_reduce_fusion
  18.6 0.0 copy-done.1
  18.6 0.0 copy-done.10
  18.6 0.8 %convolution_select_fusion.refs_0_.refs_3_ = f32[64,4096]{1,0:T(8,128)S(1)} fusion(f32[4,4224]{1,0:T(4,128)S(1)} %collective-permute-done.2, f32[4,4224]{1,0:T(4,128)S(1)} %collective-permute-done.1, f32[4,4224]{1,0:T(4,128)S(1)} %collective-permute-done, f32[64,4096]{1,0:T(8,128)S(1)} %copy-done.1, f32[4096]{0:T(1024)S(1)} %copy-done.10, ...), kind=kOutput, calls=%fused_computation | convolution fusion | flops 240538368 | bytes 2316848 | tf_op jit(solution)/shard_map/dot_general | solution.py:447
  19.5 0.0 copy-done.2
  19.5 0.0 copy-start
  19.5 0.1 add_subtract_fusion
  19.6 0.1 add_add_fusion
  19.6 0.8 %copy-done = f32[64,4096]{1,0:T(8,128)} copy-done((f32[64,4096]{1,0:T(8,128)}, f32[64,4096]{1,0:T(8,128)S(1)}, u32[]{:S(2)}) %copy-start) | copy-done | bytes 1048600
  20.4 0.0 collective-permute-start.3
  20.5 5.3 %collective-permute-start.4 = (f32[64,256]{1,0:T(8,128)S(1)}, f32[64,256]{1,0:T(8,128)S(1)}, u32[]{:S(2)}, u32[]{:S(2)}) collective-permute-start(f32[64,256]{1,0:T(8,128)S(1)} %add_subtract_fusion), channel_id=1, source_target_pairs={{8,0},{16,8},{24,16},{32,24},{40,32},{48,40},{56,48},{64,56},{72,6... | collective-permute-start | bytes 196616 | tf_op jit(solution)/shard_map/ppermute | solution.py:385
  25.8 5.6 %shard_map.136 = (f32[64,4096]{1,0:T(8,128)}, f32[64,256]{1,0:T(8,128)}, f32[64,256]{1,0:T(8,128)}) custom-call(f32[64,4096]{1,0:T(8,128)} %copy-done, f32[64,8]{1,0:T(8,128)} %bitcast.24, f32[1,4096]{1,0:T(1,128)} %constant.74.clone.refs_2_.top_ref.refs_5_, bf16[6,64,64]{2,1,0:T(8,128)(2,1)} %fusion.6.refs_3_.pick_ref.refs_6_, ...), custom_call_target="tpu_custom_call" | custom-call | flops 2500000000 | bytes 4000000 | tf_op jit(solution)/shard_map/pallas_call | solution.py:314
  31.4 0.0 collective-permute-done.3.lower_ref
  31.4 0.0 copy-start.3
  31.4 0.0 collective-permute-done.4.upper_ref
  31.4 0.0 copy-start.4
  31.4 0.6 %copy-done.3 = f32[64,256]{1,0:T(8,128)} copy-done((f32[64,256]{1,0:T(8,128)}, f32[64,256]{1,0:T(8,128)S(1)}, u32[]{:S(2)}) %copy-start.3) | copy-done | bytes 65560
  32.0 0.0 copy-done.4
  32.0 2.4 %shard_map.137 = (f32[64,256]{1,0:T(8,128)}, f32[64,256]{1,0:T(8,128)}, f32[64,256]{1,0:T(8,128)}, f32[64,256]{1,0:T(8,128)}) custom-call(f32[64,256]{1,0:T(8,128)} %copy-done.3, f32[64,256]{1,0:T(8,128)} %copy-done.4, bf16[6,64,64]{2,1,0:T(8,128)(2,1)} %fusion.6.refs_3_.pick_ref.refs_6_, s32[64,2]{1,0:T(8,128)} %bitcast.27, ...), custom_call_target="tpu_custom_call" | custom-call | tf_op jit(solution)/shard_map/pallas_call | solution.py:330
  34.4 0.0 collective-permute-start.5
  34.4 5.3 %collective-permute-start.6 = (f32[64,256]{1,0:T(8,128)}, f32[64,256]{1,0:T(8,128)S(1)}, u32[]{:S(2)}, u32[]{:S(2)}) collective-permute-start(f32[64,256]{1,0:T(8,128)} %get-tuple-element.18), channel_id=1, source_target_pairs={{8,0},{16,8},{24,16},{32,24},{40,32},{48,40},{56,48},{64,56},{72,6... | collective-permute-start | bytes 196616 | tf_op jit(solution)/shard_map/ppermute | solution.py:385
  39.8 2.4 %collective-permute-done.5.refs_10_ = f32[64,256]{1,0:T(8,128)S(1)} collective-permute-done((f32[64,256]{1,0:T(8,128)}, f32[64,256]{1,0:T(8,128)S(1)}, u32[]{:S(2)}, u32[]{:S(2)}) %collective-permute-start.5) | collective-permute-done | bytes 65568 | tf_op jit(solution)/shard_map/ppermute | solution.py:385
  42.2 0.0 copy-start.8
  42.2 0.0 collective-permute-done.6.refs_11_
  42.2 0.0 copy-start.9
  42.2 0.6 %copy-done.8 = f32[64,256]{1,0:T(8,128)} copy-done((f32[64,256]{1,0:T(8,128)}, f32[64,256]{1,0:T(8,128)S(1)}, u32[]{:S(2)}) %copy-start.8) | copy-done | bytes 65560
  42.8 0.0 copy-done.9
  42.9 6.2 %shard_map.138 = f32[64,4096]{1,0:T(8,128)} custom-call(f32[64,4096]{1,0:T(8,128)} %get-tuple-element.12.refs_0_, f32[64,256]{1,0:T(8,128)} %get-tuple-element.15.refs_1_, f32[64,256]{1,0:T(8,128)} %get-tuple-element.16.refs_2_, f32[64,4096]{1,0:T(8,128)} %copy-done, f32[64,8]{1,0:T(8,128)} %bitcast.26, f32[1,4096]{1,0:T(1,128)} %constant.74.clone.refs_2_.top_ref.refs_5_, ...), custom_call_target="tpu_custom_call" | custom-call | flops 2500000000 | bytes 4000000 | tf_op jit(solution)/shard_map/pallas_call | solution.py:314
  (5 shorter events, 0.0 us)
Async XLA Ops:
  2.0 13.9 %copy-start.5 = (s32[1,4,64]{2,1,0:T(4,128)S(1)}, s32[1,4,64]{2,1,0:T(4,128)}, u32[]{:S(2)}) copy-start(s32[1,4,64]{2,1,0:T(4,128)} %param.19) | copy-start | bytes 3076
  2.0 13.9 %copy-start.6 = (s32[1,2,64]{2,1,0:T(2,128)S(1)}, s32[1,2,64]{2,1,0:T(2,128)}, u32[]{:S(2)}) copy-start(s32[1,2,64]{2,1,0:T(2,128)} %param.20) | copy-start | bytes 1540
  3.3 13.3 %copy-start.7 = (s32[1,2,64]{2,1,0:T(2,128)S(1)}, s32[1,2,64]{2,1,0:T(2,128)}, u32[]{:S(2)}) copy-start(s32[1,2,64]{2,1,0:T(2,128)} %param.21) | copy-start | bytes 1540
  4.4 14.3 %copy-start.1 = (f32[64,4096]{1,0:T(8,128)S(1)}, f32[64,4096]{1,0:T(8,128)}, u32[]{:S(2)}) copy-start(f32[64,4096]{1,0:T(8,128)} %param.14) | copy-start | bytes 3145732
  4.4 14.3 %copy-start.10 = (f32[4096]{0:T(1024)S(1)}, f32[4096]{0:T(1024)}, u32[]{:S(2)}) copy-start(f32[4096]{0:T(1024)} %constant.87) | copy-start | bytes 49156
  6.2 11.1 %collective-permute-start = (f32[4,4224]{1,0:T(4,128)S(1)}, f32[4,4224]{1,0:T(4,128)S(1)}, u32[]{:S(2)}, u32[]{:S(2)}) collective-permute-start(f32[4,4224]{1,0:T(4,128)S(1)} %get-tuple-element.24), channel_id=1, source_target_pairs={{0,1},{1,2},{2,3},{3,4},{4,5},{5,6},{6,7},{7,8},{8,9},{9,10},{10,1... | collective-permute-start | bytes 202760 | tf_op jit(solution)/shard_map/ppermute | solution.py:438
  6.3 11.2 %collective-permute-start.2 = (f32[4,4224]{1,0:T(4,128)S(1)}, f32[4,4224]{1,0:T(4,128)S(1)}, u32[]{:S(2)}, u32[]{:S(2)}) collective-permute-start(f32[4,4224]{1,0:T(4,128)S(1)} %get-tuple-element.25), channel_id=1, source_target_pairs={{0,64},{1,65},{2,66},{3,67},{4,68},{5,69},{6,70},{7,71},{8,72},{9,... | collective-permute-start | bytes 202760 | tf_op jit(solution)/shard_map/ppermute | solution.py:438
  9.7 8.1 %collective-permute-start.1 = (f32[4,4224]{1,0:T(4,128)S(1)}, f32[4,4224]{1,0:T(4,128)S(1)}, u32[]{:S(2)}, u32[]{:S(2)}) collective-permute-start(f32[4,4224]{1,0:T(4,128)S(1)} %get-tuple-element.26), channel_id=1, source_target_pairs={{0,127},{1,0},{2,1},{3,2},{4,3},{5,4},{6,5},{7,6},{8,7},{9,8},{10,... | collective-permute-start | bytes 202760 | tf_op jit(solution)/shard_map/ppermute | solution.py:438
  18.4 1.0 %copy-start.2 = (f32[64,128]{1,0:T(8,128)}, f32[64,128]{1,0:T(8,128)S(1)}, u32[]{:S(2)}) copy-start(f32[64,128]{1,0:T(8,128)S(1)} %convolution_add_fusion) | copy-start | bytes 98308
  19.5 1.0 %copy-start = (f32[64,4096]{1,0:T(8,128)}, f32[64,4096]{1,0:T(8,128)S(1)}, u32[]{:S(2)}) copy-start(f32[64,4096]{1,0:T(8,128)S(1)} %convolution_select_fusion.refs_0_.refs_3_) | copy-start | bytes 3145732
  20.4 10.9 %collective-permute-start.3 = (f32[64,256]{1,0:T(8,128)S(1)}, f32[64,256]{1,0:T(8,128)S(1)}, u32[]{:S(2)}, u32[]{:S(2)}) collective-permute-start(f32[64,256]{1,0:T(8,128)S(1)} %add_add_fusion), channel_id=1, source_target_pairs={{0,8},{8,16},{16,24},{24,32},{32,40},{40,48},{48,56},{56,64},{64,7... | collective-permute-start | bytes 196616 | tf_op jit(solution)/shard_map/ppermute | solution.py:385
  20.5 10.9 %collective-permute-start.4 = (f32[64,256]{1,0:T(8,128)S(1)}, f32[64,256]{1,0:T(8,128)S(1)}, u32[]{:S(2)}, u32[]{:S(2)}) collective-permute-start(f32[64,256]{1,0:T(8,128)S(1)} %add_subtract_fusion), channel_id=1, source_target_pairs={{8,0},{16,8},{24,16},{32,24},{40,32},{48,40},{56,48},{64,56},{72,6... | collective-permute-start | bytes 196616 | tf_op jit(solution)/shard_map/ppermute | solution.py:385
  31.4 0.6 %copy-start.3 = (f32[64,256]{1,0:T(8,128)}, f32[64,256]{1,0:T(8,128)S(1)}, u32[]{:S(2)}) copy-start(f32[64,256]{1,0:T(8,128)S(1)} %collective-permute-done.3.lower_ref) | copy-start | bytes 196612
  31.4 0.6 %copy-start.4 = (f32[64,256]{1,0:T(8,128)}, f32[64,256]{1,0:T(8,128)S(1)}, u32[]{:S(2)}) copy-start(f32[64,256]{1,0:T(8,128)S(1)} %collective-permute-done.4.upper_ref) | copy-start | bytes 196612
  34.4 7.8 %collective-permute-start.5 = (f32[64,256]{1,0:T(8,128)}, f32[64,256]{1,0:T(8,128)S(1)}, u32[]{:S(2)}, u32[]{:S(2)}) collective-permute-start(f32[64,256]{1,0:T(8,128)} %get-tuple-element.17), channel_id=1, source_target_pairs={{0,8},{8,16},{16,24},{24,32},{32,40},{40,48},{48,56},{56,64},{64,7... | collective-permute-start | bytes 196616 | tf_op jit(solution)/shard_map/ppermute | solution.py:385
  34.4 7.8 %collective-permute-start.6 = (f32[64,256]{1,0:T(8,128)}, f32[64,256]{1,0:T(8,128)S(1)}, u32[]{:S(2)}, u32[]{:S(2)}) collective-permute-start(f32[64,256]{1,0:T(8,128)} %get-tuple-element.18), channel_id=1, source_target_pairs={{8,0},{16,8},{24,16},{32,24},{40,32},{48,40},{56,48},{64,56},{72,6... | collective-permute-start | bytes 196616 | tf_op jit(solution)/shard_map/ppermute | solution.py:385
  42.2 0.6 %copy-start.8 = (f32[64,256]{1,0:T(8,128)}, f32[64,256]{1,0:T(8,128)S(1)}, u32[]{:S(2)}) copy-start(f32[64,256]{1,0:T(8,128)S(1)} %collective-permute-done.5.refs_10_) | copy-start | bytes 196612
  42.2 0.7 %copy-start.9 = (f32[64,256]{1,0:T(8,128)}, f32[64,256]{1,0:T(8,128)S(1)}, u32[]{:S(2)}) copy-start(f32[64,256]{1,0:T(8,128)S(1)} %collective-permute-done.6.refs_11_) | copy-start | bytes 196612

commit v15 on v14

--- a/solution.py
+++ b/solution.py
@@ -413,21 +413,17 @@
     )
     width = P_SIZE**3
     exact = lax.Precision.HIGHEST
-    side_lanes = jnp.concatenate(
-        [
-            diffusion.T,
-            velocity.T,
-            new_slot[None, :].astype(jnp.float32),
-            orders[None, :].astype(jnp.float32),
-            jnp.zeros((128 - side_width, element_count), jnp.float32),
-        ],
-        axis=0,
+    counts = jnp.concatenate(
+        [new_slot[None, :].astype(jnp.float32), orders[None, :].astype(jnp.float32)], axis=0
     )
     hit_values = hit.astype(jnp.float32)
     parcels = jnp.concatenate(
         [
             jnp.einsum("qjr,rc->qjc", hit_values, coefficients, precision=exact),
-            jnp.einsum("qjr,cr->qjc", hit_values, side_lanes, precision=exact),
+            jnp.einsum("qjr,rc->qjc", hit_values, diffusion, precision=exact),
+            jnp.einsum("qjr,rc->qjc", hit_values, velocity, precision=exact),
+            jnp.einsum("qjr,cr->qjc", hit_values, counts, precision=exact),
+            jnp.zeros(hit.shape[:2] + (128 - side_width,), jnp.float32),
         ],
         axis=2,
     )
@@ -447,10 +443,14 @@
     placed = jnp.dot(
         placing, jnp.concatenate([coefficients, arrivals[:, :width]], axis=0), precision=exact
     )
-    placed_side = jnp.einsum("sr,cr->sc", staying, side_lanes, precision=exact) + jnp.dot(
-        coming, arrivals[:, width:], precision=exact
-    )
-    placed_side = placed_side[:, :side_width]
+    placed_side = jnp.concatenate(
+        [
+            jnp.dot(staying, diffusion, precision=exact),
+            jnp.dot(staying, velocity, precision=exact),
+            jnp.einsum("sr,cr->sc", staying, counts, precision=exact),
+        ],
+        axis=1,
+    ) + jnp.dot(coming, arrivals[:, width : width + side_width], precision=exact)
     weight = placed_side
     top = jnp.asarray(top_modes().astype(np.float32))
     tables = kernel_tables()

time: 49.4 us -> 48.5 us (0.982)
  local copies, waits for them, and re-layouts: 4.85 us -> 3.28 us
  matrix products: 3.11 us -> 4.38 us
  other arithmetic: 3.92 us -> 3.29 us
    unnamed x24 -> x28, local copies, waits for them, and re-layouts: 3.67 us -> 2.15 us
    dot_general x3 -> x7, matrix products: 0.51 us -> 1.76 us  [the longest x1 0.82 us: shards(): jnp.einsum('qjr,rc->qjc', hit_values, diffusion, precision=exact)]
    convert_element_type x1, other arithmetic: 0.66 us -> 0.01 us  [shards(): orders[None, :].astype(jnp.float32)]
  transfers between devices with their start and end apart: 7 -> 7, of which waited for: 1 -> 2; matrix products, arithmetic and copies ran while one was open for 4% -> 4% of each run, Pallas kernels for 11% -> 12%
where the time goes in v15:
time: 48.5 us; the launch traced here: 48.2 us
  starting transfers between devices  20.3 us (42%)
  Pallas kernels  14.2 us (29%)
  matrix products  4.38 us (9%)
  other arithmetic  3.29 us (7%)
  local copies, waits for them, and re-layouts  3.28 us (7%)
  waiting for transfers between devices  2.53 us (5%)
    pallas_call x2, Pallas kernels, inner(): pl.pallas_call(functools.partial(inner_body, scale=scale, carried=carried...  11.8 us
    ppermute x4, starting transfers between devices, exchange(): return (lax.ppermute(total, 'dom', up), lax.ppermute(even, 'dom', down))  10.7 us
    ppermute x3, starting transfers between devices, shards(): arrived = lax.ppermute(parcels[index], ('dom', 'face'), pairs)  9.63 us
    ppermute x4, waiting for transfers between devices, exchange(): return (lax.ppermute(total, 'dom', up), lax.ppermute(even, 'dom', down))  2.46 us
    pallas_call x1, Pallas kernels, faces(): pl.pallas_call(functools.partial(faces_body, scale=scale), out_shape=(squ...  2.43 us
    unnamed x28, local copies, waits for them, and re-layouts  2.15 us
    dot_general x1, matrix products, shards(): jnp.einsum('qjr,rc->qjc', hit_values, coefficients, precision=exact)  1.78 us
  transfers between devices with their start and end apart: 7, of which 2 were waited for; matrix products, arithmetic and copies ran while one was open for 4% of the time, Pallas kernels for 12%

profile of v15, /device:TPU:0, one launch (start us, length us, event | category | flops | bytes accessed | tf_op | source)
XLA Modules:
  0.0 48.2 jit_solution(16248659160328757622)
XLA Ops:
  0.0 0.0 copy-start
  0.0 0.7 %and_select_fusion = s32[3]{0:T(128)S(1)} fusion(s32[3]{0:T(128)} %constant.73.clone, s32[]{:T(128)S(6)} %add.96), kind=kLoop, calls=%fused_computation.46 | loop fusion | flops 36 | bytes 28 | tf_op jit(solution)/shard_map/jit(remainder)/select_n | solution.py:408
  0.7 0.7 %compare_select_fusion.2 = (s32[64]{0:T(128)S(1)}, s32[64]{0:T(128)S(1)}, s32[64]{0:T(128)S(1)}) fusion(s32[]{:T(128)S(6)} %add.96, s32[64]{0:T(128)} %param.18), kind=kLoop, calls=%fused_computation.48 | loop fusion | flops 1344 | bytes 1028 | tf_op jit(solution)/shard_map/jit(_where)/select_n | solution.py:431
  1.4 0.1 fusion.34
  1.4 0.2 reduce_window_sum.11
  1.7 0.0 copy-done
  1.7 0.1 fusion.23
  1.8 0.8 %fusion.25 = f32[3,4,3]{2,1,0:T(4,128)S(1)} fusion(pred[3,4,64]{2,1,0:T(4,128)(4,1)S(1)} %fusion.19, f32[64,3]{0,1:T(4,128)} %param.15), kind=kOutput, calls=%fused_computation.44 | convolution fusion | flops 27648 | bytes 1680 | tf_op jit(solution)/shard_map/qjr,rc->qjc/dot_general | solution.py:423
  2.7 0.0 copy-start.8
  2.7 0.0 copy-start.9
  2.7 0.0 copy-start.7
  2.7 0.0 copy-start.2
  2.7 0.0 copy-start.13
  2.7 1.8 %fusion.4 = f32[3,4,4096]{2,1,0:T(4,128)S(1)} fusion(pred[3,4,64]{2,1,0:T(4,128)(4,1)S(1)} %fusion.19, f32[64,4096]{1,0:T(8,128)} %param.14), kind=kOutput, calls=%fused_computation.7 | convolution fusion | flops 37748736 | bytes 1245952 | tf_op jit(solution)/shard_map/qjr,rc->qjc/dot_general | solution.py:422
  4.5 0.0 copy-done.10
  4.5 0.1 fusion.27
  4.7 0.1 concatenate.22
  4.9 0.1 collective-permute-start
  4.9 3.4 %collective-permute-start.2 = (f32[4,4224]{1,0:T(4,128)S(1)}, f32[4,4224]{1,0:T(4,128)S(1)}, u32[]{:S(2)}, u32[]{:S(2)}) collective-permute-start(f32[4,4224]{1,0:T(4,128)S(1)} %get-tuple-element.25), channel_id=1, source_target_pairs={{0,64},{1,65},{2,66},{3,67},{4,68},{5,69},{6,70},{7,71},{8,72},{9,... | collective-permute-start | bytes 202760 | tf_op jit(solution)/shard_map/ppermute | solution.py:434
  8.3 6.2 %collective-permute-start.1 = (f32[4,4224]{1,0:T(4,128)S(1)}, f32[4,4224]{1,0:T(4,128)S(1)}, u32[]{:S(2)}, u32[]{:S(2)}) collective-permute-start(f32[4,4224]{1,0:T(4,128)S(1)} %get-tuple-element.26), channel_id=1, source_target_pairs={{0,127},{1,0},{2,1},{3,2},{4,3},{5,4},{6,5},{7,6},{8,7},{9,8},{10,... | collective-permute-start | bytes 202760 | tf_op jit(solution)/shard_map/ppermute | solution.py:434
  14.5 0.0 copy-done.6
  14.5 0.0 copy-done.8
  14.5 0.8 %fusion.6.refs_3_.pick_ref.refs_6_ = bf16[6,64,64]{2,1,0:T(8,128)(2,1)} fusion(s32[6,64]{1,0:T(8,128)S(1)} %pad_add_fusion), kind=kLoop, calls=%fused_computation.10 | loop fusion | flops 49152 | bytes 50688 | tf_op jit(solution)/shard_map/convert_element_type | solution.py:460
  15.3 0.0 copy-done.9
  15.3 0.7 %copy.36 = s32[2,64]{0,1:T(8,128)} copy(s32[2,64]{1,0:T(2,128)S(1)} %bitcast.36) | data formatting | bytes 1024 | tf_op jit(solution)/shard_map/squeeze | solution.py:461
  16.0 0.0 collective-permute-done
  16.0 0.2 fusion.22
  16.2 0.0 collective-permute-done.2
  16.2 0.2 fusion.20
  16.4 0.1 collective-permute-done.1
  16.4 0.2 fusion.21
  16.6 0.1 pad_add_fusion.1
  16.7 0.1 fusion.8
  16.8 0.2 fusion.10
  17.0 0.0 copy-done.7
  17.0 0.2 fusion.12
  17.1 0.1 pad_maximum_fusion.3
  17.2 0.1 copy.34
  17.3 0.2 convolution_add_fusion.refs_1_.weight_ref.refs_4_
  17.5 0.2 slice_reduce_fusion
  17.7 0.0 copy-done.2
  17.7 0.0 copy-done.13
  17.7 0.8 %convolution_select_fusion.refs_0_.refs_3_ = f32[64,4096]{1,0:T(8,128)S(1)} fusion(f32[4,4224]{1,0:T(4,128)S(1)} %collective-permute-done.2, f32[4,4224]{1,0:T(4,128)S(1)} %collective-permute-done.1, f32[4,4224]{1,0:T(4,128)S(1)} %collective-permute-done, f32[64,4096]{1,0:T(8,128)S(1)} %copy-done.2, f32[4096]{0:T(1024)S(1)} %copy-done.13, ...), kind=kOutput, calls=%fused_computation | convolution fusion | flops 240538368 | bytes 2316848 | tf_op jit(solution)/shard_map/dot_general | solution.py:443
  18.6 0.0 copy-done.3
  18.6 0.0 copy-start.1
  18.6 0.1 add_subtract_fusion
  18.7 0.1 add_add_fusion
  18.7 0.8 %copy-done.1 = f32[64,4096]{1,0:T(8,128)} copy-done((f32[64,4096]{1,0:T(8,128)}, f32[64,4096]{1,0:T(8,128)S(1)}, u32[]{:S(2)}) %copy-start.1) | copy-done | bytes 1048600
  19.6 0.0 collective-permute-start.3
  19.6 5.3 %collective-permute-start.4 = (f32[64,256]{1,0:T(8,128)S(1)}, f32[64,256]{1,0:T(8,128)S(1)}, u32[]{:S(2)}, u32[]{:S(2)}) collective-permute-start(f32[64,256]{1,0:T(8,128)S(1)} %add_subtract_fusion), channel_id=1, source_target_pairs={{8,0},{16,8},{24,16},{32,24},{40,32},{48,40},{56,48},{64,56},{72,6... | collective-permute-start | bytes 196616 | tf_op jit(solution)/shard_map/ppermute | solution.py:385
  24.9 5.5 %shard_map.136 = (f32[64,4096]{1,0:T(8,128)}, f32[64,256]{1,0:T(8,128)}, f32[64,256]{1,0:T(8,128)}) custom-call(f32[64,4096]{1,0:T(8,128)} %copy-done.1, f32[64,8]{1,0:T(8,128)} %copy-done.3, f32[1,4096]{1,0:T(1,128)} %constant.74.clone.refs_2_.top_ref.refs_5_, bf16[6,64,64]{2,1,0:T(8,128)(2,1)} %fusion.6.refs_3_.pick_ref.refs_6_, ...), custom_call_target="tpu_custom_call" | custom-call | flops 2500000000 | bytes 4000000 | tf_op jit(solution)/shard_map/pallas_call | solution.py:314
  30.4 0.0 collective-permute-done.3.lower_ref
  30.5 0.0 collective-permute-done.4.upper_ref
  30.5 0.0 copy-start.5
  30.5 0.6 %copy-done.4 = f32[64,256]{1,0:T(8,128)} copy-done((f32[64,256]{1,0:T(8,128)}, f32[64,256]{1,0:T(8,128)S(1)}, u32[]{:S(2)}) %copy-start.4) | copy-done | bytes 65560
  31.1 0.0 copy-done.5
  31.1 2.4 %shard_map.137 = (f32[64,256]{1,0:T(8,128)}, f32[64,256]{1,0:T(8,128)}, f32[64,256]{1,0:T(8,128)}, f32[64,256]{1,0:T(8,128)}) custom-call(f32[64,256]{1,0:T(8,128)} %copy-done.4, f32[64,256]{1,0:T(8,128)} %copy-done.5, bf16[6,64,64]{2,1,0:T(8,128)(2,1)} %fusion.6.refs_3_.pick_ref.refs_6_, s32[64,2]{1,0:T(8,128)} %bitcast.32, ...), custom_call_target="tpu_custom_call" | custom-call | tf_op jit(solution)/shard_map/pallas_call | solution.py:330
  33.5 0.0 collective-permute-start.5
  33.5 5.3 %collective-permute-start.6 = (f32[64,256]{1,0:T(8,128)}, f32[64,256]{1,0:T(8,128)S(1)}, u32[]{:S(2)}, u32[]{:S(2)}) collective-permute-start(f32[64,256]{1,0:T(8,128)} %get-tuple-element.18), channel_id=1, source_target_pairs={{8,0},{16,8},{24,16},{32,24},{40,32},{48,40},{56,48},{64,56},{72,6... | collective-permute-start | bytes 196616 | tf_op jit(solution)/shard_map/ppermute | solution.py:385
  38.9 2.4 %collective-permute-done.5.refs_10_ = f32[64,256]{1,0:T(8,128)S(1)} collective-permute-done((f32[64,256]{1,0:T(8,128)}, f32[64,256]{1,0:T(8,128)S(1)}, u32[]{:S(2)}, u32[]{:S(2)}) %collective-permute-start.5) | collective-permute-done | bytes 65568 | tf_op jit(solution)/shard_map/ppermute | solution.py:385
  41.3 0.0 collective-permute-done.6.refs_11_
  41.3 0.6 %copy-done.11 = f32[64,256]{1,0:T(8,128)} copy-done((f32[64,256]{1,0:T(8,128)}, f32[64,256]{1,0:T(8,128)S(1)}, u32[]{:S(2)}) %copy-start.11) | copy-done | bytes 65560
  42.0 0.0 copy-done.12
  42.0 6.2 %shard_map.138 = f32[64,4096]{1,0:T(8,128)} custom-call(f32[64,4096]{1,0:T(8,128)} %get-tuple-element.12.refs_0_, f32[64,256]{1,0:T(8,128)} %get-tuple-element.15.refs_1_, f32[64,256]{1,0:T(8,128)} %get-tuple-element.16.refs_2_, f32[64,4096]{1,0:T(8,128)} %copy-done.1, f32[64,8]{1,0:T(8,128)} %copy-done.3, f32[1,4096]{1,0:T(1,128)} %constant.74.clone.refs_2_.top_ref.refs_5_, ...), custom_call_target="tpu_custom_call" | custom-call | flops 2500000000 | bytes 4000000 | tf_op jit(solution)/shard_map/pallas_call | solution.py:314
  (13 shorter events, 0.1 us)
Async XLA Ops:
  0.0 1.7 %copy-start = (f32[64,3]{0,1:T(4,128)S(1)}, f32[64,3]{0,1:T(4,128)}, u32[]{:S(2)}) copy-start(f32[64,3]{0,1:T(4,128)} %param.16) | copy-start | bytes 2308
  0.0 4.5 %copy-start.10 = (s32[64]{0:T(128)S(1)}, s32[64]{0:T(128)}, u32[]{:S(2)}) copy-start(s32[64]{0:T(128)} %param.17) | copy-start | bytes 772
  2.7 11.8 %copy-start.6 = (s32[1,4,64]{2,1,0:T(4,128)S(1)}, s32[1,4,64]{2,1,0:T(4,128)}, u32[]{:S(2)}) copy-start(s32[1,4,64]{2,1,0:T(4,128)} %param.19) | copy-start | bytes 3076
  2.7 11.8 %copy-start.8 = (s32[1,2,64]{2,1,0:T(2,128)S(1)}, s32[1,2,64]{2,1,0:T(2,128)}, u32[]{:S(2)}) copy-start(s32[1,2,64]{2,1,0:T(2,128)} %param.20) | copy-start | bytes 1540
  2.7 12.6 %copy-start.9 = (s32[1,2,64]{2,1,0:T(2,128)S(1)}, s32[1,2,64]{2,1,0:T(2,128)}, u32[]{:S(2)}) copy-start(s32[1,2,64]{2,1,0:T(2,128)} %param.21) | copy-start | bytes 1540
  2.7 14.3 %copy-start.7 = (f32[64,3]{0,1:T(4,128)S(1)}, f32[64,3]{0,1:T(4,128)}, u32[]{:S(2)}) copy-start(f32[64,3]{0,1:T(4,128)} %param.15) | copy-start | bytes 2308
  2.7 15.0 %copy-start.2 = (f32[64,4096]{1,0:T(8,128)S(1)}, f32[64,4096]{1,0:T(8,128)}, u32[]{:S(2)}) copy-start(f32[64,4096]{1,0:T(8,128)} %param.14) | copy-start | bytes 3145732
  2.7 15.0 %copy-start.13 = (f32[4096]{0:T(1024)S(1)}, f32[4096]{0:T(1024)}, u32[]{:S(2)}) copy-start(f32[4096]{0:T(1024)} %constant.87) | copy-start | bytes 49156
  4.9 11.1 %collective-permute-start = (f32[4,4224]{1,0:T(4,128)S(1)}, f32[4,4224]{1,0:T(4,128)S(1)}, u32[]{:S(2)}, u32[]{:S(2)}) collective-permute-start(f32[4,4224]{1,0:T(4,128)S(1)} %get-tuple-element.24), channel_id=1, source_target_pairs={{0,1},{1,2},{2,3},{3,4},{4,5},{5,6},{6,7},{7,8},{8,9},{9,10},{10,1... | collective-permute-start | bytes 202760 | tf_op jit(solution)/shard_map/ppermute | solution.py:434
  4.9 11.2 %collective-permute-start.2 = (f32[4,4224]{1,0:T(4,128)S(1)}, f32[4,4224]{1,0:T(4,128)S(1)}, u32[]{:S(2)}, u32[]{:S(2)}) collective-permute-start(f32[4,4224]{1,0:T(4,128)S(1)} %get-tuple-element.25), channel_id=1, source_target_pairs={{0,64},{1,65},{2,66},{3,67},{4,68},{5,69},{6,70},{7,71},{8,72},{9,... | collective-permute-start | bytes 202760 | tf_op jit(solution)/shard_map/ppermute | solution.py:434
  8.3 8.1 %collective-permute-start.1 = (f32[4,4224]{1,0:T(4,128)S(1)}, f32[4,4224]{1,0:T(4,128)S(1)}, u32[]{:S(2)}, u32[]{:S(2)}) collective-permute-start(f32[4,4224]{1,0:T(4,128)S(1)} %get-tuple-element.26), channel_id=1, source_target_pairs={{0,127},{1,0},{2,1},{3,2},{4,3},{5,4},{6,5},{7,6},{8,7},{9,8},{10,... | collective-permute-start | bytes 202760 | tf_op jit(solution)/shard_map/ppermute | solution.py:434
  17.5 1.1 %copy-start.3 = (f32[64,8]{1,0:T(8,128)}, f32[64,8]{1,0:T(8,128)S(1)}, u32[]{:S(2)}) copy-start(f32[64,8]{1,0:T(8,128)S(1)} %convolution_add_fusion.refs_1_.weight_ref.refs_4_) | copy-start | bytes 6148
  18.6 1.0 %copy-start.1 = (f32[64,4096]{1,0:T(8,128)}, f32[64,4096]{1,0:T(8,128)S(1)}, u32[]{:S(2)}) copy-start(f32[64,4096]{1,0:T(8,128)S(1)} %convolution_select_fusion.refs_0_.refs_3_) | copy-start | bytes 3145732
  19.6 10.9 %collective-permute-start.3 = (f32[64,256]{1,0:T(8,128)S(1)}, f32[64,256]{1,0:T(8,128)S(1)}, u32[]{:S(2)}, u32[]{:S(2)}) collective-permute-start(f32[64,256]{1,0:T(8,128)S(1)} %add_add_fusion), channel_id=1, source_target_pairs={{0,8},{8,16},{16,24},{24,32},{32,40},{40,48},{48,56},{56,64},{64,7... | collective-permute-start | bytes 196616 | tf_op jit(solution)/shard_map/ppermute | solution.py:385
  19.6 10.9 %collective-permute-start.4 = (f32[64,256]{1,0:T(8,128)S(1)}, f32[64,256]{1,0:T(8,128)S(1)}, u32[]{:S(2)}, u32[]{:S(2)}) collective-permute-start(f32[64,256]{1,0:T(8,128)S(1)} %add_subtract_fusion), channel_id=1, source_target_pairs={{8,0},{16,8},{24,16},{32,24},{40,32},{48,40},{56,48},{64,56},{72,6... | collective-permute-start | bytes 196616 | tf_op jit(solution)/shard_map/ppermute | solution.py:385
  30.4 0.6 %copy-start.4 = (f32[64,256]{1,0:T(8,128)}, f32[64,256]{1,0:T(8,128)S(1)}, u32[]{:S(2)}) copy-start(f32[64,256]{1,0:T(8,128)S(1)} %collective-permute-done.3.lower_ref) | copy-start | bytes 196612
  30.5 0.6 %copy-start.5 = (f32[64,256]{1,0:T(8,128)}, f32[64,256]{1,0:T(8,128)S(1)}, u32[]{:S(2)}) copy-start(f32[64,256]{1,0:T(8,128)S(1)} %collective-permute-done.4.upper_ref) | copy-start | bytes 196612
  33.5 7.8 %collective-permute-start.5 = (f32[64,256]{1,0:T(8,128)}, f32[64,256]{1,0:T(8,128)S(1)}, u32[]{:S(2)}, u32[]{:S(2)}) collective-permute-start(f32[64,256]{1,0:T(8,128)} %get-tuple-element.17), channel_id=1, source_target_pairs={{0,8},{8,16},{16,24},{24,32},{32,40},{40,48},{48,56},{56,64},{64,7... | collective-permute-start | bytes 196616 | tf_op jit(solution)/shard_map/ppermute | solution.py:385
  33.5 7.8 %collective-permute-start.6 = (f32[64,256]{1,0:T(8,128)}, f32[64,256]{1,0:T(8,128)S(1)}, u32[]{:S(2)}, u32[]{:S(2)}) collective-permute-start(f32[64,256]{1,0:T(8,128)} %get-tuple-element.18), channel_id=1, source_target_pairs={{8,0},{16,8},{24,16},{32,24},{40,32},{48,40},{56,48},{64,56},{72,6... | collective-permute-start | bytes 196616 | tf_op jit(solution)/shard_map/ppermute | solution.py:385
  41.3 0.6 %copy-start.11 = (f32[64,256]{1,0:T(8,128)}, f32[64,256]{1,0:T(8,128)S(1)}, u32[]{:S(2)}) copy-start(f32[64,256]{1,0:T(8,128)S(1)} %collective-permute-done.5.refs_10_) | copy-start | bytes 196612
  41.3 0.6 %copy-start.12 = (f32[64,256]{1,0:T(8,128)}, f32[64,256]{1,0:T(8,128)S(1)}, u32[]{:S(2)}) copy-start(f32[64,256]{1,0:T(8,128)S(1)} %collective-permute-done.6.refs_11_) | copy-start | bytes 196612

commit v16 on v15

--- a/solution.py
+++ b/solution.py
@@ -407,9 +407,11 @@
     shifts = (1, blocks_all - 1, blocks_all // 2)
     goal = (here + jnp.asarray(shifts, jnp.int32)) % blocks_all
     chosen = destination[None, :] == goal[:, None]
-    rank = jnp.cumsum(chosen.astype(jnp.int32), axis=1) - 1
+    ladder = np.arange(element_count)
+    before = jnp.asarray((ladder[:, None] < ladder[None, :]).astype(np.float32))
+    rank = jnp.dot(chosen.astype(jnp.float32), before, precision=lax.Precision.HIGHEST)
     hit = chosen[:, None, :] & (
-        rank[:, None, :] == jnp.arange(moving, dtype=jnp.int32)[None, :, None]
+        rank[:, None, :] == jnp.arange(moving, dtype=jnp.float32)[None, :, None]
     )
     width = P_SIZE**3
     exact = lax.Precision.HIGHEST

time: 48.5 us -> 49.2 us (1.014)
  matrix products: 4.38 us -> 5.26 us
    dot_general x0 -> x1, matrix products: none -> 0.88 us  [shards(): jnp.dot(chosen.astype(jnp.float32), before, precision=lax.Precision.HIGHEST)]
  transfers between devices with their start and end apart: 7 -> 7, of which waited for: 2 -> 2; matrix products, arithmetic and copies ran while one was open for 4% -> 4% of each run, Pallas kernels for 12% -> 11%
where the time goes in v16:
time: 49.2 us; the launch traced here: 48.9 us
  starting transfers between devices  20.3 us (41%)
  Pallas kernels  14.2 us (29%)
  matrix products  5.26 us (11%)
  local copies, waits for them, and re-layouts  3.28 us (7%)
  other arithmetic  3.05 us (6%)
  waiting for transfers between devices  2.54 us (5%)
    pallas_call x2, Pallas kernels, inner(): pl.pallas_call(functools.partial(inner_body, scale=scale, carried=carried...  11.8 us
    ppermute x4, starting transfers between devices, exchange(): return (lax.ppermute(total, 'dom', up), lax.ppermute(even, 'dom', down))  10.7 us
    ppermute x3, starting transfers between devices, shards(): arrived = lax.ppermute(parcels[index], ('dom', 'face'), pairs)  9.63 us
    ppermute x4, waiting for transfers between devices, exchange(): return (lax.ppermute(total, 'dom', up), lax.ppermute(even, 'dom', down))  2.46 us
    pallas_call x1, Pallas kernels, faces(): pl.pallas_call(functools.partial(faces_body, scale=scale), out_shape=(squ...  2.42 us
    unnamed x28, local copies, waits for them, and re-layouts  2.16 us
    dot_general x1, matrix products, shards(): jnp.einsum('qjr,rc->qjc', hit_values, coefficients, precision=exact)  1.78 us
  transfers between devices with their start and end apart: 7, of which 2 were waited for; matrix products, arithmetic and copies ran while one was open for 4% of the time, Pallas kernels for 11%

profile of v16, /device:TPU:0, one launch (start us, length us, event | category | flops | bytes accessed | tf_op | source)
XLA Modules:
  0.0 48.9 jit_solution(16844773940352506872)
XLA Ops:
  0.0 0.0 copy-start
  0.0 0.7 %and_select_fusion = s32[3]{0:T(128)S(1)} fusion(s32[3]{0:T(128)} %constant.70.clone, s32[]{:T(128)S(6)} %add.91), kind=kLoop, calls=%fused_computation.46 | loop fusion | flops 36 | bytes 28 | tf_op jit(solution)/shard_map/jit(remainder)/select_n | solution.py:408
  0.7 0.7 %compare_select_fusion.2 = (s32[64]{0:T(128)S(1)}, s32[64]{0:T(128)S(1)}, s32[64]{0:T(128)S(1)}) fusion(s32[]{:T(128)S(6)} %add.91, s32[64]{0:T(128)} %param.19), kind=kLoop, calls=%fused_computation.48 | loop fusion | flops 1344 | bytes 1028 | tf_op jit(solution)/shard_map/jit(_where)/select_n | solution.py:433
  1.4 0.1 broadcast_compare_fusion
  1.4 0.9 %fusion.34 = f32[3,64]{1,0:T(4,128)S(1)} fusion(pred[3,64]{1,0:T(4,128)(4,1)S(1)} %broadcast_compare_fusion, f32[64,64]{1,0:T(8,128)} %constant.71.clone), kind=kOutput, calls=%fused_computation.65 | convolution fusion | flops 147456 | bytes 17344 | tf_op jit(solution)/shard_map/dot_general | solution.py:412
  2.3 0.0 copy-done
  2.4 0.1 fusion.23
  2.5 0.8 %fusion.25 = f32[3,4,3]{2,1,0:T(4,128)S(1)} fusion(pred[3,4,64]{2,1,0:T(4,128)(4,1)S(1)} %fusion.19, f32[64,3]{0,1:T(4,128)} %param.16), kind=kOutput, calls=%fused_computation.44 | convolution fusion | flops 27648 | bytes 1680 | tf_op jit(solution)/shard_map/qjr,rc->qjc/dot_general | solution.py:425
  3.3 0.0 copy-start.8
  3.3 0.0 copy-start.9
  3.4 0.0 copy-start.7
  3.4 0.0 copy-start.2
  3.4 0.0 copy-start.13
  3.4 1.8 %fusion.4 = f32[3,4,4096]{2,1,0:T(4,128)S(1)} fusion(pred[3,4,64]{2,1,0:T(4,128)(4,1)S(1)} %fusion.19, f32[64,4096]{1,0:T(8,128)} %param.15), kind=kOutput, calls=%fused_computation.7 | convolution fusion | flops 37748736 | bytes 1245952 | tf_op jit(solution)/shard_map/qjr,rc->qjc/dot_general | solution.py:424
  5.2 0.0 copy-done.10
  5.2 0.1 fusion.27
  5.3 0.1 concatenate.22
  5.5 0.1 collective-permute-start
  5.6 3.4 %collective-permute-start.2 = (f32[4,4224]{1,0:T(4,128)S(1)}, f32[4,4224]{1,0:T(4,128)S(1)}, u32[]{:S(2)}, u32[]{:S(2)}) collective-permute-start(f32[4,4224]{1,0:T(4,128)S(1)} %get-tuple-element.23), channel_id=1, source_target_pairs={{0,64},{1,65},{2,66},{3,67},{4,68},{5,69},{6,70},{7,71},{8,72},{9,... | collective-permute-start | bytes 202760 | tf_op jit(solution)/shard_map/ppermute | solution.py:436
  9.0 6.2 %collective-permute-start.1 = (f32[4,4224]{1,0:T(4,128)S(1)}, f32[4,4224]{1,0:T(4,128)S(1)}, u32[]{:S(2)}, u32[]{:S(2)}) collective-permute-start(f32[4,4224]{1,0:T(4,128)S(1)} %get-tuple-element.24), channel_id=1, source_target_pairs={{0,127},{1,0},{2,1},{3,2},{4,3},{5,4},{6,5},{7,6},{8,7},{9,8},{10,... | collective-permute-start | bytes 202760 | tf_op jit(solution)/shard_map/ppermute | solution.py:436
  15.2 0.0 copy-done.6
  15.2 0.0 copy-done.8
  15.2 0.8 %fusion.6.refs_3_.pick_ref.refs_6_ = bf16[6,64,64]{2,1,0:T(8,128)(2,1)} fusion(s32[6,64]{1,0:T(8,128)S(1)} %pad_add_fusion), kind=kLoop, calls=%fused_computation.10 | loop fusion | flops 49152 | bytes 50688 | tf_op jit(solution)/shard_map/convert_element_type | solution.py:462
  15.9 0.0 copy-done.9
  15.9 0.7 %copy.37 = s32[2,64]{0,1:T(8,128)} copy(s32[2,64]{1,0:T(2,128)S(1)} %bitcast.38) | data formatting | bytes 1024 | tf_op jit(solution)/shard_map/squeeze | solution.py:463
  16.6 0.0 collective-permute-done
  16.6 0.2 fusion.22
  16.8 0.0 collective-permute-done.2
  16.8 0.2 fusion.20
  17.0 0.1 collective-permute-done.1
  17.1 0.2 fusion.21
  17.3 0.1 pad_add_fusion.1
  17.4 0.1 fusion.8
  17.5 0.2 fusion.10
  17.6 0.0 copy-done.7
  17.6 0.2 fusion.12
  17.8 0.1 pad_maximum_fusion.3
  17.9 0.1 copy.35
  17.9 0.2 convolution_add_fusion.refs_1_.weight_ref.refs_4_
  18.2 0.0 copy-start.3
  18.2 0.2 slice_reduce_fusion
  18.3 0.0 copy-done.2
  18.4 0.0 copy-done.13
  18.4 0.8 %convolution_select_fusion.refs_0_.refs_3_ = f32[64,4096]{1,0:T(8,128)S(1)} fusion(f32[4,4224]{1,0:T(4,128)S(1)} %collective-permute-done.2, f32[4,4224]{1,0:T(4,128)S(1)} %collective-permute-done.1, f32[4,4224]{1,0:T(4,128)S(1)} %collective-permute-done, f32[64,4096]{1,0:T(8,128)S(1)} %copy-done.2, f32[4096]{0:T(1024)S(1)} %copy-done.13, ...), kind=kOutput, calls=%fused_computation | convolution fusion | flops 240538368 | bytes 2316848 | tf_op jit(solution)/shard_map/dot_general | solution.py:445
  19.2 0.0 copy-done.3
  19.2 0.1 add_subtract_fusion
  19.3 0.1 add_add_fusion
  19.4 0.8 %copy-done.1 = f32[64,4096]{1,0:T(8,128)} copy-done((f32[64,4096]{1,0:T(8,128)}, f32[64,4096]{1,0:T(8,128)S(1)}, u32[]{:S(2)}) %copy-start.1) | copy-done | bytes 1048600
  20.2 0.0 collective-permute-start.3
  20.2 5.3 %collective-permute-start.4 = (f32[64,256]{1,0:T(8,128)S(1)}, f32[64,256]{1,0:T(8,128)S(1)}, u32[]{:S(2)}, u32[]{:S(2)}) collective-permute-start(f32[64,256]{1,0:T(8,128)S(1)} %add_subtract_fusion), channel_id=1, source_target_pairs={{8,0},{16,8},{24,16},{32,24},{40,32},{48,40},{56,48},{64,56},{72,6... | collective-permute-start | bytes 196616 | tf_op jit(solution)/shard_map/ppermute | solution.py:385
  25.6 5.5 %shard_map.145 = (f32[64,4096]{1,0:T(8,128)}, f32[64,256]{1,0:T(8,128)}, f32[64,256]{1,0:T(8,128)}) custom-call(f32[64,4096]{1,0:T(8,128)} %copy-done.1, f32[64,8]{1,0:T(8,128)} %copy-done.3, f32[1,4096]{1,0:T(1,128)} %constant.72.clone.refs_2_.top_ref.refs_5_, bf16[6,64,64]{2,1,0:T(8,128)(2,1)} %fusion.6.refs_3_.pick_ref.refs_6_, ...), custom_call_target="tpu_custom_call" | custom-call | flops 2500000000 | bytes 4000000 | tf_op jit(solution)/shard_map/pallas_call | solution.py:314
  31.1 0.0 collective-permute-done.3.lower_ref
  31.1 0.0 collective-permute-done.4.upper_ref
  31.1 0.0 copy-start.5
  31.1 0.6 %copy-done.4 = f32[64,256]{1,0:T(8,128)} copy-done((f32[64,256]{1,0:T(8,128)}, f32[64,256]{1,0:T(8,128)S(1)}, u32[]{:S(2)}) %copy-start.4) | copy-done | bytes 65560
  31.7 0.0 copy-done.5
  31.8 2.4 %shard_map.146 = (f32[64,256]{1,0:T(8,128)}, f32[64,256]{1,0:T(8,128)}, f32[64,256]{1,0:T(8,128)}, f32[64,256]{1,0:T(8,128)}) custom-call(f32[64,256]{1,0:T(8,128)} %copy-done.4, f32[64,256]{1,0:T(8,128)} %copy-done.5, bf16[6,64,64]{2,1,0:T(8,128)(2,1)} %fusion.6.refs_3_.pick_ref.refs_6_, s32[64,2]{1,0:T(8,128)} %bitcast.34, ...), custom_call_target="tpu_custom_call" | custom-call | tf_op jit(solution)/shard_map/pallas_call | solution.py:330
  34.2 0.0 collective-permute-start.5
  34.2 5.3 %collective-permute-start.6 = (f32[64,256]{1,0:T(8,128)}, f32[64,256]{1,0:T(8,128)S(1)}, u32[]{:S(2)}, u32[]{:S(2)}) collective-permute-start(f32[64,256]{1,0:T(8,128)} %get-tuple-element.18), channel_id=1, source_target_pairs={{8,0},{16,8},{24,16},{32,24},{40,32},{48,40},{56,48},{64,56},{72,6... | collective-permute-start | bytes 196616 | tf_op jit(solution)/shard_map/ppermute | solution.py:385
  39.5 2.4 %collective-permute-done.5.refs_10_ = f32[64,256]{1,0:T(8,128)S(1)} collective-permute-done((f32[64,256]{1,0:T(8,128)}, f32[64,256]{1,0:T(8,128)S(1)}, u32[]{:S(2)}, u32[]{:S(2)}) %collective-permute-start.5) | collective-permute-done | bytes 65568 | tf_op jit(solution)/shard_map/ppermute | solution.py:385
  42.0 0.0 collective-permute-done.6.refs_11_
  42.0 0.6 %copy-done.11 = f32[64,256]{1,0:T(8,128)} copy-done((f32[64,256]{1,0:T(8,128)}, f32[64,256]{1,0:T(8,128)S(1)}, u32[]{:S(2)}) %copy-start.11) | copy-done | bytes 65560
  42.6 0.0 copy-done.12
  42.6 6.2 %shard_map.147 = f32[64,4096]{1,0:T(8,128)} custom-call(f32[64,4096]{1,0:T(8,128)} %get-tuple-element.12.refs_0_, f32[64,256]{1,0:T(8,128)} %get-tuple-element.15.refs_1_, f32[64,256]{1,0:T(8,128)} %get-tuple-element.16.refs_2_, f32[64,4096]{1,0:T(8,128)} %copy-done.1, f32[64,8]{1,0:T(8,128)} %copy-done.3, f32[1,4096]{1,0:T(1,128)} %constant.72.clone.refs_2_.top_ref.refs_5_, ...), custom_call_target="tpu_custom_call" | custom-call | flops 2500000000 | bytes 4000000 | tf_op jit(solution)/shard_map/pallas_call | solution.py:314
  (12 shorter events, 0.1 us)
Async XLA Ops:
  0.0 2.3 %copy-start = (f32[64,3]{0,1:T(4,128)S(1)}, f32[64,3]{0,1:T(4,128)}, u32[]{:S(2)}) copy-start(f32[64,3]{0,1:T(4,128)} %param.17) | copy-start | bytes 2308
  0.0 5.2 %copy-start.10 = (s32[64]{0:T(128)S(1)}, s32[64]{0:T(128)}, u32[]{:S(2)}) copy-start(s32[64]{0:T(128)} %param.18) | copy-start | bytes 772
  3.3 11.8 %copy-start.6 = (s32[1,4,64]{2,1,0:T(4,128)S(1)}, s32[1,4,64]{2,1,0:T(4,128)}, u32[]{:S(2)}) copy-start(s32[1,4,64]{2,1,0:T(4,128)} %param.20) | copy-start | bytes 3076
  3.3 11.8 %copy-start.8 = (s32[1,2,64]{2,1,0:T(2,128)S(1)}, s32[1,2,64]{2,1,0:T(2,128)}, u32[]{:S(2)}) copy-start(s32[1,2,64]{2,1,0:T(2,128)} %param.21) | copy-start | bytes 1540
  3.3 12.6 %copy-start.9 = (s32[1,2,64]{2,1,0:T(2,128)S(1)}, s32[1,2,64]{2,1,0:T(2,128)}, u32[]{:S(2)}) copy-start(s32[1,2,64]{2,1,0:T(2,128)} %param.22) | copy-start | bytes 1540
  3.4 14.3 %copy-start.7 = (f32[64,3]{0,1:T(4,128)S(1)}, f32[64,3]{0,1:T(4,128)}, u32[]{:S(2)}) copy-start(f32[64,3]{0,1:T(4,128)} %param.16) | copy-start | bytes 2308
  3.4 15.0 %copy-start.2 = (f32[64,4096]{1,0:T(8,128)S(1)}, f32[64,4096]{1,0:T(8,128)}, u32[]{:S(2)}) copy-start(f32[64,4096]{1,0:T(8,128)} %param.15) | copy-start | bytes 3145732
  3.4 15.0 %copy-start.13 = (f32[4096]{0:T(1024)S(1)}, f32[4096]{0:T(1024)}, u32[]{:S(2)}) copy-start(f32[4096]{0:T(1024)} %constant.85) | copy-start | bytes 49156
  5.5 11.1 %collective-permute-start = (f32[4,4224]{1,0:T(4,128)S(1)}, f32[4,4224]{1,0:T(4,128)S(1)}, u32[]{:S(2)}, u32[]{:S(2)}) collective-permute-start(f32[4,4224]{1,0:T(4,128)S(1)} %get-tuple-element.22), channel_id=1, source_target_pairs={{0,1},{1,2},{2,3},{3,4},{4,5},{5,6},{6,7},{7,8},{8,9},{9,10},{10,1... | collective-permute-start | bytes 202760 | tf_op jit(solution)/shard_map/ppermute | solution.py:436
  5.6 11.2 %collective-permute-start.2 = (f32[4,4224]{1,0:T(4,128)S(1)}, f32[4,4224]{1,0:T(4,128)S(1)}, u32[]{:S(2)}, u32[]{:S(2)}) collective-permute-start(f32[4,4224]{1,0:T(4,128)S(1)} %get-tuple-element.23), channel_id=1, source_target_pairs={{0,64},{1,65},{2,66},{3,67},{4,68},{5,69},{6,70},{7,71},{8,72},{9,... | collective-permute-start | bytes 202760 | tf_op jit(solution)/shard_map/ppermute | solution.py:436
  9.0 8.1 %collective-permute-start.1 = (f32[4,4224]{1,0:T(4,128)S(1)}, f32[4,4224]{1,0:T(4,128)S(1)}, u32[]{:S(2)}, u32[]{:S(2)}) collective-permute-start(f32[4,4224]{1,0:T(4,128)S(1)} %get-tuple-element.24), channel_id=1, source_target_pairs={{0,127},{1,0},{2,1},{3,2},{4,3},{5,4},{6,5},{7,6},{8,7},{9,8},{10,... | collective-permute-start | bytes 202760 | tf_op jit(solution)/shard_map/ppermute | solution.py:436
  18.2 1.1 %copy-start.3 = (f32[64,8]{1,0:T(8,128)}, f32[64,8]{1,0:T(8,128)S(1)}, u32[]{:S(2)}) copy-start(f32[64,8]{1,0:T(8,128)S(1)} %convolution_add_fusion.refs_1_.weight_ref.refs_4_) | copy-start | bytes 6148
  19.2 1.0 %copy-start.1 = (f32[64,4096]{1,0:T(8,128)}, f32[64,4096]{1,0:T(8,128)S(1)}, u32[]{:S(2)}) copy-start(f32[64,4096]{1,0:T(8,128)S(1)} %convolution_select_fusion.refs_0_.refs_3_) | copy-start | bytes 3145732
  20.2 10.9 %collective-permute-start.3 = (f32[64,256]{1,0:T(8,128)S(1)}, f32[64,256]{1,0:T(8,128)S(1)}, u32[]{:S(2)}, u32[]{:S(2)}) collective-permute-start(f32[64,256]{1,0:T(8,128)S(1)} %add_add_fusion), channel_id=1, source_target_pairs={{0,8},{8,16},{16,24},{24,32},{32,40},{40,48},{48,56},{56,64},{64,7... | collective-permute-start | bytes 196616 | tf_op jit(solution)/shard_map/ppermute | solution.py:385
  20.2 10.9 %collective-permute-start.4 = (f32[64,256]{1,0:T(8,128)S(1)}, f32[64,256]{1,0:T(8,128)S(1)}, u32[]{:S(2)}, u32[]{:S(2)}) collective-permute-start(f32[64,256]{1,0:T(8,128)S(1)} %add_subtract_fusion), channel_id=1, source_target_pairs={{8,0},{16,8},{24,16},{32,24},{40,32},{48,40},{56,48},{64,56},{72,6... | collective-permute-start | bytes 196616 | tf_op jit(solution)/shard_map/ppermute | solution.py:385
  31.1 0.6 %copy-start.4 = (f32[64,256]{1,0:T(8,128)}, f32[64,256]{1,0:T(8,128)S(1)}, u32[]{:S(2)}) copy-start(f32[64,256]{1,0:T(8,128)S(1)} %collective-permute-done.3.lower_ref) | copy-start | bytes 196612
  31.1 0.6 %copy-start.5 = (f32[64,256]{1,0:T(8,128)}, f32[64,256]{1,0:T(8,128)S(1)}, u32[]{:S(2)}) copy-start(f32[64,256]{1,0:T(8,128)S(1)} %collective-permute-done.4.upper_ref) | copy-start | bytes 196612
  34.2 7.8 %collective-permute-start.5 = (f32[64,256]{1,0:T(8,128)}, f32[64,256]{1,0:T(8,128)S(1)}, u32[]{:S(2)}, u32[]{:S(2)}) collective-permute-start(f32[64,256]{1,0:T(8,128)} %get-tuple-element.17), channel_id=1, source_target_pairs={{0,8},{8,16},{16,24},{24,32},{32,40},{40,48},{48,56},{56,64},{64,7... | collective-permute-start | bytes 196616 | tf_op jit(solution)/shard_map/ppermute | solution.py:385
  34.2 7.8 %collective-permute-start.6 = (f32[64,256]{1,0:T(8,128)}, f32[64,256]{1,0:T(8,128)S(1)}, u32[]{:S(2)}, u32[]{:S(2)}) collective-permute-start(f32[64,256]{1,0:T(8,128)} %get-tuple-element.18), channel_id=1, source_target_pairs={{8,0},{16,8},{24,16},{32,24},{40,32},{48,40},{56,48},{64,56},{72,6... | collective-permute-start | bytes 196616 | tf_op jit(solution)/shard_map/ppermute | solution.py:385
  42.0 0.6 %copy-start.11 = (f32[64,256]{1,0:T(8,128)}, f32[64,256]{1,0:T(8,128)S(1)}, u32[]{:S(2)}) copy-start(f32[64,256]{1,0:T(8,128)S(1)} %collective-permute-done.5.refs_10_) | copy-start | bytes 196612
  42.0 0.6 %copy-start.12 = (f32[64,256]{1,0:T(8,128)}, f32[64,256]{1,0:T(8,128)S(1)}, u32[]{:S(2)}) copy-start(f32[64,256]{1,0:T(8,128)S(1)} %collective-permute-done.6.refs_11_) | copy-start | bytes 196612

commit v17 on v15

--- a/solution.py
+++ b/solution.py
@@ -405,8 +405,8 @@
     )
     side_width = side_info.shape[1]
     shifts = (1, blocks_all - 1, blocks_all // 2)
-    goal = (here + jnp.asarray(shifts, jnp.int32)) % blocks_all
-    chosen = destination[None, :] == goal[:, None]
+    offset = (destination - here + blocks_all) % blocks_all
+    chosen = offset[None, :] == jnp.asarray(shifts, jnp.int32)[:, None]
     rank = jnp.cumsum(chosen.astype(jnp.int32), axis=1) - 1
     hit = chosen[:, None, :] & (
         rank[:, None, :] == jnp.arange(moving, dtype=jnp.int32)[None, :, None]

time: 48.5 us -> 48.5 us (level)
    eq x0 -> x1, other arithmetic: none -> 0.73 us  [shards(): chosen = offset[None, :] == jnp.asarray(shifts, jnp.int32)[:, None]]
    select_n x1, other arithmetic: 0.69 us -> 0.01 us  [shards(): offset = (destination - here + blocks_all) % blocks_all]
where the time goes in v17:
time: 48.5 us; the launch traced here: 48.2 us
  starting transfers between devices  20.3 us (42%)
  Pallas kernels  14.2 us (29%)
  matrix products  4.38 us (9%)
  other arithmetic  3.3 us (7%)
  local copies, waits for them, and re-layouts  3.28 us (7%)
  waiting for transfers between devices  2.53 us (5%)
    pallas_call x2, Pallas kernels, inner(): pl.pallas_call(functools.partial(inner_body, scale=scale, carried=carried...  11.8 us
    ppermute x4, starting transfers between devices, exchange(): return (lax.ppermute(total, 'dom', up), lax.ppermute(even, 'dom', down))  10.7 us
    ppermute x3, starting transfers between devices, shards(): arrived = lax.ppermute(parcels[index], ('dom', 'face'), pairs)  9.63 us
    ppermute x4, waiting for transfers between devices, exchange(): return (lax.ppermute(total, 'dom', up), lax.ppermute(even, 'dom', down))  2.46 us
    pallas_call x1, Pallas kernels, faces(): pl.pallas_call(functools.partial(faces_body, scale=scale), out_shape=(squ...  2.43 us
    unnamed x28, local copies, waits for them, and re-layouts  2.15 us
    dot_general x1, matrix products, shards(): jnp.einsum('qjr,rc->qjc', hit_values, coefficients, precision=exact)  1.78 us
  transfers between devices with their start and end apart: 7, of which 2 were waited for; matrix products, arithmetic and copies ran while one was open for 4% of the time, Pallas kernels for 12%

profile of v17, /device:TPU:0, one launch (start us, length us, event | category | flops | bytes accessed | tf_op | source)
XLA Modules:
  0.0 48.2 jit_solution(7663769882662068711)
XLA Ops:
  0.0 0.0 copy-start
  0.0 0.7 %compare_select_fusion.2 = (s32[64]{0:T(128)S(1)}, s32[64]{0:T(128)S(1)}, s32[64]{0:T(128)S(1)}) fusion(s32[]{:T(128)S(6)} %add.94, s32[64]{0:T(128)} %param.18), kind=kLoop, calls=%fused_computation.48 | loop fusion | flops 1344 | bytes 1028 | tf_op jit(solution)/shard_map/jit(_where)/select_n | solution.py:431
  0.7 0.7 %broadcast_compare_fusion = (pred[3,64]{1,0:T(4,128)(4,1)S(1)}, s32[3,64]{1,0:T(4,128)S(1)}) fusion(s32[64]{0:T(128)S(1)} %and_select_fusion, s32[3]{0:T(128)} %constant.71.clone), kind=kLoop, calls=%fused_computation.57 | loop fusion | flops 384 | bytes 1228 | tf_op jit(solution)/shard_map/eq | solution.py:409
  1.4 0.2 reduce_window_sum.11
  1.7 0.0 copy-done
  1.7 0.1 fusion.23
  1.8 0.8 %fusion.25 = f32[3,4,3]{2,1,0:T(4,128)S(1)} fusion(pred[3,4,64]{2,1,0:T(4,128)(4,1)S(1)} %fusion.19, f32[64,3]{0,1:T(4,128)} %param.15), kind=kOutput, calls=%fused_computation.44 | convolution fusion | flops 27648 | bytes 1680 | tf_op jit(solution)/shard_map/qjr,rc->qjc/dot_general | solution.py:423
  2.7 0.0 copy-start.8
  2.7 0.0 copy-start.9
  2.7 0.0 copy-start.7
  2.7 0.0 copy-start.2
  2.7 0.0 copy-start.13
  2.7 1.8 %fusion.4 = f32[3,4,4096]{2,1,0:T(4,128)S(1)} fusion(pred[3,4,64]{2,1,0:T(4,128)(4,1)S(1)} %fusion.19, f32[64,4096]{1,0:T(8,128)} %param.14), kind=kOutput, calls=%fused_computation.7 | convolution fusion | flops 37748736 | bytes 1245952 | tf_op jit(solution)/shard_map/qjr,rc->qjc/dot_general | solution.py:422
  4.5 0.0 copy-done.10
  4.5 0.1 fusion.27
  4.7 0.1 concatenate.22
  4.9 0.1 collective-permute-start
  4.9 3.4 %collective-permute-start.2 = (f32[4,4224]{1,0:T(4,128)S(1)}, f32[4,4224]{1,0:T(4,128)S(1)}, u32[]{:S(2)}, u32[]{:S(2)}) collective-permute-start(f32[4,4224]{1,0:T(4,128)S(1)} %get-tuple-element.23), channel_id=1, source_target_pairs={{0,64},{1,65},{2,66},{3,67},{4,68},{5,69},{6,70},{7,71},{8,72},{9,... | collective-permute-start | bytes 202760 | tf_op jit(solution)/shard_map/ppermute | solution.py:434
  8.3 6.2 %collective-permute-start.1 = (f32[4,4224]{1,0:T(4,128)S(1)}, f32[4,4224]{1,0:T(4,128)S(1)}, u32[]{:S(2)}, u32[]{:S(2)}) collective-permute-start(f32[4,4224]{1,0:T(4,128)S(1)} %get-tuple-element.24), channel_id=1, source_target_pairs={{0,127},{1,0},{2,1},{3,2},{4,3},{5,4},{6,5},{7,6},{8,7},{9,8},{10,... | collective-permute-start | bytes 202760 | tf_op jit(solution)/shard_map/ppermute | solution.py:434
  14.5 0.0 copy-done.6
  14.5 0.0 copy-done.8
  14.5 0.8 %fusion.6.refs_3_.pick_ref.refs_6_ = bf16[6,64,64]{2,1,0:T(8,128)(2,1)} fusion(s32[6,64]{1,0:T(8,128)S(1)} %pad_add_fusion), kind=kLoop, calls=%fused_computation.10 | loop fusion | flops 49152 | bytes 50688 | tf_op jit(solution)/shard_map/convert_element_type | solution.py:460
  15.3 0.0 copy-done.9
  15.3 0.7 %copy.36 = s32[2,64]{0,1:T(8,128)} copy(s32[2,64]{1,0:T(2,128)S(1)} %bitcast.36) | data formatting | bytes 1024 | tf_op jit(solution)/shard_map/squeeze | solution.py:461
  16.0 0.0 collective-permute-done
  16.0 0.2 fusion.22
  16.2 0.0 collective-permute-done.2
  16.2 0.2 fusion.20
  16.4 0.1 collective-permute-done.1
  16.4 0.2 fusion.21
  16.6 0.1 pad_add_fusion.1
  16.7 0.1 fusion.8
  16.8 0.2 fusion.10
  17.0 0.0 copy-done.7
  17.0 0.2 fusion.12
  17.2 0.1 pad_maximum_fusion.3
  17.2 0.1 copy.34
  17.3 0.2 convolution_add_fusion.refs_1_.weight_ref.refs_4_
  17.5 0.0 copy-start.3
  17.5 0.2 slice_reduce_fusion
  17.7 0.0 copy-done.2
  17.7 0.0 copy-done.13
  17.7 0.8 %convolution_select_fusion.refs_0_.refs_3_ = f32[64,4096]{1,0:T(8,128)S(1)} fusion(f32[4,4224]{1,0:T(4,128)S(1)} %collective-permute-done.2, f32[4,4224]{1,0:T(4,128)S(1)} %collective-permute-done.1, f32[4,4224]{1,0:T(4,128)S(1)} %collective-permute-done, f32[64,4096]{1,0:T(8,128)S(1)} %copy-done.2, f32[4096]{0:T(1024)S(1)} %copy-done.13, ...), kind=kOutput, calls=%fused_computation | convolution fusion | flops 240538368 | bytes 2316848 | tf_op jit(solution)/shard_map/dot_general | solution.py:443
  18.6 0.0 copy-done.3
  18.6 0.0 copy-start.1
  18.6 0.1 add_subtract_fusion
  18.7 0.1 add_add_fusion
  18.7 0.8 %copy-done.1 = f32[64,4096]{1,0:T(8,128)} copy-done((f32[64,4096]{1,0:T(8,128)}, f32[64,4096]{1,0:T(8,128)S(1)}, u32[]{:S(2)}) %copy-start.1) | copy-done | bytes 1048600
  19.6 0.0 collective-permute-start.3
  19.6 5.3 %collective-permute-start.4 = (f32[64,256]{1,0:T(8,128)S(1)}, f32[64,256]{1,0:T(8,128)S(1)}, u32[]{:S(2)}, u32[]{:S(2)}) collective-permute-start(f32[64,256]{1,0:T(8,128)S(1)} %add_subtract_fusion), channel_id=1, source_target_pairs={{8,0},{16,8},{24,16},{32,24},{40,32},{48,40},{56,48},{64,56},{72,6... | collective-permute-start | bytes 196616 | tf_op jit(solution)/shard_map/ppermute | solution.py:385
  24.9 5.5 %shard_map.136 = (f32[64,4096]{1,0:T(8,128)}, f32[64,256]{1,0:T(8,128)}, f32[64,256]{1,0:T(8,128)}) custom-call(f32[64,4096]{1,0:T(8,128)} %copy-done.1, f32[64,8]{1,0:T(8,128)} %copy-done.3, f32[1,4096]{1,0:T(1,128)} %constant.72.clone.refs_2_.top_ref.refs_5_, bf16[6,64,64]{2,1,0:T(8,128)(2,1)} %fusion.6.refs_3_.pick_ref.refs_6_, ...), custom_call_target="tpu_custom_call" | custom-call | flops 2500000000 | bytes 4000000 | tf_op jit(solution)/shard_map/pallas_call | solution.py:314
  30.4 0.0 collective-permute-done.3.lower_ref
  30.5 0.0 collective-permute-done.4.upper_ref
  30.5 0.0 copy-start.5
  30.5 0.6 %copy-done.4 = f32[64,256]{1,0:T(8,128)} copy-done((f32[64,256]{1,0:T(8,128)}, f32[64,256]{1,0:T(8,128)S(1)}, u32[]{:S(2)}) %copy-start.4) | copy-done | bytes 65560
  31.1 0.0 copy-done.5
  31.1 2.4 %shard_map.137 = (f32[64,256]{1,0:T(8,128)}, f32[64,256]{1,0:T(8,128)}, f32[64,256]{1,0:T(8,128)}, f32[64,256]{1,0:T(8,128)}) custom-call(f32[64,256]{1,0:T(8,128)} %copy-done.4, f32[64,256]{1,0:T(8,128)} %copy-done.5, bf16[6,64,64]{2,1,0:T(8,128)(2,1)} %fusion.6.refs_3_.pick_ref.refs_6_, s32[64,2]{1,0:T(8,128)} %bitcast.32, ...), custom_call_target="tpu_custom_call" | custom-call | tf_op jit(solution)/shard_map/pallas_call | solution.py:330
  33.5 0.0 collective-permute-start.5
  33.5 5.3 %collective-permute-start.6 = (f32[64,256]{1,0:T(8,128)}, f32[64,256]{1,0:T(8,128)S(1)}, u32[]{:S(2)}, u32[]{:S(2)}) collective-permute-start(f32[64,256]{1,0:T(8,128)} %get-tuple-element.18), channel_id=1, source_target_pairs={{8,0},{16,8},{24,16},{32,24},{40,32},{48,40},{56,48},{64,56},{72,6... | collective-permute-start | bytes 196616 | tf_op jit(solution)/shard_map/ppermute | solution.py:385
  38.9 2.4 %collective-permute-done.5.refs_10_ = f32[64,256]{1,0:T(8,128)S(1)} collective-permute-done((f32[64,256]{1,0:T(8,128)}, f32[64,256]{1,0:T(8,128)S(1)}, u32[]{:S(2)}, u32[]{:S(2)}) %collective-permute-start.5) | collective-permute-done | bytes 65568 | tf_op jit(solution)/shard_map/ppermute | solution.py:385
  41.3 0.0 collective-permute-done.6.refs_11_
  41.3 0.6 %copy-done.11 = f32[64,256]{1,0:T(8,128)} copy-done((f32[64,256]{1,0:T(8,128)}, f32[64,256]{1,0:T(8,128)S(1)}, u32[]{:S(2)}) %copy-start.11) | copy-done | bytes 65560
  42.0 0.0 copy-done.12
  42.0 6.2 %shard_map.138 = f32[64,4096]{1,0:T(8,128)} custom-call(f32[64,4096]{1,0:T(8,128)} %get-tuple-element.12.refs_0_, f32[64,256]{1,0:T(8,128)} %get-tuple-element.15.refs_1_, f32[64,256]{1,0:T(8,128)} %get-tuple-element.16.refs_2_, f32[64,4096]{1,0:T(8,128)} %copy-done.1, f32[64,8]{1,0:T(8,128)} %copy-done.3, f32[1,4096]{1,0:T(1,128)} %constant.72.clone.refs_2_.top_ref.refs_5_, ...), custom_call_target="tpu_custom_call" | custom-call | flops 2500000000 | bytes 4000000 | tf_op jit(solution)/shard_map/pallas_call | solution.py:314
  (13 shorter events, 0.1 us)
Async XLA Ops:
  0.0 1.7 %copy-start = (f32[64,3]{0,1:T(4,128)S(1)}, f32[64,3]{0,1:T(4,128)}, u32[]{:S(2)}) copy-start(f32[64,3]{0,1:T(4,128)} %param.16) | copy-start | bytes 2308
  0.0 4.5 %copy-start.10 = (s32[64]{0:T(128)S(1)}, s32[64]{0:T(128)}, u32[]{:S(2)}) copy-start(s32[64]{0:T(128)} %param.17) | copy-start | bytes 772
  2.7 11.8 %copy-start.6 = (s32[1,4,64]{2,1,0:T(4,128)S(1)}, s32[1,4,64]{2,1,0:T(4,128)}, u32[]{:S(2)}) copy-start(s32[1,4,64]{2,1,0:T(4,128)} %param.19) | copy-start | bytes 3076
  2.7 11.8 %copy-start.8 = (s32[1,2,64]{2,1,0:T(2,128)S(1)}, s32[1,2,64]{2,1,0:T(2,128)}, u32[]{:S(2)}) copy-start(s32[1,2,64]{2,1,0:T(2,128)} %param.20) | copy-start | bytes 1540
  2.7 12.6 %copy-start.9 = (s32[1,2,64]{2,1,0:T(2,128)S(1)}, s32[1,2,64]{2,1,0:T(2,128)}, u32[]{:S(2)}) copy-start(s32[1,2,64]{2,1,0:T(2,128)} %param.21) | copy-start | bytes 1540
  2.7 14.3 %copy-start.7 = (f32[64,3]{0,1:T(4,128)S(1)}, f32[64,3]{0,1:T(4,128)}, u32[]{:S(2)}) copy-start(f32[64,3]{0,1:T(4,128)} %param.15) | copy-start | bytes 2308
  2.7 15.0 %copy-start.2 = (f32[64,4096]{1,0:T(8,128)S(1)}, f32[64,4096]{1,0:T(8,128)}, u32[]{:S(2)}) copy-start(f32[64,4096]{1,0:T(8,128)} %param.14) | copy-start | bytes 3145732
  2.7 15.0 %copy-start.13 = (f32[4096]{0:T(1024)S(1)}, f32[4096]{0:T(1024)}, u32[]{:S(2)}) copy-start(f32[4096]{0:T(1024)} %constant.85) | copy-start | bytes 49156
  4.9 11.1 %collective-permute-start = (f32[4,4224]{1,0:T(4,128)S(1)}, f32[4,4224]{1,0:T(4,128)S(1)}, u32[]{:S(2)}, u32[]{:S(2)}) collective-permute-start(f32[4,4224]{1,0:T(4,128)S(1)} %get-tuple-element.22), channel_id=1, source_target_pairs={{0,1},{1,2},{2,3},{3,4},{4,5},{5,6},{6,7},{7,8},{8,9},{9,10},{10,1... | collective-permute-start | bytes 202760 | tf_op jit(solution)/shard_map/ppermute | solution.py:434
  4.9 11.2 %collective-permute-start.2 = (f32[4,4224]{1,0:T(4,128)S(1)}, f32[4,4224]{1,0:T(4,128)S(1)}, u32[]{:S(2)}, u32[]{:S(2)}) collective-permute-start(f32[4,4224]{1,0:T(4,128)S(1)} %get-tuple-element.23), channel_id=1, source_target_pairs={{0,64},{1,65},{2,66},{3,67},{4,68},{5,69},{6,70},{7,71},{8,72},{9,... | collective-permute-start | bytes 202760 | tf_op jit(solution)/shard_map/ppermute | solution.py:434
  8.3 8.1 %collective-permute-start.1 = (f32[4,4224]{1,0:T(4,128)S(1)}, f32[4,4224]{1,0:T(4,128)S(1)}, u32[]{:S(2)}, u32[]{:S(2)}) collective-permute-start(f32[4,4224]{1,0:T(4,128)S(1)} %get-tuple-element.24), channel_id=1, source_target_pairs={{0,127},{1,0},{2,1},{3,2},{4,3},{5,4},{6,5},{7,6},{8,7},{9,8},{10,... | collective-permute-start | bytes 202760 | tf_op jit(solution)/shard_map/ppermute | solution.py:434
  17.5 1.1 %copy-start.3 = (f32[64,8]{1,0:T(8,128)}, f32[64,8]{1,0:T(8,128)S(1)}, u32[]{:S(2)}) copy-start(f32[64,8]{1,0:T(8,128)S(1)} %convolution_add_fusion.refs_1_.weight_ref.refs_4_) | copy-start | bytes 6148
  18.6 1.0 %copy-start.1 = (f32[64,4096]{1,0:T(8,128)}, f32[64,4096]{1,0:T(8,128)S(1)}, u32[]{:S(2)}) copy-start(f32[64,4096]{1,0:T(8,128)S(1)} %convolution_select_fusion.refs_0_.refs_3_) | copy-start | bytes 3145732
  19.6 10.9 %collective-permute-start.3 = (f32[64,256]{1,0:T(8,128)S(1)}, f32[64,256]{1,0:T(8,128)S(1)}, u32[]{:S(2)}, u32[]{:S(2)}) collective-permute-start(f32[64,256]{1,0:T(8,128)S(1)} %add_add_fusion), channel_id=1, source_target_pairs={{0,8},{8,16},{16,24},{24,32},{32,40},{40,48},{48,56},{56,64},{64,7... | collective-permute-start | bytes 196616 | tf_op jit(solution)/shard_map/ppermute | solution.py:385
  19.6 10.9 %collective-permute-start.4 = (f32[64,256]{1,0:T(8,128)S(1)}, f32[64,256]{1,0:T(8,128)S(1)}, u32[]{:S(2)}, u32[]{:S(2)}) collective-permute-start(f32[64,256]{1,0:T(8,128)S(1)} %add_subtract_fusion), channel_id=1, source_target_pairs={{8,0},{16,8},{24,16},{32,24},{40,32},{48,40},{56,48},{64,56},{72,6... | collective-permute-start | bytes 196616 | tf_op jit(solution)/shard_map/ppermute | solution.py:385
  30.5 0.6 %copy-start.4 = (f32[64,256]{1,0:T(8,128)}, f32[64,256]{1,0:T(8,128)S(1)}, u32[]{:S(2)}) copy-start(f32[64,256]{1,0:T(8,128)S(1)} %collective-permute-done.3.lower_ref) | copy-start | bytes 196612
  30.5 0.6 %copy-start.5 = (f32[64,256]{1,0:T(8,128)}, f32[64,256]{1,0:T(8,128)S(1)}, u32[]{:S(2)}) copy-start(f32[64,256]{1,0:T(8,128)S(1)} %collective-permute-done.4.upper_ref) | copy-start | bytes 196612
  33.5 7.8 %collective-permute-start.5 = (f32[64,256]{1,0:T(8,128)}, f32[64,256]{1,0:T(8,128)S(1)}, u32[]{:S(2)}, u32[]{:S(2)}) collective-permute-start(f32[64,256]{1,0:T(8,128)} %get-tuple-element.17), channel_id=1, source_target_pairs={{0,8},{8,16},{16,24},{24,32},{32,40},{40,48},{48,56},{56,64},{64,7... | collective-permute-start | bytes 196616 | tf_op jit(solution)/shard_map/ppermute | solution.py:385
  33.5 7.8 %collective-permute-start.6 = (f32[64,256]{1,0:T(8,128)}, f32[64,256]{1,0:T(8,128)S(1)}, u32[]{:S(2)}, u32[]{:S(2)}) collective-permute-start(f32[64,256]{1,0:T(8,128)} %get-tuple-element.18), channel_id=1, source_target_pairs={{8,0},{16,8},{24,16},{32,24},{40,32},{48,40},{56,48},{64,56},{72,6... | collective-permute-start | bytes 196616 | tf_op jit(solution)/shard_map/ppermute | solution.py:385
  41.3 0.6 %copy-start.11 = (f32[64,256]{1,0:T(8,128)}, f32[64,256]{1,0:T(8,128)S(1)}, u32[]{:S(2)}) copy-start(f32[64,256]{1,0:T(8,128)S(1)} %collective-permute-done.5.refs_10_) | copy-start | bytes 196612
  41.3 0.6 %copy-start.12 = (f32[64,256]{1,0:T(8,128)}, f32[64,256]{1,0:T(8,128)S(1)}, u32[]{:S(2)}) copy-start(f32[64,256]{1,0:T(8,128)S(1)} %collective-permute-done.6.refs_11_) | copy-start | bytes 196612

commit v18 on v15

--- a/solution.py
+++ b/solution.py
@@ -51,7 +51,7 @@
             np.kron(second.T, identity),
             np.kron(identity, derivative.T),
             np.kron(derivative.T, identity),
-            traces, pad, swapped, pad,
+            traces, swapped,
         ],
         axis=1,
     ).astype(np.float32)
@@ -223,11 +223,11 @@
         return rows if a < low else jnp.concatenate([blank, rows], axis=0)
 
     own = jnp.concatenate([trace_block(a, 4 * PLANE) for a in range(P_SIZE)], axis=1)
-    other = jnp.concatenate([trace_block(a, 4 * PLANE + 128) for a in range(P_SIZE)], axis=1)
+    other = own
     lane = lax.broadcasted_iota(jnp.int32, (1, P_SIZE * 128), 1) % 128
     across = jnp.zeros_like(own)
     for face in range(4):
-        gathered = exact_pick(pick_ref[face], other)
+        gathered = pltpu.roll(exact_pick(pick_ref[face], other), P_SIZE * 128 - 64, 1)
         across = jnp.where(lane // P_SIZE == face, gathered, across)
     jump = own - across
     jump_rows = jnp.concatenate(

time: 48.5 us -> 49.1 us (1.012)
  Pallas kernels: 14.2 us -> 14.8 us
    pallas_call x2, Pallas kernels: 11.8 us -> 12.4 us  [inner(): pl.pallas_call(functools.partial(inner_body, scale=scale, carried=carried...]
where the time goes in v18:
time: 49.1 us; the launch traced here: 48.8 us
  starting transfers between devices  20.3 us (41%)
  Pallas kernels  14.8 us (30%)
  matrix products  4.38 us (9%)
  other arithmetic  3.29 us (7%)
  local copies, waits for them, and re-layouts  3.28 us (7%)
  waiting for transfers between devices  2.53 us (5%)
    pallas_call x2, Pallas kernels, inner(): pl.pallas_call(functools.partial(inner_body, scale=scale, carried=carried...  12.4 us
    ppermute x4, starting transfers between devices, exchange(): return (lax.ppermute(total, 'dom', up), lax.ppermute(even, 'dom', down))  10.7 us
    ppermute x3, starting transfers between devices, shards(): arrived = lax.ppermute(parcels[index], ('dom', 'face'), pairs)  9.63 us
    ppermute x4, waiting for transfers between devices, exchange(): return (lax.ppermute(total, 'dom', up), lax.ppermute(even, 'dom', down))  2.46 us
    pallas_call x1, Pallas kernels, faces(): pl.pallas_call(functools.partial(faces_body, scale=scale), out_shape=(squ...  2.43 us
    unnamed x28, local copies, waits for them, and re-layouts  2.15 us
    dot_general x1, matrix products, shards(): jnp.einsum('qjr,rc->qjc', hit_values, coefficients, precision=exact)  1.78 us
  transfers between devices with their start and end apart: 7, of which 2 were waited for; matrix products, arithmetic and copies ran while one was open for 4% of the time, Pallas kernels for 12%

profile of v18, /device:TPU:0, one launch (start us, length us, event | category | flops | bytes accessed | tf_op | source)
XLA Modules:
  0.0 48.8 jit_solution(15360112718712467656)
XLA Ops:
  0.0 0.0 copy-start
  0.0 0.7 %and_select_fusion = s32[3]{0:T(128)S(1)} fusion(s32[3]{0:T(128)} %constant.73.clone, s32[]{:T(128)S(6)} %add.96), kind=kLoop, calls=%fused_computation.46 | loop fusion | flops 36 | bytes 28 | tf_op jit(solution)/shard_map/jit(remainder)/select_n | solution.py:408
  0.7 0.7 %compare_select_fusion.2 = (s32[64]{0:T(128)S(1)}, s32[64]{0:T(128)S(1)}, s32[64]{0:T(128)S(1)}) fusion(s32[]{:T(128)S(6)} %add.96, s32[64]{0:T(128)} %param.18), kind=kLoop, calls=%fused_computation.48 | loop fusion | flops 1344 | bytes 1028 | tf_op jit(solution)/shard_map/jit(_where)/select_n | solution.py:431
  1.4 0.1 fusion.34
  1.4 0.2 reduce_window_sum.11
  1.7 0.0 copy-done
  1.7 0.1 fusion.23
  1.8 0.8 %fusion.25 = f32[3,4,3]{2,1,0:T(4,128)S(1)} fusion(pred[3,4,64]{2,1,0:T(4,128)(4,1)S(1)} %fusion.19, f32[64,3]{0,1:T(4,128)} %param.15), kind=kOutput, calls=%fused_computation.44 | convolution fusion | flops 27648 | bytes 1680 | tf_op jit(solution)/shard_map/qjr,rc->qjc/dot_general | solution.py:423
  2.7 0.0 copy-start.8
  2.7 0.0 copy-start.9
  2.7 0.0 copy-start.7
  2.7 0.0 copy-start.2
  2.7 0.0 copy-start.13
  2.7 1.8 %fusion.4 = f32[3,4,4096]{2,1,0:T(4,128)S(1)} fusion(pred[3,4,64]{2,1,0:T(4,128)(4,1)S(1)} %fusion.19, f32[64,4096]{1,0:T(8,128)} %param.14), kind=kOutput, calls=%fused_computation.7 | convolution fusion | flops 37748736 | bytes 1245952 | tf_op jit(solution)/shard_map/qjr,rc->qjc/dot_general | solution.py:422
  4.5 0.0 copy-done.10
  4.5 0.1 fusion.27
  4.7 0.1 concatenate.22
  4.9 0.1 collective-permute-start
  4.9 3.4 %collective-permute-start.2 = (f32[4,4224]{1,0:T(4,128)S(1)}, f32[4,4224]{1,0:T(4,128)S(1)}, u32[]{:S(2)}, u32[]{:S(2)}) collective-permute-start(f32[4,4224]{1,0:T(4,128)S(1)} %get-tuple-element.25), channel_id=1, source_target_pairs={{0,64},{1,65},{2,66},{3,67},{4,68},{5,69},{6,70},{7,71},{8,72},{9,... | collective-permute-start | bytes 202760 | tf_op jit(solution)/shard_map/ppermute | solution.py:434
  8.3 6.2 %collective-permute-start.1 = (f32[4,4224]{1,0:T(4,128)S(1)}, f32[4,4224]{1,0:T(4,128)S(1)}, u32[]{:S(2)}, u32[]{:S(2)}) collective-permute-start(f32[4,4224]{1,0:T(4,128)S(1)} %get-tuple-element.26), channel_id=1, source_target_pairs={{0,127},{1,0},{2,1},{3,2},{4,3},{5,4},{6,5},{7,6},{8,7},{9,8},{10,... | collective-permute-start | bytes 202760 | tf_op jit(solution)/shard_map/ppermute | solution.py:434
  14.5 0.0 copy-done.6
  14.5 0.0 copy-done.8
  14.5 0.8 %fusion.6.refs_3_.pick_ref.refs_6_ = bf16[6,64,64]{2,1,0:T(8,128)(2,1)} fusion(s32[6,64]{1,0:T(8,128)S(1)} %pad_add_fusion), kind=kLoop, calls=%fused_computation.10 | loop fusion | flops 49152 | bytes 50688 | tf_op jit(solution)/shard_map/convert_element_type | solution.py:460
  15.3 0.0 copy-done.9
  15.3 0.7 %copy.36 = s32[2,64]{0,1:T(8,128)} copy(s32[2,64]{1,0:T(2,128)S(1)} %bitcast.36) | data formatting | bytes 1024 | tf_op jit(solution)/shard_map/squeeze | solution.py:461
  16.0 0.0 collective-permute-done
  16.0 0.2 fusion.22
  16.2 0.0 collective-permute-done.2
  16.2 0.2 fusion.20
  16.4 0.1 collective-permute-done.1
  16.4 0.2 fusion.21
  16.6 0.1 pad_add_fusion.1
  16.7 0.1 fusion.8
  16.8 0.2 fusion.10
  17.0 0.0 copy-done.7
  17.0 0.2 fusion.12
  17.1 0.1 pad_maximum_fusion.3
  17.2 0.1 copy.34
  17.3 0.2 convolution_add_fusion.refs_1_.weight_ref.refs_4_
  17.5 0.0 copy-start.3
  17.5 0.2 slice_reduce_fusion
  17.7 0.0 copy-done.2
  17.7 0.0 copy-done.13
  17.7 0.8 %convolution_select_fusion.refs_0_.refs_3_ = f32[64,4096]{1,0:T(8,128)S(1)} fusion(f32[4,4224]{1,0:T(4,128)S(1)} %collective-permute-done.2, f32[4,4224]{1,0:T(4,128)S(1)} %collective-permute-done.1, f32[4,4224]{1,0:T(4,128)S(1)} %collective-permute-done, f32[64,4096]{1,0:T(8,128)S(1)} %copy-done.2, f32[4096]{0:T(1024)S(1)} %copy-done.13, ...), kind=kOutput, calls=%fused_computation | convolution fusion | flops 240538368 | bytes 2316848 | tf_op jit(solution)/shard_map/dot_general | solution.py:443
  18.6 0.0 copy-done.3
  18.6 0.1 add_subtract_fusion
  18.7 0.1 add_add_fusion
  18.7 0.8 %copy-done.1 = f32[64,4096]{1,0:T(8,128)} copy-done((f32[64,4096]{1,0:T(8,128)}, f32[64,4096]{1,0:T(8,128)S(1)}, u32[]{:S(2)}) %copy-start.1) | copy-done | bytes 1048600
  19.6 0.0 collective-permute-start.3
  19.6 5.3 %collective-permute-start.4 = (f32[64,256]{1,0:T(8,128)S(1)}, f32[64,256]{1,0:T(8,128)S(1)}, u32[]{:S(2)}, u32[]{:S(2)}) collective-permute-start(f32[64,256]{1,0:T(8,128)S(1)} %add_subtract_fusion), channel_id=1, source_target_pairs={{8,0},{16,8},{24,16},{32,24},{40,32},{48,40},{56,48},{64,56},{72,6... | collective-permute-start | bytes 196616 | tf_op jit(solution)/shard_map/ppermute | solution.py:385
  24.9 6.1 %shard_map.136 = (f32[64,4096]{1,0:T(8,128)}, f32[64,256]{1,0:T(8,128)}, f32[64,256]{1,0:T(8,128)}) custom-call(f32[64,4096]{1,0:T(8,128)} %copy-done.1, f32[64,8]{1,0:T(8,128)} %copy-done.3, f32[1,4096]{1,0:T(1,128)} %constant.74.clone.refs_2_.top_ref.refs_5_, bf16[6,64,64]{2,1,0:T(8,128)(2,1)} %fusion.6.refs_3_.pick_ref.refs_6_, ...), custom_call_target="tpu_custom_call" | custom-call | flops 2500000000 | bytes 4000000 | tf_op jit(solution)/shard_map/pallas_call | solution.py:314
  31.0 0.0 collective-permute-done.3.lower_ref
  31.0 0.0 collective-permute-done.4.upper_ref
  31.0 0.0 copy-start.5
  31.0 0.6 %copy-done.4 = f32[64,256]{1,0:T(8,128)} copy-done((f32[64,256]{1,0:T(8,128)}, f32[64,256]{1,0:T(8,128)S(1)}, u32[]{:S(2)}) %copy-start.4) | copy-done | bytes 65560
  31.6 0.0 copy-done.5
  31.6 2.4 %shard_map.137 = (f32[64,256]{1,0:T(8,128)}, f32[64,256]{1,0:T(8,128)}, f32[64,256]{1,0:T(8,128)}, f32[64,256]{1,0:T(8,128)}) custom-call(f32[64,256]{1,0:T(8,128)} %copy-done.4, f32[64,256]{1,0:T(8,128)} %copy-done.5, bf16[6,64,64]{2,1,0:T(8,128)(2,1)} %fusion.6.refs_3_.pick_ref.refs_6_, s32[64,2]{1,0:T(8,128)} %bitcast.32, ...), custom_call_target="tpu_custom_call" | custom-call | tf_op jit(solution)/shard_map/pallas_call | solution.py:330
  34.0 0.0 collective-permute-start.5
  34.0 5.3 %collective-permute-start.6 = (f32[64,256]{1,0:T(8,128)}, f32[64,256]{1,0:T(8,128)S(1)}, u32[]{:S(2)}, u32[]{:S(2)}) collective-permute-start(f32[64,256]{1,0:T(8,128)} %get-tuple-element.18), channel_id=1, source_target_pairs={{8,0},{16,8},{24,16},{32,24},{40,32},{48,40},{56,48},{64,56},{72,6... | collective-permute-start | bytes 196616 | tf_op jit(solution)/shard_map/ppermute | solution.py:385
  39.4 2.4 %collective-permute-done.5.refs_10_ = f32[64,256]{1,0:T(8,128)S(1)} collective-permute-done((f32[64,256]{1,0:T(8,128)}, f32[64,256]{1,0:T(8,128)S(1)}, u32[]{:S(2)}, u32[]{:S(2)}) %collective-permute-start.5) | collective-permute-done | bytes 65568 | tf_op jit(solution)/shard_map/ppermute | solution.py:385
  41.8 0.0 collective-permute-done.6.refs_11_
  41.8 0.6 %copy-done.11 = f32[64,256]{1,0:T(8,128)} copy-done((f32[64,256]{1,0:T(8,128)}, f32[64,256]{1,0:T(8,128)S(1)}, u32[]{:S(2)}) %copy-start.11) | copy-done | bytes 65560
  42.5 0.0 copy-done.12
  42.5 6.3 %shard_map.138 = f32[64,4096]{1,0:T(8,128)} custom-call(f32[64,4096]{1,0:T(8,128)} %get-tuple-element.12.refs_0_, f32[64,256]{1,0:T(8,128)} %get-tuple-element.15.refs_1_, f32[64,256]{1,0:T(8,128)} %get-tuple-element.16.refs_2_, f32[64,4096]{1,0:T(8,128)} %copy-done.1, f32[64,8]{1,0:T(8,128)} %copy-done.3, f32[1,4096]{1,0:T(1,128)} %constant.74.clone.refs_2_.top_ref.refs_5_, ...), custom_call_target="tpu_custom_call" | custom-call | flops 2500000000 | bytes 4000000 | tf_op jit(solution)/shard_map/pallas_call | solution.py:314
  (13 shorter events, 0.1 us)
Async XLA Ops:
  0.0 1.7 %copy-start = (f32[64,3]{0,1:T(4,128)S(1)}, f32[64,3]{0,1:T(4,128)}, u32[]{:S(2)}) copy-start(f32[64,3]{0,1:T(4,128)} %param.16) | copy-start | bytes 2308
  0.0 4.5 %copy-start.10 = (s32[64]{0:T(128)S(1)}, s32[64]{0:T(128)}, u32[]{:S(2)}) copy-start(s32[64]{0:T(128)} %param.17) | copy-start | bytes 772
  2.7 11.8 %copy-start.6 = (s32[1,4,64]{2,1,0:T(4,128)S(1)}, s32[1,4,64]{2,1,0:T(4,128)}, u32[]{:S(2)}) copy-start(s32[1,4,64]{2,1,0:T(4,128)} %param.19) | copy-start | bytes 3076
  2.7 11.8 %copy-start.8 = (s32[1,2,64]{2,1,0:T(2,128)S(1)}, s32[1,2,64]{2,1,0:T(2,128)}, u32[]{:S(2)}) copy-start(s32[1,2,64]{2,1,0:T(2,128)} %param.20) | copy-start | bytes 1540
  2.7 12.6 %copy-start.9 = (s32[1,2,64]{2,1,0:T(2,128)S(1)}, s32[1,2,64]{2,1,0:T(2,128)}, u32[]{:S(2)}) copy-start(s32[1,2,64]{2,1,0:T(2,128)} %param.21) | copy-start | bytes 1540
  2.7 14.3 %copy-start.7 = (f32[64,3]{0,1:T(4,128)S(1)}, f32[64,3]{0,1:T(4,128)}, u32[]{:S(2)}) copy-start(f32[64,3]{0,1:T(4,128)} %param.15) | copy-start | bytes 2308
  2.7 15.0 %copy-start.2 = (f32[64,4096]{1,0:T(8,128)S(1)}, f32[64,4096]{1,0:T(8,128)}, u32[]{:S(2)}) copy-start(f32[64,4096]{1,0:T(8,128)} %param.14) | copy-start | bytes 3145732
  2.7 15.0 %copy-start.13 = (f32[4096]{0:T(1024)S(1)}, f32[4096]{0:T(1024)}, u32[]{:S(2)}) copy-start(f32[4096]{0:T(1024)} %constant.87) | copy-start | bytes 49156
  4.9 11.1 %collective-permute-start = (f32[4,4224]{1,0:T(4,128)S(1)}, f32[4,4224]{1,0:T(4,128)S(1)}, u32[]{:S(2)}, u32[]{:S(2)}) collective-permute-start(f32[4,4224]{1,0:T(4,128)S(1)} %get-tuple-element.24), channel_id=1, source_target_pairs={{0,1},{1,2},{2,3},{3,4},{4,5},{5,6},{6,7},{7,8},{8,9},{9,10},{10,1... | collective-permute-start | bytes 202760 | tf_op jit(solution)/shard_map/ppermute | solution.py:434
  4.9 11.2 %collective-permute-start.2 = (f32[4,4224]{1,0:T(4,128)S(1)}, f32[4,4224]{1,0:T(4,128)S(1)}, u32[]{:S(2)}, u32[]{:S(2)}) collective-permute-start(f32[4,4224]{1,0:T(4,128)S(1)} %get-tuple-element.25), channel_id=1, source_target_pairs={{0,64},{1,65},{2,66},{3,67},{4,68},{5,69},{6,70},{7,71},{8,72},{9,... | collective-permute-start | bytes 202760 | tf_op jit(solution)/shard_map/ppermute | solution.py:434
  8.3 8.1 %collective-permute-start.1 = (f32[4,4224]{1,0:T(4,128)S(1)}, f32[4,4224]{1,0:T(4,128)S(1)}, u32[]{:S(2)}, u32[]{:S(2)}) collective-permute-start(f32[4,4224]{1,0:T(4,128)S(1)} %get-tuple-element.26), channel_id=1, source_target_pairs={{0,127},{1,0},{2,1},{3,2},{4,3},{5,4},{6,5},{7,6},{8,7},{9,8},{10,... | collective-permute-start | bytes 202760 | tf_op jit(solution)/shard_map/ppermute | solution.py:434
  17.5 1.1 %copy-start.3 = (f32[64,8]{1,0:T(8,128)}, f32[64,8]{1,0:T(8,128)S(1)}, u32[]{:S(2)}) copy-start(f32[64,8]{1,0:T(8,128)S(1)} %convolution_add_fusion.refs_1_.weight_ref.refs_4_) | copy-start | bytes 6148
  18.6 1.0 %copy-start.1 = (f32[64,4096]{1,0:T(8,128)}, f32[64,4096]{1,0:T(8,128)S(1)}, u32[]{:S(2)}) copy-start(f32[64,4096]{1,0:T(8,128)S(1)} %convolution_select_fusion.refs_0_.refs_3_) | copy-start | bytes 3145732
  19.6 11.4 %collective-permute-start.3 = (f32[64,256]{1,0:T(8,128)S(1)}, f32[64,256]{1,0:T(8,128)S(1)}, u32[]{:S(2)}, u32[]{:S(2)}) collective-permute-start(f32[64,256]{1,0:T(8,128)S(1)} %add_add_fusion), channel_id=1, source_target_pairs={{0,8},{8,16},{16,24},{24,32},{32,40},{40,48},{48,56},{56,64},{64,7... | collective-permute-start | bytes 196616 | tf_op jit(solution)/shard_map/ppermute | solution.py:385
  19.6 11.4 %collective-permute-start.4 = (f32[64,256]{1,0:T(8,128)S(1)}, f32[64,256]{1,0:T(8,128)S(1)}, u32[]{:S(2)}, u32[]{:S(2)}) collective-permute-start(f32[64,256]{1,0:T(8,128)S(1)} %add_subtract_fusion), channel_id=1, source_target_pairs={{8,0},{16,8},{24,16},{32,24},{40,32},{48,40},{56,48},{64,56},{72,6... | collective-permute-start | bytes 196616 | tf_op jit(solution)/shard_map/ppermute | solution.py:385
  31.0 0.6 %copy-start.4 = (f32[64,256]{1,0:T(8,128)}, f32[64,256]{1,0:T(8,128)S(1)}, u32[]{:S(2)}) copy-start(f32[64,256]{1,0:T(8,128)S(1)} %collective-permute-done.3.lower_ref) | copy-start | bytes 196612
  31.0 0.6 %copy-start.5 = (f32[64,256]{1,0:T(8,128)}, f32[64,256]{1,0:T(8,128)S(1)}, u32[]{:S(2)}) copy-start(f32[64,256]{1,0:T(8,128)S(1)} %collective-permute-done.4.upper_ref) | copy-start | bytes 196612
  34.0 7.8 %collective-permute-start.5 = (f32[64,256]{1,0:T(8,128)}, f32[64,256]{1,0:T(8,128)S(1)}, u32[]{:S(2)}, u32[]{:S(2)}) collective-permute-start(f32[64,256]{1,0:T(8,128)} %get-tuple-element.17), channel_id=1, source_target_pairs={{0,8},{8,16},{16,24},{24,32},{32,40},{40,48},{48,56},{56,64},{64,7... | collective-permute-start | bytes 196616 | tf_op jit(solution)/shard_map/ppermute | solution.py:385
  34.0 7.8 %collective-permute-start.6 = (f32[64,256]{1,0:T(8,128)}, f32[64,256]{1,0:T(8,128)S(1)}, u32[]{:S(2)}, u32[]{:S(2)}) collective-permute-start(f32[64,256]{1,0:T(8,128)} %get-tuple-element.18), channel_id=1, source_target_pairs={{8,0},{16,8},{24,16},{32,24},{40,32},{48,40},{56,48},{64,56},{72,6... | collective-permute-start | bytes 196616 | tf_op jit(solution)/shard_map/ppermute | solution.py:385
  41.8 0.6 %copy-start.11 = (f32[64,256]{1,0:T(8,128)}, f32[64,256]{1,0:T(8,128)S(1)}, u32[]{:S(2)}) copy-start(f32[64,256]{1,0:T(8,128)S(1)} %collective-permute-done.5.refs_10_) | copy-start | bytes 196612
  41.8 0.6 %copy-start.12 = (f32[64,256]{1,0:T(8,128)}, f32[64,256]{1,0:T(8,128)S(1)}, u32[]{:S(2)}) copy-start(f32[64,256]{1,0:T(8,128)S(1)} %collective-permute-done.6.refs_11_) | copy-start | bytes 196612

commit v19 on v15

--- a/solution.py
+++ b/solution.py
@@ -268,9 +268,17 @@
 
 def faces_body(
     lower_ref, upper_ref, pick_ref, turn_ref, flip_ref, top_ref, weight_ref, even_ref, total_ref,
-    below_ref, above_ref, new_even_ref, new_total_ref, *, scale
+    below_ref, above_ref, new_even_ref, new_total_ref, held_ref, held_sems, *, scale
 ):
-    below, above = turn_pair(lower_ref[...], upper_ref[...], pick_ref, turn_ref[...], flip_ref[...])
+    arrivals = [
+        pltpu.make_async_copy(source, held_ref.at[index], held_sems.at[index])
+        for index, source in enumerate((lower_ref, upper_ref))
+    ]
+    for copy in arrivals:
+        copy.start()
+    for copy in arrivals:
+        copy.wait()
+    below, above = turn_pair(held_ref[0], held_ref[1], pick_ref, turn_ref[...], flip_ref[...])
     below_ref[...] = below
     above_ref[...] = above
     top = top_ref[...]
@@ -330,8 +338,9 @@
     return pl.pallas_call(
         functools.partial(faces_body, scale=scale),
         out_shape=(square,) * 4,
-        in_specs=[spec] * 9,
+        in_specs=[pl.BlockSpec(memory_space=pl.ANY)] * 2 + [spec] * 7,
         out_specs=(spec,) * 4,
+        scratch_shapes=[pltpu.VMEM((2, count, PLANE), jnp.float32), pltpu.SemaphoreType.DMA((2,))],
     )(lower, upper, picks, codes, flip, top, weight, even, total)
 
 

time: 48.5 us -> 49.4 us (1.019)
  Pallas kernels: 14.2 us -> 15 us
    pallas_call x1, Pallas kernels: 2.43 us -> 3.25 us  [faces(): pl.pallas_call(functools.partial(faces_body, scale=scale), out_shape=(squ...]
  transfers between devices with their start and end apart: 7 -> 7, of which waited for: 2 -> 2; matrix products, arithmetic and copies ran while one was open for 4% -> 4% of each run, Pallas kernels for 12% -> 11%
where the time goes in v19:
time: 49.4 us; the launch traced here: 49.1 us
  starting transfers between devices  20.4 us (41%)
  Pallas kernels  15 us (30%)
  matrix products  4.38 us (9%)
  other arithmetic  3.29 us (7%)
  local copies, waits for them, and re-layouts  3.28 us (7%)
  waiting for transfers between devices  2.53 us (5%)
    pallas_call x2, Pallas kernels, inner(): pl.pallas_call(functools.partial(inner_body, scale=scale, carried=carried...  11.8 us
    ppermute x4, starting transfers between devices, exchange(): return (lax.ppermute(total, 'dom', up), lax.ppermute(even, 'dom', down))  10.8 us
    ppermute x3, starting transfers between devices, shards(): arrived = lax.ppermute(parcels[index], ('dom', 'face'), pairs)  9.63 us
    pallas_call x1, Pallas kernels, faces(): pl.pallas_call(functools.partial(faces_body, scale=scale), out_shape=(squ...  3.25 us
    ppermute x4, waiting for transfers between devices, exchange(): return (lax.ppermute(total, 'dom', up), lax.ppermute(even, 'dom', down))  2.46 us
    unnamed x28, local copies, waits for them, and re-layouts  2.15 us
    dot_general x1, matrix products, shards(): jnp.einsum('qjr,rc->qjc', hit_values, coefficients, precision=exact)  1.78 us
  transfers between devices with their start and end apart: 7, of which 2 were waited for; matrix products, arithmetic and copies ran while one was open for 4% of the time, Pallas kernels for 11%

profile of v19, /device:TPU:0, one launch (start us, length us, event | category | flops | bytes accessed | tf_op | source)
XLA Modules:
  0.0 49.1 jit_solution(7762280575884052123)
XLA Ops:
  0.0 0.0 copy-start
  0.0 0.7 %and_select_fusion = s32[3]{0:T(128)S(1)} fusion(s32[3]{0:T(128)} %constant.73.clone, s32[]{:T(128)S(6)} %add.96), kind=kLoop, calls=%fused_computation.46 | loop fusion | flops 36 | bytes 28 | tf_op jit(solution)/shard_map/jit(remainder)/select_n | solution.py:417
  0.7 0.7 %compare_select_fusion.2 = (s32[64]{0:T(128)S(1)}, s32[64]{0:T(128)S(1)}, s32[64]{0:T(128)S(1)}) fusion(s32[]{:T(128)S(6)} %add.96, s32[64]{0:T(128)} %param.18), kind=kLoop, calls=%fused_computation.48 | loop fusion | flops 1344 | bytes 1028 | tf_op jit(solution)/shard_map/jit(_where)/select_n | solution.py:440
  1.4 0.1 fusion.34
  1.4 0.2 reduce_window_sum.11
  1.7 0.0 copy-done
  1.7 0.1 fusion.23
  1.8 0.8 %fusion.25 = f32[3,4,3]{2,1,0:T(4,128)S(1)} fusion(pred[3,4,64]{2,1,0:T(4,128)(4,1)S(1)} %fusion.19, f32[64,3]{0,1:T(4,128)} %param.15), kind=kOutput, calls=%fused_computation.44 | convolution fusion | flops 27648 | bytes 1680 | tf_op jit(solution)/shard_map/qjr,rc->qjc/dot_general | solution.py:432
  2.7 0.0 copy-start.8
  2.7 0.0 copy-start.9
  2.7 0.0 copy-start.7
  2.7 0.0 copy-start.2
  2.7 0.0 copy-start.13
  2.7 1.8 %fusion.4 = f32[3,4,4096]{2,1,0:T(4,128)S(1)} fusion(pred[3,4,64]{2,1,0:T(4,128)(4,1)S(1)} %fusion.19, f32[64,4096]{1,0:T(8,128)} %param.14), kind=kOutput, calls=%fused_computation.7 | convolution fusion | flops 37748736 | bytes 1245952 | tf_op jit(solution)/shard_map/qjr,rc->qjc/dot_general | solution.py:431
  4.5 0.0 copy-done.10
  4.5 0.1 fusion.27
  4.7 0.1 concatenate.22
  4.9 0.1 collective-permute-start
  4.9 3.4 %collective-permute-start.2 = (f32[4,4224]{1,0:T(4,128)S(1)}, f32[4,4224]{1,0:T(4,128)S(1)}, u32[]{:S(2)}, u32[]{:S(2)}) collective-permute-start(f32[4,4224]{1,0:T(4,128)S(1)} %get-tuple-element.25), channel_id=1, source_target_pairs={{0,64},{1,65},{2,66},{3,67},{4,68},{5,69},{6,70},{7,71},{8,72},{9,... | collective-permute-start | bytes 202760 | tf_op jit(solution)/shard_map/ppermute | solution.py:443
  8.3 6.2 %collective-permute-start.1 = (f32[4,4224]{1,0:T(4,128)S(1)}, f32[4,4224]{1,0:T(4,128)S(1)}, u32[]{:S(2)}, u32[]{:S(2)}) collective-permute-start(f32[4,4224]{1,0:T(4,128)S(1)} %get-tuple-element.26), channel_id=1, source_target_pairs={{0,127},{1,0},{2,1},{3,2},{4,3},{5,4},{6,5},{7,6},{8,7},{9,8},{10,... | collective-permute-start | bytes 202760 | tf_op jit(solution)/shard_map/ppermute | solution.py:443
  14.5 0.0 copy-done.6
  14.5 0.0 copy-done.8
  14.5 0.8 %fusion.6.refs_3_.pick_ref.refs_6_ = bf16[6,64,64]{2,1,0:T(8,128)(2,1)} fusion(s32[6,64]{1,0:T(8,128)S(1)} %pad_add_fusion), kind=kLoop, calls=%fused_computation.10 | loop fusion | flops 49152 | bytes 50688 | tf_op jit(solution)/shard_map/convert_element_type | solution.py:469
  15.3 0.0 copy-done.9
  15.3 0.7 %copy.36 = s32[2,64]{0,1:T(8,128)} copy(s32[2,64]{1,0:T(2,128)S(1)} %bitcast.36) | data formatting | bytes 1024 | tf_op jit(solution)/shard_map/squeeze | solution.py:470
  16.0 0.0 collective-permute-done
  16.0 0.2 fusion.22
  16.2 0.0 collective-permute-done.2
  16.2 0.2 fusion.20
  16.4 0.1 collective-permute-done.1
  16.4 0.2 fusion.21
  16.6 0.1 pad_add_fusion.1
  16.7 0.1 fusion.8
  16.8 0.2 fusion.10
  17.0 0.0 copy-done.7
  17.0 0.2 fusion.12
  17.1 0.1 pad_maximum_fusion.3
  17.2 0.1 copy.34
  17.3 0.2 convolution_add_fusion.refs_1_.weight_ref.refs_4_
  17.5 0.2 slice_reduce_fusion
  17.7 0.0 copy-done.2
  17.7 0.0 copy-done.13
  17.7 0.8 %convolution_select_fusion.refs_0_.refs_3_ = f32[64,4096]{1,0:T(8,128)S(1)} fusion(f32[4,4224]{1,0:T(4,128)S(1)} %collective-permute-done.2, f32[4,4224]{1,0:T(4,128)S(1)} %collective-permute-done.1, f32[4,4224]{1,0:T(4,128)S(1)} %collective-permute-done, f32[64,4096]{1,0:T(8,128)S(1)} %copy-done.2, f32[4096]{0:T(1024)S(1)} %copy-done.13, ...), kind=kOutput, calls=%fused_computation | convolution fusion | flops 240538368 | bytes 2316848 | tf_op jit(solution)/shard_map/dot_general | solution.py:452
  18.6 0.0 copy-done.3
  18.6 0.0 copy-start.1
  18.6 0.1 add_subtract_fusion
  18.7 0.1 add_add_fusion
  18.7 0.8 %copy-done.1 = f32[64,4096]{1,0:T(8,128)} copy-done((f32[64,4096]{1,0:T(8,128)}, f32[64,4096]{1,0:T(8,128)S(1)}, u32[]{:S(2)}) %copy-start.1) | copy-done | bytes 1048600
  19.6 0.0 collective-permute-start.3
  19.6 5.3 %collective-permute-start.4 = (f32[64,256]{1,0:T(8,128)S(1)}, f32[64,256]{1,0:T(8,128)S(1)}, u32[]{:S(2)}, u32[]{:S(2)}) collective-permute-start(f32[64,256]{1,0:T(8,128)S(1)} %add_subtract_fusion), channel_id=1, source_target_pairs={{8,0},{16,8},{24,16},{32,24},{40,32},{48,40},{56,48},{64,56},{72,6... | collective-permute-start | bytes 196616 | tf_op jit(solution)/shard_map/ppermute | solution.py:394
  24.9 5.5 %shard_map.136 = (f32[64,4096]{1,0:T(8,128)}, f32[64,256]{1,0:T(8,128)}, f32[64,256]{1,0:T(8,128)}) custom-call(f32[64,4096]{1,0:T(8,128)} %copy-done.1, f32[64,8]{1,0:T(8,128)} %copy-done.3, f32[1,4096]{1,0:T(1,128)} %constant.74.clone.refs_2_.top_ref.refs_5_, bf16[6,64,64]{2,1,0:T(8,128)(2,1)} %fusion.6.refs_3_.pick_ref.refs_6_, ...), custom_call_target="tpu_custom_call" | custom-call | flops 2500000000 | bytes 4000000 | tf_op jit(solution)/shard_map/pallas_call | solution.py:322
  30.4 0.0 collective-permute-done.3.lower_ref
  30.5 0.0 collective-permute-done.4.upper_ref
  30.5 0.0 copy-start.5
  30.5 0.6 %copy-done.4 = f32[64,256]{1,0:T(8,128)} copy-done((f32[64,256]{1,0:T(8,128)}, f32[64,256]{1,0:T(8,128)S(1)}, u32[]{:S(2)}) %copy-start.4) | copy-done | bytes 65560
  31.1 0.0 copy-done.5
  31.1 3.3 %shard_map.137 = (f32[64,256]{1,0:T(8,128)}, f32[64,256]{1,0:T(8,128)}, f32[64,256]{1,0:T(8,128)}, f32[64,256]{1,0:T(8,128)}) custom-call(f32[64,256]{1,0:T(8,128)} %copy-done.4, f32[64,256]{1,0:T(8,128)} %copy-done.5, bf16[6,64,64]{2,1,0:T(8,128)(2,1)} %fusion.6.refs_3_.pick_ref.refs_6_, s32[64,2]{1,0:T(8,128)} %bitcast.32, ...), custom_call_target="tpu_custom_call" | custom-call | tf_op jit(solution)/shard_map/pallas_call | solution.py:338
  34.4 0.1 collective-permute-start.5
  34.4 5.3 %collective-permute-start.6 = (f32[64,256]{1,0:T(8,128)}, f32[64,256]{1,0:T(8,128)S(1)}, u32[]{:S(2)}, u32[]{:S(2)}) collective-permute-start(f32[64,256]{1,0:T(8,128)} %get-tuple-element.18), channel_id=1, source_target_pairs={{8,0},{16,8},{24,16},{32,24},{40,32},{48,40},{56,48},{64,56},{72,6... | collective-permute-start | bytes 196616 | tf_op jit(solution)/shard_map/ppermute | solution.py:394
  39.8 2.4 %collective-permute-done.5.refs_10_ = f32[64,256]{1,0:T(8,128)S(1)} collective-permute-done((f32[64,256]{1,0:T(8,128)}, f32[64,256]{1,0:T(8,128)S(1)}, u32[]{:S(2)}, u32[]{:S(2)}) %collective-permute-start.5) | collective-permute-done | bytes 65568 | tf_op jit(solution)/shard_map/ppermute | solution.py:394
  42.2 0.0 collective-permute-done.6.refs_11_
  42.2 0.6 %copy-done.11 = f32[64,256]{1,0:T(8,128)} copy-done((f32[64,256]{1,0:T(8,128)}, f32[64,256]{1,0:T(8,128)S(1)}, u32[]{:S(2)}) %copy-start.11) | copy-done | bytes 65560
  42.9 0.0 copy-done.12
  42.9 6.2 %shard_map.138 = f32[64,4096]{1,0:T(8,128)} custom-call(f32[64,4096]{1,0:T(8,128)} %get-tuple-element.12.refs_0_, f32[64,256]{1,0:T(8,128)} %get-tuple-element.15.refs_1_, f32[64,256]{1,0:T(8,128)} %get-tuple-element.16.refs_2_, f32[64,4096]{1,0:T(8,128)} %copy-done.1, f32[64,8]{1,0:T(8,128)} %copy-done.3, f32[1,4096]{1,0:T(1,128)} %constant.74.clone.refs_2_.top_ref.refs_5_, ...), custom_call_target="tpu_custom_call" | custom-call | flops 2500000000 | bytes 4000000 | tf_op jit(solution)/shard_map/pallas_call | solution.py:322
  (13 shorter events, 0.1 us)
Async XLA Ops:
  0.0 1.7 %copy-start = (f32[64,3]{0,1:T(4,128)S(1)}, f32[64,3]{0,1:T(4,128)}, u32[]{:S(2)}) copy-start(f32[64,3]{0,1:T(4,128)} %param.16) | copy-start | bytes 2308
  0.0 4.5 %copy-start.10 = (s32[64]{0:T(128)S(1)}, s32[64]{0:T(128)}, u32[]{:S(2)}) copy-start(s32[64]{0:T(128)} %param.17) | copy-start | bytes 772
  2.7 11.8 %copy-start.6 = (s32[1,4,64]{2,1,0:T(4,128)S(1)}, s32[1,4,64]{2,1,0:T(4,128)}, u32[]{:S(2)}) copy-start(s32[1,4,64]{2,1,0:T(4,128)} %param.19) | copy-start | bytes 3076
  2.7 11.8 %copy-start.8 = (s32[1,2,64]{2,1,0:T(2,128)S(1)}, s32[1,2,64]{2,1,0:T(2,128)}, u32[]{:S(2)}) copy-start(s32[1,2,64]{2,1,0:T(2,128)} %param.20) | copy-start | bytes 1540
  2.7 12.6 %copy-start.9 = (s32[1,2,64]{2,1,0:T(2,128)S(1)}, s32[1,2,64]{2,1,0:T(2,128)}, u32[]{:S(2)}) copy-start(s32[1,2,64]{2,1,0:T(2,128)} %param.21) | copy-start | bytes 1540
  2.7 14.3 %copy-start.7 = (f32[64,3]{0,1:T(4,128)S(1)}, f32[64,3]{0,1:T(4,128)}, u32[]{:S(2)}) copy-start(f32[64,3]{0,1:T(4,128)} %param.15) | copy-start | bytes 2308
  2.7 15.0 %copy-start.2 = (f32[64,4096]{1,0:T(8,128)S(1)}, f32[64,4096]{1,0:T(8,128)}, u32[]{:S(2)}) copy-start(f32[64,4096]{1,0:T(8,128)} %param.14) | copy-start | bytes 3145732
  2.7 15.0 %copy-start.13 = (f32[4096]{0:T(1024)S(1)}, f32[4096]{0:T(1024)}, u32[]{:S(2)}) copy-start(f32[4096]{0:T(1024)} %constant.87) | copy-start | bytes 49156
  4.9 11.1 %collective-permute-start = (f32[4,4224]{1,0:T(4,128)S(1)}, f32[4,4224]{1,0:T(4,128)S(1)}, u32[]{:S(2)}, u32[]{:S(2)}) collective-permute-start(f32[4,4224]{1,0:T(4,128)S(1)} %get-tuple-element.24), channel_id=1, source_target_pairs={{0,1},{1,2},{2,3},{3,4},{4,5},{5,6},{6,7},{7,8},{8,9},{9,10},{10,1... | collective-permute-start | bytes 202760 | tf_op jit(solution)/shard_map/ppermute | solution.py:443
  4.9 11.2 %collective-permute-start.2 = (f32[4,4224]{1,0:T(4,128)S(1)}, f32[4,4224]{1,0:T(4,128)S(1)}, u32[]{:S(2)}, u32[]{:S(2)}) collective-permute-start(f32[4,4224]{1,0:T(4,128)S(1)} %get-tuple-element.25), channel_id=1, source_target_pairs={{0,64},{1,65},{2,66},{3,67},{4,68},{5,69},{6,70},{7,71},{8,72},{9,... | collective-permute-start | bytes 202760 | tf_op jit(solution)/shard_map/ppermute | solution.py:443
  8.3 8.1 %collective-permute-start.1 = (f32[4,4224]{1,0:T(4,128)S(1)}, f32[4,4224]{1,0:T(4,128)S(1)}, u32[]{:S(2)}, u32[]{:S(2)}) collective-permute-start(f32[4,4224]{1,0:T(4,128)S(1)} %get-tuple-element.26), channel_id=1, source_target_pairs={{0,127},{1,0},{2,1},{3,2},{4,3},{5,4},{6,5},{7,6},{8,7},{9,8},{10,... | collective-permute-start | bytes 202760 | tf_op jit(solution)/shard_map/ppermute | solution.py:443
  17.5 1.1 %copy-start.3 = (f32[64,8]{1,0:T(8,128)}, f32[64,8]{1,0:T(8,128)S(1)}, u32[]{:S(2)}) copy-start(f32[64,8]{1,0:T(8,128)S(1)} %convolution_add_fusion.refs_1_.weight_ref.refs_4_) | copy-start | bytes 6148
  18.6 1.0 %copy-start.1 = (f32[64,4096]{1,0:T(8,128)}, f32[64,4096]{1,0:T(8,128)S(1)}, u32[]{:S(2)}) copy-start(f32[64,4096]{1,0:T(8,128)S(1)} %convolution_select_fusion.refs_0_.refs_3_) | copy-start | bytes 3145732
  19.6 10.9 %collective-permute-start.3 = (f32[64,256]{1,0:T(8,128)S(1)}, f32[64,256]{1,0:T(8,128)S(1)}, u32[]{:S(2)}, u32[]{:S(2)}) collective-permute-start(f32[64,256]{1,0:T(8,128)S(1)} %add_add_fusion), channel_id=1, source_target_pairs={{0,8},{8,16},{16,24},{24,32},{32,40},{40,48},{48,56},{56,64},{64,7... | collective-permute-start | bytes 196616 | tf_op jit(solution)/shard_map/ppermute | solution.py:394
  19.6 10.9 %collective-permute-start.4 = (f32[64,256]{1,0:T(8,128)S(1)}, f32[64,256]{1,0:T(8,128)S(1)}, u32[]{:S(2)}, u32[]{:S(2)}) collective-permute-start(f32[64,256]{1,0:T(8,128)S(1)} %add_subtract_fusion), channel_id=1, source_target_pairs={{8,0},{16,8},{24,16},{32,24},{40,32},{48,40},{56,48},{64,56},{72,6... | collective-permute-start | bytes 196616 | tf_op jit(solution)/shard_map/ppermute | solution.py:394
  30.4 0.6 %copy-start.4 = (f32[64,256]{1,0:T(8,128)}, f32[64,256]{1,0:T(8,128)S(1)}, u32[]{:S(2)}) copy-start(f32[64,256]{1,0:T(8,128)S(1)} %collective-permute-done.3.lower_ref) | copy-start | bytes 196612
  30.5 0.6 %copy-start.5 = (f32[64,256]{1,0:T(8,128)}, f32[64,256]{1,0:T(8,128)S(1)}, u32[]{:S(2)}) copy-start(f32[64,256]{1,0:T(8,128)S(1)} %collective-permute-done.4.upper_ref) | copy-start | bytes 196612
  34.4 7.9 %collective-permute-start.5 = (f32[64,256]{1,0:T(8,128)}, f32[64,256]{1,0:T(8,128)S(1)}, u32[]{:S(2)}, u32[]{:S(2)}) collective-permute-start(f32[64,256]{1,0:T(8,128)} %get-tuple-element.17), channel_id=1, source_target_pairs={{0,8},{8,16},{16,24},{24,32},{32,40},{40,48},{48,56},{56,64},{64,7... | collective-permute-start | bytes 196616 | tf_op jit(solution)/shard_map/ppermute | solution.py:394
  34.4 7.8 %collective-permute-start.6 = (f32[64,256]{1,0:T(8,128)}, f32[64,256]{1,0:T(8,128)S(1)}, u32[]{:S(2)}, u32[]{:S(2)}) collective-permute-start(f32[64,256]{1,0:T(8,128)} %get-tuple-element.18), channel_id=1, source_target_pairs={{8,0},{16,8},{24,16},{32,24},{40,32},{48,40},{56,48},{64,56},{72,6... | collective-permute-start | bytes 196616 | tf_op jit(solution)/shard_map/ppermute | solution.py:394
  42.2 0.6 %copy-start.11 = (f32[64,256]{1,0:T(8,128)}, f32[64,256]{1,0:T(8,128)S(1)}, u32[]{:S(2)}) copy-start(f32[64,256]{1,0:T(8,128)S(1)} %collective-permute-done.5.refs_10_) | copy-start | bytes 196612
  42.2 0.6 %copy-start.12 = (f32[64,256]{1,0:T(8,128)}, f32[64,256]{1,0:T(8,128)S(1)}, u32[]{:S(2)}) copy-start(f32[64,256]{1,0:T(8,128)S(1)} %collective-permute-done.6.refs_11_) | copy-start | bytes 196612

commit v20 on v15

--- a/solution.py
+++ b/solution.py
@@ -332,6 +332,7 @@
         out_shape=(square,) * 4,
         in_specs=[spec] * 9,
         out_specs=(spec,) * 4,
+        input_output_aliases={7: 2, 8: 3},
     )(lower, upper, picks, codes, flip, top, weight, even, total)
 
 

time: 48.5 us -> 48.5 us (level)
  no operation moved by 1% of the time
where the time goes in v20:
time: 48.5 us; the launch traced here: 48.2 us
  starting transfers between devices  20.3 us (42%)
  Pallas kernels  14.2 us (29%)
  matrix products  4.38 us (9%)
  other arithmetic  3.29 us (7%)
  local copies, waits for them, and re-layouts  3.27 us (7%)
  waiting for transfers between devices  2.53 us (5%)
    pallas_call x2, Pallas kernels, inner(): pl.pallas_call(functools.partial(inner_body, scale=scale, carried=carried...  11.8 us
    ppermute x4, starting transfers between devices, exchange(): return (lax.ppermute(total, 'dom', up), lax.ppermute(even, 'dom', down))  10.7 us
    ppermute x3, starting transfers between devices, shards(): arrived = lax.ppermute(parcels[index], ('dom', 'face'), pairs)  9.63 us
    ppermute x4, waiting for transfers between devices, exchange(): return (lax.ppermute(total, 'dom', up), lax.ppermute(even, 'dom', down))  2.46 us
    pallas_call x1, Pallas kernels, faces(): pl.pallas_call(functools.partial(faces_body, scale=scale), out_shape=(squ...  2.43 us
    unnamed x28, local copies, waits for them, and re-layouts  2.14 us
    dot_general x1, matrix products, shards(): jnp.einsum('qjr,rc->qjc', hit_values, coefficients, precision=exact)  1.78 us
  transfers between devices with their start and end apart: 7, of which 2 were waited for; matrix products, arithmetic and copies ran while one was open for 4% of the time, Pallas kernels for 12%

profile of v20, /device:TPU:0, one launch (start us, length us, event | category | flops | bytes accessed | tf_op | source)
XLA Modules:
  0.0 48.2 jit_solution(12774111287652896080)
XLA Ops:
  0.0 0.0 copy-start
  0.0 0.7 %and_select_fusion = s32[3]{0:T(128)S(1)} fusion(s32[3]{0:T(128)} %constant.73.clone, s32[]{:T(128)S(6)} %add.96), kind=kLoop, calls=%fused_computation.46 | loop fusion | flops 36 | bytes 28 | tf_op jit(solution)/shard_map/jit(remainder)/select_n | solution.py:409
  0.7 0.7 %compare_select_fusion.2 = (s32[64]{0:T(128)S(1)}, s32[64]{0:T(128)S(1)}, s32[64]{0:T(128)S(1)}) fusion(s32[]{:T(128)S(6)} %add.96, s32[64]{0:T(128)} %param.18), kind=kLoop, calls=%fused_computation.48 | loop fusion | flops 1344 | bytes 1028 | tf_op jit(solution)/shard_map/jit(_where)/select_n | solution.py:432
  1.4 0.1 fusion.34
  1.4 0.2 reduce_window_sum.11
  1.7 0.0 copy-done
  1.7 0.1 fusion.23
  1.8 0.8 %fusion.25 = f32[3,4,3]{2,1,0:T(4,128)S(1)} fusion(pred[3,4,64]{2,1,0:T(4,128)(4,1)S(1)} %fusion.19, f32[64,3]{0,1:T(4,128)} %param.15), kind=kOutput, calls=%fused_computation.44 | convolution fusion | flops 27648 | bytes 1680 | tf_op jit(solution)/shard_map/qjr,rc->qjc/dot_general | solution.py:424
  2.7 0.0 copy-start.8
  2.7 0.0 copy-start.9
  2.7 0.0 copy-start.7
  2.7 0.0 copy-start.2
  2.7 0.0 copy-start.13
  2.7 1.8 %fusion.4 = f32[3,4,4096]{2,1,0:T(4,128)S(1)} fusion(pred[3,4,64]{2,1,0:T(4,128)(4,1)S(1)} %fusion.19, f32[64,4096]{1,0:T(8,128)} %param.14), kind=kOutput, calls=%fused_computation.7 | convolution fusion | flops 37748736 | bytes 1245952 | tf_op jit(solution)/shard_map/qjr,rc->qjc/dot_general | solution.py:423
  4.5 0.0 copy-done.10
  4.5 0.1 fusion.27
  4.7 0.1 concatenate.22
  4.9 0.1 collective-permute-start
  4.9 3.4 %collective-permute-start.2 = (f32[4,4224]{1,0:T(4,128)S(1)}, f32[4,4224]{1,0:T(4,128)S(1)}, u32[]{:S(2)}, u32[]{:S(2)}) collective-permute-start(f32[4,4224]{1,0:T(4,128)S(1)} %get-tuple-element.25), channel_id=1, source_target_pairs={{0,64},{1,65},{2,66},{3,67},{4,68},{5,69},{6,70},{7,71},{8,72},{9,... | collective-permute-start | bytes 202760 | tf_op jit(solution)/shard_map/ppermute | solution.py:435
  8.3 6.2 %collective-permute-start.1 = (f32[4,4224]{1,0:T(4,128)S(1)}, f32[4,4224]{1,0:T(4,128)S(1)}, u32[]{:S(2)}, u32[]{:S(2)}) collective-permute-start(f32[4,4224]{1,0:T(4,128)S(1)} %get-tuple-element.26), channel_id=1, source_target_pairs={{0,127},{1,0},{2,1},{3,2},{4,3},{5,4},{6,5},{7,6},{8,7},{9,8},{10,... | collective-permute-start | bytes 202760 | tf_op jit(solution)/shard_map/ppermute | solution.py:435
  14.5 0.0 copy-done.6
  14.5 0.0 copy-done.8
  14.5 0.8 %fusion.6.refs_3_.pick_ref.refs_6_ = bf16[6,64,64]{2,1,0:T(8,128)(2,1)} fusion(s32[6,64]{1,0:T(8,128)S(1)} %pad_add_fusion), kind=kLoop, calls=%fused_computation.10 | loop fusion | flops 49152 | bytes 50688 | tf_op jit(solution)/shard_map/convert_element_type | solution.py:461
  15.3 0.0 copy-done.9
  15.3 0.7 %copy.38 = s32[2,64]{0,1:T(8,128)} copy(s32[2,64]{1,0:T(2,128)S(1)} %bitcast.36) | data formatting | bytes 1024 | tf_op jit(solution)/shard_map/squeeze | solution.py:462
  16.0 0.0 collective-permute-done
  16.0 0.2 fusion.22
  16.2 0.0 collective-permute-done.2
  16.2 0.2 fusion.20
  16.4 0.1 collective-permute-done.1
  16.4 0.2 fusion.21
  16.6 0.1 pad_add_fusion.1
  16.7 0.1 fusion.8
  16.8 0.2 fusion.10
  17.0 0.0 copy-done.7
  17.0 0.2 fusion.12
  17.1 0.1 pad_maximum_fusion.3
  17.2 0.1 copy.36
  17.3 0.2 convolution_add_fusion.refs_1_.weight_ref.refs_4_
  17.5 0.0 copy-start.3
  17.5 0.2 slice_reduce_fusion
  17.7 0.0 copy-done.2
  17.7 0.0 copy-done.13
  17.7 0.8 %convolution_select_fusion.refs_0_.refs_3_ = f32[64,4096]{1,0:T(8,128)S(1)} fusion(f32[4,4224]{1,0:T(4,128)S(1)} %collective-permute-done.2, f32[4,4224]{1,0:T(4,128)S(1)} %collective-permute-done.1, f32[4,4224]{1,0:T(4,128)S(1)} %collective-permute-done, f32[64,4096]{1,0:T(8,128)S(1)} %copy-done.2, f32[4096]{0:T(1024)S(1)} %copy-done.13, ...), kind=kOutput, calls=%fused_computation | convolution fusion | flops 240538368 | bytes 2316848 | tf_op jit(solution)/shard_map/dot_general | solution.py:444
  18.6 0.0 copy-done.3
  18.6 0.0 copy-start.1
  18.6 0.1 add_subtract_fusion
  18.7 0.1 add_add_fusion
  18.7 0.8 %copy-done.1 = f32[64,4096]{1,0:T(8,128)} copy-done((f32[64,4096]{1,0:T(8,128)}, f32[64,4096]{1,0:T(8,128)S(1)}, u32[]{:S(2)}) %copy-start.1) | copy-done | bytes 1048600
  19.6 0.0 collective-permute-start.3
  19.6 5.3 %collective-permute-start.4 = (f32[64,256]{1,0:T(8,128)S(1)}, f32[64,256]{1,0:T(8,128)S(1)}, u32[]{:S(2)}, u32[]{:S(2)}) collective-permute-start(f32[64,256]{1,0:T(8,128)S(1)} %add_subtract_fusion), channel_id=1, source_target_pairs={{8,0},{16,8},{24,16},{32,24},{40,32},{48,40},{56,48},{64,56},{72,6... | collective-permute-start | bytes 196616 | tf_op jit(solution)/shard_map/ppermute | solution.py:386
  24.9 5.5 %shard_map.136 = (f32[64,4096]{1,0:T(8,128)}, f32[64,256]{1,0:T(8,128)}, f32[64,256]{1,0:T(8,128)}) custom-call(f32[64,4096]{1,0:T(8,128)} %copy-done.1, f32[64,8]{1,0:T(8,128)} %copy-done.3, f32[1,4096]{1,0:T(1,128)} %constant.74.clone.refs_2_.top_ref.refs_5_, bf16[6,64,64]{2,1,0:T(8,128)(2,1)} %fusion.6.refs_3_.pick_ref.refs_6_, ...), custom_call_target="tpu_custom_call" | custom-call | flops 2500000000 | bytes 4000000 | tf_op jit(solution)/shard_map/pallas_call | solution.py:314
  30.4 0.0 collective-permute-done.3.lower_ref
  30.5 0.0 collective-permute-done.4.upper_ref
  30.5 0.6 %copy-done.4 = f32[64,256]{1,0:T(8,128)} copy-done((f32[64,256]{1,0:T(8,128)}, f32[64,256]{1,0:T(8,128)S(1)}, u32[]{:S(2)}) %copy-start.4) | copy-done | bytes 65560
  31.1 0.0 copy-done.5
  31.1 2.4 %shard_map.137 = (f32[64,256]{1,0:T(8,128)}, f32[64,256]{1,0:T(8,128)}, f32[64,256]{1,0:T(8,128)}, f32[64,256]{1,0:T(8,128)}) custom-call(f32[64,256]{1,0:T(8,128)} %copy-done.4, f32[64,256]{1,0:T(8,128)} %copy-done.5, bf16[6,64,64]{2,1,0:T(8,128)(2,1)} %fusion.6.refs_3_.pick_ref.refs_6_, ...), custom_call_target="tpu_custom_call", output_to_operand_aliasing={{2}: (7, {}), {3}: (8, {})} | custom-call | tf_op jit(solution)/shard_map/pallas_call | solution.py:330
  33.5 0.0 collective-permute-start.5
  33.5 5.3 %collective-permute-start.6 = (f32[64,256]{1,0:T(8,128)}, f32[64,256]{1,0:T(8,128)S(1)}, u32[]{:S(2)}, u32[]{:S(2)}) collective-permute-start(f32[64,256]{1,0:T(8,128)} %get-tuple-element.18), channel_id=1, source_target_pairs={{8,0},{16,8},{24,16},{32,24},{40,32},{48,40},{56,48},{64,56},{72,6... | collective-permute-start | bytes 196616 | tf_op jit(solution)/shard_map/ppermute | solution.py:386
  38.9 2.4 %collective-permute-done.5.refs_10_ = f32[64,256]{1,0:T(8,128)S(1)} collective-permute-done((f32[64,256]{1,0:T(8,128)}, f32[64,256]{1,0:T(8,128)S(1)}, u32[]{:S(2)}, u32[]{:S(2)}) %collective-permute-start.5) | collective-permute-done | bytes 65568 | tf_op jit(solution)/shard_map/ppermute | solution.py:386
  41.3 0.0 collective-permute-done.6.refs_11_
  41.3 0.6 %copy-done.11 = f32[64,256]{1,0:T(8,128)} copy-done((f32[64,256]{1,0:T(8,128)}, f32[64,256]{1,0:T(8,128)S(1)}, u32[]{:S(2)}) %copy-start.11) | copy-done | bytes 65560
  42.0 0.0 copy-done.12
  42.0 6.2 %shard_map.138 = f32[64,4096]{1,0:T(8,128)} custom-call(f32[64,4096]{1,0:T(8,128)} %get-tuple-element.12.refs_0_, f32[64,256]{1,0:T(8,128)} %get-tuple-element.15.refs_1_, f32[64,256]{1,0:T(8,128)} %get-tuple-element.16.refs_2_, f32[64,4096]{1,0:T(8,128)} %copy-done.1, f32[64,8]{1,0:T(8,128)} %copy-done.3, f32[1,4096]{1,0:T(1,128)} %constant.74.clone.refs_2_.top_ref.refs_5_, ...), custom_call_target="tpu_custom_call" | custom-call | flops 2500000000 | bytes 4000000 | tf_op jit(solution)/shard_map/pallas_call | solution.py:314
  (13 shorter events, 0.1 us)
Async XLA Ops:
  0.0 1.7 %copy-start = (f32[64,3]{0,1:T(4,128)S(1)}, f32[64,3]{0,1:T(4,128)}, u32[]{:S(2)}) copy-start(f32[64,3]{0,1:T(4,128)} %param.16) | copy-start | bytes 2308
  0.0 4.5 %copy-start.10 = (s32[64]{0:T(128)S(1)}, s32[64]{0:T(128)}, u32[]{:S(2)}) copy-start(s32[64]{0:T(128)} %param.17) | copy-start | bytes 772
  2.7 11.8 %copy-start.6 = (s32[1,4,64]{2,1,0:T(4,128)S(1)}, s32[1,4,64]{2,1,0:T(4,128)}, u32[]{:S(2)}) copy-start(s32[1,4,64]{2,1,0:T(4,128)} %param.19) | copy-start | bytes 3076
  2.7 11.8 %copy-start.8 = (s32[1,2,64]{2,1,0:T(2,128)S(1)}, s32[1,2,64]{2,1,0:T(2,128)}, u32[]{:S(2)}) copy-start(s32[1,2,64]{2,1,0:T(2,128)} %param.20) | copy-start | bytes 1540
  2.7 12.6 %copy-start.9 = (s32[1,2,64]{2,1,0:T(2,128)S(1)}, s32[1,2,64]{2,1,0:T(2,128)}, u32[]{:S(2)}) copy-start(s32[1,2,64]{2,1,0:T(2,128)} %param.21) | copy-start | bytes 1540
  2.7 14.3 %copy-start.7 = (f32[64,3]{0,1:T(4,128)S(1)}, f32[64,3]{0,1:T(4,128)}, u32[]{:S(2)}) copy-start(f32[64,3]{0,1:T(4,128)} %param.15) | copy-start | bytes 2308
  2.7 15.0 %copy-start.2 = (f32[64,4096]{1,0:T(8,128)S(1)}, f32[64,4096]{1,0:T(8,128)}, u32[]{:S(2)}) copy-start(f32[64,4096]{1,0:T(8,128)} %param.14) | copy-start | bytes 3145732
  2.7 15.0 %copy-start.13 = (f32[4096]{0:T(1024)S(1)}, f32[4096]{0:T(1024)}, u32[]{:S(2)}) copy-start(f32[4096]{0:T(1024)} %constant.87) | copy-start | bytes 49156
  4.9 11.1 %collective-permute-start = (f32[4,4224]{1,0:T(4,128)S(1)}, f32[4,4224]{1,0:T(4,128)S(1)}, u32[]{:S(2)}, u32[]{:S(2)}) collective-permute-start(f32[4,4224]{1,0:T(4,128)S(1)} %get-tuple-element.24), channel_id=1, source_target_pairs={{0,1},{1,2},{2,3},{3,4},{4,5},{5,6},{6,7},{7,8},{8,9},{9,10},{10,1... | collective-permute-start | bytes 202760 | tf_op jit(solution)/shard_map/ppermute | solution.py:435
  4.9 11.2 %collective-permute-start.2 = (f32[4,4224]{1,0:T(4,128)S(1)}, f32[4,4224]{1,0:T(4,128)S(1)}, u32[]{:S(2)}, u32[]{:S(2)}) collective-permute-start(f32[4,4224]{1,0:T(4,128)S(1)} %get-tuple-element.25), channel_id=1, source_target_pairs={{0,64},{1,65},{2,66},{3,67},{4,68},{5,69},{6,70},{7,71},{8,72},{9,... | collective-permute-start | bytes 202760 | tf_op jit(solution)/shard_map/ppermute | solution.py:435
  8.3 8.1 %collective-permute-start.1 = (f32[4,4224]{1,0:T(4,128)S(1)}, f32[4,4224]{1,0:T(4,128)S(1)}, u32[]{:S(2)}, u32[]{:S(2)}) collective-permute-start(f32[4,4224]{1,0:T(4,128)S(1)} %get-tuple-element.26), channel_id=1, source_target_pairs={{0,127},{1,0},{2,1},{3,2},{4,3},{5,4},{6,5},{7,6},{8,7},{9,8},{10,... | collective-permute-start | bytes 202760 | tf_op jit(solution)/shard_map/ppermute | solution.py:435
  17.5 1.1 %copy-start.3 = (f32[64,8]{1,0:T(8,128)}, f32[64,8]{1,0:T(8,128)S(1)}, u32[]{:S(2)}) copy-start(f32[64,8]{1,0:T(8,128)S(1)} %convolution_add_fusion.refs_1_.weight_ref.refs_4_) | copy-start | bytes 6148
  18.6 1.0 %copy-start.1 = (f32[64,4096]{1,0:T(8,128)}, f32[64,4096]{1,0:T(8,128)S(1)}, u32[]{:S(2)}) copy-start(f32[64,4096]{1,0:T(8,128)S(1)} %convolution_select_fusion.refs_0_.refs_3_) | copy-start | bytes 3145732
  19.6 10.9 %collective-permute-start.3 = (f32[64,256]{1,0:T(8,128)S(1)}, f32[64,256]{1,0:T(8,128)S(1)}, u32[]{:S(2)}, u32[]{:S(2)}) collective-permute-start(f32[64,256]{1,0:T(8,128)S(1)} %add_add_fusion), channel_id=1, source_target_pairs={{0,8},{8,16},{16,24},{24,32},{32,40},{40,48},{48,56},{56,64},{64,7... | collective-permute-start | bytes 196616 | tf_op jit(solution)/shard_map/ppermute | solution.py:386
  19.6 10.9 %collective-permute-start.4 = (f32[64,256]{1,0:T(8,128)S(1)}, f32[64,256]{1,0:T(8,128)S(1)}, u32[]{:S(2)}, u32[]{:S(2)}) collective-permute-start(f32[64,256]{1,0:T(8,128)S(1)} %add_subtract_fusion), channel_id=1, source_target_pairs={{8,0},{16,8},{24,16},{32,24},{40,32},{48,40},{56,48},{64,56},{72,6... | collective-permute-start | bytes 196616 | tf_op jit(solution)/shard_map/ppermute | solution.py:386
  30.4 0.6 %copy-start.4 = (f32[64,256]{1,0:T(8,128)}, f32[64,256]{1,0:T(8,128)S(1)}, u32[]{:S(2)}) copy-start(f32[64,256]{1,0:T(8,128)S(1)} %collective-permute-done.3.lower_ref) | copy-start | bytes 196612
  30.5 0.6 %copy-start.5 = (f32[64,256]{1,0:T(8,128)}, f32[64,256]{1,0:T(8,128)S(1)}, u32[]{:S(2)}) copy-start(f32[64,256]{1,0:T(8,128)S(1)} %collective-permute-done.4.upper_ref) | copy-start | bytes 196612
  33.5 7.8 %collective-permute-start.5 = (f32[64,256]{1,0:T(8,128)}, f32[64,256]{1,0:T(8,128)S(1)}, u32[]{:S(2)}, u32[]{:S(2)}) collective-permute-start(f32[64,256]{1,0:T(8,128)} %get-tuple-element.17), channel_id=1, source_target_pairs={{0,8},{8,16},{16,24},{24,32},{32,40},{40,48},{48,56},{56,64},{64,7... | collective-permute-start | bytes 196616 | tf_op jit(solution)/shard_map/ppermute | solution.py:386
  33.5 7.8 %collective-permute-start.6 = (f32[64,256]{1,0:T(8,128)}, f32[64,256]{1,0:T(8,128)S(1)}, u32[]{:S(2)}, u32[]{:S(2)}) collective-permute-start(f32[64,256]{1,0:T(8,128)} %get-tuple-element.18), channel_id=1, source_target_pairs={{8,0},{16,8},{24,16},{32,24},{40,32},{48,40},{56,48},{64,56},{72,6... | collective-permute-start | bytes 196616 | tf_op jit(solution)/shard_map/ppermute | solution.py:386
  41.3 0.6 %copy-start.11 = (f32[64,256]{1,0:T(8,128)}, f32[64,256]{1,0:T(8,128)S(1)}, u32[]{:S(2)}) copy-start(f32[64,256]{1,0:T(8,128)S(1)} %collective-permute-done.5.refs_10_) | copy-start | bytes 196612
  41.3 0.6 %copy-start.12 = (f32[64,256]{1,0:T(8,128)}, f32[64,256]{1,0:T(8,128)S(1)}, u32[]{:S(2)}) copy-start(f32[64,256]{1,0:T(8,128)S(1)} %collective-permute-done.6.refs_11_) | copy-start | bytes 196612
